TPU v7x, 128 devices: a whole 4x4x4 slice. The times are simulated.
128 devices in a mesh: batch: 16 (over z, y_hi, core), tm: 8 (over y_lo, x).
Axes of the slice: x: 4, y: 4 (y_hi: 2, y_lo: 2; y = y_hi * 2 + y_lo), z: 4, core: 2. Of those that a mesh axis runs over, the one named last changes fastest.
Arguments:
- x_in: bfloat16 [16, 16, 256, 1280], P('batch', 'tm'), may hold values from -6 to 6
- norm_gain: float32 [1280], replicated, may hold values from 0.5 to 1.5
- w_query: bfloat16 [1280, 640], replicated, may hold values from -1 to 1
- w_key: bfloat16 [1280, 640], replicated, may hold values from -16 to 16
- w_value: bfloat16 [1280, 640], replicated, may hold values from -0.15625 to 0.15625
- w_out: bfloat16 [640, 1280], replicated, may hold values from -0.25 to 0.25
- w_time: bfloat16 [1280, 3, 1280], replicated, may hold values from -0.09375 to 0.09375
- cotangent: bfloat16 [16, 16, 256, 1280], P('batch', 'tm'), may hold values from -6 to 6
Outputs:
- output: bfloat16 [16, 16, 256, 1280], P('batch', 'tm')
- grad_input: bfloat16 [16, 16, 256, 1280], P('batch', 'tm')
- grad_query: float32 [1280, 640], P(('batch', 'tm'))
- grad_key: float32 [1280, 640], P(('batch', 'tm'))
- grad_value: float32 [1280, 640], P(('batch', 'tm'))
- grad_out: float32 [640, 1280], P(('batch', 'tm'))
- grad_gain: float32 [1280], P(('batch', 'tm'))
All inputs are finite; a program needn't handle non-finite values.
Results may differ from a plain program's by a relative error of at most 0.014.
The roundings to bfloat16 on the way count: a program that leaves them out, or rounds other values in their place, can miss the bound.
Values may be sent and summed in bfloat16 or wider, within the bound.
No kernel may reach another device: no remote copies, remote signals or barrier semaphores. Data moves between devices by JAX's collectives and lax.ppermute only.
A program may use at most 192 MiB of HBM per device.

v0:
```python
import jax
import jax.numpy as jnp
from jax import lax
from jax.sharding import PartitionSpec as P

HEADS = 10
HD = 64


eps_norm = 1e-05
highest = lax.Precision.HIGHEST


def broadcast(block, axis, holder):
    block = jnp.where(lax.axis_index(axis) == holder, block, jnp.zeros_like(block))
    return lax.psum(block, axis)


def padded_2(value, sides, width):
    for axis, dim in sides:
        size, length = (lax.axis_size(axis), value.shape[dim])
        up = [(i, (i + 1) % size) for i in range(size - 1)]
        down = [(j, i) for i, j in up]
        last = lax.slice_in_dim(value, length - width, length, axis=dim)
        leading = lax.slice_in_dim(value, 0, width, axis=dim)
        before = lax.ppermute(last, axis, up)
        after = lax.ppermute(leading, axis, down)
        value = jnp.concatenate([before, value, after], axis=dim)
    return value


def layer_norm(inputs, norm_gain):
    wide = inputs.astype(jnp.float32)
    centre = jnp.mean(wide, axis=-1, keepdims=True)
    spread = jnp.mean((wide - centre) ** 2, axis=-1, keepdims=True)
    inv_std = lax.rsqrt(spread + eps_norm)
    x_hat = (wide - centre) * inv_std
    return ((x_hat * norm_gain).astype(jnp.bfloat16), x_hat, inv_std)


def project(inputs, matrix):
    return jnp.dot(inputs, matrix, preferred_element_type=jnp.float32).astype(jnp.bfloat16)


def split_heads(tensor):
    return tensor.reshape(tensor.shape[:-1] + (HEADS, HD))


def attend(queries, key_rows, val_rows, key_first, val_first):
    key_all = jnp.concatenate(
        [key_rows, jnp.broadcast_to(key_first[:, None], key_rows.shape)], axis=2
    )
    val_all = jnp.concatenate(
        [val_rows, jnp.broadcast_to(val_first[:, None], val_rows.shape)], axis=2
    )
    scores = jnp.einsum(
        "lfshd,lfthd->lfhst",
        split_heads(queries),
        split_heads(key_all),
        preferred_element_type=jnp.float32,
    ) * HD ** (-0.5)
    top_score = jnp.max(scores, axis=-1, keepdims=True)
    expd = jnp.exp(scores - top_score)
    prob_f32 = expd / jnp.sum(expd, axis=-1, keepdims=True)
    prob_b = prob_f32.astype(jnp.bfloat16)
    mixed = jnp.einsum(
        "lfhst,lfthd->lfshd", prob_b, split_heads(val_all), preferred_element_type=jnp.float32
    )
    attended = mixed.reshape(queries.shape).astype(jnp.bfloat16)
    return (attended, prob_f32, prob_b, key_all, val_all)


def attend_back(grad_att, queries, key_all, val_all, prob_f32, prob_b):
    grad_heads = split_heads(grad_att)
    grad_prob = jnp.einsum(
        "lfshd,lfthd->lfhst", grad_heads, split_heads(val_all), preferred_element_type=jnp.float32
    )
    centre = jnp.sum(grad_prob * prob_f32, axis=-1, keepdims=True)
    grad_score = (prob_f32 * (grad_prob - centre) * HD ** (-0.5)).astype(jnp.bfloat16)
    grad_queries = jnp.einsum(
        "lfhst,lfthd->lfshd", grad_score, split_heads(key_all), preferred_element_type=jnp.float32
    )
    grad_queries = grad_queries.reshape(queries.shape).astype(jnp.bfloat16)
    grad_keys = jnp.einsum(
        "lfhst,lfshd->lfthd", grad_score, split_heads(queries), preferred_element_type=jnp.float32
    ).reshape(key_all.shape)
    grad_vals = jnp.einsum(
        "lfhst,lfshd->lfthd", prob_b, grad_heads, preferred_element_type=jnp.float32
    ).reshape(val_all.shape)
    frame_len = queries.shape[2]
    return (
        grad_queries,
        grad_keys[:, :, :frame_len],
        grad_vals[:, :, :frame_len],
        jnp.sum(grad_keys[:, :, frame_len:], axis=1),
        jnp.sum(grad_vals[:, :, frame_len:], axis=1),
    )


def gram_rows(left, right, precision=None):
    flat_left = left.reshape(-1, left.shape[-1])
    flat_right = right.reshape(-1, right.shape[-1])
    return lax.dot_general(
        flat_left,
        flat_right,
        (((0,), (0,)), ((), ())),
        preferred_element_type=jnp.float32,
        precision=precision,
    )


def silu_slope(hidden_wide):
    sigma = jax.nn.sigmoid(hidden_wide)
    return sigma * (1.0 + hidden_wide * (1.0 - sigma))


def time_stack(padded, frames):
    return jnp.stack(
        [padded[:, 0:frames], padded[:, 1 : frames + 1], padded[:, 2 : frames + 2]], axis=3
    )


def first_terms(normed_first, key_grad, val_grad, key_wide, val_wide):
    rows = jnp.einsum("lsh,ch->lsc", key_grad, key_wide, precision=highest)
    rows = rows + jnp.einsum("lsh,ch->lsc", val_grad, val_wide, precision=highest)
    extra_key = gram_rows(normed_first.astype(jnp.float32), key_grad, highest)
    extra_val = gram_rows(normed_first.astype(jnp.float32), val_grad, highest)
    return (rows, extra_key, extra_val)


def on_device(x_in, norm_gain, w_query, w_key, w_value, w_out, w_time, cotangent):
    frames = x_in.shape[1]
    is_owner = lax.axis_index("tm") == 0
    normed, x_hat, inv_std = layer_norm(x_in, norm_gain)
    queries = project(normed, w_query)
    key_rows = project(normed, w_key)
    val_rows = project(normed, w_value)
    shared = broadcast(jnp.stack([key_rows[:, 0], val_rows[:, 0]]), "tm", 0)
    key_first = shared[0]
    val_first = shared[1]
    normed_first = normed[:, 0]
    attended, prob_f32, prob_b, key_all, val_all = attend(
        queries, key_rows, val_rows, key_first, val_first
    )
    hidden = (
        x_in.astype(jnp.float32) + jnp.dot(attended, w_out, preferred_element_type=jnp.float32)
    ).astype(jnp.bfloat16)
    active = jax.nn.silu(hidden.astype(jnp.float32)).astype(jnp.bfloat16)
    padded = padded_2(jnp.stack([active, cotangent]), (("tm", 2),), 1)
    act_stack = time_stack(padded[0], frames)
    conv = jnp.einsum("lfsjc,cjo->lfso", act_stack, w_time, preferred_element_type=jnp.float32)
    output = (hidden.astype(jnp.float32) + conv).astype(jnp.bfloat16)
    grad_pad = padded[1]
    grad_stack = jnp.stack(
        [grad_pad[:, 2 : frames + 2], grad_pad[:, 1 : frames + 1], grad_pad[:, 0:frames]], axis=3
    )
    grad_act = jnp.einsum("lfsjo,cjo->lfsc", grad_stack, w_time, preferred_element_type=jnp.float32)
    grad_hidden = (
        cotangent.astype(jnp.float32) + grad_act * silu_slope(hidden.astype(jnp.float32))
    ).astype(jnp.bfloat16)
    grad_out = gram_rows(attended, grad_hidden)
    grad_att = jnp.einsum(
        "lfso,ho->lfsh", grad_hidden, w_out, preferred_element_type=jnp.float32
    ).astype(jnp.bfloat16)
    grad_queries, key_own, val_own, key_first_grad, val_first_grad = attend_back(
        grad_att, queries, key_all, val_all, prob_f32, prob_b
    )
    key_b = key_own.astype(jnp.bfloat16)
    val_b = val_own.astype(jnp.bfloat16)
    grad_normed = jnp.einsum(
        "lfsh,ch->lfsc", grad_queries, w_query, preferred_element_type=jnp.float32
    )
    grad_normed = grad_normed + jnp.einsum(
        "lfsh,ch->lfsc", key_b, w_key, preferred_element_type=jnp.float32
    )
    grad_normed = grad_normed + jnp.einsum(
        "lfsh,ch->lfsc", val_b, w_value, preferred_element_type=jnp.float32
    )
    key_wide = w_key.astype(jnp.float32)
    val_wide = w_value.astype(jnp.float32)
    summed = (
        lax.psum(key_first_grad.astype(jnp.bfloat16), "tm").astype(jnp.float32),
        lax.psum(val_first_grad.astype(jnp.bfloat16), "tm").astype(jnp.float32),
    )

    def owner_terms(operands):
        return first_terms(normed_first, operands[0], operands[1], key_wide, val_wide)

    def no_terms(operands):
        return (
            jnp.zeros(normed_first.shape, jnp.float32),
            jnp.zeros(key_wide.shape, jnp.float32),
            jnp.zeros(val_wide.shape, jnp.float32),
        )

    first_rows, extra_key, extra_val = lax.cond(is_owner, owner_terms, no_terms, summed)
    grad_normed = grad_normed.at[:, 0].add(first_rows)
    grad_wq = gram_rows(normed, grad_queries)
    grad_wk = gram_rows(normed, key_b) + extra_key
    grad_wv = gram_rows(normed, val_b) + extra_val
    grad_gain = jnp.sum(grad_normed * x_hat, axis=(0, 1, 2))
    grad_hat = grad_normed * norm_gain
    grad_x = inv_std * (
        grad_hat
        - jnp.mean(grad_hat, axis=-1, keepdims=True)
        - x_hat * jnp.mean(grad_hat * x_hat, axis=-1, keepdims=True)
    )
    grad_input = (grad_hidden.astype(jnp.float32) + grad_x).astype(jnp.bfloat16)
    grad_wq, grad_wk, grad_wv, grad_out, grad_gain = (
        lax.psum_scatter(grad_wq, ("batch", "tm"), scatter_dimension=0, tiled=True),
        lax.psum_scatter(grad_wk, ("batch", "tm"), scatter_dimension=0, tiled=True),
        lax.psum_scatter(grad_wv, ("batch", "tm"), scatter_dimension=0, tiled=True),
        lax.psum_scatter(grad_out, ("batch", "tm"), scatter_dimension=0, tiled=True),
        lax.psum_scatter(grad_gain, ("batch", "tm"), scatter_dimension=0, tiled=True),
    )
    return (output, grad_input, grad_wq, grad_wk, grad_wv, grad_out, grad_gain)


def solution(mesh):
    in_specs = (
        P("batch", "tm", None, None),
        P(),
        P(),
        P(),
        P(),
        P(),
        P(),
        P("batch", "tm", None, None),
    )
    out_specs = (
        P("batch", "tm", None, None),
        P("batch", "tm", None, None),
        P(("batch", "tm"), None),
        P(("batch", "tm"), None),
        P(("batch", "tm"), None),
        P(("batch", "tm"), None),
        P(("batch", "tm")),
    )
    return jax.shard_map(
        on_device, mesh=mesh, in_specs=in_specs, out_specs=out_specs, check_vma=False
    )
```

profile of v0, /device:TPU:0, one launch (start us, length us, event | category | flops | bytes accessed | tf_op | source)
XLA Modules:
  0.0 543.0 jit_solution(7023471474250597642)
XLA Ops:
  7.3 1.7 convert_reduce_fusion
  9.0 1.8 fusion.75
  11.3 1.2 fusion.102
  12.8 1.2 fusion.105
  15.6 1.9 maximum_select_fusion
  17.7 2.2 copy.52
  19.9 2.2 copy.55
  22.0 3.5 fusion.108
  25.5 2.2 copy.54
  27.6 68.1 %all-reduce.11.cloned.1.call-done = bf16[2,1,256,640]{3,2,1,0:T(8,128)(2,1)} async-done(((bf16[2,1,256,640]{3,2,1,0:T(8,128)(2,1)}), bf16[2,1,256,640]{3,2,1,0:T(8,128)(2,1)}) %all-reduce.11.cloned.1.call-update) | async-done | bytes 655376 | tf_op jit(solution)/shard_map/psum | solution.py:16
  95.8 2.0 fusion.163
  97.7 1.1 copy.53
  98.9 1.9 copy.56
  102.7 6.7 %fusion.135 = f32[2,10,256,512]{3,2,1,0:T(8,128)} fusion(bf16[2,256,10,64]{1,3,2,0:T(8,128)(2,1)} %bitcast.239, bf16[1,2,256,10,64]{2,4,3,1,0:T(8,128)(2,1)S(1)} %broadcast_in_dim.32, bf16[1,2,256,10,64]{2,4,3,1,0:T(8,128)(2,1)} %bitcast.235), kind=kOutput, calls=%fused_computation.141 | convolution fusion | flops 338165760 | bytes 12451840 | tf_op jit(solution)/shard_map/lfshd,lfthd->lfhst/dot_general | solution.py:56
  109.3 13.1 %fusion.164 = (f32[2,10,256]{2,1,0:T(8,128)S(1)}, f32[2,10,256,512]{3,2,1,0:T(8,128)}) fusion(f32[2,10,256,512]{3,2,1,0:T(8,128)} %fusion.135), kind=kOutput, calls=%fused_computation.173 | output fusion | flops 10486271 | bytes 20992000 | tf_op jit(solution)/shard_map/sub | solution.py:63
  123.4 17.5 %fusion.99 = bf16[2,10,64,256]{3,2,1,0:T(8,128)(2,1)} fusion(bf16[1,2,256,10,64]{2,4,3,1,0:T(8,128)(2,1)} %broadcast_in_dim.14, bf16[1,2,256,10,64]{2,4,3,1,0:T(8,128)(2,1)} %bitcast.237, f32[2,10,256]{2,1,0:T(8,128)S(1)} %get-tuple-element.71, f32[2,10,256,512]{3,2,1,0:T(8,128)} %fusion.135), kind=kOutput, calls=%fused_computation.105 | convolution fusion | flops 351606272 | bytes 12472320 | tf_op jit(solution)/shard_map/lfhst,lfthd->lfshd/dot_general | solution.py:66
  140.9 2.7 fusion.61
  143.7 1.1 copy-done.29
  146.1 1.7 fusion.117
  147.8 1.3 collective-permute-start.1
  149.1 6.0 %collective-permute-start = (bf16[2,1,1,256,1280]{4,3,2,1,0:T(8,128)(2,1)}, bf16[2,1,1,256,1280]{4,3,2,1,0:T(8,128)(2,1)}, u32[]{:S(2)}, u32[]{:S(2)}) collective-permute-start(bf16[2,1,1,256,1280]{4,3,2,1,0:T(8,128)(2,1)} %get-tuple-element.67), channel_id=1, source_target_pairs={{0,1},{1,2},{2,3},{3,4},{4,5},{5,6},{6,7},{8,9},{9,10},{10,11},{11... | collective-permute-start | bytes 3932168 | tf_op jit(solution)/shard_map/ppermute | solution.py:26
  155.1 3.5 convert_element_type.178
  158.6 2.0 convert_element_type.179
  160.6 14.6 %collective-permute-done.1 = bf16[2,1,1,256,1280]{4,3,2,1,0:T(8,128)(2,1)} collective-permute-done((bf16[2,1,1,256,1280]{4,3,2,1,0:T(8,128)(2,1)}, bf16[2,1,1,256,1280]{4,3,2,1,0:T(8,128)(2,1)}, u32[]{:S(2)}, u32[]{:S(2)}) %collective-permute-start.1) | collective-permute-done | bytes 1310752 | tf_op jit(solution)/shard_map/ppermute | solution.py:27
  175.2 1.2 collective-permute-done
  176.3 2.8 pad_maximum_fusion
  179.5 2.0 slice_bitcast_fusion.5
  181.6 9.6 %fusion.65 = bf16[1,2,256,1280]{3,2,1,0:T(8,128)(2,1)S(1)} fusion(bf16[1280,3,1280]{2,0,1:T(8,128)(2,1)} %param.18, bf16[1,2,256,1,1280]{4,2,1,3,0:T(8,128)(2,1)S(1)} %get-tuple-element.62, bf16[1,2,256,1,1280]{4,2,1,3,0:T(8,128)(2,1)S(1)} %get-tuple-element.63, bf16[1,2,256,1,1280]{4,2,1,3,0:T(8,128)(2,1)S(1)} %get-tuple-element.61, ...), kind=kOutput, calls=%fused_computation.68 | convolution fusion | flops 5044961280 | bytes 17694720 | tf_op jit(solution)/shard_map/lfsjo,cjo->lfsc/dot_general | solution.py:157
  192.3 2.1 fusion.111
  194.3 1.3 copy.58
  195.7 17.6 %fusion.82 = f32[2,10,64,512]{3,2,1,0:T(8,128)} fusion(bf16[2,256,10,64]{1,3,2,0:T(8,128)(2,1)S(1)} %bitcast.241, f32[2,10,256]{2,1,0:T(8,128)S(1)} %get-tuple-element.71, f32[2,10,256,512]{3,2,1,0:T(8,128)} %fusion.135), kind=kOutput, calls=%fused_computation.87 | convolution fusion | flops 348657152 | bytes 13783040 | tf_op jit(solution)/shard_map/lfhst,lfshd->lfthd/dot_general | solution.py:87
  213.3 6.6 %fusion.123 = f32[2,10,256,512]{3,2,1,0:T(8,128)} fusion(bf16[2,256,10,64]{1,3,2,0:T(8,128)(2,1)} %bitcast.242, bf16[2,256,10,64]{1,3,2,0:T(8,128)(2,1)S(1)} %broadcast_in_dim.33, bf16[2,256,10,64]{1,3,2,0:T(8,128)(2,1)S(1)} %bitcast.238), kind=kOutput, calls=%fused_computation.129 | convolution fusion | flops 338165760 | bytes 12451840 | tf_op jit(solution)/shard_map/lfshd,lfthd->lfhst/dot_general | solution.py:75
  219.9 43.1 %fusion.26 = f32[2,10,64,512]{3,2,1,0:T(8,128)} fusion(bf16[2,256,10,64]{1,3,2,0:T(8,128)(2,1)S(1)} %bitcast.240, f32[2,10,256,512]{3,2,1,0:T(8,128)} %fusion.123, f32[2,10,256,512]{3,2,1,0:T(8,128)} %get-tuple-element.72, f32[2,10,256]{2,1,0:T(8,128)S(1)} %get-tuple-element.71), kind=kOutput, calls=%fused_computation.28 | convolution fusion | flops 353900032 | bytes 24268800 | tf_op jit(solution)/shard_map/lfhst,lfshd->lfthd/dot_general | solution.py:84
  263.0 2.3 slice_reduce_fusion.1
  265.3 2.2 slice_reduce_fusion
  267.7 42.3 %fusion.114 = bf16[2,10,64,256]{3,2,1,0:T(8,128)(2,1)} fusion(f32[2,10,256,512]{3,2,1,0:T(8,128)} %fusion.123, bf16[1,2,256,10,64]{2,4,3,1,0:T(8,128)(2,1)S(1)} %copy-done.24, bf16[1,2,256,10,64]{2,4,3,1,0:T(8,128)(2,1)S(1)} %bitcast.236, f32[2,10,256,512]{3,2,1,0:T(8,128)} %get-tuple-element.72, f32[2,10,256]{2,1,0:T(8,128)S(1)} %get-tuple-element.71), kind=kOutput, calls=%fused_computation.110 | convolution fusion | flops 356849152 | bytes 22958080 | tf_op jit(solution)/shard_map/lfhst,lfthd->lfshd/dot_general | solution.py:80
  309.9 1.4 slice.120
  311.3 2.2 slice.121
  313.8 1.6 copy.77
  315.5 4.5 convolution_bitcast_fusion
  319.9 3.0 convolution_bitcast_fusion.3
  322.9 23.3 %all-reduce.15.cloned.1.call-done = (bf16[1,256,640]{1,2,0:T(8,128)(2,1)}, bf16[1,256,640]{1,2,0:T(8,128)(2,1)}) async-done(((bf16[1,256,640]{1,2,0:T(8,128)(2,1)}, bf16[1,256,640]{1,2,0:T(8,128)(2,1)}), (bf16[1,256,640]{1,2,0:T(8,128)(2,1)}, bf16[1,256,640]{1,2,0:T(8,128)(2,1)})) %all-reduce.15.cloned.1.call-update) | async-done | bytes 655376 | tf_op jit(solution)/shard_map/psum | solution.py:182
  346.2 8.2 %conditional.1 = (f32[1280,640]{1,0:T(8,128)S(1)}, f32[1280,640]{1,0:T(8,128)S(1)}, f32[1,1,256,1280]{3,2,1,0:T(8,128)S(1)}) conditional(s32[]{:T(128)} %convert_element_type.173, () %tuple.22, (bf16[1,2,256,1280]{3,2,1,0:T(8,128)(2,1)S(1)}, bf16[1,256,640]{1,2,0:T(8,128)(2,1)}, bf16[1,256,640]{1,2,0:T(8,128)(2,1)}, f32[1280,640]{1,0:T(8,128)}, ...), branch_computations={%region_10.11_spmd, %region_11.12_spmd} | conditional | flops 5872353280 | bytes 48496776 | solution.py:196
  346.3 1.7 fusion.3
  348.7 1.2 copy-done.4
  349.9 2.1 fusion.9
  352.1 2.2 fusion
  354.5 3.0 fusion.40
  357.5 3.0 fusion.39
  360.5 1.4 copy-done.42
  362.0 1.2 fusion.89
  363.3 3.0 convolution_add_fusion.2
  366.3 1.2 convolution_add_fusion.1
  367.6 1.5 copy.87
  371.2 10.5 %fusion.62 = bf16[1,2,256,1280]{3,2,1,0:T(8,128)(2,1)} fusion(bf16[1280,3,1280]{2,0,1:T(8,128)(2,1)} %param.18, bf16[1,2,256,1,1280]{4,2,1,3,0:T(8,128)(2,1)S(1)} %copy-done.34, bf16[1,2,256,1,1280]{4,2,1,3,0:T(8,128)(2,1)S(1)} %copy-done.33, bf16[1,2,256,1,1280]{4,2,1,3,0:T(8,128)(2,1)S(1)} %copy-done.35, bf16[1,2,256,1280]{3,2,1,0:T(8,128)(2,1)S(1)} %copy-done.31), kind=kOutput, calls=%fused_computation.67 | convolution fusion | flops 5039063040 | bytes 16384000 | tf_op jit(solution)/shard_map/lfsjc,cjo->lfso/dot_general | solution.py:151
  381.7 1.3 fusion.120
  383.5 3.0 fusion.74
  386.4 63.6 %all-reduce.4 = f32[1280]{0:T(1024)S(1)} all-reduce(f32[1280]{0:T(1024)S(1)} %get-tuple-element.50), channel_id=6, replica_groups=mesh['batch'=16,'tm'=8] {'batch','tm'}, use_global_device_ids=true, to_apply=%region_19.20.clone | all-reduce | flops 1280 | bytes 10240
  450.6 4.4 fusion.73
  455.0 75.3 %all-reduce.13.cloned.1.call-done = (f32[1280,640]{1,0:T(8,128)}, f32[1280,640]{1,0:T(8,128)}, f32[1280,640]{1,0:T(8,128)}, f32[640,1280]{1,0:T(8,128)}) async-done(((f32[1280,640]{1,0:T(8,128)}, f32[1280,640]{1,0:T(8,128)}, f32[1280,640]{1,0:T(8,128)}, f32[640,1280]{1,0:T(8,128)}), (f32[1280,640]{1,0:T(8,128)}, f32[1280,640]{1,0:T(8,128)}, f32[1280,640]{1,0:T(8,128)}, ...) | async-done | bytes 13107216
  530.3 1.5 constant_dynamic-slice_fusion.3
  531.8 1.5 constant_dynamic-slice_fusion.2
  533.2 1.5 constant_dynamic-slice_fusion.1
  534.7 1.5 constant_dynamic-slice_fusion
  (108 shorter events, 12.7 us)
Async XLA Ops:
  7.2 133.8 %copy-start = (bf16[640,1280]{1,0:T(8,128)(2,1)S(1)}, bf16[640,1280]{1,0:T(8,128)(2,1)}, u32[]{:S(2)}) copy-start(bf16[640,1280]{1,0:T(8,128)(2,1)} %param.17) | copy-start | bytes 4915204
  7.2 3.6 copy-start.36
  7.2 88.6 %all-reduce.11.cloned.1.call-start = ((), (), s32[]{:S(2)}) async-start(), calls=%async_computation | async-start | bytes 1310720 | tf_op jit(solution)/shard_map/psum | solution.py:16
  7.2 3.6 copy-start.2
  7.3 4.1 copy-start.9
  9.0 3.6 copy-start.38
  10.8 1.7 copy-start.40
  11.3 1.4 copy-start.8
  12.6 1.4 copy-start.25
  14.0 0.8 copy-start.26
  17.5 328.8 %all-reduce.15.cloned.1.call-start = ((), (), s32[]{:S(2)}) async-start(), calls=%async_computation.2 | async-start | bytes 1310720 | tf_op jit(solution)/shard_map/psum | solution.py:182
  101.8 0.9 copy-start.23
  143.7 1.1 copy-start.29
  144.8 1.3 copy-start.15
  145.5 2.3 copy-start.6
  147.8 27.4 %collective-permute-start.1 = (bf16[2,1,1,256,1280]{4,3,2,1,0:T(8,128)(2,1)}, bf16[2,1,1,256,1280]{4,3,2,1,0:T(8,128)(2,1)}, u32[]{:S(2)}, u32[]{:S(2)}) collective-permute-start(bf16[2,1,1,256,1280]{4,3,2,1,0:T(8,128)(2,1)} %get-tuple-element.68), channel_id=1, source_target_pairs={{1,0},{2,1},{3,2},{4,3},{5,4},{6,5},{7,6},{9,8},{10,9},{11,10},{12... | collective-permute-start | bytes 3932168 | tf_op jit(solution)/shard_map/ppermute | solution.py:27
  149.1 27.2 %collective-permute-start = (bf16[2,1,1,256,1280]{4,3,2,1,0:T(8,128)(2,1)}, bf16[2,1,1,256,1280]{4,3,2,1,0:T(8,128)(2,1)}, u32[]{:S(2)}, u32[]{:S(2)}) collective-permute-start(bf16[2,1,1,256,1280]{4,3,2,1,0:T(8,128)(2,1)} %get-tuple-element.67), channel_id=1, source_target_pairs={{0,1},{1,2},{2,3},{3,4},{4,5},{5,6},{6,7},{8,9},{9,10},{10,11},{11... | collective-permute-start | bytes 3932168 | tf_op jit(solution)/shard_map/ppermute | solution.py:26
  155.1 3.5 copy-start.10
  158.6 17.8 %copy-start.7 = (bf16[1,1,2,256,1280]{4,3,2,1,0:T(8,128)(2,1)S(1)}, bf16[1,1,2,256,1280]{4,3,2,1,0:T(8,128)(2,1)}, u32[]{:S(2)}) copy-start(bf16[1,1,2,256,1280]{4,3,2,1,0:T(8,128)(2,1)} %copy-done.6) | copy-start | bytes 3932164
  158.6 17.8 %copy-start.16 = (bf16[1,2,256,1280]{3,2,1,0:T(8,128)(2,1)S(1)}, bf16[1,2,256,1280]{3,2,1,0:T(8,128)(2,1)}, u32[]{:S(2)}) copy-start(bf16[1,2,256,1280]{3,2,1,0:T(8,128)(2,1)} %param.19) | copy-start | bytes 3932164
  179.5 2.1 copy-start.30
  191.2 1.1 copy-start.32
  195.7 17.6 %copy-start.22 = (bf16[2,256,640]{1,2,0:T(8,128)(2,1)}, bf16[2,256,640]{1,2,0:T(8,128)(2,1)S(1)}, u32[]{:S(2)}) copy-start(bf16[2,256,640]{1,2,0:T(8,128)(2,1)S(1)} %copy.58) | copy-start | bytes 1966084
  195.7 17.7 %copy-start.20 = (bf16[2,256,640]{1,2,0:T(8,128)(2,1)S(1)}, bf16[2,256,640]{1,2,0:T(8,128)(2,1)}, u32[]{:S(2)}) copy-start(bf16[2,256,640]{1,2,0:T(8,128)(2,1)} %copy.52) | copy-start | bytes 1966084
  213.3 6.6 %copy-start.21 = (bf16[2,256,640]{1,2,0:T(8,128)(2,1)S(1)}, bf16[2,256,640]{1,2,0:T(8,128)(2,1)}, u32[]{:S(2)}) copy-start(bf16[2,256,640]{1,2,0:T(8,128)(2,1)} %copy.54) | copy-start | bytes 1966084
  263.0 4.6 copy-start.19
  263.0 4.6 copy-start.24
  267.6 262.7 %all-reduce.13.cloned.1.call-start = ((), (), s32[]{:S(2)}) async-start(), calls=%async_computation.1 | async-start | bytes 26214400
  313.8 40.7 %copy-start.14 = (bf16[1,2,256,640]{3,2,1,0:T(8,128)(2,1)}, bf16[1,2,256,640]{3,2,1,0:T(8,128)(2,1)S(1)}, u32[]{:S(2)}) copy-start(bf16[1,2,256,640]{3,2,1,0:T(8,128)(2,1)S(1)} %copy.76) | copy-start | bytes 1966084
  315.5 42.0 %copy-start.12 = (bf16[1,2,256,640]{3,2,1,0:T(8,128)(2,1)}, bf16[1,2,256,640]{3,2,1,0:T(8,128)(2,1)S(1)}, u32[]{:S(2)}) copy-start(bf16[1,2,256,640]{3,2,1,0:T(8,128)(2,1)S(1)} %copy.77) | copy-start | bytes 1966084
  315.5 4.5 copy-start.43
  346.2 1.8 copy-start.28
  348.0 1.9 copy-start.4
  348.0 1.9 copy-start.27
  348.7 3.3 copy-start.5
  354.5 3.0 copy-start.17
  360.5 1.4 copy-start.42
  360.5 1.6 copy-start.44
  363.3 3.0 copy-start.11
  363.3 3.0 copy-start.13
  367.6 2.3 copy-start.31
  367.6 2.8 copy-start.33
  367.6 3.1 copy-start.34
  367.6 3.5 copy-start.35
  371.2 10.5 %copy-start.18 = (f32[1,1,256,1280]{3,2,1,0:T(8,128)S(1)}, f32[1,1,256,1280]{3,2,1,0:T(8,128)}, u32[]{:S(2)}) copy-start(f32[1,1,256,1280]{3,2,1,0:T(8,128)} %copy-done.17) | copy-start | bytes 3932164
  381.7 1.8 copy-start.3
  381.7 1.8 copy-start.37
  381.7 1.8 copy-start.39
  381.7 1.8 copy-start.41
  450.6 85.6 %copy-start.1 = (bf16[640,1280]{1,0:T(8,128)(2,1)S(1)}, bf16[640,1280]{1,0:T(8,128)(2,1)}, u32[]{:S(2)}) copy-start(bf16[640,1280]{1,0:T(8,128)(2,1)} %param.17) | copy-start | bytes 4915204
Sparse Core Ops, SparseCore 0:
  17.6 78.1 all-reduce.10
  267.7 78.4 all-reduce.14
  360.6 169.6 all-reduce.12
where the time goes:
time: 548 us; the launch traced here: 543 us
  matrix products  190 us (35%)
  waiting for transfers between devices  183 us (33%)
  blocking collectives  63.6 us (12%)
  other arithmetic  42.9 us (8%)
  local copies, waits for them, and re-layouts  41.4 us (8%)
  between operations  14.5 us (3%)
  starting transfers between devices  7.56 us (1%)
    unnamed x4, waiting for transfers between devices  75.4 us
    psum x1, waiting for transfers between devices, broadcast(): return lax.psum(block, axis)  68.1 us
    unnamed x1, blocking collectives  63.6 us
    dot_general x1, matrix products, attend_back(): jnp.einsum('lfhst,lfshd->lfthd', grad_score, split_heads(queries), prefer...  43.1 us
    dot_general x1, matrix products, attend_back(): jnp.einsum('lfhst,lfthd->lfshd', grad_score, split_heads(key_all), prefer...  42.3 us
    psum x1, waiting for transfers between devices, on_device(): lax.psum(key_first_grad.astype(jnp.bfloat16), 'tm').astype(jnp.float32)  23.3 us
    unnamed x90, local copies, waits for them, and re-layouts  18.7 us
    dot_general x1, matrix products, attend_back(): jnp.einsum('lfhst,lfshd->lfthd', prob_b, grad_heads, preferred_element_ty...  17.6 us
  transfers between devices with their start and end apart: 5, of which 5 were waited for; matrix products, arithmetic and copies ran while one was open for 18% of the time, Pallas kernels for 0%

commit v1 on v0

--- a/solution.py
+++ b/solution.py
@@ -1,3 +1,5 @@
+import functools
+
 import jax
 import jax.numpy as jnp
 from jax import lax
@@ -11,9 +13,39 @@
 highest = lax.Precision.HIGHEST
 
 
-def broadcast(block, axis, holder):
-    block = jnp.where(lax.axis_index(axis) == holder, block, jnp.zeros_like(block))
-    return lax.psum(block, axis)
+def tree_broadcast(block, axis):
+    index = lax.axis_index(axis)
+    have = block
+    for pairs in (((0, 4),), ((0, 3), (4, 7)), ((0, 1), (3, 2), (4, 5), (7, 6))):
+        got = lax.ppermute(have, axis, list(pairs))
+        hit = functools.reduce(jnp.logical_or, [index == dst for _, dst in pairs])
+        have = jnp.where(hit, got, have)
+    return have
+
+
+def tree_reduce(block, axis):
+    index = lax.axis_index(axis)
+    total = block
+    for pairs in (((1, 0), (2, 3), (5, 4), (6, 7)), ((3, 0), (7, 4)), ((4, 0),)):
+        got = lax.ppermute(total.astype(jnp.bfloat16), axis, list(pairs))
+        hit = functools.reduce(jnp.logical_or, [index == dst for _, dst in pairs])
+        total = jnp.where(hit, total + got.astype(jnp.float32), total)
+    return total
+
+
+def scatter_sum(parts, outer, inner):
+    count = lax.axis_size(outer) * lax.axis_size(inner)
+    packed = jnp.concatenate([p.reshape(count, -1) for p in parts], axis=1)
+    share = packed.reshape((lax.axis_size(outer), -1) + packed.shape[1:])
+    share = lax.psum_scatter(share, outer, scatter_dimension=0, tiled=True)[0]
+    share = lax.all_to_all(share, inner, 0, 0, tiled=True)
+    share = jnp.sum(share, axis=0)
+    outs, start = [], 0
+    for p in parts:
+        width = p.size // count
+        outs.append(share[start : start + width].reshape((p.shape[0] // count,) + p.shape[1:]))
+        start += width
+    return outs
 
 
 def padded_2(value, sides, width):
@@ -135,10 +167,10 @@
     queries = project(normed, w_query)
     key_rows = project(normed, w_key)
     val_rows = project(normed, w_value)
-    shared = broadcast(jnp.stack([key_rows[:, 0], val_rows[:, 0]]), "tm", 0)
-    key_first = shared[0]
-    val_first = shared[1]
-    normed_first = normed[:, 0]
+    x_first = tree_broadcast(x_in[:, 0], "tm")
+    normed_first = layer_norm(x_first, norm_gain)[0]
+    key_first = project(normed_first, w_key)
+    val_first = project(normed_first, w_value)
     attended, prob_f32, prob_b, key_all, val_all = attend(
         queries, key_rows, val_rows, key_first, val_first
     )
@@ -146,11 +178,10 @@
         x_in.astype(jnp.float32) + jnp.dot(attended, w_out, preferred_element_type=jnp.float32)
     ).astype(jnp.bfloat16)
     active = jax.nn.silu(hidden.astype(jnp.float32)).astype(jnp.bfloat16)
-    padded = padded_2(jnp.stack([active, cotangent]), (("tm", 2),), 1)
-    act_stack = time_stack(padded[0], frames)
+    grad_pad = padded_2(cotangent, (("tm", 1),), 1)
+    act_stack = time_stack(padded_2(active, (("tm", 1),), 1), frames)
     conv = jnp.einsum("lfsjc,cjo->lfso", act_stack, w_time, preferred_element_type=jnp.float32)
     output = (hidden.astype(jnp.float32) + conv).astype(jnp.bfloat16)
-    grad_pad = padded[1]
     grad_stack = jnp.stack(
         [grad_pad[:, 2 : frames + 2], grad_pad[:, 1 : frames + 1], grad_pad[:, 0:frames]], axis=3
     )
@@ -178,22 +209,19 @@
     )
     key_wide = w_key.astype(jnp.float32)
     val_wide = w_value.astype(jnp.float32)
-    summed = (
-        lax.psum(key_first_grad.astype(jnp.bfloat16), "tm").astype(jnp.float32),
-        lax.psum(val_first_grad.astype(jnp.bfloat16), "tm").astype(jnp.float32),
-    )
+    first_sum = tree_reduce(jnp.concatenate([key_first_grad, val_first_grad], axis=-1), "tm")
+    width = key_first_grad.shape[-1]
 
     def owner_terms(operands):
-        return first_terms(normed_first, operands[0], operands[1], key_wide, val_wide)
+        rows = jnp.einsum("lsh,ch->lsc", operands[..., :width], key_wide, precision=highest)
+        return rows + jnp.einsum("lsh,ch->lsc", operands[..., width:], val_wide, precision=highest)
 
     def no_terms(operands):
-        return (
-            jnp.zeros(normed_first.shape, jnp.float32),
-            jnp.zeros(key_wide.shape, jnp.float32),
-            jnp.zeros(val_wide.shape, jnp.float32),
-        )
-
-    first_rows, extra_key, extra_val = lax.cond(is_owner, owner_terms, no_terms, summed)
+        return jnp.zeros(normed_first.shape, jnp.float32)
+
+    first_rows = lax.cond(is_owner, owner_terms, no_terms, first_sum)
+    extra_key = gram_rows(normed_first.astype(jnp.float32), key_first_grad, highest)
+    extra_val = gram_rows(normed_first.astype(jnp.float32), val_first_grad, highest)
     grad_normed = grad_normed.at[:, 0].add(first_rows)
     grad_wq = gram_rows(normed, grad_queries)
     grad_wk = gram_rows(normed, key_b) + extra_key
@@ -206,12 +234,8 @@
         - x_hat * jnp.mean(grad_hat * x_hat, axis=-1, keepdims=True)
     )
     grad_input = (grad_hidden.astype(jnp.float32) + grad_x).astype(jnp.bfloat16)
-    grad_wq, grad_wk, grad_wv, grad_out, grad_gain = (
-        lax.psum_scatter(grad_wq, ("batch", "tm"), scatter_dimension=0, tiled=True),
-        lax.psum_scatter(grad_wk, ("batch", "tm"), scatter_dimension=0, tiled=True),
-        lax.psum_scatter(grad_wv, ("batch", "tm"), scatter_dimension=0, tiled=True),
-        lax.psum_scatter(grad_out, ("batch", "tm"), scatter_dimension=0, tiled=True),
-        lax.psum_scatter(grad_gain, ("batch", "tm"), scatter_dimension=0, tiled=True),
+    grad_wq, grad_wk, grad_wv, grad_out, grad_gain = scatter_sum(
+        (grad_wq, grad_wk, grad_wv, grad_out, grad_gain), "batch", "tm"
     )
     return (output, grad_input, grad_wq, grad_wk, grad_wv, grad_out, grad_gain)
 

time: 548 us -> 546 us (level)
  blocking collectives: 63.6 us -> 0 us
  local copies, waits for them, and re-layouts: 41.4 us -> 71.9 us
  starting transfers between devices: 7.56 us -> 27 us
  matrix products: 190 us -> 206 us
  waiting for transfers between devices: 183 us -> 170 us
  other arithmetic: 42.9 us -> 48.8 us
    psum x2 -> x0, waiting for transfers between devices: 91.4 us -> none  [the longest x1 68.1 us: broadcast(): return lax.psum(block, axis)]
    unnamed x1 -> x0, blocking collectives: 63.6 us -> none
    ppermute x0 -> x6, waiting for transfers between devices: none -> 54.6 us  [the longest x3 32.3 us: tree_reduce(): got = lax.ppermute(total.astype(jnp.bfloat16), axis, list(pairs))]
    concatenate x0 -> x6, local copies, waits for them, and re-layouts: none -> 19 us  [scatter_sum(): packed = jnp.concatenate([p.reshape(count, -1) for p in parts], axis=1)]
    unnamed x4 -> x2, waiting for transfers between devices: 75.4 us -> 94.2 us
    ppermute x0 -> x6, starting transfers between devices: none -> 13.1 us  [the longest x3 8.86 us: tree_broadcast(): got = lax.ppermute(have, axis, list(pairs))]
    ppermute x1 -> x2, waiting for transfers between devices: 14.6 us -> 4.3 us  [padded_2(): after = lax.ppermute(leading, axis, down)]
    all_to_all x0 -> x1, waiting for transfers between devices: none -> 8.37 us  [scatter_sum(): share = lax.all_to_all(share, inner, 0, 0, tiled=True)]
  transfers between devices with their start and end apart: 5 -> 12, of which waited for: 5 -> 9; matrix products, arithmetic and copies ran while one was open for 18% -> 11% of each run, Pallas kernels for 0% -> 0%
where the time goes in v1:
time: 546 us; the launch traced here: 540 us
  matrix products  206 us (38%)
  waiting for transfers between devices  170 us (31%)
  local copies, waits for them, and re-layouts  71.9 us (13%)
  other arithmetic  48.8 us (9%)
  starting transfers between devices  27 us (5%)
  between operations  14.7 us (3%)
    unnamed x2, waiting for transfers between devices  94.2 us
    dot_general x1, matrix products, attend_back(): jnp.einsum('lfhst,lfshd->lfthd', grad_score, split_heads(queries), prefer...  43 us
    dot_general x1, matrix products, attend_back(): jnp.einsum('lfhst,lfthd->lfshd', grad_score, split_heads(key_all), prefer...  42.8 us
    ppermute x3, waiting for transfers between devices, tree_reduce(): got = lax.ppermute(total.astype(jnp.bfloat16), axis, list(pairs))  32.3 us
    ppermute x3, waiting for transfers between devices, tree_broadcast(): got = lax.ppermute(have, axis, list(pairs))  22.3 us
    unnamed x75, local copies, waits for them, and re-layouts  21.7 us
    dot_general x6, matrix products, gram_rows(): lax.dot_general(flat_left, flat_right, (((0,), (0,)), ((), ())), preferre...  20.7 us
    concatenate x6, local copies, waits for them, and re-layouts, scatter_sum(): packed = jnp.concatenate([p.reshape(count, -1) for p in parts], axis=1)  19 us
  transfers between devices with their start and end apart: 12, of which 9 were waited for; matrix products, arithmetic and copies ran while one was open for 11% of the time, Pallas kernels for 0%

profile of v1, /device:TPU:0, one launch (start us, length us, event | category | flops | bytes accessed | tf_op | source)
XLA Modules:
  0.0 539.5 jit_solution(11139450685441663099)
XLA Ops:
  7.2 2.1 slice_bitcast_fusion.5
  9.4 4.4 collective-permute-start
  13.8 2.4 fusion.167
  17.7 5.4 %collective-permute-start.6 = (bf16[1,1,256,1280]{3,2,1,0:T(8,128)(2,1)}, bf16[1,1,256,1280]{3,2,1,0:T(8,128)(2,1)}, u32[]{:S(2)}, u32[]{:S(2)}) collective-permute-start(bf16[1,1,256,1280]{3,2,1,0:T(8,128)(2,1)} %get-tuple-element.57), channel_id=1, source_target_pairs={{0,1},{1,2},{2,3},{3,4},{4,5},{5,6},{6,7},{8,9},{9,10},{10,11},{11... | collective-permute-start | bytes 1966088 | tf_op jit(solution)/shard_map/ppermute | solution.py:58
  23.8 17.4 %collective-permute-done = bf16[1,256,1280]{2,1,0:T(8,128)(2,1)} collective-permute-done((bf16[1,256,1280]{2,1,0:T(8,128)(2,1)}, bf16[1,256,1280]{2,1,0:T(8,128)(2,1)}, u32[]{:S(2)}, u32[]{:S(2)}) %collective-permute-start) | collective-permute-done | bytes 655392 | tf_op jit(solution)/shard_map/ppermute | solution.py:20
  42.2 2.1 collective-permute-start.1
  44.3 2.1 fusion.95
  46.5 2.2 copy.52
  48.6 3.5 convert_element_type.186
  52.1 2.1 fusion.98
  54.3 2.2 copy.53
  56.4 3.5 convert_element_type.187
  60.0 2.0 broadcast_select_fusion.1
  62.0 2.3 collective-permute-start.2
  64.3 2.1 fusion.92
  66.4 2.2 copy.50
  68.6 3.5 fusion.114
  72.1 4.9 collective-permute-done.2
  83.7 6.7 %fusion.125 = f32[2,10,256,512]{3,2,1,0:T(8,128)} fusion(bf16[2,256,10,64]{1,3,2,0:T(8,128)(2,1)} %bitcast.225, bf16[1,2,256,10,64]{2,4,3,1,0:T(8,128)(2,1)S(1)} %broadcast_in_dim.13, bf16[1,2,256,10,64]{2,4,3,1,0:T(8,128)(2,1)} %bitcast.223), kind=kOutput, calls=%fused_computation.135 | convolution fusion | flops 338165760 | bytes 12451840 | tf_op jit(solution)/shard_map/lfshd,lfthd->lfhst/dot_general | solution.py:88
  90.4 13.1 %fusion.170 = (f32[2,10,256]{2,1,0:T(8,128)S(1)}, f32[2,10,256,512]{3,2,1,0:T(8,128)}) fusion(f32[2,10,256,512]{3,2,1,0:T(8,128)} %fusion.125), kind=kOutput, calls=%fused_computation.177 | output fusion | flops 10486271 | bytes 20992000 | tf_op jit(solution)/shard_map/sub | solution.py:95
  105.5 17.6 %fusion.89 = bf16[2,10,64,256]{3,2,1,0:T(8,128)(2,1)} fusion(bf16[1,2,256,10,64]{2,4,3,1,0:T(8,128)(2,1)} %broadcast_in_dim.11, bf16[1,2,256,10,64]{2,4,3,1,0:T(8,128)(2,1)} %bitcast.227, f32[2,10,256]{2,1,0:T(8,128)S(1)} %get-tuple-element.66, f32[2,10,256,512]{3,2,1,0:T(8,128)} %fusion.125), kind=kOutput, calls=%fused_computation.99 | convolution fusion | flops 351606272 | bytes 12472320 | tf_op jit(solution)/shard_map/lfhst,lfthd->lfshd/dot_general | solution.py:98
  123.2 3.9 fusion.67
  127.0 10.1 %fusion.53 = bf16[1,2,256,1280]{3,2,1,0:T(8,128)(2,1)S(1)} fusion(bf16[1280,3,1280]{2,0,1:T(8,128)(2,1)} %param.18, bf16[1,2,256,1,1280]{4,2,3,1,0:T(8,128)(2,1)S(1)} %copy-done.28, bf16[1,2,256,1,1280]{4,2,3,1,0:T(8,128)(2,1)S(1)} %bitcast.219, bf16[1,2,256,1,1280]{4,2,3,1,0:T(8,128)(2,1)S(1)} %copy-done.27, ...), kind=kOutput, calls=%fused_computation.60 | convolution fusion | flops 5044961280 | bytes 17694720 | tf_op jit(solution)/shard_map/lfsjo,cjo->lfsc/dot_general | solution.py:188
  138.2 2.1 fusion.101
  141.6 17.9 %fusion.70 = f32[2,10,64,512]{3,2,1,0:T(8,128)} fusion(bf16[2,256,10,64]{1,3,2,0:T(8,128)(2,1)S(1)} %bitcast.229, f32[2,10,256]{2,1,0:T(8,128)S(1)} %get-tuple-element.66, f32[2,10,256,512]{3,2,1,0:T(8,128)} %fusion.125), kind=kOutput, calls=%fused_computation.75 | convolution fusion | flops 348657152 | bytes 13783040 | tf_op jit(solution)/shard_map/lfhst,lfshd->lfthd/dot_general | solution.py:119
  159.6 2.3 slice.117
  163.5 5.4 fusion.119
  168.9 43.0 %fusion.16 = f32[2,10,64,512]{3,2,1,0:T(8,128)} fusion(bf16[2,256,10,64]{1,3,2,0:T(8,128)(2,1)S(1)} %bitcast.226, f32[2,10,256,512]{3,2,1,0:T(8,128)} %fusion.119, f32[2,10,256,512]{3,2,1,0:T(8,128)} %get-tuple-element.67, f32[2,10,256]{2,1,0:T(8,128)S(1)} %get-tuple-element.66), kind=kOutput, calls=%fused_computation.20 | convolution fusion | flops 353900032 | bytes 24268800 | tf_op jit(solution)/shard_map/lfhst,lfshd->lfthd/dot_general | solution.py:116
  211.9 2.2 slice.116
  215.6 42.8 %fusion.104 = bf16[2,10,64,256]{3,2,1,0:T(8,128)(2,1)} fusion(f32[2,10,256,512]{3,2,1,0:T(8,128)} %fusion.119, bf16[1,2,256,10,64]{2,4,3,1,0:T(8,128)(2,1)} %copy-done.26, bf16[1,2,256,10,64]{2,4,3,1,0:T(8,128)(2,1)} %bitcast.224, f32[2,10,256,512]{3,2,1,0:T(8,128)} %get-tuple-element.67, f32[2,10,256]{2,1,0:T(8,128)S(1)} %get-tuple-element.66), kind=kOutput, calls=%fused_computation.104 | convolution fusion | flops 356849152 | bytes 22958080 | tf_op jit(solution)/shard_map/lfhst,lfthd->lfshd/dot_general | solution.py:112
  258.4 4.3 convolution_bitcast_fusion
  262.7 3.1 convolution_bitcast_fusion.3
  265.8 2.7 fusion.80
  268.5 2.2 copy.77
  270.7 2.6 convolution_bitcast_fusion.1
  273.2 4.1 convolution_add_fusion.1
  277.3 4.8 concatenate.71
  282.1 2.2 copy.76
  284.3 2.5 convolution_bitcast_fusion.2
  286.9 4.2 convolution_add_fusion.2
  291.1 4.4 concatenate.70
  295.5 4.4 concatenate.69
  299.9 3.8 constant_dynamic-update-slice_fusion.4
  303.7 4.5 concatenate.72
  309.9 3.2 convolution_add_fusion.4
  320.6 5.0 collective-permute-done.7
  329.1 14.1 %collective-permute-done.8 = bf16[1,256,1280]{1,2,0:T(8,128)(2,1)S(1)} collective-permute-done((bf16[1,256,1280]{1,2,0:T(8,128)(2,1)S(1)}, bf16[1,256,1280]{1,2,0:T(8,128)(2,1)S(1)}, u32[]{:S(2)}, u32[]{:S(2)}) %collective-permute-start.8) | collective-permute-done | bytes 655392 | tf_op jit(solution)/shard_map/ppermute | solution.py:30
  346.0 2.0 constant_dynamic-update-slice_fusion.1
  348.0 13.2 %collective-permute-done.9 = bf16[1,256,1280]{1,2,0:T(8,128)(2,1)S(1)} collective-permute-done((bf16[1,256,1280]{1,2,0:T(8,128)(2,1)S(1)}, bf16[1,256,1280]{1,2,0:T(8,128)(2,1)S(1)}, u32[]{:S(2)}, u32[]{:S(2)}) %collective-permute-start.9) | collective-permute-done | bytes 655392 | tf_op jit(solution)/shard_map/ppermute | solution.py:30
  362.3 15.1 %conditional.1 = (f32[1,1,256,1280]{3,2,1,0:T(8,128)}) conditional(s32[]{:T(128)} %convert_element_type.179, () %tuple.20, (pred[]{:T(512)}, f32[1,256,1280]{1,2,0:T(8,128)S(1)}, f32[1,256,1280]{1,2,0:T(8,128)}, f32[1280,640]{1,0:T(8,128)}, f32[1280,640]{1,0:T(8,128)}) %tuple.42), branch_computations={%region_9.10_spmd, %region_10.11_spmd} | conditional | flops 5034147840 | bytes 47185984 | solution.py:222
  363.8 2.8 copy.62
  366.6 2.0 add_select_fusion
  369.3 3.4 fusion.1
  372.7 4.5 fusion
  377.4 2.9 fusion.112
  380.3 2.8 fusion.62
  388.1 9.0 %collective-permute-done.3 = bf16[1,1,256,1280]{3,2,1,0:T(8,128)(2,1)S(1)} collective-permute-done((bf16[1,1,256,1280]{3,2,1,0:T(8,128)(2,1)S(1)}, bf16[1,1,256,1280]{3,2,1,0:T(8,128)(2,1)S(1)}, u32[]{:S(2)}, u32[]{:S(2)}) %collective-permute-start.3) | collective-permute-done | bytes 655392 | tf_op jit(solution)/shard_map/ppermute | solution.py:58
  397.1 4.3 collective-permute-done.4
  401.7 11.9 %fusion.50 = bf16[1,2,256,1280]{3,2,1,0:T(8,128)(2,1)} fusion(bf16[1280,3,1280]{2,0,1:T(8,128)(2,1)} %param.18, bf16[1,2,256,1,1280]{4,2,1,3,0:T(8,128)(2,1)S(1)} %get-tuple-element.59, bf16[1,2,256,1,1280]{4,2,1,3,0:T(8,128)(2,1)S(1)} %bitcast.220, bf16[1,2,256,1,1280]{4,2,1,3,0:T(8,128)(2,1)S(1)} %get-tuple-element.58, ...), kind=kOutput, calls=%fused_computation.59 | convolution fusion | flops 5039063040 | bytes 16384000 | tf_op jit(solution)/shard_map/lfsjc,cjo->lfso/dot_general | solution.py:183
  413.6 94.2 %reduce-scatter.4.cloned.1.call-done = f32[1,8,25610]{2,1,0:T(8,128)} async-done(((f32[16,8,25610]{2,1,0:T(8,128)}), f32[1,8,25610]{2,1,0:T(8,128)}) %reduce-scatter.4.cloned.1.call-update) | async-done | bytes 819536
  507.8 2.9 copy.67
  510.7 4.3 all-to-all-start
  515.0 4.4 fusion.61
  519.4 8.4 %all-to-all-done = f32[8,1,25610]{2,1,0:T(1,128)} async-done(((f32[8,1,25610]{2,1,0:T(1,128)}), f32[8,1,25610]{2,1,0:T(1,128)}, u32[]{:S(2)}, u32[]{:S(2)}) %all-to-all-start) | async-done | bytes 819552 | tf_op jit(solution)/shard_map/all_to_all | solution.py:41
  (123 shorter events, 46.0 us)
Async XLA Ops:
  7.2 116.0 %copy-start = (bf16[640,1280]{1,0:T(8,128)(2,1)S(1)}, bf16[640,1280]{1,0:T(8,128)(2,1)}, u32[]{:S(2)}) copy-start(bf16[640,1280]{1,0:T(8,128)(2,1)} %param.17) | copy-start | bytes 4915204
  7.2 15.9 %copy-start.2 = (bf16[1,2,256,1280]{3,2,1,0:T(8,128)(2,1)S(1)}, bf16[1,2,256,1280]{3,2,1,0:T(8,128)(2,1)}, u32[]{:S(2)}) copy-start(bf16[1,2,256,1280]{3,2,1,0:T(8,128)(2,1)} %param.12) | copy-start | bytes 3932164
  7.2 500.6 %reduce-scatter.4.cloned.1.call-start = ((), (), s32[]{:S(2)}) async-start(), calls=%async_computation.2 | async-start | bytes 13996032
  9.4 31.9 %collective-permute-start = (bf16[1,256,1280]{2,1,0:T(8,128)(2,1)}, bf16[1,256,1280]{2,1,0:T(8,128)(2,1)}, u32[]{:S(2)}, u32[]{:S(2)}) collective-permute-start(bf16[1,256,1280]{2,1,0:T(8,128)(2,1)} %slice_bitcast_fusion.5), channel_id=1, source_target_pairs={{0,4},{8,12},{16,20},{24,28},{32,36},{40,44},{48,52},{56,60},{64,6... | collective-permute-start | bytes 1966088 | tf_op jit(solution)/shard_map/ppermute | solution.py:20
  16.2 28.1 %copy-start.30 = (f32[1280]{0:T(1024)S(1)}, f32[1280]{0:T(1024)}, u32[]{:S(2)}) copy-start(f32[1280]{0:T(1024)} %param.13) | copy-start | bytes 15364
  16.2 52.3 %collective-permute-start.5 = (bf16[1,1,256,1280]{3,2,1,0:T(8,128)(2,1)}, bf16[1,1,256,1280]{3,2,1,0:T(8,128)(2,1)}, u32[]{:S(2)}, u32[]{:S(2)}) collective-permute-start(bf16[1,1,256,1280]{3,2,1,0:T(8,128)(2,1)} %get-tuple-element.56), channel_id=1, source_target_pairs={{1,0},{2,1},{3,2},{4,3},{5,4},{6,5},{7,6},{9,8},{10,9},{11,10},{12... | collective-permute-start | bytes 1966088 | tf_op jit(solution)/shard_map/ppermute | solution.py:59
  17.7 50.9 %collective-permute-start.6 = (bf16[1,1,256,1280]{3,2,1,0:T(8,128)(2,1)}, bf16[1,1,256,1280]{3,2,1,0:T(8,128)(2,1)}, u32[]{:S(2)}, u32[]{:S(2)}) collective-permute-start(bf16[1,1,256,1280]{3,2,1,0:T(8,128)(2,1)} %get-tuple-element.57), channel_id=1, source_target_pairs={{0,1},{1,2},{2,3},{3,4},{4,5},{5,6},{6,7},{8,9},{9,10},{10,11},{11... | collective-permute-start | bytes 1966088 | tf_op jit(solution)/shard_map/ppermute | solution.py:58
  23.3 21.0 %copy-start.31 = (bf16[1280,640]{1,0:T(8,128)(2,1)S(1)}, bf16[1280,640]{1,0:T(8,128)(2,1)}, u32[]{:S(2)}) copy-start(bf16[1280,640]{1,0:T(8,128)(2,1)} %param.14) | copy-start | bytes 4915204
  42.2 17.8 %collective-permute-start.1 = (bf16[1,256,1280]{2,1,0:T(8,128)(2,1)}, bf16[1,256,1280]{2,1,0:T(8,128)(2,1)}, u32[]{:S(2)}, u32[]{:S(2)}) collective-permute-start(bf16[1,256,1280]{2,1,0:T(8,128)(2,1)} %broadcast_select_fusion), channel_id=1, source_target_pairs={{0,3},{4,7},{8,11},{12,15},{16,19},{20,23},{24,27},{28,31},{32,35}... | collective-permute-start | bytes 1966088 | tf_op jit(solution)/shard_map/ppermute | solution.py:20
  48.6 3.5 copy-start.12
  56.4 7.8 %copy-start.15 = (bf16[1280,640]{1,0:T(8,128)(2,1)S(1)}, bf16[1280,640]{1,0:T(8,128)(2,1)}, u32[]{:S(2)}) copy-start(bf16[1280,640]{1,0:T(8,128)(2,1)} %param.16) | copy-start | bytes 4915204
  62.0 15.0 %collective-permute-start.2 = (bf16[1,256,1280]{2,1,0:T(8,128)(2,1)}, bf16[1,256,1280]{2,1,0:T(8,128)(2,1)}, u32[]{:S(2)}, u32[]{:S(2)}) collective-permute-start(bf16[1,256,1280]{2,1,0:T(8,128)(2,1)} %broadcast_select_fusion.1), channel_id=1, source_target_pairs={{0,1},{3,2},{4,5},{7,6},{8,9},{11,10},{12,13},{15,14},{16,17},{19,... | collective-permute-start | bytes 1966088 | tf_op jit(solution)/shard_map/ppermute | solution.py:20
  72.1 6.6 %copy-start.13 = (bf16[1280,640]{1,0:T(8,128)(2,1)S(1)}, bf16[1280,640]{1,0:T(8,128)(2,1)}, u32[]{:S(2)}) copy-start(bf16[1280,640]{1,0:T(8,128)(2,1)} %param.15) | copy-start | bytes 4915204
  78.3 1.8 copy-start.9
  78.3 1.8 copy-start.16
  82.9 0.8 copy-start.26
  123.1 3.9 copy-start.18
  123.1 3.9 copy-start.27
  123.1 3.9 copy-start.28
  127.0 10.1 %copy-start.34 = (bf16[1,2,256,1280]{3,2,1,0:T(8,128)(2,1)}, bf16[1,2,256,1280]{3,2,1,0:T(8,128)(2,1)S(1)}, u32[]{:S(2)}) copy-start(bf16[1,2,256,1280]{3,2,1,0:T(8,128)(2,1)S(1)} %get-tuple-element.69) | copy-start | bytes 3932164
  137.1 1.1 copy-start.29
  141.6 17.9 %copy-start.24 = (bf16[2,256,640]{1,2,0:T(8,128)(2,1)}, bf16[2,256,640]{1,2,0:T(8,128)(2,1)S(1)}, u32[]{:S(2)}) copy-start(bf16[2,256,640]{1,2,0:T(8,128)(2,1)S(1)} %copy.56) | copy-start | bytes 1966084
  159.6 3.9 copy-start.22
  159.6 3.9 copy-start.25
  163.5 5.4 %copy-start.21 = (bf16[2,256,640]{1,2,0:T(8,128)(2,1)S(1)}, bf16[2,256,640]{1,2,0:T(8,128)(2,1)}, u32[]{:S(2)}) copy-start(bf16[2,256,640]{1,2,0:T(8,128)(2,1)} %copy.52) | copy-start | bytes 1966084
  258.4 4.3 copy-start.33
  262.7 3.1 copy-start.32
  270.7 2.6 copy-start.10
  284.3 2.6 copy-start.11
  308.3 1.7 copy-start.14
  308.3 4.8 copy-start.17
  308.3 4.8 copy-start.23
  308.3 17.3 %collective-permute-start.7 = (bf16[1,256,1280]{1,2,0:T(8,128)(2,1)S(1)}, bf16[1,256,1280]{1,2,0:T(8,128)(2,1)S(1)}, u32[]{:S(2)}, u32[]{:S(2)}) collective-permute-start(bf16[1,256,1280]{1,2,0:T(8,128)(2,1)S(1)} %fusion.126), channel_id=1, source_target_pairs={{1,0},{2,3},{5,4},{6,7},{9,8},{10,11},{13,12},{14,15},{17,16},{18,... | collective-permute-start | bytes 1966088 | tf_op jit(solution)/shard_map/ppermute | solution.py:30
  314.4 1.5 copy-start.3
  315.8 2.9 copy-start.8
  318.7 8.5 %copy-start.7 = (f32[16,8,6400]{2,1,0:T(8,128)S(1)}, f32[16,8,6400]{2,1,0:T(8,128)}, u32[]{:S(2)}) copy-start(f32[16,8,6400]{2,1,0:T(8,128)} %concatenate.71) | copy-start | bytes 9830404
  325.9 17.3 %collective-permute-start.8 = (bf16[1,256,1280]{1,2,0:T(8,128)(2,1)S(1)}, bf16[1,256,1280]{1,2,0:T(8,128)(2,1)S(1)}, u32[]{:S(2)}, u32[]{:S(2)}) collective-permute-start(bf16[1,256,1280]{1,2,0:T(8,128)(2,1)S(1)} %fusion.132), channel_id=1, source_target_pairs={{3,0},{7,4},{11,8},{15,12},{19,16},{23,20},{27,24},{31,28},{35,32}... | collective-permute-start | bytes 1966088 | tf_op jit(solution)/shard_map/ppermute | solution.py:30
  329.1 16.9 %copy-start.6 = (f32[16,8,6400]{2,1,0:T(8,128)S(1)}, f32[16,8,6400]{2,1,0:T(8,128)}, u32[]{:S(2)}) copy-start(f32[16,8,6400]{2,1,0:T(8,128)} %concatenate.72) | copy-start | bytes 9830404
  344.6 17.7 %copy-start.20 = (f32[1,256,1280]{1,2,0:T(8,128)S(1)}, f32[1,256,1280]{1,2,0:T(8,128)}, u32[]{:S(2)}) copy-start(f32[1,256,1280]{1,2,0:T(8,128)} %get-tuple-element.51) | copy-start | bytes 3932164
  344.6 16.5 %collective-permute-start.9 = (bf16[1,256,1280]{1,2,0:T(8,128)(2,1)S(1)}, bf16[1,256,1280]{1,2,0:T(8,128)(2,1)S(1)}, u32[]{:S(2)}, u32[]{:S(2)}) collective-permute-start(bf16[1,256,1280]{1,2,0:T(8,128)(2,1)S(1)} %get-tuple-element.50), channel_id=1, source_target_pairs={{4,0},{12,8},{20,16},{28,24},{36,32},{44,40},{52,48},{60,56},{68,6... | collective-permute-start | bytes 1966088 | tf_op jit(solution)/shard_map/ppermute | solution.py:30
  366.6 2.7 copy-start.4
  369.3 3.4 copy-start.5
  383.9 1.3 copy-start.19
  385.3 11.8 %collective-permute-start.3 = (bf16[1,1,256,1280]{3,2,1,0:T(8,128)(2,1)S(1)}, bf16[1,1,256,1280]{3,2,1,0:T(8,128)(2,1)S(1)}, u32[]{:S(2)}, u32[]{:S(2)}) collective-permute-start(bf16[1,1,256,1280]{3,2,1,0:T(8,128)(2,1)S(1)} %get-tuple-element.60), channel_id=1, source_target_pairs={{0,1},{1,2},{2,3},{3,4},{4,5},{5,6},{6,7},{8,9},{9,10},{10,11},{11... | collective-permute-start | bytes 1966088 | tf_op jit(solution)/shard_map/ppermute | solution.py:58
  386.6 15.1 %copy-start.35 = (bf16[1,2,256,1280]{3,2,1,0:T(8,128)(2,1)S(1)}, bf16[1,2,256,1280]{3,2,1,0:T(8,128)(2,1)}, u32[]{:S(2)}) copy-start(bf16[1,2,256,1280]{3,2,1,0:T(8,128)(2,1)} %copy-done.34) | copy-start | bytes 3932164
  386.7 14.8 %collective-permute-start.4 = (bf16[1,1,256,1280]{3,2,1,0:T(8,128)(2,1)S(1)}, bf16[1,1,256,1280]{3,2,1,0:T(8,128)(2,1)S(1)}, u32[]{:S(2)}, u32[]{:S(2)}) collective-permute-start(bf16[1,1,256,1280]{3,2,1,0:T(8,128)(2,1)S(1)} %get-tuple-element.61), channel_id=1, source_target_pairs={{1,0},{2,1},{3,2},{4,3},{5,4},{6,5},{7,6},{9,8},{10,9},{11,10},{12... | collective-permute-start | bytes 1966088 | tf_op jit(solution)/shard_map/ppermute | solution.py:59
  510.7 17.0 %all-to-all-start = ((f32[8,1,25610]{2,1,0:T(1,128)}), f32[8,1,25610]{2,1,0:T(1,128)}, u32[]{:S(2)}, u32[]{:S(2)}) async-start(f32[8,1,25610]{2,1,0:T(1,128)} %copy.67), calls=%async_computation | async-start | bytes 1646592 | tf_op jit(solution)/shard_map/all_to_all | solution.py:41
  515.0 17.5 %copy-start.1 = (bf16[640,1280]{1,0:T(8,128)(2,1)S(1)}, bf16[640,1280]{1,0:T(8,128)(2,1)}, u32[]{:S(2)}) copy-start(bf16[640,1280]{1,0:T(8,128)(2,1)} %param.17) | copy-start | bytes 4915204
Sparse Core Ops, SparseCore 0:
  384.0 123.7 reduce-scatter.3

commit v2 on v1

--- a/solution.py
+++ b/solution.py
@@ -13,39 +13,30 @@
 highest = lax.Precision.HIGHEST
 
 
-def tree_broadcast(block, axis):
+def from_owner(block, axis):
     index = lax.axis_index(axis)
     have = block
-    for pairs in (((0, 4),), ((0, 3), (4, 7)), ((0, 1), (3, 2), (4, 5), (7, 6))):
-        got = lax.ppermute(have, axis, list(pairs))
-        hit = functools.reduce(jnp.logical_or, [index == dst for _, dst in pairs])
-        have = jnp.where(hit, got, have)
+    for target in range(1, lax.axis_size(axis)):
+        got = lax.ppermute(block, axis, [(0, target)])
+        have = jnp.where(index == target, got, have)
     return have
 
 
-def tree_reduce(block, axis):
-    index = lax.axis_index(axis)
+def to_owner(block, axis):
     total = block
-    for pairs in (((1, 0), (2, 3), (5, 4), (6, 7)), ((3, 0), (7, 4)), ((4, 0),)):
-        got = lax.ppermute(total.astype(jnp.bfloat16), axis, list(pairs))
-        hit = functools.reduce(jnp.logical_or, [index == dst for _, dst in pairs])
-        total = jnp.where(hit, total + got.astype(jnp.float32), total)
+    for source in range(1, lax.axis_size(axis)):
+        got = lax.ppermute(block.astype(jnp.bfloat16), axis, [(source, 0)])
+        total = total + got.astype(jnp.float32)
     return total
 
 
-def scatter_sum(parts, outer, inner):
+def scatter_sum(value, outer, inner):
     count = lax.axis_size(outer) * lax.axis_size(inner)
-    packed = jnp.concatenate([p.reshape(count, -1) for p in parts], axis=1)
-    share = packed.reshape((lax.axis_size(outer), -1) + packed.shape[1:])
+    share = value.reshape((lax.axis_size(outer), lax.axis_size(inner), -1) + value.shape[1:])
     share = lax.psum_scatter(share, outer, scatter_dimension=0, tiled=True)[0]
     share = lax.all_to_all(share, inner, 0, 0, tiled=True)
     share = jnp.sum(share, axis=0)
-    outs, start = [], 0
-    for p in parts:
-        width = p.size // count
-        outs.append(share[start : start + width].reshape((p.shape[0] // count,) + p.shape[1:]))
-        start += width
-    return outs
+    return share.reshape((value.shape[0] // count,) + value.shape[1:])
 
 
 def padded_2(value, sides, width):
@@ -167,7 +158,7 @@
     queries = project(normed, w_query)
     key_rows = project(normed, w_key)
     val_rows = project(normed, w_value)
-    x_first = tree_broadcast(x_in[:, 0], "tm")
+    x_first = from_owner(x_in[:, 0], "tm")
     normed_first = layer_norm(x_first, norm_gain)[0]
     key_first = project(normed_first, w_key)
     val_first = project(normed_first, w_value)
@@ -209,7 +200,7 @@
     )
     key_wide = w_key.astype(jnp.float32)
     val_wide = w_value.astype(jnp.float32)
-    first_sum = tree_reduce(jnp.concatenate([key_first_grad, val_first_grad], axis=-1), "tm")
+    first_sum = to_owner(jnp.concatenate([key_first_grad, val_first_grad], axis=-1), "tm")
     width = key_first_grad.shape[-1]
 
     def owner_terms(operands):
@@ -234,9 +225,13 @@
         - x_hat * jnp.mean(grad_hat * x_hat, axis=-1, keepdims=True)
     )
     grad_input = (grad_hidden.astype(jnp.float32) + grad_x).astype(jnp.bfloat16)
-    grad_wq, grad_wk, grad_wv, grad_out, grad_gain = scatter_sum(
-        (grad_wq, grad_wk, grad_wv, grad_out, grad_gain), "batch", "tm"
-    )
+    grad_wq, grad_wk, grad_wv, grad_out = (
+        scatter_sum(grad_wq, "batch", "tm"),
+        scatter_sum(grad_wk, "batch", "tm"),
+        scatter_sum(grad_wv, "batch", "tm"),
+        scatter_sum(grad_out, "batch", "tm"),
+    )
+    grad_gain = scatter_sum(grad_gain, "batch", "tm")
     return (output, grad_input, grad_wq, grad_wk, grad_wv, grad_out, grad_gain)
 
 

time: 546 us -> 570 us (1.044)
  waiting for transfers between devices: 170 us -> 62.3 us
  blocking collectives: 0 us -> 72 us
  starting transfers between devices: 27 us -> 60.4 us
  other arithmetic: 48.8 us -> 66.2 us
  local copies, waits for them, and re-layouts: 71.9 us -> 82.2 us
    unnamed x2 -> x4, waiting for transfers between devices: 94.2 us -> 0.07 us
    unnamed x0 -> x1, blocking collectives: none -> 72 us
    concatenate x6 -> x0, local copies, waits for them, and re-layouts: 19 us -> none  [scatter_sum(): packed = jnp.concatenate([p.reshape(count, -1) for p in parts], axis=1)]
    another operation x2 -> x8, local copies, waits for them, and re-layouts: 4.26 us -> 22.4 us
    all_to_all x1 -> x5, starting transfers between devices: 4.28 us -> 20.5 us  [scatter_sum(): share = lax.all_to_all(share, inner, 0, 0, tiled=True)]
    ppermute x6 -> x14, starting transfers between devices: 13.1 us -> 25.5 us  [the longest x7 16.5 us: from_owner(): got = lax.ppermute(block, axis, [(0, target)])]
    convert_element_type x4 -> x9, other arithmetic: 2.85 us -> 15.1 us  [the longest x7 13.7 us: to_owner(): total = total + got.astype(jnp.float32)]
    ppermute x6 -> x14, waiting for transfers between devices: 54.6 us -> 44.3 us  [the longest x7 24 us: to_owner(): got = lax.ppermute(block.astype(jnp.bfloat16), axis, [(source, 0)])]
  transfers between devices with their start and end apart: 12 -> 27, of which waited for: 9 -> 8; matrix products, arithmetic and copies ran while one was open for 11% -> 59% of each run, Pallas kernels for 0% -> 0%
where the time goes in v2:
time: 570 us; the launch traced here: 562 us
  matrix products  204 us (36%)
  local copies, waits for them, and re-layouts  82.2 us (14%)
  blocking collectives  72 us (13%)
  other arithmetic  66.2 us (12%)
  waiting for transfers between devices  62.3 us (11%)
  starting transfers between devices  60.4 us (11%)
  between operations  14.7 us (3%)
    unnamed x1, blocking collectives  72 us
    dot_general x1, matrix products, attend_back(): jnp.einsum('lfhst,lfshd->lfthd', grad_score, split_heads(queries), prefer...  43.3 us
    dot_general x1, matrix products, attend_back(): jnp.einsum('lfhst,lfthd->lfshd', grad_score, split_heads(key_all), prefer...  42.6 us
    ppermute x7, waiting for transfers between devices, to_owner(): got = lax.ppermute(block.astype(jnp.bfloat16), axis, [(source, 0)])  24 us
    another operation x8, local copies, waits for them, and re-layouts  22.4 us
    all_to_all x5, starting transfers between devices, scatter_sum(): share = lax.all_to_all(share, inner, 0, 0, tiled=True)  20.5 us
    ppermute x7, waiting for transfers between devices, from_owner(): got = lax.ppermute(block, axis, [(0, target)])  20.3 us
    dot_general x6, matrix products, gram_rows(): lax.dot_general(flat_left, flat_right, (((0,), (0,)), ((), ())), preferre...  20.1 us
  transfers between devices with their start and end apart: 27, of which 8 were waited for; matrix products, arithmetic and copies ran while one was open for 59% of the time, Pallas kernels for 0%

profile of v2, /device:TPU:0, one launch (start us, length us, event | category | flops | bytes accessed | tf_op | source)
XLA Modules:
  0.0 562.2 jit_solution(17484349653256234583)
XLA Ops:
  9.4 3.5 collective-permute-start.6
  12.9 2.2 collective-permute-start.5
  30.4 11.9 %collective-permute-done.5 = bf16[1,256,1280]{2,1,0:T(8,128)(2,1)S(1)} collective-permute-done((bf16[1,256,1280]{2,1,0:T(8,128)(2,1)}, bf16[1,256,1280]{2,1,0:T(8,128)(2,1)S(1)}, u32[]{:S(2)}, u32[]{:S(2)}) %collective-permute-start.5) | collective-permute-done | bytes 655392 | tf_op jit(solution)/shard_map/ppermute | solution.py:20
  53.0 2.6 fusion.167
  56.9 6.1 %collective-permute-start.10 = (bf16[1,1,256,1280]{3,2,1,0:T(8,128)(2,1)}, bf16[1,1,256,1280]{3,2,1,0:T(8,128)(2,1)}, u32[]{:S(2)}, u32[]{:S(2)}) collective-permute-start(bf16[1,1,256,1280]{3,2,1,0:T(8,128)(2,1)} %get-tuple-element.78), channel_id=1, source_target_pairs={{0,1},{1,2},{2,3},{3,4},{4,5},{5,6},{6,7},{8,9},{9,10},{10,11},{11... | collective-permute-start | bytes 1966088 | tf_op jit(solution)/shard_map/ppermute | solution.py:49
  63.0 7.5 %collective-permute-done.1 = bf16[1,256,1280]{2,1,0:T(8,128)(2,1)} collective-permute-done((bf16[1,256,1280]{2,1,0:T(8,128)(2,1)}, bf16[1,256,1280]{2,1,0:T(8,128)(2,1)}, u32[]{:S(2)}, u32[]{:S(2)}) %collective-permute-start.1) | collective-permute-done | bytes 655392 | tf_op jit(solution)/shard_map/ppermute | solution.py:20
  78.5 6.7 %fusion.130 = f32[2,10,256,512]{3,2,1,0:T(8,128)} fusion(bf16[2,256,10,64]{1,3,2,0:T(8,128)(2,1)} %bitcast.249, bf16[1,2,256,10,64]{2,4,3,1,0:T(8,128)(2,1)S(1)} %broadcast_in_dim.13, bf16[1,2,256,10,64]{2,4,3,1,0:T(8,128)(2,1)} %bitcast.251), kind=kOutput, calls=%fused_computation.136 | convolution fusion | flops 338165760 | bytes 12451840 | tf_op jit(solution)/shard_map/lfshd,lfthd->lfhst/dot_general | solution.py:79
  85.1 13.1 %fusion.169 = (f32[2,10,256]{2,1,0:T(8,128)S(1)}, f32[2,10,256,512]{3,2,1,0:T(8,128)}) fusion(f32[2,10,256,512]{3,2,1,0:T(8,128)} %fusion.130), kind=kOutput, calls=%fused_computation.172 | output fusion | flops 10486271 | bytes 20992000 | tf_op jit(solution)/shard_map/sub | solution.py:86
  99.2 17.7 %fusion.89 = bf16[2,10,64,256]{3,2,1,0:T(8,128)(2,1)} fusion(bf16[1,2,256,10,64]{2,4,3,1,0:T(8,128)(2,1)} %broadcast_in_dim.11, bf16[1,2,256,10,64]{2,4,3,1,0:T(8,128)(2,1)} %bitcast.253, f32[2,10,256]{2,1,0:T(8,128)S(1)} %get-tuple-element.83, f32[2,10,256,512]{3,2,1,0:T(8,128)} %fusion.130), kind=kOutput, calls=%fused_computation.95 | convolution fusion | flops 351606272 | bytes 12472320 | tf_op jit(solution)/shard_map/lfhst,lfthd->lfshd/dot_general | solution.py:89
  121.7 3.8 fusion.67
  127.6 9.7 %fusion.53 = bf16[1,2,256,1280]{3,2,1,0:T(8,128)(2,1)S(1)} fusion(bf16[1280,3,1280]{2,0,1:T(8,128)(2,1)} %param.18, bf16[1,2,256,1,1280]{4,2,3,1,0:T(8,128)(2,1)S(1)} %get-tuple-element.76, bf16[1,2,256,1,1280]{4,2,3,1,0:T(8,128)(2,1)S(1)} %bitcast.242, bf16[1,2,256,1,1280]{4,2,3,1,0:T(8,128)(2,1)S(1)} %get-tuple-element.75, ...), kind=kOutput, calls=%fused_computation.58 | convolution fusion | flops 5044961280 | bytes 17694720 | tf_op jit(solution)/shard_map/lfsjo,cjo->lfsc/dot_general | solution.py:179
  138.4 2.8 fusion.137
  141.3 3.4 fusion.101
  146.0 17.7 %fusion.70 = f32[2,10,64,512]{3,2,1,0:T(8,128)} fusion(bf16[2,256,10,64]{1,3,2,0:T(8,128)(2,1)S(1)} %bitcast.255, f32[2,10,256]{2,1,0:T(8,128)S(1)} %get-tuple-element.83, f32[2,10,256,512]{3,2,1,0:T(8,128)} %fusion.130), kind=kOutput, calls=%fused_computation.73 | convolution fusion | flops 348657152 | bytes 13783040 | tf_op jit(solution)/shard_map/lfhst,lfshd->lfthd/dot_general | solution.py:110
  167.8 2.8 convolution_bitcast_fusion
  170.6 4.2 convolution_add_fusion.1
  174.8 4.9 reshape.391
  179.8 2.8 copy.71
  182.6 3.6 dot_general.120
  186.3 6.7 %fusion.118 = f32[2,10,256,512]{3,2,1,0:T(8,128)} fusion(bf16[2,256,10,64]{1,3,2,0:T(8,128)(2,1)} %bitcast.256, bf16[2,256,10,64]{1,3,2,0:T(8,128)(2,1)S(1)} %broadcast_in_dim.14, bf16[2,256,10,64]{1,3,2,0:T(8,128)(2,1)} %bitcast.254), kind=kOutput, calls=%fused_computation.121 | convolution fusion | flops 338165760 | bytes 12451840 | tf_op jit(solution)/shard_map/lfshd,lfthd->lfhst/dot_general | solution.py:98
  193.0 42.6 %fusion.104 = bf16[2,10,64,256]{3,2,1,0:T(8,128)(2,1)} fusion(f32[2,10,256,512]{3,2,1,0:T(8,128)} %fusion.118, bf16[1,2,256,10,64]{2,4,3,1,0:T(8,128)(2,1)} %copy-done.27, bf16[1,2,256,10,64]{2,4,3,1,0:T(8,128)(2,1)} %bitcast.252, f32[2,10,256,512]{3,2,1,0:T(8,128)} %get-tuple-element.84, f32[2,10,256]{2,1,0:T(8,128)S(1)} %get-tuple-element.83), kind=kOutput, calls=%fused_computation.100 | convolution fusion | flops 356849152 | bytes 22958080 | tf_op jit(solution)/shard_map/lfhst,lfthd->lfshd/dot_general | solution.py:103
  237.8 3.4 fusion.128
  241.2 3.6 convert_element_type.200
  247.2 43.3 %fusion.16 = f32[2,10,64,512]{3,2,1,0:T(8,128)} fusion(bf16[2,256,10,64]{1,3,2,0:T(8,128)(2,1)} %bitcast.250, f32[2,10,256,512]{3,2,1,0:T(8,128)} %fusion.118, f32[2,10,256,512]{3,2,1,0:T(8,128)} %get-tuple-element.84, f32[2,10,256]{2,1,0:T(8,128)S(1)} %get-tuple-element.83), kind=kOutput, calls=%fused_computation.20 | convolution fusion | flops 353900032 | bytes 24268800 | tf_op jit(solution)/shard_map/lfhst,lfshd->lfthd/dot_general | solution.py:107
  290.6 2.2 slice.96
  302.6 2.2 copy.91
  304.7 2.8 convolution_bitcast_fusion.1
  307.5 4.1 convolution_add_fusion.2
  311.6 4.8 reshape.390
  316.5 3.0 fusion.80
  322.4 20.9 %collective-permute-done.17 = bf16[1,256,1280]{1,2,0:T(8,128)(2,1)} collective-permute-done((bf16[1,256,1280]{1,2,0:T(8,128)(2,1)}, bf16[1,256,1280]{1,2,0:T(8,128)(2,1)}, u32[]{:S(2)}, u32[]{:S(2)}) %collective-permute-start.17) | collective-permute-done | bytes 655392 | tf_op jit(solution)/shard_map/ppermute | solution.py:28
  350.4 2.3 convert_element_type.199
  352.7 2.2 convert_element_type.198
  355.0 5.4 collective-permute-start.7
  360.4 2.3 convert_element_type.197
  362.7 3.2 collective-permute-done.14
  367.4 2.3 convert_element_type.196
  369.7 2.2 convert_element_type.195
  374.2 35.6 %conditional.1 = (f32[1,1,256,1280]{3,2,1,0:T(8,128)}) conditional(s32[]{:T(128)} %convert_element_type.191, () %tuple.20, (f32[1,256,1280]{1,2,0:T(8,128)}, f32[1,256,1280]{1,2,0:T(8,128)}, f32[1,256,1280]{1,2,0:T(8,128)}, f32[1,256,1280]{1,2,0:T(8,128)}, f32[1,256,1280]{1,2,0:T(8,128)}, /*index=5*/f32[1,256,1280]{1,2,0:T(8,128)}, ...), branch_computations={%region_9.10_spmd, %region_10.11_spmd} | conditional | flops 5035786240 | bytes 70778944 | solution.py:213
  374.2 2.8 copy.70
  377.0 2.8 copy.69
  379.8 2.8 copy.68
  382.6 2.8 copy.67
  385.4 2.8 copy.66
  388.2 2.8 copy.65
  391.0 2.8 copy.64
  393.8 2.8 copy.63
  396.6 4.8 add_add_fusion
  401.6 3.4 fusion.1
  405.0 4.5 fusion
  409.8 3.2 fusion.111
  413.0 3.0 fusion.62
  416.1 72.0 %all-reduce = f32[16,8,10]{2,1,0:T(8,128)S(1)} all-reduce(f32[16,8,10]{2,1,0:T(8,128)S(1)} %reshape.393), channel_id=6, replica_groups=mesh['batch'=16,'tm'=8] {'batch'}, use_global_device_ids=true, to_apply=%region_22.23.clone | all-reduce | flops 1280 | bytes 10240
  489.4 3.3 all-to-all-start.4
  494.5 4.3 all-to-all-done.4
  498.8 3.4 all-to-all-start.3
  502.2 3.0 fusion.115
  505.3 4.5 all-to-all-done.3
  509.8 4.1 all-to-all-start.2
  513.9 10.7 %fusion.50 = bf16[1,2,256,1280]{3,2,1,0:T(8,128)(2,1)} fusion(bf16[1280,3,1280]{2,0,1:T(8,128)(2,1)} %param.18, bf16[1,2,256,1,1280]{4,2,1,3,0:T(8,128)(2,1)} %get-tuple-element.80, bf16[1,2,256,1,1280]{4,2,1,3,0:T(8,128)(2,1)S(1)} %bitcast.243, bf16[1,2,256,1,1280]{4,2,1,3,0:T(8,128)(2,1)} %get-tuple-element.79, bf16[1,2,256,1280]{3,2,1,0:T(8,128)(2,1)} %copy-done.39), kind=kOutput, calls=%fused_computation.57 | convolution fusion | flops 5039063040 | bytes 16384000 | tf_op jit(solution)/shard_map/lfsjc,cjo->lfso/dot_general | solution.py:174
  526.3 5.6 all-to-all-start
  531.9 9.0 %all-to-all-done = f32[8,10,640]{2,1,0:T(8,128)} async-done(((f32[8,10,640]{2,1,0:T(8,128)}), f32[8,10,640]{2,1,0:T(8,128)}, u32[]{:S(2)}, u32[]{:S(2)}) %all-to-all-start) | async-done | bytes 204832 | tf_op jit(solution)/shard_map/all_to_all | solution.py:37
  541.0 4.1 all-to-all-start.1
  545.1 4.4 fusion.61
  (176 shorter events, 91.0 us)
Async XLA Ops:
  7.2 114.6 %copy-start = (bf16[640,1280]{1,0:T(8,128)(2,1)S(1)}, bf16[640,1280]{1,0:T(8,128)(2,1)}, u32[]{:S(2)}) copy-start(bf16[640,1280]{1,0:T(8,128)(2,1)} %param.17) | copy-start | bytes 4915204
  7.2 14.4 %copy-start.2 = (bf16[1,2,256,1280]{3,2,1,0:T(8,128)(2,1)S(1)}, bf16[1,2,256,1280]{3,2,1,0:T(8,128)(2,1)}, u32[]{:S(2)}) copy-start(bf16[1,2,256,1280]{3,2,1,0:T(8,128)(2,1)} %param.12) | copy-start | bytes 3932164
  7.2 15.2 %copy-start.32 = (f32[1280]{0:T(1024)S(1)}, f32[1280]{0:T(1024)}, u32[]{:S(2)}) copy-start(f32[1280]{0:T(1024)} %param.13) | copy-start | bytes 15364
  7.2 485.5 %reduce-scatter.11.cloned.1.call-start = ((), (), s32[]{:S(2)}) async-start(), calls=%async_computation.12 | async-start | bytes 3481600 | tf_op jit(solution)/shard_map/reduce_scatter | solution.py:36
  9.4 18.9 %collective-permute-start.6 = (bf16[1,256,1280]{2,1,0:T(8,128)(2,1)}, bf16[1,256,1280]{2,1,0:T(8,128)(2,1)S(1)}, u32[]{:S(2)}, u32[]{:S(2)}) collective-permute-start(bf16[1,256,1280]{2,1,0:T(8,128)(2,1)} %slice_bitcast_fusion.5), channel_id=1, source_target_pairs={{0,1},{8,9},{16,17},{24,25},{32,33},{40,41},{48,49},{56,57},{64,65... | collective-permute-start | bytes 1966088 | tf_op jit(solution)/shard_map/ppermute | solution.py:20
  12.9 29.4 %collective-permute-start.5 = (bf16[1,256,1280]{2,1,0:T(8,128)(2,1)}, bf16[1,256,1280]{2,1,0:T(8,128)(2,1)S(1)}, u32[]{:S(2)}, u32[]{:S(2)}) collective-permute-start(bf16[1,256,1280]{2,1,0:T(8,128)(2,1)} %slice_bitcast_fusion.5), channel_id=1, source_target_pairs={{0,2},{8,10},{16,18},{24,26},{32,34},{40,42},{48,50},{56,58},{64,6... | collective-permute-start | bytes 1966088 | tf_op jit(solution)/shard_map/ppermute | solution.py:20
  15.2 40.5 %collective-permute-start.4 = (bf16[1,256,1280]{2,1,0:T(8,128)(2,1)}, bf16[1,256,1280]{2,1,0:T(8,128)(2,1)}, u32[]{:S(2)}, u32[]{:S(2)}) collective-permute-start(bf16[1,256,1280]{2,1,0:T(8,128)(2,1)} %slice_bitcast_fusion.5), channel_id=1, source_target_pairs={{0,3},{8,11},{16,19},{24,27},{32,35},{40,43},{48,51},{56,59},{64,6... | collective-permute-start | bytes 1966088 | tf_op jit(solution)/shard_map/ppermute | solution.py:20
  17.3 39.6 %collective-permute-start.3 = (bf16[1,256,1280]{2,1,0:T(8,128)(2,1)}, bf16[1,256,1280]{2,1,0:T(8,128)(2,1)}, u32[]{:S(2)}, u32[]{:S(2)}) collective-permute-start(bf16[1,256,1280]{2,1,0:T(8,128)(2,1)} %slice_bitcast_fusion.5), channel_id=1, source_target_pairs={{0,4},{8,12},{16,20},{24,28},{32,36},{40,44},{48,52},{56,60},{64,6... | collective-permute-start | bytes 1966088 | tf_op jit(solution)/shard_map/ppermute | solution.py:20
  19.5 43.5 %collective-permute-start.2 = (bf16[1,256,1280]{2,1,0:T(8,128)(2,1)}, bf16[1,256,1280]{2,1,0:T(8,128)(2,1)}, u32[]{:S(2)}, u32[]{:S(2)}) collective-permute-start(bf16[1,256,1280]{2,1,0:T(8,128)(2,1)} %slice_bitcast_fusion.5), channel_id=1, source_target_pairs={{0,5},{8,13},{16,21},{24,29},{32,37},{40,45},{48,53},{56,61},{64,6... | collective-permute-start | bytes 1966088 | tf_op jit(solution)/shard_map/ppermute | solution.py:20
  21.8 1.4 copy-start.37
  21.9 1.0 copy-start.33
  23.3 21.2 %copy-start.22 = (bf16[1,2,256,1280]{3,2,1,0:T(8,128)(2,1)}, bf16[1,2,256,1280]{3,2,1,0:T(8,128)(2,1)S(1)}, u32[]{:S(2)}) copy-start(bf16[1,2,256,1280]{3,2,1,0:T(8,128)(2,1)S(1)} %fusion.56) | copy-start | bytes 3932164
  23.3 2.1 copy-start.11
  25.3 19.1 %copy-start.14 = (bf16[1280,640]{1,0:T(8,128)(2,1)S(1)}, bf16[1280,640]{1,0:T(8,128)(2,1)}, u32[]{:S(2)}) copy-start(bf16[1280,640]{1,0:T(8,128)(2,1)} %param.16) | copy-start | bytes 4915204
  28.3 18.2 %copy-start.28 = (bf16[1,256,1280]{2,1,0:T(8,128)(2,1)}, bf16[1,256,1280]{2,1,0:T(8,128)(2,1)S(1)}, u32[]{:S(2)}) copy-start(bf16[1,256,1280]{2,1,0:T(8,128)(2,1)S(1)} %collective-permute-done.6) | copy-start | bytes 1966084
  28.3 42.2 %collective-permute-start.1 = (bf16[1,256,1280]{2,1,0:T(8,128)(2,1)}, bf16[1,256,1280]{2,1,0:T(8,128)(2,1)}, u32[]{:S(2)}, u32[]{:S(2)}) collective-permute-start(bf16[1,256,1280]{2,1,0:T(8,128)(2,1)} %slice_bitcast_fusion.5), channel_id=1, source_target_pairs={{0,6},{8,14},{16,22},{24,30},{32,38},{40,46},{48,54},{56,62},{64,7... | collective-permute-start | bytes 1966088 | tf_op jit(solution)/shard_map/ppermute | solution.py:20
  42.3 4.2 copy-start.30
  42.3 28.1 %collective-permute-start = (bf16[1,256,1280]{2,1,0:T(8,128)(2,1)}, bf16[1,256,1280]{2,1,0:T(8,128)(2,1)}, u32[]{:S(2)}, u32[]{:S(2)}) collective-permute-start(bf16[1,256,1280]{2,1,0:T(8,128)(2,1)} %slice_bitcast_fusion.5), channel_id=1, source_target_pairs={{0,7},{8,15},{16,23},{24,31},{32,39},{40,47},{48,55},{56,63},{64,7... | collective-permute-start | bytes 1966088 | tf_op jit(solution)/shard_map/ppermute | solution.py:20
  53.0 17.4 %copy-start.29 = (bf16[1,256,1280]{2,1,0:T(8,128)(2,1)S(1)}, bf16[1,256,1280]{2,1,0:T(8,128)(2,1)}, u32[]{:S(2)}) copy-start(bf16[1,256,1280]{2,1,0:T(8,128)(2,1)} %copy-done.28) | copy-start | bytes 1966084
  53.0 17.4 %copy-start.31 = (bf16[1,256,1280]{2,1,0:T(8,128)(2,1)S(1)}, bf16[1,256,1280]{2,1,0:T(8,128)(2,1)}, u32[]{:S(2)}) copy-start(bf16[1,256,1280]{2,1,0:T(8,128)(2,1)} %copy-done.30) | copy-start | bytes 1966084
  55.6 69.9 %collective-permute-start.9 = (bf16[1,1,256,1280]{3,2,1,0:T(8,128)(2,1)}, bf16[1,1,256,1280]{3,2,1,0:T(8,128)(2,1)}, u32[]{:S(2)}, u32[]{:S(2)}) collective-permute-start(bf16[1,1,256,1280]{3,2,1,0:T(8,128)(2,1)} %get-tuple-element.77), channel_id=1, source_target_pairs={{1,0},{2,1},{3,2},{4,3},{5,4},{6,5},{7,6},{9,8},{10,9},{11,10},{12... | collective-permute-start | bytes 1966088 | tf_op jit(solution)/shard_map/ppermute | solution.py:50
  56.9 14.8 %copy-start.12 = (bf16[1280,640]{1,0:T(8,128)(2,1)S(1)}, bf16[1280,640]{1,0:T(8,128)(2,1)}, u32[]{:S(2)}) copy-start(bf16[1280,640]{1,0:T(8,128)(2,1)} %param.15) | copy-start | bytes 4915204
  56.9 68.6 %collective-permute-start.10 = (bf16[1,1,256,1280]{3,2,1,0:T(8,128)(2,1)}, bf16[1,1,256,1280]{3,2,1,0:T(8,128)(2,1)}, u32[]{:S(2)}, u32[]{:S(2)}) collective-permute-start(bf16[1,1,256,1280]{3,2,1,0:T(8,128)(2,1)} %get-tuple-element.78), channel_id=1, source_target_pairs={{0,1},{1,2},{2,3},{3,4},{4,5},{5,6},{6,7},{8,9},{9,10},{10,11},{11... | collective-permute-start | bytes 1966088 | tf_op jit(solution)/shard_map/ppermute | solution.py:49
  71.4 1.1 copy-start.6
  71.4 1.7 copy-start.15
  121.7 3.8 copy-start.19
  125.6 2.1 copy-start.39
  127.6 10.8 %copy-start.23 = (bf16[16,8,5,512]{3,2,1,0:T(8,128)(2,1)S(1)}, bf16[16,8,5,512]{3,2,1,0:T(8,128)(2,1)}, u32[]{:S(2)}) copy-start(bf16[16,8,5,512]{3,2,1,0:T(8,128)(2,1)} %dot_general.127) | copy-start | bytes 1966084
  137.3 1.0 copy-start.21
  141.2 364.0 %reduce-scatter.9.cloned.1.call-start = ((), (), s32[]{:S(2)}) async-start(), calls=%async_computation.11 | async-start | bytes 5570560 | tf_op jit(solution)/shard_map/reduce_scatter | solution.py:36
  146.0 17.7 %copy-start.25 = (bf16[2,256,640]{1,2,0:T(8,128)(2,1)}, bf16[2,256,640]{1,2,0:T(8,128)(2,1)S(1)}, u32[]{:S(2)}) copy-start(bf16[2,256,640]{1,2,0:T(8,128)(2,1)S(1)} %copy.58) | copy-start | bytes 1966084
  167.8 2.8 copy-start.7
  179.8 344.9 %reduce-scatter.5.cloned.1.call-start = ((), (), s32[]{:S(2)}) async-start(), calls=%async_computation.9 | async-start | bytes 3481600 | tf_op jit(solution)/shard_map/reduce_scatter | solution.py:36
  235.7 2.1 copy-start.18
  241.2 290.8 %reduce-scatter.7.cloned.1.call-start = ((), (), s32[]{:S(2)}) async-start(), calls=%async_computation.10 | async-start | bytes 5570560 | tf_op jit(solution)/shard_map/reduce_scatter | solution.py:36
  241.2 3.6 copy-start.16
  244.8 1.9 copy-start.38
  296.1 47.1 %collective-permute-start.17 = (bf16[1,256,1280]{1,2,0:T(8,128)(2,1)}, bf16[1,256,1280]{1,2,0:T(8,128)(2,1)}, u32[]{:S(2)}, u32[]{:S(2)}) collective-permute-start(bf16[1,256,1280]{1,2,0:T(8,128)(2,1)} %fusion.154), channel_id=1, source_target_pairs={{7,0},{15,8},{23,16},{31,24},{39,32},{47,40},{55,48},{63,56},{71,6... | collective-permute-start | bytes 1966088 | tf_op jit(solution)/shard_map/ppermute | solution.py:28
  297.4 47.2 %collective-permute-start.16 = (bf16[1,256,1280]{1,2,0:T(8,128)(2,1)}, bf16[1,256,1280]{1,2,0:T(8,128)(2,1)}, u32[]{:S(2)}, u32[]{:S(2)}) collective-permute-start(bf16[1,256,1280]{1,2,0:T(8,128)(2,1)} %fusion.154), channel_id=1, source_target_pairs={{6,0},{14,8},{22,16},{30,24},{38,32},{46,40},{54,48},{62,56},{70,6... | collective-permute-start | bytes 1966088 | tf_op jit(solution)/shard_map/ppermute | solution.py:28
  298.7 56.3 %collective-permute-start.15 = (bf16[1,256,1280]{1,2,0:T(8,128)(2,1)}, bf16[1,256,1280]{1,2,0:T(8,128)(2,1)}, u32[]{:S(2)}, u32[]{:S(2)}) collective-permute-start(bf16[1,256,1280]{1,2,0:T(8,128)(2,1)} %fusion.154), channel_id=1, source_target_pairs={{5,0},{13,8},{21,16},{29,24},{37,32},{45,40},{53,48},{61,56},{69,6... | collective-permute-start | bytes 1966088 | tf_op jit(solution)/shard_map/ppermute | solution.py:28
  300.0 65.9 %collective-permute-start.14 = (bf16[1,256,1280]{1,2,0:T(8,128)(2,1)}, bf16[1,256,1280]{1,2,0:T(8,128)(2,1)}, u32[]{:S(2)}, u32[]{:S(2)}) collective-permute-start(bf16[1,256,1280]{1,2,0:T(8,128)(2,1)} %fusion.154), channel_id=1, source_target_pairs={{4,0},{12,8},{20,16},{28,24},{36,32},{44,40},{52,48},{60,56},{68,6... | collective-permute-start | bytes 1966088 | tf_op jit(solution)/shard_map/ppermute | solution.py:28
  301.3 68.4 %collective-permute-start.13 = (bf16[1,256,1280]{1,2,0:T(8,128)(2,1)}, bf16[1,256,1280]{1,2,0:T(8,128)(2,1)}, u32[]{:S(2)}, u32[]{:S(2)}) collective-permute-start(bf16[1,256,1280]{1,2,0:T(8,128)(2,1)} %fusion.154), channel_id=1, source_target_pairs={{3,0},{11,8},{19,16},{27,24},{35,32},{43,40},{51,48},{59,56},{67,6... | collective-permute-start | bytes 1966088 | tf_op jit(solution)/shard_map/ppermute | solution.py:28
  304.7 2.8 copy-start.9
  316.5 3.0 copy-start.13
  316.5 3.0 copy-start.26
  319.5 1.4 copy-start.17
  319.6 1.6 copy-start.24
  321.1 24.7 %copy-start.10 = (f32[256,640]{0,1:T(8,128)S(1)}, f32[256,640]{0,1:T(8,128)}, u32[]{:S(2)}) copy-start(f32[256,640]{0,1:T(8,128)} %copy-done.8) | copy-start | bytes 1966084
  322.4 26.2 %copy-start.3 = (f32[2,256,1280]{2,1,0:T(8,128)}, f32[2,256,1280]{2,1,0:T(8,128)S(1)}, u32[]{:S(2)}) copy-start(f32[2,256,1280]{2,1,0:T(8,128)S(1)} %convolution_add_fusion.3) | copy-start | bytes 7864324
  343.2 28.7 %collective-permute-start.12 = (bf16[1,256,1280]{1,2,0:T(8,128)(2,1)}, bf16[1,256,1280]{1,2,0:T(8,128)(2,1)S(1)}, u32[]{:S(2)}, u32[]{:S(2)}) collective-permute-start(bf16[1,256,1280]{1,2,0:T(8,128)(2,1)} %fusion.154), channel_id=1, source_target_pairs={{2,0},{10,8},{18,16},{26,24},{34,32},{42,40},{50,48},{58,56},{66,6... | collective-permute-start | bytes 1966088 | tf_op jit(solution)/shard_map/ppermute | solution.py:28
  344.5 28.6 %collective-permute-start.11 = (bf16[1,256,1280]{1,2,0:T(8,128)(2,1)}, bf16[1,256,1280]{1,2,0:T(8,128)(2,1)S(1)}, u32[]{:S(2)}, u32[]{:S(2)}) collective-permute-start(bf16[1,256,1280]{1,2,0:T(8,128)(2,1)} %fusion.154), channel_id=1, source_target_pairs={{1,0},{9,8},{17,16},{25,24},{33,32},{41,40},{49,48},{57,56},{65,64... | collective-permute-start | bytes 1966088 | tf_op jit(solution)/shard_map/ppermute | solution.py:28
  347.0 2.3 copy-start.20
  355.0 147.2 %collective-permute-start.7 = (bf16[1,1,256,1280]{3,2,1,0:T(8,128)(2,1)}, bf16[1,1,256,1280]{3,2,1,0:T(8,128)(2,1)}, u32[]{:S(2)}, u32[]{:S(2)}) collective-permute-start(bf16[1,1,256,1280]{3,2,1,0:T(8,128)(2,1)} %get-tuple-element.81), channel_id=1, source_target_pairs={{0,1},{1,2},{2,3},{3,4},{4,5},{5,6},{6,7},{8,9},{9,10},{10,11},{11... | collective-permute-start | bytes 1966088 | tf_op jit(solution)/shard_map/ppermute | solution.py:49
  365.9 136.3 %collective-permute-start.8 = (bf16[1,1,256,1280]{3,2,1,0:T(8,128)(2,1)}, bf16[1,1,256,1280]{3,2,1,0:T(8,128)(2,1)}, u32[]{:S(2)}, u32[]{:S(2)}) collective-permute-start(bf16[1,1,256,1280]{3,2,1,0:T(8,128)(2,1)} %get-tuple-element.82), channel_id=1, source_target_pairs={{1,0},{2,1},{3,2},{4,3},{5,4},{6,5},{7,6},{9,8},{10,9},{11,10},{12... | collective-permute-start | bytes 1966088 | tf_op jit(solution)/shard_map/ppermute | solution.py:50
  396.6 5.0 copy-start.4
  401.6 3.4 copy-start.5
  409.8 3.2 copy-start.34
  409.8 3.2 copy-start.36
  489.4 9.4 %all-to-all-start.4 = ((f32[8,1,10]{2,1,0:T(1,128)}), f32[8,1,10]{2,1,0:T(1,128)S(1)}, u32[]{:S(2)}, u32[]{:S(2)}) async-start(f32[8,1,10]{2,1,0:T(1,128)} %bitcast.74), calls=%async_computation.8 | async-start | bytes 8192 | tf_op jit(solution)/shard_map/all_to_all | solution.py:37
  498.8 11.1 %all-to-all-start.3 = ((f32[8,5,1280]{2,1,0:T(8,128)}), f32[8,5,1280]{2,1,0:T(8,128)S(1)}, u32[]{:S(2)}, u32[]{:S(2)}) async-start(f32[8,5,1280]{2,1,0:T(8,128)} %copy.80), calls=%async_computation.7 | async-start | bytes 655360 | tf_op jit(solution)/shard_map/all_to_all | solution.py:37
  509.8 16.5 %all-to-all-start.2 = ((f32[8,10,640]{2,1,0:T(8,128)}), f32[8,10,640]{2,1,0:T(8,128)}, u32[]{:S(2)}, u32[]{:S(2)}) async-start(f32[8,10,640]{2,1,0:T(8,128)} %bitcast.270), calls=%async_computation.5 | async-start | bytes 655360 | tf_op jit(solution)/shard_map/all_to_all | solution.py:37
  526.3 14.6 %all-to-all-start = ((f32[8,10,640]{2,1,0:T(8,128)}), f32[8,10,640]{2,1,0:T(8,128)}, u32[]{:S(2)}, u32[]{:S(2)}) async-start(f32[8,10,640]{2,1,0:T(8,128)} %copy.75), calls=%async_computation.1 | async-start | bytes 655360 | tf_op jit(solution)/shard_map/all_to_all | solution.py:37
  541.0 12.9 %all-to-all-start.1 = ((f32[8,10,640]{2,1,0:T(8,128)}), f32[8,10,640]{2,1,0:T(8,128)}, u32[]{:S(2)}, u32[]{:S(2)}) async-start(f32[8,10,640]{2,1,0:T(8,128)} %bitcast.271), calls=%async_computation.3 | async-start | bytes 655360 | tf_op jit(solution)/shard_map/all_to_all | solution.py:37
  545.0 10.4 %copy-start.1 = (bf16[640,1280]{1,0:T(8,128)(2,1)S(1)}, bf16[640,1280]{1,0:T(8,128)(2,1)}, u32[]{:S(2)}) copy-start(bf16[640,1280]{1,0:T(8,128)(2,1)} %param.17) | copy-start | bytes 4915204
  (3 other events, 2.3 us)
Sparse Core Ops, SparseCore 0:
  141.4 80.6 reduce-scatter.10
  226.1 84.2 reduce-scatter.8
  314.5 81.3 reduce-scatter.4
  399.9 84.2 reduce-scatter.6

commit v3 on v2

--- a/solution.py
+++ b/solution.py
@@ -10,7 +10,6 @@
 
 
 eps_norm = 1e-05
-highest = lax.Precision.HIGHEST
 
 
 def from_owner(block, axis):
@@ -30,13 +29,28 @@
     return total
 
 
-def scatter_sum(value, outer, inner):
+def scatter_sum(parts, outer, inner):
     count = lax.axis_size(outer) * lax.axis_size(inner)
-    share = value.reshape((lax.axis_size(outer), lax.axis_size(inner), -1) + value.shape[1:])
-    share = lax.psum_scatter(share, outer, scatter_dimension=0, tiled=True)[0]
-    share = lax.all_to_all(share, inner, 0, 0, tiled=True)
-    share = jnp.sum(share, axis=0)
-    return share.reshape((value.shape[0] // count,) + value.shape[1:])
+    packed = jnp.concatenate([p.reshape(count, -1) for p in parts], axis=1)
+    share = packed.reshape((lax.axis_size(outer), lax.axis_size(inner), -1))
+    share = lax.psum_scatter(share, inner, scatter_dimension=1, tiled=True)
+    share = lax.all_to_all(share, outer, 0, 0, tiled=True)
+    share = jnp.sum(share, axis=(0, 1))
+    outs, start = [], 0
+    for p in parts:
+        width = p.size // count
+        outs.append(share[start : start + width].reshape((p.shape[0] // count,) + p.shape[1:]))
+        start += width
+    return outs
+
+
+def split_dot(wide, narrow, dims):
+    high = wide.astype(jnp.bfloat16)
+    low = (wide - high.astype(jnp.float32)).astype(jnp.bfloat16)
+    return sum(
+        lax.dot_general(part, narrow, dims, preferred_element_type=jnp.float32)
+        for part in (high, low)
+    )
 
 
 def padded_2(value, sides, width):
@@ -143,14 +157,6 @@
     )
 
 
-def first_terms(normed_first, key_grad, val_grad, key_wide, val_wide):
-    rows = jnp.einsum("lsh,ch->lsc", key_grad, key_wide, precision=highest)
-    rows = rows + jnp.einsum("lsh,ch->lsc", val_grad, val_wide, precision=highest)
-    extra_key = gram_rows(normed_first.astype(jnp.float32), key_grad, highest)
-    extra_val = gram_rows(normed_first.astype(jnp.float32), val_grad, highest)
-    return (rows, extra_key, extra_val)
-
-
 def on_device(x_in, norm_gain, w_query, w_key, w_value, w_out, w_time, cotangent):
     frames = x_in.shape[1]
     is_owner = lax.axis_index("tm") == 0
@@ -198,21 +204,20 @@
     grad_normed = grad_normed + jnp.einsum(
         "lfsh,ch->lfsc", val_b, w_value, preferred_element_type=jnp.float32
     )
-    key_wide = w_key.astype(jnp.float32)
-    val_wide = w_value.astype(jnp.float32)
     first_sum = to_owner(jnp.concatenate([key_first_grad, val_first_grad], axis=-1), "tm")
     width = key_first_grad.shape[-1]
 
     def owner_terms(operands):
-        rows = jnp.einsum("lsh,ch->lsc", operands[..., :width], key_wide, precision=highest)
-        return rows + jnp.einsum("lsh,ch->lsc", operands[..., width:], val_wide, precision=highest)
+        both = jnp.concatenate([w_key, w_value], axis=1)
+        return split_dot(operands, both, (((2,), (1,)), ((), ())))
 
     def no_terms(operands):
         return jnp.zeros(normed_first.shape, jnp.float32)
 
     first_rows = lax.cond(is_owner, owner_terms, no_terms, first_sum)
-    extra_key = gram_rows(normed_first.astype(jnp.float32), key_first_grad, highest)
-    extra_val = gram_rows(normed_first.astype(jnp.float32), val_first_grad, highest)
+    first_flat = normed_first.reshape(-1, normed_first.shape[-1])
+    extra_key = split_dot(key_first_grad.reshape(-1, width), first_flat, (((0,), (0,)), ((), ()))).T
+    extra_val = split_dot(val_first_grad.reshape(-1, width), first_flat, (((0,), (0,)), ((), ()))).T
     grad_normed = grad_normed.at[:, 0].add(first_rows)
     grad_wq = gram_rows(normed, grad_queries)
     grad_wk = gram_rows(normed, key_b) + extra_key
@@ -225,13 +230,9 @@
         - x_hat * jnp.mean(grad_hat * x_hat, axis=-1, keepdims=True)
     )
     grad_input = (grad_hidden.astype(jnp.float32) + grad_x).astype(jnp.bfloat16)
-    grad_wq, grad_wk, grad_wv, grad_out = (
-        scatter_sum(grad_wq, "batch", "tm"),
-        scatter_sum(grad_wk, "batch", "tm"),
-        scatter_sum(grad_wv, "batch", "tm"),
-        scatter_sum(grad_out, "batch", "tm"),
-    )
-    grad_gain = scatter_sum(grad_gain, "batch", "tm")
+    grad_wq, grad_wk, grad_wv, grad_out, grad_gain = scatter_sum(
+        (grad_wq, grad_wk, grad_wv, grad_out, grad_gain), "batch", "tm"
+    )
     return (output, grad_input, grad_wq, grad_wk, grad_wv, grad_out, grad_gain)
 
 

time: 570 us -> 588 us (1.032)
  waiting for transfers between devices: 62.3 us -> 168 us
  blocking collectives: 72 us -> 0 us
  starting transfers between devices: 60.4 us -> 44 us
  other arithmetic: 66.2 us -> 55.7 us
  local copies, waits for them, and re-layouts: 82.2 us -> 92.7 us
    reduce_scatter x4 -> x1, waiting for transfers between devices: 0.04 us -> 137 us  [scatter_sum(): share = lax.psum_scatter(share, inner, scatter_dimension=1, tiled=True)]
    unnamed x1 -> x0, blocking collectives: 72 us -> none
    ppermute x7, waiting for transfers between devices: 24 us -> 0.02 us  [to_owner(): got = lax.ppermute(block.astype(jnp.bfloat16), axis, [(source, 0)])]
    concatenate x0 -> x7, local copies, waits for them, and re-layouts: none -> 20.7 us  [the longest x6 19 us: scatter_sum(): packed = jnp.concatenate([p.reshape(count, -1) for p in parts], axis=1)]
    all_to_all x5 -> x1, starting transfers between devices: 20.5 us -> 8.09 us  [scatter_sum(): share = lax.all_to_all(share, outer, 0, 0, tiled=True)]
    reshape x4, local copies, waits for them, and re-layouts: 12.7 us -> 2.49 us  [scatter_sum(): share[start:start + width].reshape((p.shape[0] // count,) + p.shape[1:])]
    dot_general x2 -> x6, matrix products: 7.96 us -> 16.9 us  [split_dot(): lax.dot_general(part, narrow, dims, preferred_element_type=jnp.float32)]
    unnamed x83 -> x91, local copies, waits for them, and re-layouts: 12.5 us -> 21.1 us
  transfers between devices with their start and end apart: 27 -> 20, of which waited for: 8 -> 5; matrix products, arithmetic and copies ran while one was open for 59% -> 28% of each run, Pallas kernels for 0% -> 0%
where the time goes in v3:
time: 588 us; the launch traced here: 581 us
  matrix products  206 us (35%)
  waiting for transfers between devices  168 us (29%)
  local copies, waits for them, and re-layouts  92.7 us (16%)
  other arithmetic  55.7 us (9%)
  starting transfers between devices  44 us (7%)
  between operations  15.1 us (3%)
    reduce_scatter x1, waiting for transfers between devices, scatter_sum(): share = lax.psum_scatter(share, inner, scatter_dimension=1, tiled=True)  137 us
    dot_general x1, matrix products, attend_back(): jnp.einsum('lfhst,lfshd->lfthd', grad_score, split_heads(queries), prefer...  43.3 us
    dot_general x1, matrix products, attend_back(): jnp.einsum('lfhst,lfthd->lfshd', grad_score, split_heads(key_all), prefer...  42.5 us
    unnamed x91, local copies, waits for them, and re-layouts  21.1 us
    another operation x8, local copies, waits for them, and re-layouts  21 us
    concatenate x6, local copies, waits for them, and re-layouts, scatter_sum(): packed = jnp.concatenate([p.reshape(count, -1) for p in parts], axis=1)  19 us
    ppermute x7, waiting for transfers between devices, from_owner(): got = lax.ppermute(block, axis, [(0, target)])  18.4 us
    dot_general x1, matrix products, attend_back(): jnp.einsum('lfhst,lfshd->lfthd', prob_b, grad_heads, preferred_element_ty...  17.8 us
  transfers between devices with their start and end apart: 20, of which 5 were waited for; matrix products, arithmetic and copies ran while one was open for 28% of the time, Pallas kernels for 0%

profile of v3, /device:TPU:0, one launch (start us, length us, event | category | flops | bytes accessed | tf_op | source)
XLA Modules:
  0.0 581.1 jit_solution(3945494671595582840)
XLA Ops:
  9.4 3.5 collective-permute-start.6
  12.9 2.2 collective-permute-start.5
  19.4 2.2 collective-permute-start.2
  23.7 2.2 fusion.110
  30.4 11.9 %collective-permute-done.5 = bf16[1,256,1280]{2,1,0:T(8,128)(2,1)S(1)} collective-permute-done((bf16[1,256,1280]{2,1,0:T(8,128)(2,1)}, bf16[1,256,1280]{2,1,0:T(8,128)(2,1)S(1)}, u32[]{:S(2)}, u32[]{:S(2)}) %collective-permute-start.5) | collective-permute-done | bytes 655392 | tf_op jit(solution)/shard_map/ppermute | solution.py:19
  44.5 3.6 fusion.104
  48.1 2.2 copy.81
  50.3 2.2 copy.80
  52.5 2.2 copy.78
  54.6 2.6 fusion.185
  58.5 5.7 collective-permute-start.10
  64.2 6.2 %collective-permute-done.1 = bf16[1,256,1280]{2,1,0:T(8,128)(2,1)} collective-permute-done((bf16[1,256,1280]{2,1,0:T(8,128)(2,1)}, bf16[1,256,1280]{2,1,0:T(8,128)(2,1)}, u32[]{:S(2)}, u32[]{:S(2)}) %collective-permute-start.1) | collective-permute-done | bytes 655392 | tf_op jit(solution)/shard_map/ppermute | solution.py:19
  72.5 2.9 convolution_convert_fusion.1
  79.4 6.7 %fusion.137 = f32[2,10,256,512]{3,2,1,0:T(8,128)} fusion(bf16[2,256,10,64]{1,3,2,0:T(8,128)(2,1)} %bitcast.220, bf16[1,2,256,10,64]{2,4,3,1,0:T(8,128)(2,1)S(1)} %broadcast_in_dim.13, bf16[1,2,256,10,64]{2,4,3,1,0:T(8,128)(2,1)} %bitcast.222), kind=kOutput, calls=%fused_computation.149 | convolution fusion | flops 338165760 | bytes 12451840 | tf_op jit(solution)/shard_map/lfshd,lfthd->lfhst/dot_general | solution.py:93
  86.1 13.2 %fusion.188 = (f32[2,10,256]{2,1,0:T(8,128)S(1)}, f32[2,10,256,512]{3,2,1,0:T(8,128)}) fusion(f32[2,10,256,512]{3,2,1,0:T(8,128)} %fusion.137), kind=kOutput, calls=%fused_computation.191 | output fusion | flops 10486271 | bytes 20992000 | tf_op jit(solution)/shard_map/sub | solution.py:100
  100.2 17.7 %fusion.101 = bf16[2,10,64,256]{3,2,1,0:T(8,128)(2,1)} fusion(bf16[1,2,256,10,64]{2,4,3,1,0:T(8,128)(2,1)} %broadcast_in_dim.11, bf16[1,2,256,10,64]{2,4,3,1,0:T(8,128)(2,1)} %bitcast.224, f32[2,10,256]{2,1,0:T(8,128)S(1)} %get-tuple-element.83, f32[2,10,256,512]{3,2,1,0:T(8,128)} %fusion.137), kind=kOutput, calls=%fused_computation.113 | convolution fusion | flops 351606272 | bytes 12472320 | tf_op jit(solution)/shard_map/lfhst,lfthd->lfshd/dot_general | solution.py:103
  118.0 3.8 fusion.79
  123.8 9.6 %fusion.65 = bf16[1,2,256,1280]{3,2,1,0:T(8,128)(2,1)S(1)} fusion(bf16[1280,3,1280]{2,0,1:T(8,128)(2,1)} %param.18, bf16[1,2,256,1,1280]{4,2,3,1,0:T(8,128)(2,1)S(1)} %get-tuple-element.72, bf16[1,2,256,1,1280]{4,2,3,1,0:T(8,128)(2,1)S(1)} %bitcast.216, bf16[1,2,256,1,1280]{4,2,3,1,0:T(8,128)(2,1)S(1)} %get-tuple-element.71, ...), kind=kOutput, calls=%fused_computation.76 | convolution fusion | flops 5044961280 | bytes 17694720 | tf_op jit(solution)/shard_map/lfsjo,cjo->lfsc/dot_general | solution.py:185
  137.9 17.8 %fusion.82 = f32[2,10,64,512]{3,2,1,0:T(8,128)} fusion(bf16[2,256,10,64]{1,3,2,0:T(8,128)(2,1)S(1)} %bitcast.226, f32[2,10,256]{2,1,0:T(8,128)S(1)} %get-tuple-element.83, f32[2,10,256,512]{3,2,1,0:T(8,128)} %fusion.137), kind=kOutput, calls=%fused_computation.91 | convolution fusion | flops 348657152 | bytes 13783040 | tf_op jit(solution)/shard_map/lfhst,lfshd->lfthd/dot_general | solution.py:124
  157.3 2.2 slice.109
  159.5 2.7 convolution_bitcast_fusion
  162.4 5.4 fusion.131
  167.8 42.5 %fusion.116 = bf16[2,10,64,256]{3,2,1,0:T(8,128)(2,1)} fusion(f32[2,10,256,512]{3,2,1,0:T(8,128)} %fusion.131, bf16[1,2,256,10,64]{2,4,3,1,0:T(8,128)(2,1)} %copy-done.28, bf16[1,2,256,10,64]{2,4,3,1,0:T(8,128)(2,1)} %bitcast.223, f32[2,10,256,512]{3,2,1,0:T(8,128)} %get-tuple-element.84, f32[2,10,256]{2,1,0:T(8,128)S(1)} %get-tuple-element.83), kind=kOutput, calls=%fused_computation.118 | convolution fusion | flops 356849152 | bytes 22958080 | tf_op jit(solution)/shard_map/lfhst,lfthd->lfshd/dot_general | solution.py:117
  210.3 43.3 %fusion.26 = f32[2,10,64,512]{3,2,1,0:T(8,128)} fusion(bf16[2,256,10,64]{1,3,2,0:T(8,128)(2,1)S(1)} %bitcast.221, f32[2,10,256,512]{3,2,1,0:T(8,128)} %fusion.131, f32[2,10,256,512]{3,2,1,0:T(8,128)} %get-tuple-element.84, f32[2,10,256]{2,1,0:T(8,128)S(1)} %get-tuple-element.83), kind=kOutput, calls=%fused_computation.30 | convolution fusion | flops 353900032 | bytes 24268800 | tf_op jit(solution)/shard_map/lfhst,lfshd->lfthd/dot_general | solution.py:121
  255.2 2.4 slice.108
  257.7 2.6 fusion.148
  267.7 2.6 fusion.151
  270.3 2.2 copy.116
  272.5 4.7 concatenate.75
  277.2 2.6 convolution_bitcast_fusion.1
  279.9 2.6 fusion.39
  282.5 4.4 concatenate.74
  286.9 2.2 copy.115
  289.1 4.2 convolution_bitcast_fusion.2
  293.3 3.1 convolution_bitcast_fusion.3
  296.4 4.5 concatenate.72
  300.9 5.9 %fusion.40 = f32[1280,640]{1,0:T(8,128)} fusion(f32[1280,640]{1,0:T(8,128)} %convolution_bitcast_fusion.2, f32[1280,640]{1,0:T(8,128)} %fusion.151, f32[256,640]{0,1:T(8,128)} %copy-done.8, bf16[1,256,1280]{2,1,0:T(8,128)(2,1)S(1)} %copy-done.5, f32[1280]{0:T(1024)S(1)} %copy-done.35, f32[256]{0:T(256)S(1)} %add_rsqrt_fusion.1, ...), kind=kOutput, calls=%fused_computation.52 | convolution fusion | flops 423362560 | bytes 11148288 | tf_op jit(solution)/shard_map/dot_general | solution.py:51
  306.8 4.6 concatenate.73
  311.4 3.1 copy_dynamic-update-slice_fusion.3
  327.1 2.7 convolution_add_fusion.3
  333.4 2.2 convert_element_type.248
  335.6 2.2 convert_element_type.247
  337.9 2.3 convert_element_type.246
  340.1 2.3 convert_element_type.245
  342.5 2.4 convert_element_type.244
  347.3 31.1 %conditional.1 = (f32[1,1,256,1280]{3,2,1,0:T(8,128)}) conditional(s32[]{:T(128)} %convert_element_type.240, () %tuple.20, (bf16[1280,640]{1,0:T(8,128)(2,1)}, bf16[1280,640]{1,0:T(8,128)(2,1)}, f32[1,256,1280]{1,2,0:T(8,128)S(1)}, f32[1,256,1280]{1,2,0:T(8,128)}, f32[1,256,1280]{1,2,0:T(8,128)}, /*index=5*/f32[1,256,1280]{1,2,0:T(8,128)}, ...), branch_computations={%region_9.10_spmd, %region_10.11_spmd} | conditional | flops 1681981440 | bytes 58982436 | solution.py:217
  347.3 2.8 copy.96
  350.1 2.8 copy.95
  352.9 2.8 copy.94
  355.7 2.8 copy.93
  358.5 2.8 copy.92
  361.3 2.8 copy.91
  364.0 2.8 copy.90
  368.3 4.8 fusion.5
  376.0 2.2 fusion
  378.4 2.9 fusion.124
  381.3 2.8 fusion.74
  390.9 3.4 fusion.73
  394.3 137.1 %reduce-scatter.2.cloned.1.call-done = f32[16,1,25610]{2,0,1:T(8,128)} async-done(((f32[16,8,25610]{2,0,1:T(8,128)}), f32[16,1,25610]{2,0,1:T(8,128)}) %reduce-scatter.2.cloned.1.call-update) | async-done | bytes 1639056 | tf_op jit(solution)/shard_map/reduce_scatter | solution.py:36
  531.4 4.3 copy.106
  535.7 8.1 %all-to-all-start = ((f32[16,1,25610]{2,1,0:T(1,128)}), f32[16,1,25610]{2,1,0:T(1,128)}, u32[]{:S(2)}, u32[]{:S(2)}) async-start(f32[16,1,25610]{2,1,0:T(1,128)} %copy.106), calls=%async_computation.1 | async-start | bytes 3293184 | tf_op jit(solution)/shard_map/all_to_all | solution.py:37
  545.9 10.2 %fusion.62 = bf16[1,2,256,1280]{3,2,1,0:T(8,128)(2,1)} fusion(bf16[1280,3,1280]{2,0,1:T(8,128)(2,1)} %param.18, bf16[1,2,256,1,1280]{4,2,1,3,0:T(8,128)(2,1)S(1)} %get-tuple-element.76, bf16[1,2,256,1,1280]{4,2,1,3,0:T(8,128)(2,1)S(1)} %bitcast.217, bf16[1,2,256,1,1280]{4,2,1,3,0:T(8,128)(2,1)S(1)} %get-tuple-element.75, ...), kind=kOutput, calls=%fused_computation.75 | convolution fusion | flops 5039063040 | bytes 16384000 | tf_op jit(solution)/shard_map/lfsjc,cjo->lfso/dot_general | solution.py:180
  556.2 12.2 %all-to-all-done = f32[16,1,25610]{2,1,0:T(1,128)} async-done(((f32[16,1,25610]{2,1,0:T(1,128)}), f32[16,1,25610]{2,1,0:T(1,128)}, u32[]{:S(2)}, u32[]{:S(2)}) %all-to-all-start) | async-done | bytes 1639072 | tf_op jit(solution)/shard_map/all_to_all | solution.py:37
  568.3 2.5 reduce_sum.125
  (164 shorter events, 75.1 us)
Async XLA Ops:
  7.2 110.8 %copy-start = (bf16[640,1280]{1,0:T(8,128)(2,1)S(1)}, bf16[640,1280]{1,0:T(8,128)(2,1)}, u32[]{:S(2)}) copy-start(bf16[640,1280]{1,0:T(8,128)(2,1)} %param.17) | copy-start | bytes 4915204
  7.2 16.0 %copy-start.2 = (bf16[1,2,256,1280]{3,2,1,0:T(8,128)(2,1)S(1)}, bf16[1,2,256,1280]{3,2,1,0:T(8,128)(2,1)}, u32[]{:S(2)}) copy-start(bf16[1,2,256,1280]{3,2,1,0:T(8,128)(2,1)} %param.12) | copy-start | bytes 3932164
  7.2 16.5 %copy-start.35 = (f32[1280]{0:T(1024)S(1)}, f32[1280]{0:T(1024)}, u32[]{:S(2)}) copy-start(f32[1280]{0:T(1024)} %param.13) | copy-start | bytes 15364
  7.2 524.2 %reduce-scatter.2.cloned.1.call-start = ((), (), s32[]{:S(2)}) async-start(), calls=%async_computation.2 | async-start | bytes 14819328 | tf_op jit(solution)/shard_map/reduce_scatter | solution.py:36
  7.3 16.4 %copy-start.14 = (bf16[1280,640]{1,0:T(8,128)(2,1)S(1)}, bf16[1280,640]{1,0:T(8,128)(2,1)}, u32[]{:S(2)}) copy-start(bf16[1280,640]{1,0:T(8,128)(2,1)} %param.15) | copy-start | bytes 4915204
  9.4 18.9 %collective-permute-start.6 = (bf16[1,256,1280]{2,1,0:T(8,128)(2,1)}, bf16[1,256,1280]{2,1,0:T(8,128)(2,1)S(1)}, u32[]{:S(2)}, u32[]{:S(2)}) collective-permute-start(bf16[1,256,1280]{2,1,0:T(8,128)(2,1)} %slice_bitcast_fusion.1), channel_id=1, source_target_pairs={{0,1},{8,9},{16,17},{24,25},{32,33},{40,41},{48,49},{56,57},{64,65... | collective-permute-start | bytes 1966088 | tf_op jit(solution)/shard_map/ppermute | solution.py:19
  12.9 29.4 %collective-permute-start.5 = (bf16[1,256,1280]{2,1,0:T(8,128)(2,1)}, bf16[1,256,1280]{2,1,0:T(8,128)(2,1)S(1)}, u32[]{:S(2)}, u32[]{:S(2)}) collective-permute-start(bf16[1,256,1280]{2,1,0:T(8,128)(2,1)} %slice_bitcast_fusion.1), channel_id=1, source_target_pairs={{0,2},{8,10},{16,18},{24,26},{32,34},{40,42},{48,50},{56,58},{64,6... | collective-permute-start | bytes 1966088 | tf_op jit(solution)/shard_map/ppermute | solution.py:19
  15.2 42.0 %collective-permute-start.4 = (bf16[1,256,1280]{2,1,0:T(8,128)(2,1)}, bf16[1,256,1280]{2,1,0:T(8,128)(2,1)}, u32[]{:S(2)}, u32[]{:S(2)}) collective-permute-start(bf16[1,256,1280]{2,1,0:T(8,128)(2,1)} %slice_bitcast_fusion.1), channel_id=1, source_target_pairs={{0,3},{8,11},{16,19},{24,27},{32,35},{40,43},{48,51},{56,59},{64,6... | collective-permute-start | bytes 1966088 | tf_op jit(solution)/shard_map/ppermute | solution.py:19
  17.3 41.2 %collective-permute-start.3 = (bf16[1,256,1280]{2,1,0:T(8,128)(2,1)}, bf16[1,256,1280]{2,1,0:T(8,128)(2,1)}, u32[]{:S(2)}, u32[]{:S(2)}) collective-permute-start(bf16[1,256,1280]{2,1,0:T(8,128)(2,1)} %slice_bitcast_fusion.1), channel_id=1, source_target_pairs={{0,4},{8,12},{16,20},{24,28},{32,36},{40,44},{48,52},{56,60},{64,6... | collective-permute-start | bytes 1966088 | tf_op jit(solution)/shard_map/ppermute | solution.py:19
  19.4 44.8 %collective-permute-start.2 = (bf16[1,256,1280]{2,1,0:T(8,128)(2,1)}, bf16[1,256,1280]{2,1,0:T(8,128)(2,1)}, u32[]{:S(2)}, u32[]{:S(2)}) collective-permute-start(bf16[1,256,1280]{2,1,0:T(8,128)(2,1)} %slice_bitcast_fusion.1), channel_id=1, source_target_pairs={{0,5},{8,13},{16,21},{24,29},{32,37},{40,45},{48,53},{56,61},{64,6... | collective-permute-start | bytes 1966088 | tf_op jit(solution)/shard_map/ppermute | solution.py:19
  23.7 2.2 copy-start.36
  28.3 19.8 %copy-start.31 = (bf16[1,256,1280]{2,1,0:T(8,128)(2,1)}, bf16[1,256,1280]{2,1,0:T(8,128)(2,1)S(1)}, u32[]{:S(2)}) copy-start(bf16[1,256,1280]{2,1,0:T(8,128)(2,1)S(1)} %collective-permute-done.6) | copy-start | bytes 1966084
  28.3 42.2 %collective-permute-start.1 = (bf16[1,256,1280]{2,1,0:T(8,128)(2,1)}, bf16[1,256,1280]{2,1,0:T(8,128)(2,1)}, u32[]{:S(2)}, u32[]{:S(2)}) collective-permute-start(bf16[1,256,1280]{2,1,0:T(8,128)(2,1)} %slice_bitcast_fusion.1), channel_id=1, source_target_pairs={{0,6},{8,14},{16,22},{24,30},{32,38},{40,46},{48,54},{56,62},{64,7... | collective-permute-start | bytes 1966088 | tf_op jit(solution)/shard_map/ppermute | solution.py:19
  42.3 5.7 copy-start.33
  42.3 28.1 %collective-permute-start = (bf16[1,256,1280]{2,1,0:T(8,128)(2,1)}, bf16[1,256,1280]{2,1,0:T(8,128)(2,1)}, u32[]{:S(2)}, u32[]{:S(2)}) collective-permute-start(bf16[1,256,1280]{2,1,0:T(8,128)(2,1)} %slice_bitcast_fusion.1), channel_id=1, source_target_pairs={{0,7},{8,15},{16,23},{24,31},{32,39},{40,47},{48,55},{56,63},{64,7... | collective-permute-start | bytes 1966088 | tf_op jit(solution)/shard_map/ppermute | solution.py:19
  54.6 15.8 %copy-start.32 = (bf16[1,256,1280]{2,1,0:T(8,128)(2,1)S(1)}, bf16[1,256,1280]{2,1,0:T(8,128)(2,1)}, u32[]{:S(2)}) copy-start(bf16[1,256,1280]{2,1,0:T(8,128)(2,1)} %copy-done.31) | copy-start | bytes 1966084
  54.6 15.8 %copy-start.34 = (bf16[1,256,1280]{2,1,0:T(8,128)(2,1)S(1)}, bf16[1,256,1280]{2,1,0:T(8,128)(2,1)}, u32[]{:S(2)}) copy-start(bf16[1,256,1280]{2,1,0:T(8,128)(2,1)} %copy-done.33) | copy-start | bytes 1966084
  57.2 64.6 %collective-permute-start.9 = (bf16[1,1,256,1280]{3,2,1,0:T(8,128)(2,1)}, bf16[1,1,256,1280]{3,2,1,0:T(8,128)(2,1)}, u32[]{:S(2)}, u32[]{:S(2)}) collective-permute-start(bf16[1,1,256,1280]{3,2,1,0:T(8,128)(2,1)} %get-tuple-element.73), channel_id=1, source_target_pairs={{1,0},{2,1},{3,2},{4,3},{5,4},{6,5},{7,6},{9,8},{10,9},{11,10},{12... | collective-permute-start | bytes 1966088 | tf_op jit(solution)/shard_map/ppermute | solution.py:64
  58.5 13.2 %copy-start.15 = (bf16[1280,640]{1,0:T(8,128)(2,1)S(1)}, bf16[1280,640]{1,0:T(8,128)(2,1)}, u32[]{:S(2)}) copy-start(bf16[1280,640]{1,0:T(8,128)(2,1)} %param.15) | copy-start | bytes 4915204
  58.5 63.2 %collective-permute-start.10 = (bf16[1,1,256,1280]{3,2,1,0:T(8,128)(2,1)}, bf16[1,1,256,1280]{3,2,1,0:T(8,128)(2,1)}, u32[]{:S(2)}, u32[]{:S(2)}) collective-permute-start(bf16[1,1,256,1280]{3,2,1,0:T(8,128)(2,1)} %get-tuple-element.74), channel_id=1, source_target_pairs={{0,1},{1,2},{2,3},{3,4},{4,5},{5,6},{6,7},{8,9},{9,10},{10,11},{11... | collective-permute-start | bytes 1966088 | tf_op jit(solution)/shard_map/ppermute | solution.py:63
  71.4 1.1 copy-start.4
  78.5 0.9 copy-start.28
  118.0 3.8 copy-start.18
  121.8 2.1 copy-start.41
  133.4 1.1 copy-start.29
  137.9 17.8 %copy-start.26 = (bf16[2,256,640]{1,2,0:T(8,128)(2,1)}, bf16[2,256,640]{1,2,0:T(8,128)(2,1)S(1)}, u32[]{:S(2)}) copy-start(bf16[2,256,640]{1,2,0:T(8,128)(2,1)S(1)} %copy.84) | copy-start | bytes 1966084
  155.7 3.9 copy-start.30
  155.7 3.9 copy-start.40
  159.5 2.8 copy-start.23
  159.5 2.8 copy-start.27
  167.8 42.5 %copy-start.22 = (bf16[2,256,640]{1,2,0:T(8,128)(2,1)S(1)}, bf16[2,256,640]{1,2,0:T(8,128)(2,1)}, u32[]{:S(2)}) copy-start(bf16[2,256,640]{1,2,0:T(8,128)(2,1)} %copy.80) | copy-start | bytes 1966084
  253.7 4.0 copy-start.5
  255.2 12.5 %copy-start.8 = (f32[256,640]{0,1:T(8,128)}, f32[256,640]{0,1:T(8,128)S(1)}, u32[]{:S(2)}) copy-start(f32[256,640]{0,1:T(8,128)S(1)} %slice_reduce_fusion.1) | copy-start | bytes 1966084
  261.2 63.3 %collective-permute-start.17 = (bf16[1,256,1280]{1,2,0:T(8,128)(2,1)}, bf16[1,256,1280]{1,2,0:T(8,128)(2,1)}, u32[]{:S(2)}, u32[]{:S(2)}) collective-permute-start(bf16[1,256,1280]{1,2,0:T(8,128)(2,1)} %fusion.164), channel_id=1, source_target_pairs={{7,0},{15,8},{23,16},{31,24},{39,32},{47,40},{55,48},{63,56},{71,6... | collective-permute-start | bytes 1966088 | tf_op jit(solution)/shard_map/ppermute | solution.py:27
  262.5 63.3 %collective-permute-start.16 = (bf16[1,256,1280]{1,2,0:T(8,128)(2,1)}, bf16[1,256,1280]{1,2,0:T(8,128)(2,1)}, u32[]{:S(2)}, u32[]{:S(2)}) collective-permute-start(bf16[1,256,1280]{1,2,0:T(8,128)(2,1)} %fusion.164), channel_id=1, source_target_pairs={{6,0},{14,8},{22,16},{30,24},{38,32},{46,40},{54,48},{62,56},{70,6... | collective-permute-start | bytes 1966088 | tf_op jit(solution)/shard_map/ppermute | solution.py:27
  263.8 74.1 %collective-permute-start.15 = (bf16[1,256,1280]{1,2,0:T(8,128)(2,1)}, bf16[1,256,1280]{1,2,0:T(8,128)(2,1)}, u32[]{:S(2)}, u32[]{:S(2)}) collective-permute-start(bf16[1,256,1280]{1,2,0:T(8,128)(2,1)} %fusion.164), channel_id=1, source_target_pairs={{5,0},{13,8},{21,16},{29,24},{37,32},{45,40},{53,48},{61,56},{69,6... | collective-permute-start | bytes 1966088 | tf_op jit(solution)/shard_map/ppermute | solution.py:27
  265.1 75.1 %collective-permute-start.14 = (bf16[1,256,1280]{1,2,0:T(8,128)(2,1)}, bf16[1,256,1280]{1,2,0:T(8,128)(2,1)}, u32[]{:S(2)}, u32[]{:S(2)}) collective-permute-start(bf16[1,256,1280]{1,2,0:T(8,128)(2,1)} %fusion.164), channel_id=1, source_target_pairs={{4,0},{12,8},{20,16},{28,24},{36,32},{44,40},{52,48},{60,56},{68,6... | collective-permute-start | bytes 1966088 | tf_op jit(solution)/shard_map/ppermute | solution.py:27
  266.4 76.1 %collective-permute-start.13 = (bf16[1,256,1280]{1,2,0:T(8,128)(2,1)}, bf16[1,256,1280]{1,2,0:T(8,128)(2,1)}, u32[]{:S(2)}, u32[]{:S(2)}) collective-permute-start(bf16[1,256,1280]{1,2,0:T(8,128)(2,1)} %fusion.164), channel_id=1, source_target_pairs={{3,0},{11,8},{19,16},{27,24},{35,32},{43,40},{51,48},{59,56},{67,6... | collective-permute-start | bytes 1966088 | tf_op jit(solution)/shard_map/ppermute | solution.py:27
  277.2 2.7 copy-start.13
  289.1 4.2 copy-start.38
  311.4 3.1 copy-start.12
  314.5 1.9 copy-start.11
  316.5 1.9 copy-start.10
  318.4 1.4 copy-start.37
  318.4 1.6 copy-start.39
  320.0 9.8 %copy-start.6 = (f32[16,8,25610]{2,0,1:T(8,128)}, f32[16,8,25610]{2,0,1:T(8,128)S(1)}, u32[]{:S(2)}) copy-start(f32[16,8,25610]{2,0,1:T(8,128)S(1)} %copy_dynamic-update-slice_fusion) | copy-start | bytes 39336964
  320.0 2.6 copy-start.16
  320.0 3.3 copy-start.25
  323.2 3.9 copy-start.24
  324.5 20.3 %collective-permute-start.12 = (bf16[1,256,1280]{1,2,0:T(8,128)(2,1)}, bf16[1,256,1280]{1,2,0:T(8,128)(2,1)S(1)}, u32[]{:S(2)}, u32[]{:S(2)}) collective-permute-start(bf16[1,256,1280]{1,2,0:T(8,128)(2,1)} %fusion.164), channel_id=1, source_target_pairs={{2,0},{10,8},{18,16},{26,24},{34,32},{42,40},{50,48},{58,56},{66,6... | collective-permute-start | bytes 1966088 | tf_op jit(solution)/shard_map/ppermute | solution.py:27
  325.8 20.3 %collective-permute-start.11 = (bf16[1,256,1280]{1,2,0:T(8,128)(2,1)}, bf16[1,256,1280]{1,2,0:T(8,128)(2,1)S(1)}, u32[]{:S(2)}, u32[]{:S(2)}) collective-permute-start(bf16[1,256,1280]{1,2,0:T(8,128)(2,1)} %fusion.164), channel_id=1, source_target_pairs={{1,0},{9,8},{17,16},{25,24},{33,32},{41,40},{49,48},{57,56},{65,64... | collective-permute-start | bytes 1966088 | tf_op jit(solution)/shard_map/ppermute | solution.py:27
  329.8 2.4 copy-start.7
  329.8 2.4 copy-start.9
  342.4 4.9 copy-start.21
  368.3 4.8 copy-start.17
  384.9 1.3 copy-start.19
  384.9 5.9 %copy-start.3 = (f32[1,2,256,1280]{3,2,1,0:T(8,128)S(1)}, f32[1,2,256,1280]{3,2,1,0:T(8,128)}, u32[]{:S(2)}) copy-start(f32[1,2,256,1280]{3,2,1,0:T(8,128)} %fusion.124) | copy-start | bytes 7864324
  387.4 156.4 %collective-permute-start.7 = (bf16[1,1,256,1280]{3,2,1,0:T(8,128)(2,1)}, bf16[1,1,256,1280]{3,2,1,0:T(8,128)(2,1)}, u32[]{:S(2)}, u32[]{:S(2)}) collective-permute-start(bf16[1,1,256,1280]{3,2,1,0:T(8,128)(2,1)} %get-tuple-element.77), channel_id=1, source_target_pairs={{0,1},{1,2},{2,3},{3,4},{4,5},{5,6},{6,7},{8,9},{9,10},{10,11},{11... | collective-permute-start | bytes 1966088 | tf_op jit(solution)/shard_map/ppermute | solution.py:63
  389.6 154.3 %collective-permute-start.8 = (bf16[1,1,256,1280]{3,2,1,0:T(8,128)(2,1)}, bf16[1,1,256,1280]{3,2,1,0:T(8,128)(2,1)}, u32[]{:S(2)}, u32[]{:S(2)}) collective-permute-start(bf16[1,1,256,1280]{3,2,1,0:T(8,128)(2,1)} %get-tuple-element.78), channel_id=1, source_target_pairs={{1,0},{2,1},{3,2},{4,3},{5,4},{6,5},{7,6},{9,8},{10,9},{11,10},{12... | collective-permute-start | bytes 1966088 | tf_op jit(solution)/shard_map/ppermute | solution.py:64
  535.7 32.6 %all-to-all-start = ((f32[16,1,25610]{2,1,0:T(1,128)}), f32[16,1,25610]{2,1,0:T(1,128)}, u32[]{:S(2)}, u32[]{:S(2)}) async-start(f32[16,1,25610]{2,1,0:T(1,128)} %copy.106), calls=%async_computation.1 | async-start | bytes 3293184 | tf_op jit(solution)/shard_map/all_to_all | solution.py:37
  543.8 1.7 copy-start.20
  543.8 2.1 copy-start.42
  545.9 27.9 %copy-start.1 = (bf16[640,1280]{1,0:T(8,128)(2,1)S(1)}, bf16[640,1280]{1,0:T(8,128)(2,1)}, u32[]{:S(2)}) copy-start(bf16[640,1280]{1,0:T(8,128)(2,1)} %param.17) | copy-start | bytes 4915204
Sparse Core Ops, SparseCore 0:
  385.1 146.2 reduce-scatter.1

commit v4 on v3

--- a/solution.py
+++ b/solution.py
@@ -32,10 +32,10 @@
 def scatter_sum(parts, outer, inner):
     count = lax.axis_size(outer) * lax.axis_size(inner)
     packed = jnp.concatenate([p.reshape(count, -1) for p in parts], axis=1)
-    share = packed.reshape((lax.axis_size(outer), lax.axis_size(inner), -1))
-    share = lax.psum_scatter(share, inner, scatter_dimension=1, tiled=True)
-    share = lax.all_to_all(share, outer, 0, 0, tiled=True)
-    share = jnp.sum(share, axis=(0, 1))
+    share = packed.reshape((lax.axis_size(outer), -1) + packed.shape[1:])
+    share = lax.psum_scatter(share, outer, scatter_dimension=0, tiled=True)[0]
+    share = lax.all_to_all(share, inner, 0, 0, tiled=True)
+    share = jnp.sum(share, axis=0)
     outs, start = [], 0
     for p in parts:
         width = p.size // count

time: 588 us -> 551 us (0.937)
  waiting for transfers between devices: 168 us -> 139 us
    reduce_scatter x1 -> x0, waiting for transfers between devices: 137 us -> none  [scatter_sum(): share = lax.psum_scatter(share, inner, scatter_dimension=1, tiled=True)]
    unnamed x1 -> x2, waiting for transfers between devices: 0.02 us -> 94 us
    ppermute x2, waiting for transfers between devices: 0.01 us -> 9.95 us  [padded_2(): before = lax.ppermute(last, axis, up)]
    unnamed x91 -> x93, local copies, waits for them, and re-layouts: 21.1 us -> 22.5 us
  transfers between devices with their start and end apart: 20 -> 20, of which waited for: 5 -> 8; matrix products, arithmetic and copies ran while one was open for 28% -> 29% of each run, Pallas kernels for 0% -> 0%
where the time goes in v4:
time: 551 us; the launch traced here: 544 us
  matrix products  204 us (37%)
  waiting for transfers between devices  139 us (25%)
  local copies, waits for them, and re-layouts  91.3 us (17%)
  other arithmetic  55.2 us (10%)
  starting transfers between devices  39.7 us (7%)
  between operations  15 us (3%)
    unnamed x2, waiting for transfers between devices  94 us
    dot_general x1, matrix products, attend_back(): jnp.einsum('lfhst,lfshd->lfthd', grad_score, split_heads(queries), prefer...  43.1 us
    dot_general x1, matrix products, attend_back(): jnp.einsum('lfhst,lfthd->lfshd', grad_score, split_heads(key_all), prefer...  42.4 us
    unnamed x93, local copies, waits for them, and re-layouts  22.5 us
    another operation x8, local copies, waits for them, and re-layouts  21.1 us
    ppermute x7, waiting for transfers between devices, from_owner(): got = lax.ppermute(block, axis, [(0, target)])  19.8 us
    concatenate x6, local copies, waits for them, and re-layouts, scatter_sum(): packed = jnp.concatenate([p.reshape(count, -1) for p in parts], axis=1)  18.8 us
    dot_general x1, matrix products, attend_back(): jnp.einsum('lfhst,lfshd->lfthd', prob_b, grad_heads, preferred_element_ty...  17.9 us
  transfers between devices with their start and end apart: 20, of which 8 were waited for; matrix products, arithmetic and copies ran while one was open for 29% of the time, Pallas kernels for 0%

profile of v4, /device:TPU:0, one launch (start us, length us, event | category | flops | bytes accessed | tf_op | source)
XLA Modules:
  0.0 543.9 jit_solution(12520197138776551967)
XLA Ops:
  9.4 3.5 collective-permute-start.6
  12.9 2.2 collective-permute-start.5
  15.2 2.2 collective-permute-start.4
  17.3 2.2 collective-permute-start.3
  30.4 11.9 %collective-permute-done.5 = bf16[1,256,1280]{2,1,0:T(8,128)(2,1)S(1)} collective-permute-done((bf16[1,256,1280]{2,1,0:T(8,128)(2,1)}, bf16[1,256,1280]{2,1,0:T(8,128)(2,1)S(1)}, u32[]{:S(2)}, u32[]{:S(2)}) %collective-permute-start.5) | collective-permute-done | bytes 655392 | tf_op jit(solution)/shard_map/ppermute | solution.py:19
  46.6 2.2 copy.53
  48.9 2.2 copy.52
  51.1 2.2 copy.50
  53.2 2.6 fusion.185
  57.1 5.7 %collective-permute-start.10 = (bf16[1,1,256,1280]{3,2,1,0:T(8,128)(2,1)}, bf16[1,1,256,1280]{3,2,1,0:T(8,128)(2,1)}, u32[]{:S(2)}, u32[]{:S(2)}) collective-permute-start(bf16[1,1,256,1280]{3,2,1,0:T(8,128)(2,1)} %get-tuple-element.64), channel_id=1, source_target_pairs={{0,1},{1,2},{2,3},{3,4},{4,5},{5,6},{6,7},{8,9},{9,10},{10,11},{11... | collective-permute-start | bytes 1966088 | tf_op jit(solution)/shard_map/ppermute | solution.py:63
  62.9 7.6 %collective-permute-done.1 = bf16[1,256,1280]{2,1,0:T(8,128)(2,1)} collective-permute-done((bf16[1,256,1280]{2,1,0:T(8,128)(2,1)}, bf16[1,256,1280]{2,1,0:T(8,128)(2,1)}, u32[]{:S(2)}, u32[]{:S(2)}) %collective-permute-start.1) | collective-permute-done | bytes 655392 | tf_op jit(solution)/shard_map/ppermute | solution.py:19
  78.4 6.7 %fusion.137 = f32[2,10,256,512]{3,2,1,0:T(8,128)} fusion(bf16[2,256,10,64]{1,3,2,0:T(8,128)(2,1)} %bitcast.222, bf16[1,2,256,10,64]{2,4,3,1,0:T(8,128)(2,1)S(1)} %broadcast_in_dim.13, bf16[1,2,256,10,64]{2,4,3,1,0:T(8,128)(2,1)} %bitcast.224), kind=kOutput, calls=%fused_computation.145 | convolution fusion | flops 338165760 | bytes 12451840 | tf_op jit(solution)/shard_map/lfshd,lfthd->lfhst/dot_general | solution.py:93
  85.1 13.2 %fusion.188 = (f32[2,10,256]{2,1,0:T(8,128)S(1)}, f32[2,10,256,512]{3,2,1,0:T(8,128)}) fusion(f32[2,10,256,512]{3,2,1,0:T(8,128)} %fusion.137), kind=kOutput, calls=%fused_computation.191 | output fusion | flops 10486271 | bytes 20992000 | tf_op jit(solution)/shard_map/sub | solution.py:100
  99.2 17.7 %fusion.101 = bf16[2,10,64,256]{3,2,1,0:T(8,128)(2,1)} fusion(bf16[1,2,256,10,64]{2,4,3,1,0:T(8,128)(2,1)} %broadcast_in_dim.11, bf16[1,2,256,10,64]{2,4,3,1,0:T(8,128)(2,1)} %bitcast.226, f32[2,10,256]{2,1,0:T(8,128)S(1)} %get-tuple-element.73, f32[2,10,256,512]{3,2,1,0:T(8,128)} %fusion.137), kind=kOutput, calls=%fused_computation.109 | convolution fusion | flops 351606272 | bytes 12472320 | tf_op jit(solution)/shard_map/lfhst,lfthd->lfshd/dot_general | solution.py:103
  116.9 3.8 fusion.79
  122.8 9.6 %fusion.65 = bf16[1,2,256,1280]{3,2,1,0:T(8,128)(2,1)S(1)} fusion(bf16[1280,3,1280]{2,0,1:T(8,128)(2,1)} %param.18, bf16[1,2,256,1,1280]{4,2,3,1,0:T(8,128)(2,1)S(1)} %get-tuple-element.62, bf16[1,2,256,1,1280]{4,2,3,1,0:T(8,128)(2,1)S(1)} %bitcast.218, bf16[1,2,256,1,1280]{4,2,3,1,0:T(8,128)(2,1)S(1)} %get-tuple-element.61, ...), kind=kOutput, calls=%fused_computation.72 | convolution fusion | flops 5044961280 | bytes 17694720 | tf_op jit(solution)/shard_map/lfsjo,cjo->lfsc/dot_general | solution.py:185
  136.9 17.9 %fusion.82 = f32[2,10,64,512]{3,2,1,0:T(8,128)} fusion(bf16[2,256,10,64]{1,3,2,0:T(8,128)(2,1)S(1)} %bitcast.228, f32[2,10,256]{2,1,0:T(8,128)S(1)} %get-tuple-element.73, f32[2,10,256,512]{3,2,1,0:T(8,128)} %fusion.137), kind=kOutput, calls=%fused_computation.87 | convolution fusion | flops 348657152 | bytes 13783040 | tf_op jit(solution)/shard_map/lfhst,lfshd->lfthd/dot_general | solution.py:124
  154.9 2.5 slice_reduce_fusion
  157.3 2.2 slice.109
  159.6 2.7 convolution_bitcast_fusion
  162.4 5.4 fusion.131
  167.8 42.4 %fusion.116 = bf16[2,10,64,256]{3,2,1,0:T(8,128)(2,1)} fusion(f32[2,10,256,512]{3,2,1,0:T(8,128)} %fusion.131, bf16[1,2,256,10,64]{2,4,3,1,0:T(8,128)(2,1)} %copy-done.30, bf16[1,2,256,10,64]{2,4,3,1,0:T(8,128)(2,1)S(1)} %bitcast.225, f32[2,10,256,512]{3,2,1,0:T(8,128)} %get-tuple-element.74, f32[2,10,256]{2,1,0:T(8,128)S(1)} %get-tuple-element.73), kind=kOutput, calls=%fused_computation.114 | convolution fusion | flops 356849152 | bytes 22958080 | tf_op jit(solution)/shard_map/lfhst,lfthd->lfshd/dot_general | solution.py:117
  210.2 43.1 %fusion.26 = f32[2,10,64,512]{3,2,1,0:T(8,128)} fusion(bf16[2,256,10,64]{1,3,2,0:T(8,128)(2,1)S(1)} %bitcast.223, f32[2,10,256,512]{3,2,1,0:T(8,128)} %fusion.131, f32[2,10,256,512]{3,2,1,0:T(8,128)} %get-tuple-element.74, f32[2,10,256]{2,1,0:T(8,128)S(1)} %get-tuple-element.73), kind=kOutput, calls=%fused_computation.30 | convolution fusion | flops 353900032 | bytes 24268800 | tf_op jit(solution)/shard_map/lfhst,lfshd->lfthd/dot_general | solution.py:121
  254.8 2.3 slice.108
  257.1 2.6 fusion.148
  268.2 2.8 fusion.92
  271.0 3.1 convolution_bitcast_fusion.3
  274.2 2.5 fusion.151
  278.9 4.7 concatenate.75
  283.6 2.6 convolution_bitcast_fusion.1
  286.3 2.6 fusion.39
  288.9 4.4 concatenate.74
  293.3 2.2 copy.82
  295.5 4.4 convolution_bitcast_fusion.2
  305.6 4.4 concatenate.72
  310.1 5.5 %fusion.40 = f32[1280,640]{1,0:T(8,128)} fusion(f32[1280,640]{1,0:T(8,128)} %convolution_bitcast_fusion.2, f32[1280,640]{1,0:T(8,128)} %fusion.151, f32[256,640]{0,1:T(8,128)S(1)} %slice_reduce_fusion.1, bf16[1,256,1280]{2,1,0:T(8,128)(2,1)S(1)} %copy-done.4, f32[1280]{0:T(1024)S(1)} %copy-done.38, f32[256]{0:T(256)S(1)} %add_rsqrt_fusion.1, ...), kind=kOutput, calls=%fused_computation.52 | convolution fusion | flops 423362560 | bytes 11148288 | tf_op jit(solution)/shard_map/dot_general | solution.py:51
  315.6 4.4 concatenate.73
  320.0 4.0 constant_dynamic-update-slice_fusion.6
  333.8 2.2 convert_element_type.248
  336.0 2.3 convert_element_type.247
  338.3 2.2 convert_element_type.246
  340.5 2.3 convert_element_type.245
  342.8 2.4 convert_element_type.244
  345.1 2.2 collective-permute-done.12
  349.7 31.1 %conditional.1 = (f32[1,1,256,1280]{3,2,1,0:T(8,128)}) conditional(s32[]{:T(128)} %convert_element_type.240, () %tuple.20, (bf16[1280,640]{1,0:T(8,128)(2,1)}, bf16[1280,640]{1,0:T(8,128)(2,1)}, f32[1,256,1280]{1,2,0:T(8,128)S(1)}, f32[1,256,1280]{1,2,0:T(8,128)}, f32[1,256,1280]{1,2,0:T(8,128)}, /*index=5*/f32[1,256,1280]{1,2,0:T(8,128)}, ...), branch_computations={%region_9.10_spmd, %region_10.11_spmd} | conditional | flops 1681981440 | bytes 65536064 | solution.py:217
  349.7 2.8 copy.68
  352.5 2.8 copy.67
  355.3 2.8 copy.66
  358.1 2.8 copy.65
  360.8 2.9 copy.64
  363.7 2.8 copy.63
  366.5 2.8 copy.62
  370.8 4.8 fusion.5
  378.4 2.2 fusion
  380.8 2.9 fusion.124
  383.7 2.8 fusion.74
  391.5 10.0 %collective-permute-done.7 = bf16[1,1,256,1280]{3,2,1,0:T(8,128)(2,1)S(1)} collective-permute-done((bf16[1,1,256,1280]{3,2,1,0:T(8,128)(2,1)S(1)}, bf16[1,1,256,1280]{3,2,1,0:T(8,128)(2,1)S(1)}, u32[]{:S(2)}, u32[]{:S(2)}) %collective-permute-start.7) | collective-permute-done | bytes 655392 | tf_op jit(solution)/shard_map/ppermute | solution.py:63
  401.5 4.3 collective-permute-done.8
  406.0 11.8 %fusion.62 = bf16[1,2,256,1280]{3,2,1,0:T(8,128)(2,1)} fusion(bf16[1280,3,1280]{2,0,1:T(8,128)(2,1)} %param.18, bf16[1,2,256,1,1280]{4,2,1,3,0:T(8,128)(2,1)S(1)} %get-tuple-element.66, bf16[1,2,256,1,1280]{4,2,1,3,0:T(8,128)(2,1)S(1)} %bitcast.219, bf16[1,2,256,1,1280]{4,2,1,3,0:T(8,128)(2,1)S(1)} %get-tuple-element.65, ...), kind=kOutput, calls=%fused_computation.71 | convolution fusion | flops 5039063040 | bytes 16384000 | tf_op jit(solution)/shard_map/lfsjc,cjo->lfso/dot_general | solution.py:180
  417.9 94.0 %reduce-scatter.4.cloned.1.call-done = f32[1,8,25610]{2,1,0:T(8,128)} async-done(((f32[16,8,25610]{2,1,0:T(8,128)}), f32[1,8,25610]{2,1,0:T(8,128)}) %reduce-scatter.4.cloned.1.call-update) | async-done | bytes 819536
  511.9 2.9 copy.73
  514.8 4.3 all-to-all-start
  519.1 4.4 fusion.73
  523.5 8.4 %all-to-all-done = f32[8,1,25610]{2,1,0:T(1,128)} async-done(((f32[8,1,25610]{2,1,0:T(1,128)}), f32[8,1,25610]{2,1,0:T(1,128)}, u32[]{:S(2)}, u32[]{:S(2)}) %all-to-all-start) | async-done | bytes 819552 | tf_op jit(solution)/shard_map/all_to_all | solution.py:37
  (168 shorter events, 78.4 us)
Async XLA Ops:
  7.2 109.8 %copy-start = (bf16[640,1280]{1,0:T(8,128)(2,1)S(1)}, bf16[640,1280]{1,0:T(8,128)(2,1)}, u32[]{:S(2)}) copy-start(bf16[640,1280]{1,0:T(8,128)(2,1)} %param.17) | copy-start | bytes 4915204
  7.2 16.0 %copy-start.2 = (bf16[1,2,256,1280]{3,2,1,0:T(8,128)(2,1)S(1)}, bf16[1,2,256,1280]{3,2,1,0:T(8,128)(2,1)}, u32[]{:S(2)}) copy-start(bf16[1,2,256,1280]{3,2,1,0:T(8,128)(2,1)} %param.12) | copy-start | bytes 3932164
  7.2 16.5 %copy-start.38 = (f32[1280]{0:T(1024)S(1)}, f32[1280]{0:T(1024)}, u32[]{:S(2)}) copy-start(f32[1280]{0:T(1024)} %param.13) | copy-start | bytes 15364
  7.2 504.7 %reduce-scatter.4.cloned.1.call-start = ((), (), s32[]{:S(2)}) async-start(), calls=%async_computation.2 | async-start | bytes 13996032
  7.3 16.5 %copy-start.16 = (bf16[1280,640]{1,0:T(8,128)(2,1)S(1)}, bf16[1280,640]{1,0:T(8,128)(2,1)}, u32[]{:S(2)}) copy-start(bf16[1280,640]{1,0:T(8,128)(2,1)} %param.15) | copy-start | bytes 4915204
  9.4 18.9 %collective-permute-start.6 = (bf16[1,256,1280]{2,1,0:T(8,128)(2,1)}, bf16[1,256,1280]{2,1,0:T(8,128)(2,1)S(1)}, u32[]{:S(2)}, u32[]{:S(2)}) collective-permute-start(bf16[1,256,1280]{2,1,0:T(8,128)(2,1)} %slice_bitcast_fusion.1), channel_id=1, source_target_pairs={{0,1},{8,9},{16,17},{24,25},{32,33},{40,41},{48,49},{56,57},{64,65... | collective-permute-start | bytes 1966088 | tf_op jit(solution)/shard_map/ppermute | solution.py:19
  12.9 29.4 %collective-permute-start.5 = (bf16[1,256,1280]{2,1,0:T(8,128)(2,1)}, bf16[1,256,1280]{2,1,0:T(8,128)(2,1)S(1)}, u32[]{:S(2)}, u32[]{:S(2)}) collective-permute-start(bf16[1,256,1280]{2,1,0:T(8,128)(2,1)} %slice_bitcast_fusion.1), channel_id=1, source_target_pairs={{0,2},{8,10},{16,18},{24,26},{32,34},{40,42},{48,50},{56,58},{64,6... | collective-permute-start | bytes 1966088 | tf_op jit(solution)/shard_map/ppermute | solution.py:19
  15.2 40.6 %collective-permute-start.4 = (bf16[1,256,1280]{2,1,0:T(8,128)(2,1)}, bf16[1,256,1280]{2,1,0:T(8,128)(2,1)}, u32[]{:S(2)}, u32[]{:S(2)}) collective-permute-start(bf16[1,256,1280]{2,1,0:T(8,128)(2,1)} %slice_bitcast_fusion.1), channel_id=1, source_target_pairs={{0,3},{8,11},{16,19},{24,27},{32,35},{40,43},{48,51},{56,59},{64,6... | collective-permute-start | bytes 1966088 | tf_op jit(solution)/shard_map/ppermute | solution.py:19
  17.3 39.8 %collective-permute-start.3 = (bf16[1,256,1280]{2,1,0:T(8,128)(2,1)}, bf16[1,256,1280]{2,1,0:T(8,128)(2,1)}, u32[]{:S(2)}, u32[]{:S(2)}) collective-permute-start(bf16[1,256,1280]{2,1,0:T(8,128)(2,1)} %slice_bitcast_fusion.1), channel_id=1, source_target_pairs={{0,4},{8,12},{16,20},{24,28},{32,36},{40,44},{48,52},{56,60},{64,6... | collective-permute-start | bytes 1966088 | tf_op jit(solution)/shard_map/ppermute | solution.py:19
  19.5 43.4 %collective-permute-start.2 = (bf16[1,256,1280]{2,1,0:T(8,128)(2,1)}, bf16[1,256,1280]{2,1,0:T(8,128)(2,1)}, u32[]{:S(2)}, u32[]{:S(2)}) collective-permute-start(bf16[1,256,1280]{2,1,0:T(8,128)(2,1)} %slice_bitcast_fusion.1), channel_id=1, source_target_pairs={{0,5},{8,13},{16,21},{24,29},{32,37},{40,45},{48,53},{56,61},{64,6... | collective-permute-start | bytes 1966088 | tf_op jit(solution)/shard_map/ppermute | solution.py:19
  23.7 2.2 copy-start.39
  25.9 18.6 %copy-start.12 = (bf16[1280,640]{1,0:T(8,128)(2,1)S(1)}, bf16[1280,640]{1,0:T(8,128)(2,1)}, u32[]{:S(2)}) copy-start(bf16[1280,640]{1,0:T(8,128)(2,1)} %param.16) | copy-start | bytes 4915204
  28.3 18.3 %copy-start.34 = (bf16[1,256,1280]{2,1,0:T(8,128)(2,1)}, bf16[1,256,1280]{2,1,0:T(8,128)(2,1)S(1)}, u32[]{:S(2)}) copy-start(bf16[1,256,1280]{2,1,0:T(8,128)(2,1)S(1)} %collective-permute-done.6) | copy-start | bytes 1966084
  28.3 42.2 %collective-permute-start.1 = (bf16[1,256,1280]{2,1,0:T(8,128)(2,1)}, bf16[1,256,1280]{2,1,0:T(8,128)(2,1)}, u32[]{:S(2)}, u32[]{:S(2)}) collective-permute-start(bf16[1,256,1280]{2,1,0:T(8,128)(2,1)} %slice_bitcast_fusion.1), channel_id=1, source_target_pairs={{0,6},{8,14},{16,22},{24,30},{32,38},{40,46},{48,54},{56,62},{64,7... | collective-permute-start | bytes 1966088 | tf_op jit(solution)/shard_map/ppermute | solution.py:19
  42.3 4.3 copy-start.36
  42.3 28.1 %collective-permute-start = (bf16[1,256,1280]{2,1,0:T(8,128)(2,1)}, bf16[1,256,1280]{2,1,0:T(8,128)(2,1)}, u32[]{:S(2)}, u32[]{:S(2)}) collective-permute-start(bf16[1,256,1280]{2,1,0:T(8,128)(2,1)} %slice_bitcast_fusion.1), channel_id=1, source_target_pairs={{0,7},{8,15},{16,23},{24,31},{32,39},{40,47},{48,55},{56,63},{64,7... | collective-permute-start | bytes 1966088 | tf_op jit(solution)/shard_map/ppermute | solution.py:19
  53.2 17.2 %copy-start.35 = (bf16[1,256,1280]{2,1,0:T(8,128)(2,1)S(1)}, bf16[1,256,1280]{2,1,0:T(8,128)(2,1)}, u32[]{:S(2)}) copy-start(bf16[1,256,1280]{2,1,0:T(8,128)(2,1)} %copy-done.34) | copy-start | bytes 1966084
  53.2 17.2 %copy-start.37 = (bf16[1,256,1280]{2,1,0:T(8,128)(2,1)S(1)}, bf16[1,256,1280]{2,1,0:T(8,128)(2,1)}, u32[]{:S(2)}) copy-start(bf16[1,256,1280]{2,1,0:T(8,128)(2,1)} %copy-done.36) | copy-start | bytes 1966084
  55.8 64.9 %collective-permute-start.9 = (bf16[1,1,256,1280]{3,2,1,0:T(8,128)(2,1)}, bf16[1,1,256,1280]{3,2,1,0:T(8,128)(2,1)}, u32[]{:S(2)}, u32[]{:S(2)}) collective-permute-start(bf16[1,1,256,1280]{3,2,1,0:T(8,128)(2,1)} %get-tuple-element.63), channel_id=1, source_target_pairs={{1,0},{2,1},{3,2},{4,3},{5,4},{6,5},{7,6},{9,8},{10,9},{11,10},{12... | collective-permute-start | bytes 1966088 | tf_op jit(solution)/shard_map/ppermute | solution.py:64
  57.1 14.6 %copy-start.17 = (bf16[1280,640]{1,0:T(8,128)(2,1)S(1)}, bf16[1280,640]{1,0:T(8,128)(2,1)}, u32[]{:S(2)}) copy-start(bf16[1280,640]{1,0:T(8,128)(2,1)} %param.15) | copy-start | bytes 4915204
  57.1 63.6 %collective-permute-start.10 = (bf16[1,1,256,1280]{3,2,1,0:T(8,128)(2,1)}, bf16[1,1,256,1280]{3,2,1,0:T(8,128)(2,1)}, u32[]{:S(2)}, u32[]{:S(2)}) collective-permute-start(bf16[1,1,256,1280]{3,2,1,0:T(8,128)(2,1)} %get-tuple-element.64), channel_id=1, source_target_pairs={{0,1},{1,2},{2,3},{3,4},{4,5},{5,6},{6,7},{8,9},{9,10},{10,11},{11... | collective-permute-start | bytes 1966088 | tf_op jit(solution)/shard_map/ppermute | solution.py:63
  71.4 1.1 copy-start.3
  71.4 1.7 copy-start.13
  116.9 3.8 copy-start.20
  120.7 2.1 copy-start.43
  132.4 1.1 copy-start.32
  136.9 17.9 %copy-start.27 = (bf16[2,256,640]{1,2,0:T(8,128)(2,1)}, bf16[2,256,640]{1,2,0:T(8,128)(2,1)S(1)}, u32[]{:S(2)}) copy-start(bf16[2,256,640]{1,2,0:T(8,128)(2,1)S(1)} %copy.56) | copy-start | bytes 1966084
  154.9 4.7 copy-start.33
  154.9 4.7 copy-start.42
  159.6 2.8 copy-start.25
  159.6 2.8 copy-start.28
  162.4 5.4 copy-start.24
  167.8 42.4 %copy-start.23 = (bf16[2,256,640]{1,2,0:T(8,128)(2,1)S(1)}, bf16[2,256,640]{1,2,0:T(8,128)(2,1)}, u32[]{:S(2)}) copy-start(bf16[2,256,640]{1,2,0:T(8,128)(2,1)} %copy.52) | copy-start | bytes 1966084
  253.2 3.8 copy-start.4
  253.2 3.8 copy-start.6
  259.6 8.6 %copy-start.40 = (bf16[1280,640]{1,0:T(8,128)(2,1)S(1)}, bf16[1280,640]{1,0:T(8,128)(2,1)}, u32[]{:S(2)}) copy-start(bf16[1280,640]{1,0:T(8,128)(2,1)} %param.14) | copy-start | bytes 4915204
  259.6 8.6 %copy-start.41 = (bf16[2,10,64,256]{3,2,1,0:T(8,128)(2,1)S(1)}, bf16[2,10,64,256]{3,2,1,0:T(8,128)(2,1)}, u32[]{:S(2)}) copy-start(bf16[2,10,64,256]{3,2,1,0:T(8,128)(2,1)} %fusion.116) | copy-start | bytes 1966084
  261.7 67.4 %collective-permute-start.17 = (bf16[1,256,1280]{1,2,0:T(8,128)(2,1)}, bf16[1,256,1280]{1,2,0:T(8,128)(2,1)}, u32[]{:S(2)}, u32[]{:S(2)}) collective-permute-start(bf16[1,256,1280]{1,2,0:T(8,128)(2,1)} %fusion.164), channel_id=1, source_target_pairs={{7,0},{15,8},{23,16},{31,24},{39,32},{47,40},{55,48},{63,56},{71,6... | collective-permute-start | bytes 1966088 | tf_op jit(solution)/shard_map/ppermute | solution.py:27
  263.0 67.5 %collective-permute-start.16 = (bf16[1,256,1280]{1,2,0:T(8,128)(2,1)}, bf16[1,256,1280]{1,2,0:T(8,128)(2,1)}, u32[]{:S(2)}, u32[]{:S(2)}) collective-permute-start(bf16[1,256,1280]{1,2,0:T(8,128)(2,1)} %fusion.164), channel_id=1, source_target_pairs={{6,0},{14,8},{22,16},{30,24},{38,32},{46,40},{54,48},{62,56},{70,6... | collective-permute-start | bytes 1966088 | tf_op jit(solution)/shard_map/ppermute | solution.py:27
  264.3 73.9 %collective-permute-start.15 = (bf16[1,256,1280]{1,2,0:T(8,128)(2,1)}, bf16[1,256,1280]{1,2,0:T(8,128)(2,1)}, u32[]{:S(2)}, u32[]{:S(2)}) collective-permute-start(bf16[1,256,1280]{1,2,0:T(8,128)(2,1)} %fusion.164), channel_id=1, source_target_pairs={{5,0},{13,8},{21,16},{29,24},{37,32},{45,40},{53,48},{61,56},{69,6... | collective-permute-start | bytes 1966088 | tf_op jit(solution)/shard_map/ppermute | solution.py:27
  265.6 74.9 %collective-permute-start.14 = (bf16[1,256,1280]{1,2,0:T(8,128)(2,1)}, bf16[1,256,1280]{1,2,0:T(8,128)(2,1)}, u32[]{:S(2)}, u32[]{:S(2)}) collective-permute-start(bf16[1,256,1280]{1,2,0:T(8,128)(2,1)} %fusion.164), channel_id=1, source_target_pairs={{4,0},{12,8},{20,16},{28,24},{36,32},{44,40},{52,48},{60,56},{68,6... | collective-permute-start | bytes 1966088 | tf_op jit(solution)/shard_map/ppermute | solution.py:27
  266.9 75.9 %collective-permute-start.13 = (bf16[1,256,1280]{1,2,0:T(8,128)(2,1)}, bf16[1,256,1280]{1,2,0:T(8,128)(2,1)}, u32[]{:S(2)}, u32[]{:S(2)}) collective-permute-start(bf16[1,256,1280]{1,2,0:T(8,128)(2,1)} %fusion.164), channel_id=1, source_target_pairs={{3,0},{11,8},{19,16},{27,24},{35,32},{43,40},{51,48},{59,56},{67,6... | collective-permute-start | bytes 1966088 | tf_op jit(solution)/shard_map/ppermute | solution.py:27
  283.6 2.6 copy-start.7
  283.6 2.7 copy-start.11
  295.5 4.4 copy-start.18
  295.5 4.4 copy-start.29
  295.5 4.4 copy-start.31
  299.9 1.4 copy-start.14
  299.9 1.6 copy-start.26
  302.7 1.5 copy-start.5
  320.0 4.0 copy-start.10
  324.0 3.1 copy-start.9
  327.1 4.7 copy-start.8
  329.1 18.2 %collective-permute-start.12 = (bf16[1,256,1280]{1,2,0:T(8,128)(2,1)}, bf16[1,256,1280]{1,2,0:T(8,128)(2,1)S(1)}, u32[]{:S(2)}, u32[]{:S(2)}) collective-permute-start(bf16[1,256,1280]{1,2,0:T(8,128)(2,1)} %fusion.164), channel_id=1, source_target_pairs={{2,0},{10,8},{18,16},{26,24},{34,32},{42,40},{50,48},{58,56},{66,6... | collective-permute-start | bytes 1966088 | tf_op jit(solution)/shard_map/ppermute | solution.py:27
  330.5 18.0 %collective-permute-start.11 = (bf16[1,256,1280]{1,2,0:T(8,128)(2,1)}, bf16[1,256,1280]{1,2,0:T(8,128)(2,1)S(1)}, u32[]{:S(2)}, u32[]{:S(2)}) collective-permute-start(bf16[1,256,1280]{1,2,0:T(8,128)(2,1)} %fusion.164), channel_id=1, source_target_pairs={{1,0},{9,8},{17,16},{25,24},{33,32},{41,40},{49,48},{57,56},{65,64... | collective-permute-start | bytes 1966088 | tf_op jit(solution)/shard_map/ppermute | solution.py:27
  342.8 6.9 %copy-start.22 = (f32[1,256,1280]{1,2,0:T(8,128)S(1)}, f32[1,256,1280]{1,2,0:T(8,128)}, u32[]{:S(2)}) copy-start(f32[1,256,1280]{1,2,0:T(8,128)} %pad_maximum_fusion.4) | copy-start | bytes 3932164
  370.8 4.8 copy-start.19
  375.6 1.4 copy-start.15
  387.3 1.3 copy-start.21
  388.7 12.7 %collective-permute-start.7 = (bf16[1,1,256,1280]{3,2,1,0:T(8,128)(2,1)S(1)}, bf16[1,1,256,1280]{3,2,1,0:T(8,128)(2,1)S(1)}, u32[]{:S(2)}, u32[]{:S(2)}) collective-permute-start(bf16[1,1,256,1280]{3,2,1,0:T(8,128)(2,1)S(1)} %get-tuple-element.67), channel_id=1, source_target_pairs={{0,1},{1,2},{2,3},{3,4},{4,5},{5,6},{6,7},{8,9},{9,10},{10,11},{11... | collective-permute-start | bytes 1966088 | tf_op jit(solution)/shard_map/ppermute | solution.py:63
  390.1 16.0 %copy-start.44 = (bf16[1,2,256,1280]{3,2,1,0:T(8,128)(2,1)S(1)}, bf16[1,2,256,1280]{3,2,1,0:T(8,128)(2,1)}, u32[]{:S(2)}) copy-start(bf16[1,2,256,1280]{3,2,1,0:T(8,128)(2,1)} %copy-done.43) | copy-start | bytes 3932164
  390.1 15.7 %collective-permute-start.8 = (bf16[1,1,256,1280]{3,2,1,0:T(8,128)(2,1)S(1)}, bf16[1,1,256,1280]{3,2,1,0:T(8,128)(2,1)S(1)}, u32[]{:S(2)}, u32[]{:S(2)}) collective-permute-start(bf16[1,1,256,1280]{3,2,1,0:T(8,128)(2,1)S(1)} %get-tuple-element.68), channel_id=1, source_target_pairs={{1,0},{2,1},{3,2},{4,3},{5,4},{6,5},{7,6},{9,8},{10,9},{11,10},{12... | collective-permute-start | bytes 1966088 | tf_op jit(solution)/shard_map/ppermute | solution.py:64
  514.8 17.1 %all-to-all-start = ((f32[8,1,25610]{2,1,0:T(1,128)}), f32[8,1,25610]{2,1,0:T(1,128)}, u32[]{:S(2)}, u32[]{:S(2)}) async-start(f32[8,1,25610]{2,1,0:T(1,128)} %copy.73), calls=%async_computation | async-start | bytes 1646592 | tf_op jit(solution)/shard_map/all_to_all | solution.py:37
  519.1 17.5 %copy-start.1 = (bf16[640,1280]{1,0:T(8,128)(2,1)S(1)}, bf16[640,1280]{1,0:T(8,128)(2,1)}, u32[]{:S(2)}) copy-start(bf16[640,1280]{1,0:T(8,128)(2,1)} %param.17) | copy-start | bytes 4915204
  (1 other events, 0.8 us)
Sparse Core Ops, SparseCore 0:
  387.5 124.3 reduce-scatter.3

commit v5 on v1

--- a/solution.py
+++ b/solution.py
@@ -37,8 +37,8 @@
     count = lax.axis_size(outer) * lax.axis_size(inner)
     packed = jnp.concatenate([p.reshape(count, -1) for p in parts], axis=1)
     share = packed.reshape((lax.axis_size(outer), -1) + packed.shape[1:])
-    share = lax.psum_scatter(share, outer, scatter_dimension=0, tiled=True)[0]
-    share = lax.all_to_all(share, inner, 0, 0, tiled=True)
+    share = lax.psum_scatter(share.astype(jnp.bfloat16), outer, scatter_dimension=0, tiled=True)[0]
+    share = lax.all_to_all(share.astype(jnp.float32), inner, 0, 0, tiled=True)
     share = jnp.sum(share, axis=0)
     outs, start = [], 0
     for p in parts:

time: 546 us -> 507 us (0.929)
  waiting for transfers between devices: 170 us -> 140 us
  local copies, waits for them, and re-layouts: 71.9 us -> 65.2 us
    unnamed x2, waiting for transfers between devices: 94.2 us -> 61.1 us
where the time goes in v5:
time: 507 us; the launch traced here: 500 us
  matrix products  203 us (40%)
  waiting for transfers between devices  140 us (28%)
  local copies, waits for them, and re-layouts  65.2 us (13%)
  other arithmetic  49.5 us (10%)
  starting transfers between devices  27.8 us (5%)
  between operations  14.8 us (3%)
    unnamed x2, waiting for transfers between devices  61.1 us
    dot_general x1, matrix products, attend_back(): jnp.einsum('lfhst,lfthd->lfshd', grad_score, split_heads(key_all), prefer...  43 us
    dot_general x1, matrix products, attend_back(): jnp.einsum('lfhst,lfshd->lfthd', grad_score, split_heads(queries), prefer...  42.8 us
    ppermute x3, waiting for transfers between devices, tree_reduce(): got = lax.ppermute(total.astype(jnp.bfloat16), axis, list(pairs))  35.6 us
    ppermute x3, waiting for transfers between devices, tree_broadcast(): got = lax.ppermute(have, axis, list(pairs))  22 us
    dot_general x6, matrix products, gram_rows(): lax.dot_general(flat_left, flat_right, (((0,), (0,)), ((), ())), preferre...  18.8 us
    concatenate x6, local copies, waits for them, and re-layouts, scatter_sum(): packed = jnp.concatenate([p.reshape(count, -1) for p in parts], axis=1)  18.1 us
    dot_general x1, matrix products, attend(): jnp.einsum('lfhst,lfthd->lfshd', prob_b, split_heads(val_all), preferred_...  17.7 us
  transfers between devices with their start and end apart: 12, of which 9 were waited for; matrix products, arithmetic and copies ran while one was open for 11% of the time, Pallas kernels for 0%

profile of v5, /device:TPU:0, one launch (start us, length us, event | category | flops | bytes accessed | tf_op | source)
XLA Modules:
  0.0 500.5 jit_solution(18174340680227553225)
XLA Ops:
  7.2 2.1 slice_bitcast_fusion.5
  9.4 4.5 collective-permute-start
  13.9 2.5 fusion.171
  17.8 5.4 %collective-permute-start.6 = (bf16[1,1,256,1280]{3,2,1,0:T(8,128)(2,1)}, bf16[1,1,256,1280]{3,2,1,0:T(8,128)(2,1)}, u32[]{:S(2)}, u32[]{:S(2)}) collective-permute-start(bf16[1,1,256,1280]{3,2,1,0:T(8,128)(2,1)} %get-tuple-element.57), channel_id=1, source_target_pairs={{0,1},{1,2},{2,3},{3,4},{4,5},{5,6},{6,7},{8,9},{9,10},{10,11},{11... | collective-permute-start | bytes 1966088 | tf_op jit(solution)/shard_map/ppermute | solution.py:58
  24.0 17.3 %collective-permute-done = bf16[1,256,1280]{2,1,0:T(8,128)(2,1)} collective-permute-done((bf16[1,256,1280]{2,1,0:T(8,128)(2,1)}, bf16[1,256,1280]{2,1,0:T(8,128)(2,1)}, u32[]{:S(2)}, u32[]{:S(2)}) %collective-permute-start) | collective-permute-done | bytes 655392 | tf_op jit(solution)/shard_map/ppermute | solution.py:20
  42.2 2.1 collective-permute-start.1
  44.3 2.1 fusion.99
  46.5 2.1 copy.52
  48.6 3.5 convert_element_type.200
  52.1 2.1 fusion.102
  54.2 2.2 copy.53
  56.5 3.5 convert_element_type.201
  59.9 2.0 broadcast_select_fusion.1
  61.9 2.6 collective-permute-start.2
  64.6 2.1 fusion.96
  66.7 2.2 copy.50
  68.9 3.4 fusion.118
  72.2 4.7 collective-permute-done.2
  83.6 6.8 %fusion.129 = f32[2,10,256,512]{3,2,1,0:T(8,128)} fusion(bf16[2,256,10,64]{1,3,2,0:T(8,128)(2,1)} %bitcast.231, bf16[1,2,256,10,64]{2,4,3,1,0:T(8,128)(2,1)S(1)} %broadcast_in_dim.13, bf16[1,2,256,10,64]{2,4,3,1,0:T(8,128)(2,1)} %bitcast.229), kind=kOutput, calls=%fused_computation.139 | convolution fusion | flops 338165760 | bytes 12451840 | tf_op jit(solution)/shard_map/lfshd,lfthd->lfhst/dot_general | solution.py:88
  90.4 12.8 %fusion.174 = (f32[2,10,256]{2,1,0:T(8,128)S(1)}, f32[2,10,256,512]{3,2,1,0:T(8,128)}) fusion(f32[2,10,256,512]{3,2,1,0:T(8,128)} %fusion.129), kind=kOutput, calls=%fused_computation.182 | output fusion | flops 10486271 | bytes 20992000 | tf_op jit(solution)/shard_map/sub | solution.py:95
  105.3 17.7 %fusion.93 = bf16[2,10,64,256]{3,2,1,0:T(8,128)(2,1)} fusion(bf16[1,2,256,10,64]{2,4,3,1,0:T(8,128)(2,1)} %broadcast_in_dim.11, bf16[1,2,256,10,64]{2,4,3,1,0:T(8,128)(2,1)} %bitcast.233, f32[2,10,256]{2,1,0:T(8,128)S(1)} %get-tuple-element.66, f32[2,10,256,512]{3,2,1,0:T(8,128)} %fusion.129), kind=kOutput, calls=%fused_computation.103 | convolution fusion | flops 351606272 | bytes 12472320 | tf_op jit(solution)/shard_map/lfhst,lfthd->lfshd/dot_general | solution.py:98
  123.0 3.9 fusion.71
  126.9 10.1 %fusion.57 = bf16[1,2,256,1280]{3,2,1,0:T(8,128)(2,1)S(1)} fusion(bf16[1280,3,1280]{2,0,1:T(8,128)(2,1)} %param.18, bf16[1,2,256,1,1280]{4,2,3,1,0:T(8,128)(2,1)S(1)} %copy-done.28, bf16[1,2,256,1,1280]{4,2,3,1,0:T(8,128)(2,1)S(1)} %bitcast.225, bf16[1,2,256,1,1280]{4,2,3,1,0:T(8,128)(2,1)S(1)} %copy-done.27, ...), kind=kOutput, calls=%fused_computation.64 | convolution fusion | flops 5044961280 | bytes 17694720 | tf_op jit(solution)/shard_map/lfsjo,cjo->lfsc/dot_general | solution.py:188
  138.1 2.1 fusion.105
  141.5 17.6 %fusion.74 = f32[2,10,64,512]{3,2,1,0:T(8,128)} fusion(bf16[2,256,10,64]{1,3,2,0:T(8,128)(2,1)S(1)} %bitcast.235, f32[2,10,256]{2,1,0:T(8,128)S(1)} %get-tuple-element.66, f32[2,10,256,512]{3,2,1,0:T(8,128)} %fusion.129), kind=kOutput, calls=%fused_computation.79 | convolution fusion | flops 348657152 | bytes 13783040 | tf_op jit(solution)/shard_map/lfhst,lfshd->lfthd/dot_general | solution.py:119
  159.1 2.3 slice.117
  163.0 5.4 %fusion.123 = f32[2,10,256,512]{3,2,1,0:T(8,128)} fusion(bf16[2,256,10,64]{1,3,2,0:T(8,128)(2,1)S(1)} %bitcast.236, bf16[2,256,10,64]{1,3,2,0:T(8,128)(2,1)S(1)} %broadcast_in_dim.14, bf16[2,256,10,64]{1,3,2,0:T(8,128)(2,1)S(1)} %bitcast.234), kind=kOutput, calls=%fused_computation.130 | convolution fusion | flops 338165760 | bytes 12451840 | tf_op jit(solution)/shard_map/lfshd,lfthd->lfhst/dot_general | solution.py:107
  168.4 42.8 %fusion.16 = f32[2,10,64,512]{3,2,1,0:T(8,128)} fusion(bf16[2,256,10,64]{1,3,2,0:T(8,128)(2,1)S(1)} %bitcast.232, f32[2,10,256,512]{3,2,1,0:T(8,128)} %fusion.123, f32[2,10,256,512]{3,2,1,0:T(8,128)} %get-tuple-element.67, f32[2,10,256]{2,1,0:T(8,128)S(1)} %get-tuple-element.66), kind=kOutput, calls=%fused_computation.20 | convolution fusion | flops 353900032 | bytes 24268800 | tf_op jit(solution)/shard_map/lfhst,lfshd->lfthd/dot_general | solution.py:116
  211.2 2.2 slice.116
  214.9 43.0 %fusion.108 = bf16[2,10,64,256]{3,2,1,0:T(8,128)(2,1)} fusion(f32[2,10,256,512]{3,2,1,0:T(8,128)} %fusion.123, bf16[1,2,256,10,64]{2,4,3,1,0:T(8,128)(2,1)} %copy-done.26, bf16[1,2,256,10,64]{2,4,3,1,0:T(8,128)(2,1)} %bitcast.230, f32[2,10,256,512]{3,2,1,0:T(8,128)} %get-tuple-element.67, f32[2,10,256]{2,1,0:T(8,128)S(1)} %get-tuple-element.66), kind=kOutput, calls=%fused_computation.108 | convolution fusion | flops 356849152 | bytes 22958080 | tf_op jit(solution)/shard_map/lfhst,lfthd->lfshd/dot_general | solution.py:112
  257.9 3.8 fusion.46
  261.7 2.6 fusion.45
  264.3 2.7 fusion.84
  267.1 2.2 copy.77
  269.2 2.5 convolution_bitcast_fusion.1
  271.8 3.7 fusion.44
  275.5 4.5 concatenate.72
  280.0 2.2 copy.76
  282.2 2.5 convolution_bitcast_fusion.2
  284.8 3.6 fusion.43
  288.4 4.4 concatenate.71
  292.8 4.4 concatenate.70
  297.2 2.7 constant_dynamic-update-slice_fusion.4
  300.0 3.9 concatenate.73
  305.6 3.2 convolution_add_fusion.4
  314.0 7.3 %collective-permute-done.7 = bf16[1,256,1280]{1,2,0:T(8,128)(2,1)S(1)} collective-permute-done((bf16[1,256,1280]{1,2,0:T(8,128)(2,1)S(1)}, bf16[1,256,1280]{1,2,0:T(8,128)(2,1)S(1)}, u32[]{:S(2)}, u32[]{:S(2)}) %collective-permute-start.7) | collective-permute-done | bytes 655392 | tf_op jit(solution)/shard_map/ppermute | solution.py:30
  324.1 14.7 %collective-permute-done.8 = bf16[1,256,1280]{1,2,0:T(8,128)(2,1)S(1)} collective-permute-done((bf16[1,256,1280]{1,2,0:T(8,128)(2,1)S(1)}, bf16[1,256,1280]{1,2,0:T(8,128)(2,1)S(1)}, u32[]{:S(2)}, u32[]{:S(2)}) %collective-permute-start.8) | collective-permute-done | bytes 655392 | tf_op jit(solution)/shard_map/ppermute | solution.py:30
  343.2 13.6 %collective-permute-done.9 = bf16[1,256,1280]{1,2,0:T(8,128)(2,1)S(1)} collective-permute-done((bf16[1,256,1280]{1,2,0:T(8,128)(2,1)S(1)}, bf16[1,256,1280]{1,2,0:T(8,128)(2,1)S(1)}, u32[]{:S(2)}, u32[]{:S(2)}) %collective-permute-start.9) | collective-permute-done | bytes 655392 | tf_op jit(solution)/shard_map/ppermute | solution.py:30
  358.0 15.0 %conditional.1 = (f32[1,1,256,1280]{3,2,1,0:T(8,128)}) conditional(s32[]{:T(128)} %convert_element_type.193, () %tuple.20, (pred[]{:T(512)}, f32[1,256,1280]{1,2,0:T(8,128)S(1)}, f32[1,256,1280]{1,2,0:T(8,128)}, f32[1280,640]{1,0:T(8,128)}, f32[1280,640]{1,0:T(8,128)}) %tuple.42), branch_computations={%region_9.10_spmd, %region_10.11_spmd} | conditional | flops 5034147840 | bytes 47185984 | solution.py:222
  359.5 2.8 copy.62
  362.3 2.0 add_select_fusion
  365.0 3.4 fusion.1
  368.5 4.6 fusion
  373.0 2.9 fusion.116
  375.9 2.8 fusion.66
  384.0 8.8 %collective-permute-done.3 = bf16[1,1,256,1280]{3,2,1,0:T(8,128)(2,1)S(1)} collective-permute-done((bf16[1,1,256,1280]{3,2,1,0:T(8,128)(2,1)S(1)}, bf16[1,1,256,1280]{3,2,1,0:T(8,128)(2,1)S(1)}, u32[]{:S(2)}, u32[]{:S(2)}) %collective-permute-start.3) | collective-permute-done | bytes 655392 | tf_op jit(solution)/shard_map/ppermute | solution.py:58
  392.8 4.3 collective-permute-done.4
  397.4 10.9 %fusion.54 = bf16[1,2,256,1280]{3,2,1,0:T(8,128)(2,1)} fusion(bf16[1280,3,1280]{2,0,1:T(8,128)(2,1)} %param.18, bf16[1,2,256,1,1280]{4,2,1,3,0:T(8,128)(2,1)S(1)} %get-tuple-element.59, bf16[1,2,256,1,1280]{4,2,1,3,0:T(8,128)(2,1)S(1)} %bitcast.226, bf16[1,2,256,1,1280]{4,2,1,3,0:T(8,128)(2,1)S(1)} %get-tuple-element.58, ...), kind=kOutput, calls=%fused_computation.63 | convolution fusion | flops 5039063040 | bytes 16384000 | tf_op jit(solution)/shard_map/lfsjc,cjo->lfso/dot_general | solution.py:183
  408.2 61.1 %reduce-scatter.4.cloned.1.call-done = bf16[1,8,25610]{2,1,0:T(8,128)(2,1)} async-done(((bf16[16,8,25610]{2,1,0:T(8,128)(2,1)}), bf16[1,8,25610]{2,1,0:T(8,128)(2,1)}) %reduce-scatter.4.cloned.1.call-update) | async-done | bytes 409776
  470.4 1.8 copy.67
  472.1 4.2 all-to-all-start
  476.4 4.4 fusion.65
  480.8 7.8 %all-to-all-done = f32[8,1,25610]{2,1,0:T(1,128)} async-done(((f32[8,1,25610]{2,1,0:T(1,128)}), f32[8,1,25610]{2,1,0:T(1,128)}, u32[]{:S(2)}, u32[]{:S(2)}) %all-to-all-start) | async-done | bytes 819552 | tf_op jit(solution)/shard_map/all_to_all | solution.py:41
  488.6 1.7 reduce_sum.125
  (124 shorter events, 44.2 us)
Async XLA Ops:
  7.2 115.8 %copy-start = (bf16[640,1280]{1,0:T(8,128)(2,1)S(1)}, bf16[640,1280]{1,0:T(8,128)(2,1)}, u32[]{:S(2)}) copy-start(bf16[640,1280]{1,0:T(8,128)(2,1)} %param.17) | copy-start | bytes 4915204
  7.2 16.0 %copy-start.2 = (bf16[1,2,256,1280]{3,2,1,0:T(8,128)(2,1)S(1)}, bf16[1,2,256,1280]{3,2,1,0:T(8,128)(2,1)}, u32[]{:S(2)}) copy-start(bf16[1,2,256,1280]{3,2,1,0:T(8,128)(2,1)} %param.12) | copy-start | bytes 3932164
  7.2 462.1 %reduce-scatter.4.cloned.1.call-start = ((), (), s32[]{:S(2)}) async-start(), calls=%async_computation.2 | async-start | bytes 6998016
  9.4 31.9 %collective-permute-start = (bf16[1,256,1280]{2,1,0:T(8,128)(2,1)}, bf16[1,256,1280]{2,1,0:T(8,128)(2,1)}, u32[]{:S(2)}, u32[]{:S(2)}) collective-permute-start(bf16[1,256,1280]{2,1,0:T(8,128)(2,1)} %slice_bitcast_fusion.5), channel_id=1, source_target_pairs={{0,4},{8,12},{16,20},{24,28},{32,36},{40,44},{48,52},{56,60},{64,6... | collective-permute-start | bytes 1966088 | tf_op jit(solution)/shard_map/ppermute | solution.py:20
  16.4 27.9 %copy-start.30 = (f32[1280]{0:T(1024)S(1)}, f32[1280]{0:T(1024)}, u32[]{:S(2)}) copy-start(f32[1280]{0:T(1024)} %param.13) | copy-start | bytes 15364
  16.4 52.5 %collective-permute-start.5 = (bf16[1,1,256,1280]{3,2,1,0:T(8,128)(2,1)}, bf16[1,1,256,1280]{3,2,1,0:T(8,128)(2,1)}, u32[]{:S(2)}, u32[]{:S(2)}) collective-permute-start(bf16[1,1,256,1280]{3,2,1,0:T(8,128)(2,1)} %get-tuple-element.56), channel_id=1, source_target_pairs={{1,0},{2,1},{3,2},{4,3},{5,4},{6,5},{7,6},{9,8},{10,9},{11,10},{12... | collective-permute-start | bytes 1966088 | tf_op jit(solution)/shard_map/ppermute | solution.py:59
  17.8 51.1 %collective-permute-start.6 = (bf16[1,1,256,1280]{3,2,1,0:T(8,128)(2,1)}, bf16[1,1,256,1280]{3,2,1,0:T(8,128)(2,1)}, u32[]{:S(2)}, u32[]{:S(2)}) collective-permute-start(bf16[1,1,256,1280]{3,2,1,0:T(8,128)(2,1)} %get-tuple-element.57), channel_id=1, source_target_pairs={{0,1},{1,2},{2,3},{3,4},{4,5},{5,6},{6,7},{8,9},{9,10},{10,11},{11... | collective-permute-start | bytes 1966088 | tf_op jit(solution)/shard_map/ppermute | solution.py:58
  23.5 20.8 %copy-start.31 = (bf16[1280,640]{1,0:T(8,128)(2,1)S(1)}, bf16[1280,640]{1,0:T(8,128)(2,1)}, u32[]{:S(2)}) copy-start(bf16[1280,640]{1,0:T(8,128)(2,1)} %param.14) | copy-start | bytes 4915204
  42.2 17.7 %collective-permute-start.1 = (bf16[1,256,1280]{2,1,0:T(8,128)(2,1)}, bf16[1,256,1280]{2,1,0:T(8,128)(2,1)}, u32[]{:S(2)}, u32[]{:S(2)}) collective-permute-start(bf16[1,256,1280]{2,1,0:T(8,128)(2,1)} %broadcast_select_fusion), channel_id=1, source_target_pairs={{0,3},{4,7},{8,11},{12,15},{16,19},{20,23},{24,27},{28,31},{32,35}... | collective-permute-start | bytes 1966088 | tf_op jit(solution)/shard_map/ppermute | solution.py:20
  48.6 3.5 copy-start.9
  56.4 8.1 %copy-start.12 = (bf16[1280,640]{1,0:T(8,128)(2,1)S(1)}, bf16[1280,640]{1,0:T(8,128)(2,1)}, u32[]{:S(2)}) copy-start(bf16[1280,640]{1,0:T(8,128)(2,1)} %param.16) | copy-start | bytes 4915204
  61.9 15.0 %collective-permute-start.2 = (bf16[1,256,1280]{2,1,0:T(8,128)(2,1)}, bf16[1,256,1280]{2,1,0:T(8,128)(2,1)}, u32[]{:S(2)}, u32[]{:S(2)}) collective-permute-start(bf16[1,256,1280]{2,1,0:T(8,128)(2,1)} %broadcast_select_fusion.1), channel_id=1, source_target_pairs={{0,1},{3,2},{4,5},{7,6},{8,9},{11,10},{12,13},{15,14},{16,17},{19,... | collective-permute-start | bytes 1966088 | tf_op jit(solution)/shard_map/ppermute | solution.py:20
  72.2 6.4 %copy-start.10 = (bf16[1280,640]{1,0:T(8,128)(2,1)S(1)}, bf16[1280,640]{1,0:T(8,128)(2,1)}, u32[]{:S(2)}) copy-start(bf16[1280,640]{1,0:T(8,128)(2,1)} %param.15) | copy-start | bytes 4915204
  78.3 1.8 copy-start.6
  78.3 1.8 copy-start.13
  82.8 0.8 copy-start.26
  123.0 3.9 copy-start.18
  123.0 3.9 copy-start.27
  123.0 3.9 copy-start.28
  126.9 10.1 %copy-start.34 = (bf16[1,2,256,1280]{3,2,1,0:T(8,128)(2,1)}, bf16[1,2,256,1280]{3,2,1,0:T(8,128)(2,1)S(1)}, u32[]{:S(2)}) copy-start(bf16[1,2,256,1280]{3,2,1,0:T(8,128)(2,1)S(1)} %get-tuple-element.69) | copy-start | bytes 3932164
  137.0 1.1 copy-start.29
  141.4 17.6 %copy-start.24 = (bf16[2,256,640]{1,2,0:T(8,128)(2,1)}, bf16[2,256,640]{1,2,0:T(8,128)(2,1)S(1)}, u32[]{:S(2)}) copy-start(bf16[2,256,640]{1,2,0:T(8,128)(2,1)S(1)} %copy.56) | copy-start | bytes 1966084
  159.1 3.9 copy-start.22
  159.1 3.9 copy-start.25
  163.0 5.4 %copy-start.21 = (bf16[2,256,640]{1,2,0:T(8,128)(2,1)S(1)}, bf16[2,256,640]{1,2,0:T(8,128)(2,1)}, u32[]{:S(2)}) copy-start(bf16[2,256,640]{1,2,0:T(8,128)(2,1)} %copy.52) | copy-start | bytes 1966084
  257.9 3.8 copy-start.33
  261.7 2.6 copy-start.32
  269.2 2.6 copy-start.7
  282.2 2.6 copy-start.8
  303.9 1.7 copy-start.11
  304.0 4.8 copy-start.14
  304.0 4.8 copy-start.23
  304.0 17.3 %collective-permute-start.7 = (bf16[1,256,1280]{1,2,0:T(8,128)(2,1)S(1)}, bf16[1,256,1280]{1,2,0:T(8,128)(2,1)S(1)}, u32[]{:S(2)}, u32[]{:S(2)}) collective-permute-start(bf16[1,256,1280]{1,2,0:T(8,128)(2,1)S(1)} %fusion.130), channel_id=1, source_target_pairs={{1,0},{2,3},{5,4},{6,7},{9,8},{10,11},{13,12},{14,15},{17,16},{18,... | collective-permute-start | bytes 1966088 | tf_op jit(solution)/shard_map/ppermute | solution.py:30
  310.0 2.4 copy-start.3
  310.0 2.6 copy-start.17
  312.7 10.2 %copy-start.16 = (bf16[16,8,6400]{2,1,0:T(8,128)(2,1)S(1)}, bf16[16,8,6400]{2,1,0:T(8,128)(2,1)}, u32[]{:S(2)}) copy-start(bf16[16,8,6400]{2,1,0:T(8,128)(2,1)} %concatenate.72) | copy-start | bytes 4915204
  321.5 17.3 %collective-permute-start.8 = (bf16[1,256,1280]{1,2,0:T(8,128)(2,1)S(1)}, bf16[1,256,1280]{1,2,0:T(8,128)(2,1)S(1)}, u32[]{:S(2)}, u32[]{:S(2)}) collective-permute-start(bf16[1,256,1280]{1,2,0:T(8,128)(2,1)S(1)} %fusion.136), channel_id=1, source_target_pairs={{3,0},{7,4},{11,8},{15,12},{19,16},{23,20},{27,24},{31,28},{35,32}... | collective-permute-start | bytes 1966088 | tf_op jit(solution)/shard_map/ppermute | solution.py:30
  324.1 17.8 %copy-start.15 = (bf16[16,8,6400]{2,1,0:T(8,128)(2,1)S(1)}, bf16[16,8,6400]{2,1,0:T(8,128)(2,1)}, u32[]{:S(2)}) copy-start(bf16[16,8,6400]{2,1,0:T(8,128)(2,1)} %concatenate.73) | copy-start | bytes 4915204
  340.3 17.7 %copy-start.20 = (f32[1,256,1280]{1,2,0:T(8,128)S(1)}, f32[1,256,1280]{1,2,0:T(8,128)}, u32[]{:S(2)}) copy-start(f32[1,256,1280]{1,2,0:T(8,128)} %get-tuple-element.51) | copy-start | bytes 3932164
  340.3 16.5 %collective-permute-start.9 = (bf16[1,256,1280]{1,2,0:T(8,128)(2,1)S(1)}, bf16[1,256,1280]{1,2,0:T(8,128)(2,1)S(1)}, u32[]{:S(2)}, u32[]{:S(2)}) collective-permute-start(bf16[1,256,1280]{1,2,0:T(8,128)(2,1)S(1)} %get-tuple-element.50), channel_id=1, source_target_pairs={{4,0},{12,8},{20,16},{28,24},{36,32},{44,40},{52,48},{60,56},{68,6... | collective-permute-start | bytes 1966088 | tf_op jit(solution)/shard_map/ppermute | solution.py:30
  362.3 2.7 copy-start.4
  365.0 3.4 copy-start.5
  379.5 1.3 copy-start.19
  380.9 11.8 %collective-permute-start.3 = (bf16[1,1,256,1280]{3,2,1,0:T(8,128)(2,1)S(1)}, bf16[1,1,256,1280]{3,2,1,0:T(8,128)(2,1)S(1)}, u32[]{:S(2)}, u32[]{:S(2)}) collective-permute-start(bf16[1,1,256,1280]{3,2,1,0:T(8,128)(2,1)S(1)} %get-tuple-element.60), channel_id=1, source_target_pairs={{0,1},{1,2},{2,3},{3,4},{4,5},{5,6},{6,7},{8,9},{9,10},{10,11},{11... | collective-permute-start | bytes 1966088 | tf_op jit(solution)/shard_map/ppermute | solution.py:58
  382.3 15.1 %copy-start.35 = (bf16[1,2,256,1280]{3,2,1,0:T(8,128)(2,1)S(1)}, bf16[1,2,256,1280]{3,2,1,0:T(8,128)(2,1)}, u32[]{:S(2)}) copy-start(bf16[1,2,256,1280]{3,2,1,0:T(8,128)(2,1)} %copy-done.34) | copy-start | bytes 3932164
  382.3 14.8 %collective-permute-start.4 = (bf16[1,1,256,1280]{3,2,1,0:T(8,128)(2,1)S(1)}, bf16[1,1,256,1280]{3,2,1,0:T(8,128)(2,1)S(1)}, u32[]{:S(2)}, u32[]{:S(2)}) collective-permute-start(bf16[1,1,256,1280]{3,2,1,0:T(8,128)(2,1)S(1)} %get-tuple-element.61), channel_id=1, source_target_pairs={{1,0},{2,1},{3,2},{4,3},{5,4},{6,5},{7,6},{9,8},{10,9},{11,10},{12... | collective-permute-start | bytes 1966088 | tf_op jit(solution)/shard_map/ppermute | solution.py:59
  472.1 16.5 %all-to-all-start = ((f32[8,1,25610]{2,1,0:T(1,128)}), f32[8,1,25610]{2,1,0:T(1,128)}, u32[]{:S(2)}, u32[]{:S(2)}) async-start(f32[8,1,25610]{2,1,0:T(1,128)} %copy.67), calls=%async_computation | async-start | bytes 1646592 | tf_op jit(solution)/shard_map/all_to_all | solution.py:41
  476.4 17.0 %copy-start.1 = (bf16[640,1280]{1,0:T(8,128)(2,1)S(1)}, bf16[640,1280]{1,0:T(8,128)(2,1)}, u32[]{:S(2)}) copy-start(bf16[640,1280]{1,0:T(8,128)(2,1)} %param.17) | copy-start | bytes 4915204
Sparse Core Ops, SparseCore 0:
  379.7 89.5 reduce-scatter.3

commit v6 on v4

--- a/solution.py
+++ b/solution.py
@@ -33,8 +33,8 @@
     count = lax.axis_size(outer) * lax.axis_size(inner)
     packed = jnp.concatenate([p.reshape(count, -1) for p in parts], axis=1)
     share = packed.reshape((lax.axis_size(outer), -1) + packed.shape[1:])
-    share = lax.psum_scatter(share, outer, scatter_dimension=0, tiled=True)[0]
-    share = lax.all_to_all(share, inner, 0, 0, tiled=True)
+    share = lax.psum_scatter(share.astype(jnp.bfloat16), outer, scatter_dimension=0, tiled=True)[0]
+    share = lax.all_to_all(share.astype(jnp.float32), inner, 0, 0, tiled=True)
     share = jnp.sum(share, axis=0)
     outs, start = [], 0
     for p in parts:
@@ -207,14 +207,10 @@
     first_sum = to_owner(jnp.concatenate([key_first_grad, val_first_grad], axis=-1), "tm")
     width = key_first_grad.shape[-1]
 
-    def owner_terms(operands):
-        both = jnp.concatenate([w_key, w_value], axis=1)
-        return split_dot(operands, both, (((2,), (1,)), ((), ())))
-
-    def no_terms(operands):
-        return jnp.zeros(normed_first.shape, jnp.float32)
-
-    first_rows = lax.cond(is_owner, owner_terms, no_terms, first_sum)
+    dims = (((2,), (1,)), ((), ()))
+    first_rows = split_dot(first_sum[..., :width], w_key, dims)
+    first_rows = first_rows + split_dot(first_sum[..., width:], w_value, dims)
+    first_rows = jnp.where(is_owner, first_rows, jnp.zeros_like(first_rows))
     first_flat = normed_first.reshape(-1, normed_first.shape[-1])
     extra_key = split_dot(key_first_grad.reshape(-1, width), first_flat, (((0,), (0,)), ((), ()))).T
     extra_val = split_dot(val_first_grad.reshape(-1, width), first_flat, (((0,), (0,)), ((), ()))).T

time: 551 us -> 475 us (0.86)
  local copies, waits for them, and re-layouts: 91.3 us -> 63.3 us
  waiting for transfers between devices: 139 us -> 118 us
  other arithmetic: 55.2 us -> 34.6 us
  matrix products: 204 us -> 198 us
    unnamed x2, waiting for transfers between devices: 94 us -> 60.5 us
    another operation x8 -> x0, local copies, waits for them, and re-layouts: 21.1 us -> none
    ppermute x7, waiting for transfers between devices: 2.2 us -> 15.1 us  [to_owner(): got = lax.ppermute(block.astype(jnp.bfloat16), axis, [(source, 0)])]
    convert_element_type x7 -> x1, other arithmetic: 13.8 us -> 1.06 us  [scatter_sum(): share = lax.all_to_all(share.astype(jnp.float32), inner, 0, 0, tiled=True)]
    unnamed x93 -> x103, local copies, waits for them, and re-layouts: 22.5 us -> 17.2 us
    dot_general x6 -> x8, matrix products: 16.5 us -> 12.4 us  [split_dot(): lax.dot_general(part, narrow, dims, preferred_element_type=jnp.float32)]
  transfers between devices with their start and end apart: 20 -> 20, of which waited for: 8 -> 9; matrix products, arithmetic and copies ran while one was open for 29% -> 27% of each run, Pallas kernels for 0% -> 0%
where the time goes in v6:
time: 475 us; the launch traced here: 468 us
  matrix products  198 us (42%)
  waiting for transfers between devices  118 us (25%)
  local copies, waits for them, and re-layouts  63.3 us (13%)
  starting transfers between devices  40.2 us (8%)
  other arithmetic  34.6 us (7%)
  between operations  14.9 us (3%)
    unnamed x2, waiting for transfers between devices  60.5 us
    dot_general x1, matrix products, attend_back(): jnp.einsum('lfhst,lfshd->lfthd', grad_score, split_heads(queries), prefer...  43.1 us
    dot_general x1, matrix products, attend_back(): jnp.einsum('lfhst,lfthd->lfshd', grad_score, split_heads(key_all), prefer...  42.6 us
    ppermute x7, waiting for transfers between devices, from_owner(): got = lax.ppermute(block, axis, [(0, target)])  19.9 us
    dot_general x1, matrix products, attend_back(): jnp.einsum('lfhst,lfshd->lfthd', prob_b, grad_heads, preferred_element_ty...  18.6 us
    concatenate x6, local copies, waits for them, and re-layouts, scatter_sum(): packed = jnp.concatenate([p.reshape(count, -1) for p in parts], axis=1)  17.8 us
    dot_general x1, matrix products, attend(): jnp.einsum('lfhst,lfthd->lfshd', prob_b, split_heads(val_all), preferred_...  17.6 us
    unnamed x103, local copies, waits for them, and re-layouts  17.2 us
  transfers between devices with their start and end apart: 20, of which 9 were waited for; matrix products, arithmetic and copies ran while one was open for 27% of the time, Pallas kernels for 0%

profile of v6, /device:TPU:0, one launch (start us, length us, event | category | flops | bytes accessed | tf_op | source)
XLA Modules:
  0.0 468.2 jit_solution(15782940817955310714)
XLA Ops:
  7.3 2.1 slice_bitcast_fusion.1
  9.4 3.5 collective-permute-start.6
  12.9 2.2 collective-permute-start.5
  15.2 2.2 collective-permute-start.4
  17.3 2.2 collective-permute-start.3
  19.5 2.1 collective-permute-start.2
  21.6 1.6 convert_reduce_fusion
  23.7 2.1 fusion.107
  25.9 2.2 fusion.104
  28.3 2.1 collective-permute-start.1
  30.4 11.9 %collective-permute-done.5 = bf16[1,256,1280]{2,1,0:T(8,128)(2,1)S(1)} collective-permute-done((bf16[1,256,1280]{2,1,0:T(8,128)(2,1)}, bf16[1,256,1280]{2,1,0:T(8,128)(2,1)S(1)}, u32[]{:S(2)}, u32[]{:S(2)}) %collective-permute-start.5) | collective-permute-done | bytes 655392 | tf_op jit(solution)/shard_map/ppermute | solution.py:19
  42.3 2.1 collective-permute-start
  44.5 2.2 fusion.101
  46.7 2.2 copy.53
  48.8 2.2 copy.52
  51.0 2.2 copy.50
  53.2 2.5 fusion.188
  57.1 5.7 %collective-permute-start.10 = (bf16[1,1,256,1280]{3,2,1,0:T(8,128)(2,1)}, bf16[1,1,256,1280]{3,2,1,0:T(8,128)(2,1)}, u32[]{:S(2)}, u32[]{:S(2)}) collective-permute-start(bf16[1,1,256,1280]{3,2,1,0:T(8,128)(2,1)} %get-tuple-element.27), channel_id=1, source_target_pairs={{0,1},{1,2},{2,3},{3,4},{4,5},{5,6},{6,7},{8,9},{9,10},{10,11},{11... | collective-permute-start | bytes 1966088 | tf_op jit(solution)/shard_map/ppermute | solution.py:63
  62.8 7.7 %collective-permute-done.1 = bf16[1,256,1280]{2,1,0:T(8,128)(2,1)} collective-permute-done((bf16[1,256,1280]{2,1,0:T(8,128)(2,1)}, bf16[1,256,1280]{2,1,0:T(8,128)(2,1)}, u32[]{:S(2)}, u32[]{:S(2)}) %collective-permute-start.1) | collective-permute-done | bytes 655392 | tf_op jit(solution)/shard_map/ppermute | solution.py:19
  77.9 6.7 %fusion.132 = f32[2,10,256,512]{3,2,1,0:T(8,128)} fusion(bf16[2,256,10,64]{1,3,2,0:T(8,128)(2,1)} %bitcast.236, bf16[1,2,256,10,64]{2,4,3,1,0:T(8,128)(2,1)S(1)} %broadcast_in_dim.15, bf16[1,2,256,10,64]{2,4,3,1,0:T(8,128)(2,1)} %bitcast.238), kind=kOutput, calls=%fused_computation.139 | convolution fusion | flops 338165760 | bytes 12451840 | tf_op jit(solution)/shard_map/lfshd,lfthd->lfhst/dot_general | solution.py:93
  84.6 13.2 %fusion.191 = (f32[2,10,256]{2,1,0:T(8,128)S(1)}, f32[2,10,256,512]{3,2,1,0:T(8,128)}) fusion(f32[2,10,256,512]{3,2,1,0:T(8,128)} %fusion.132), kind=kOutput, calls=%fused_computation.196 | output fusion | flops 10486271 | bytes 20992000 | tf_op jit(solution)/shard_map/sub | solution.py:100
  98.7 17.6 %fusion.98 = bf16[2,10,64,256]{3,2,1,0:T(8,128)(2,1)} fusion(bf16[1,2,256,10,64]{2,4,3,1,0:T(8,128)(2,1)} %broadcast_in_dim.13, bf16[1,2,256,10,64]{2,4,3,1,0:T(8,128)(2,1)} %bitcast.240, f32[2,10,256]{2,1,0:T(8,128)S(1)} %get-tuple-element.36, f32[2,10,256,512]{3,2,1,0:T(8,128)} %fusion.132), kind=kOutput, calls=%fused_computation.104 | convolution fusion | flops 351606272 | bytes 12472320 | tf_op jit(solution)/shard_map/lfhst,lfthd->lfshd/dot_general | solution.py:103
  116.4 4.3 fusion.76
  120.8 2.0 fusion.121
  122.8 9.7 %fusion.57 = bf16[1,2,256,1280]{3,2,1,0:T(8,128)(2,1)S(1)} fusion(bf16[1280,3,1280]{2,0,1:T(8,128)(2,1)} %param.16, bf16[1,2,256,1,1280]{4,2,3,1,0:T(8,128)(2,1)S(1)} %get-tuple-element.25, bf16[1,2,256,1,1280]{4,2,3,1,0:T(8,128)(2,1)S(1)} %bitcast.232, bf16[1,2,256,1,1280]{4,2,3,1,0:T(8,128)(2,1)S(1)} %get-tuple-element.24, ...), kind=kOutput, calls=%fused_computation.60 | convolution fusion | flops 5044961280 | bytes 17694720 | tf_op jit(solution)/shard_map/lfsjo,cjo->lfsc/dot_general | solution.py:185
  133.7 2.1 fusion.110
  135.8 2.2 copy.56
  137.9 18.6 %fusion.79 = f32[2,10,64,512]{3,2,1,0:T(8,128)} fusion(bf16[2,256,10,64]{1,3,2,0:T(8,128)(2,1)} %bitcast.242, f32[2,10,256]{2,1,0:T(8,128)S(1)} %get-tuple-element.36, f32[2,10,256,512]{3,2,1,0:T(8,128)} %fusion.132), kind=kOutput, calls=%fused_computation.82 | convolution fusion | flops 348657152 | bytes 13783040 | tf_op jit(solution)/shard_map/lfhst,lfshd->lfthd/dot_general | solution.py:124
  156.5 2.5 slice_reduce_fusion
  159.0 2.2 slice.117
  161.2 2.3 fusion.46
  163.6 5.4 %fusion.126 = f32[2,10,256,512]{3,2,1,0:T(8,128)} fusion(bf16[2,256,10,64]{1,3,2,0:T(8,128)(2,1)S(1)} %bitcast.243, bf16[2,256,10,64]{1,3,2,0:T(8,128)(2,1)S(1)} %broadcast_in_dim.16, bf16[2,256,10,64]{1,3,2,0:T(8,128)(2,1)S(1)} %bitcast.241), kind=kOutput, calls=%fused_computation.129 | convolution fusion | flops 338165760 | bytes 12451840 | tf_op jit(solution)/shard_map/lfshd,lfthd->lfhst/dot_general | solution.py:112
  169.0 42.6 %fusion.113 = bf16[2,10,64,256]{3,2,1,0:T(8,128)(2,1)} fusion(f32[2,10,256,512]{3,2,1,0:T(8,128)} %fusion.126, bf16[1,2,256,10,64]{2,4,3,1,0:T(8,128)(2,1)} %copy-done.32, bf16[1,2,256,10,64]{2,4,3,1,0:T(8,128)(2,1)} %bitcast.239, f32[2,10,256,512]{3,2,1,0:T(8,128)} %get-tuple-element.37, f32[2,10,256]{2,1,0:T(8,128)S(1)} %get-tuple-element.36), kind=kOutput, calls=%fused_computation.109 | convolution fusion | flops 356849152 | bytes 22958080 | tf_op jit(solution)/shard_map/lfhst,lfthd->lfshd/dot_general | solution.py:117
  211.6 43.1 %fusion.14 = f32[2,10,64,512]{3,2,1,0:T(8,128)} fusion(bf16[2,256,10,64]{1,3,2,0:T(8,128)(2,1)} %bitcast.237, f32[2,10,256,512]{3,2,1,0:T(8,128)} %fusion.126, f32[2,10,256,512]{3,2,1,0:T(8,128)} %get-tuple-element.37, f32[2,10,256]{2,1,0:T(8,128)S(1)} %get-tuple-element.36), kind=kOutput, calls=%fused_computation.14 | convolution fusion | flops 353900032 | bytes 24268800 | tf_op jit(solution)/shard_map/lfhst,lfshd->lfthd/dot_general | solution.py:121
  254.7 1.6 slice_reduce_fusion.1
  256.3 2.5 slice.116
  258.8 2.6 fusion.152
  269.0 2.6 fusion.45
  271.6 2.8 fusion.89
  274.4 2.5 fusion.155
  277.0 2.2 copy.75
  279.1 3.9 concatenate.73
  283.1 2.6 convolution_bitcast_fusion.1
  285.7 2.1 fusion.44
  287.8 4.4 concatenate.72
  292.2 2.2 copy.74
  294.4 4.4 concatenate.70
  298.8 2.6 convolution_bitcast_fusion.2
  305.4 1.6 copy.76
  308.7 2.1 fusion.43
  310.8 4.4 concatenate.71
  315.1 1.7 constant_dynamic-update-slice_fusion.4
  320.8 2.5 collective-permute-done.14
  323.3 12.6 %collective-permute-done.12 = bf16[1,256,1280]{1,2,0:T(8,128)(2,1)S(1)} collective-permute-done((bf16[1,256,1280]{1,2,0:T(8,128)(2,1)}, bf16[1,256,1280]{1,2,0:T(8,128)(2,1)S(1)}, u32[]{:S(2)}, u32[]{:S(2)}) %collective-permute-start.12) | collective-permute-done | bytes 655392 | tf_op jit(solution)/shard_map/ppermute | solution.py:27
  335.9 2.6 convert_add_fusion.2
  351.4 9.9 %collective-permute-done.7 = bf16[1,1,256,1280]{3,2,1,0:T(8,128)(2,1)S(1)} collective-permute-done((bf16[1,1,256,1280]{3,2,1,0:T(8,128)(2,1)S(1)}, bf16[1,1,256,1280]{3,2,1,0:T(8,128)(2,1)S(1)}, u32[]{:S(2)}, u32[]{:S(2)}) %collective-permute-start.7) | collective-permute-done | bytes 655392 | tf_op jit(solution)/shard_map/ppermute | solution.py:63
  361.2 4.3 collective-permute-done.8
  365.8 10.8 %fusion.54 = bf16[1,2,256,1280]{3,2,1,0:T(8,128)(2,1)} fusion(bf16[1280,3,1280]{2,0,1:T(8,128)(2,1)} %param.16, bf16[1,2,256,1,1280]{4,2,1,3,0:T(8,128)(2,1)S(1)} %get-tuple-element.29, bf16[1,2,256,1,1280]{4,2,1,3,0:T(8,128)(2,1)S(1)} %bitcast.233, bf16[1,2,256,1,1280]{4,2,1,3,0:T(8,128)(2,1)S(1)} %get-tuple-element.28, ...), kind=kOutput, calls=%fused_computation.59 | convolution fusion | flops 5039063040 | bytes 16384000 | tf_op jit(solution)/shard_map/lfsjc,cjo->lfso/dot_general | solution.py:180
  376.5 60.5 %reduce-scatter.4.cloned.1.call-done = bf16[1,8,25610]{2,1,0:T(8,128)(2,1)} async-done(((bf16[16,8,25610]{2,1,0:T(8,128)(2,1)}), bf16[1,8,25610]{2,1,0:T(8,128)(2,1)}) %reduce-scatter.4.cloned.1.call-update) | async-done | bytes 409776
  438.1 1.8 copy.65
  439.9 4.3 all-to-all-start
  444.2 4.3 fusion.70
  448.4 7.9 %all-to-all-done = f32[8,1,25610]{2,1,0:T(1,128)} async-done(((f32[8,1,25610]{2,1,0:T(1,128)}), f32[8,1,25610]{2,1,0:T(1,128)}, u32[]{:S(2)}, u32[]{:S(2)}) %all-to-all-start) | async-done | bytes 819552 | tf_op jit(solution)/shard_map/all_to_all | solution.py:37
  456.3 1.7 reduce_sum.125
  (157 shorter events, 45.9 us)
Async XLA Ops:
  7.2 37.3 %copy-start = (bf16[1280,640]{1,0:T(8,128)(2,1)S(1)}, bf16[1280,640]{1,0:T(8,128)(2,1)}, u32[]{:S(2)}) copy-start(bf16[1280,640]{1,0:T(8,128)(2,1)} %param.14) | copy-start | bytes 4915204
  7.2 16.0 %copy-start.1 = (bf16[1,2,256,1280]{3,2,1,0:T(8,128)(2,1)S(1)}, bf16[1,2,256,1280]{3,2,1,0:T(8,128)(2,1)}, u32[]{:S(2)}) copy-start(bf16[1,2,256,1280]{3,2,1,0:T(8,128)(2,1)} %param.10) | copy-start | bytes 3932164
  7.2 16.5 %copy-start.40 = (f32[1280]{0:T(1024)S(1)}, f32[1280]{0:T(1024)}, u32[]{:S(2)}) copy-start(f32[1280]{0:T(1024)} %param.11) | copy-start | bytes 15364
  7.2 429.9 %reduce-scatter.4.cloned.1.call-start = ((), (), s32[]{:S(2)}) async-start(), calls=%async_computation.2 | async-start | bytes 6998016
  7.2 16.5 %copy-start.16 = (bf16[1280,640]{1,0:T(8,128)(2,1)S(1)}, bf16[1280,640]{1,0:T(8,128)(2,1)}, u32[]{:S(2)}) copy-start(bf16[1280,640]{1,0:T(8,128)(2,1)} %param.13) | copy-start | bytes 4915204
  9.4 18.9 %collective-permute-start.6 = (bf16[1,256,1280]{2,1,0:T(8,128)(2,1)}, bf16[1,256,1280]{2,1,0:T(8,128)(2,1)S(1)}, u32[]{:S(2)}, u32[]{:S(2)}) collective-permute-start(bf16[1,256,1280]{2,1,0:T(8,128)(2,1)} %slice_bitcast_fusion.1), channel_id=1, source_target_pairs={{0,1},{8,9},{16,17},{24,25},{32,33},{40,41},{48,49},{56,57},{64,65... | collective-permute-start | bytes 1966088 | tf_op jit(solution)/shard_map/ppermute | solution.py:19
  12.9 29.4 %collective-permute-start.5 = (bf16[1,256,1280]{2,1,0:T(8,128)(2,1)}, bf16[1,256,1280]{2,1,0:T(8,128)(2,1)S(1)}, u32[]{:S(2)}, u32[]{:S(2)}) collective-permute-start(bf16[1,256,1280]{2,1,0:T(8,128)(2,1)} %slice_bitcast_fusion.1), channel_id=1, source_target_pairs={{0,2},{8,10},{16,18},{24,26},{32,34},{40,42},{48,50},{56,58},{64,6... | collective-permute-start | bytes 1966088 | tf_op jit(solution)/shard_map/ppermute | solution.py:19
  15.2 40.6 %collective-permute-start.4 = (bf16[1,256,1280]{2,1,0:T(8,128)(2,1)}, bf16[1,256,1280]{2,1,0:T(8,128)(2,1)}, u32[]{:S(2)}, u32[]{:S(2)}) collective-permute-start(bf16[1,256,1280]{2,1,0:T(8,128)(2,1)} %slice_bitcast_fusion.1), channel_id=1, source_target_pairs={{0,3},{8,11},{16,19},{24,27},{32,35},{40,43},{48,51},{56,59},{64,6... | collective-permute-start | bytes 1966088 | tf_op jit(solution)/shard_map/ppermute | solution.py:19
  17.3 39.7 %collective-permute-start.3 = (bf16[1,256,1280]{2,1,0:T(8,128)(2,1)}, bf16[1,256,1280]{2,1,0:T(8,128)(2,1)}, u32[]{:S(2)}, u32[]{:S(2)}) collective-permute-start(bf16[1,256,1280]{2,1,0:T(8,128)(2,1)} %slice_bitcast_fusion.1), channel_id=1, source_target_pairs={{0,4},{8,12},{16,20},{24,28},{32,36},{40,44},{48,52},{56,60},{64,6... | collective-permute-start | bytes 1966088 | tf_op jit(solution)/shard_map/ppermute | solution.py:19
  19.5 43.3 %collective-permute-start.2 = (bf16[1,256,1280]{2,1,0:T(8,128)(2,1)}, bf16[1,256,1280]{2,1,0:T(8,128)(2,1)}, u32[]{:S(2)}, u32[]{:S(2)}) collective-permute-start(bf16[1,256,1280]{2,1,0:T(8,128)(2,1)} %slice_bitcast_fusion.1), channel_id=1, source_target_pairs={{0,5},{8,13},{16,21},{24,29},{32,37},{40,45},{48,53},{56,61},{64,6... | collective-permute-start | bytes 1966088 | tf_op jit(solution)/shard_map/ppermute | solution.py:19
  23.7 2.1 copy-start.42
  28.3 18.4 %copy-start.36 = (bf16[1,256,1280]{2,1,0:T(8,128)(2,1)}, bf16[1,256,1280]{2,1,0:T(8,128)(2,1)S(1)}, u32[]{:S(2)}) copy-start(bf16[1,256,1280]{2,1,0:T(8,128)(2,1)S(1)} %collective-permute-done.6) | copy-start | bytes 1966084
  28.3 42.2 %collective-permute-start.1 = (bf16[1,256,1280]{2,1,0:T(8,128)(2,1)}, bf16[1,256,1280]{2,1,0:T(8,128)(2,1)}, u32[]{:S(2)}, u32[]{:S(2)}) collective-permute-start(bf16[1,256,1280]{2,1,0:T(8,128)(2,1)} %slice_bitcast_fusion.1), channel_id=1, source_target_pairs={{0,6},{8,14},{16,22},{24,30},{32,38},{40,46},{48,54},{56,62},{64,7... | collective-permute-start | bytes 1966088 | tf_op jit(solution)/shard_map/ppermute | solution.py:19
  42.3 4.3 copy-start.38
  42.3 28.1 %collective-permute-start = (bf16[1,256,1280]{2,1,0:T(8,128)(2,1)}, bf16[1,256,1280]{2,1,0:T(8,128)(2,1)}, u32[]{:S(2)}, u32[]{:S(2)}) collective-permute-start(bf16[1,256,1280]{2,1,0:T(8,128)(2,1)} %slice_bitcast_fusion.1), channel_id=1, source_target_pairs={{0,7},{8,15},{16,23},{24,31},{32,39},{40,47},{48,55},{56,63},{64,7... | collective-permute-start | bytes 1966088 | tf_op jit(solution)/shard_map/ppermute | solution.py:19
  53.2 17.3 %copy-start.37 = (bf16[1,256,1280]{2,1,0:T(8,128)(2,1)S(1)}, bf16[1,256,1280]{2,1,0:T(8,128)(2,1)}, u32[]{:S(2)}) copy-start(bf16[1,256,1280]{2,1,0:T(8,128)(2,1)} %copy-done.36) | copy-start | bytes 1966084
  53.2 17.3 %copy-start.39 = (bf16[1,256,1280]{2,1,0:T(8,128)(2,1)S(1)}, bf16[1,256,1280]{2,1,0:T(8,128)(2,1)}, u32[]{:S(2)}) copy-start(bf16[1,256,1280]{2,1,0:T(8,128)(2,1)} %copy-done.38) | copy-start | bytes 1966084
  55.7 65.0 %collective-permute-start.9 = (bf16[1,1,256,1280]{3,2,1,0:T(8,128)(2,1)}, bf16[1,1,256,1280]{3,2,1,0:T(8,128)(2,1)}, u32[]{:S(2)}, u32[]{:S(2)}) collective-permute-start(bf16[1,1,256,1280]{3,2,1,0:T(8,128)(2,1)} %get-tuple-element.26), channel_id=1, source_target_pairs={{1,0},{2,1},{3,2},{4,3},{5,4},{6,5},{7,6},{9,8},{10,9},{11,10},{12... | collective-permute-start | bytes 1966088 | tf_op jit(solution)/shard_map/ppermute | solution.py:64
  57.0 14.7 %copy-start.17 = (bf16[1280,640]{1,0:T(8,128)(2,1)S(1)}, bf16[1280,640]{1,0:T(8,128)(2,1)}, u32[]{:S(2)}) copy-start(bf16[1280,640]{1,0:T(8,128)(2,1)} %param.13) | copy-start | bytes 4915204
  57.1 63.7 %collective-permute-start.10 = (bf16[1,1,256,1280]{3,2,1,0:T(8,128)(2,1)}, bf16[1,1,256,1280]{3,2,1,0:T(8,128)(2,1)}, u32[]{:S(2)}, u32[]{:S(2)}) collective-permute-start(bf16[1,1,256,1280]{3,2,1,0:T(8,128)(2,1)} %get-tuple-element.27), channel_id=1, source_target_pairs={{0,1},{1,2},{2,3},{3,4},{4,5},{5,6},{6,7},{8,9},{9,10},{10,11},{11... | collective-permute-start | bytes 1966088 | tf_op jit(solution)/shard_map/ppermute | solution.py:63
  116.4 4.4 copy-start.26
  120.8 2.1 copy-start.46
  122.8 10.9 %copy-start.41 = (bf16[640,1280]{1,0:T(8,128)(2,1)S(1)}, bf16[640,1280]{1,0:T(8,128)(2,1)}, u32[]{:S(2)}) copy-start(bf16[640,1280]{1,0:T(8,128)(2,1)} %param.15) | copy-start | bytes 4915204
  156.5 4.7 copy-start.35
  156.5 4.7 copy-start.45
  161.2 2.4 copy-start.28
  161.2 2.4 copy-start.30
  254.7 4.1 copy-start.5
  254.7 4.1 copy-start.8
  256.3 18.1 %copy-start.11 = (f32[256,640]{0,1:T(8,128)}, f32[256,640]{0,1:T(8,128)S(1)}, u32[]{:S(2)}) copy-start(f32[256,640]{0,1:T(8,128)S(1)} %slice_reduce_fusion.1) | copy-start | bytes 1966084
  258.8 10.2 %copy-start.44 = (bf16[2,10,64,256]{3,2,1,0:T(8,128)(2,1)S(1)}, bf16[2,10,64,256]{3,2,1,0:T(8,128)(2,1)}, u32[]{:S(2)}) copy-start(bf16[2,10,64,256]{3,2,1,0:T(8,128)(2,1)} %fusion.113) | copy-start | bytes 1966084
  262.3 55.3 %collective-permute-start.17 = (bf16[1,256,1280]{1,2,0:T(8,128)(2,1)}, bf16[1,256,1280]{1,2,0:T(8,128)(2,1)}, u32[]{:S(2)}, u32[]{:S(2)}) collective-permute-start(bf16[1,256,1280]{1,2,0:T(8,128)(2,1)} %fusion.133), channel_id=1, source_target_pairs={{7,0},{15,8},{23,16},{31,24},{39,32},{47,40},{55,48},{63,56},{71,6... | collective-permute-start | bytes 1966088 | tf_op jit(solution)/shard_map/ppermute | solution.py:27
  263.6 55.5 %collective-permute-start.16 = (bf16[1,256,1280]{1,2,0:T(8,128)(2,1)}, bf16[1,256,1280]{1,2,0:T(8,128)(2,1)}, u32[]{:S(2)}, u32[]{:S(2)}) collective-permute-start(bf16[1,256,1280]{1,2,0:T(8,128)(2,1)} %fusion.133), channel_id=1, source_target_pairs={{6,0},{14,8},{22,16},{30,24},{38,32},{46,40},{54,48},{62,56},{70,6... | collective-permute-start | bytes 1966088 | tf_op jit(solution)/shard_map/ppermute | solution.py:27
  265.1 55.7 %collective-permute-start.15 = (bf16[1,256,1280]{1,2,0:T(8,128)(2,1)}, bf16[1,256,1280]{1,2,0:T(8,128)(2,1)}, u32[]{:S(2)}, u32[]{:S(2)}) collective-permute-start(bf16[1,256,1280]{1,2,0:T(8,128)(2,1)} %fusion.133), channel_id=1, source_target_pairs={{5,0},{13,8},{21,16},{29,24},{37,32},{45,40},{53,48},{61,56},{69,6... | collective-permute-start | bytes 1966088 | tf_op jit(solution)/shard_map/ppermute | solution.py:27
  266.4 56.9 %collective-permute-start.14 = (bf16[1,256,1280]{1,2,0:T(8,128)(2,1)}, bf16[1,256,1280]{1,2,0:T(8,128)(2,1)}, u32[]{:S(2)}, u32[]{:S(2)}) collective-permute-start(bf16[1,256,1280]{1,2,0:T(8,128)(2,1)} %fusion.133), channel_id=1, source_target_pairs={{4,0},{12,8},{20,16},{28,24},{36,32},{44,40},{52,48},{60,56},{68,6... | collective-permute-start | bytes 1966088 | tf_op jit(solution)/shard_map/ppermute | solution.py:27
  267.7 55.6 %collective-permute-start.13 = (bf16[1,256,1280]{1,2,0:T(8,128)(2,1)}, bf16[1,256,1280]{1,2,0:T(8,128)(2,1)}, u32[]{:S(2)}, u32[]{:S(2)}) collective-permute-start(bf16[1,256,1280]{1,2,0:T(8,128)(2,1)} %fusion.133), channel_id=1, source_target_pairs={{3,0},{11,8},{19,16},{27,24},{35,32},{43,40},{51,48},{59,56},{67,6... | collective-permute-start | bytes 1966088 | tf_op jit(solution)/shard_map/ppermute | solution.py:27
  269.0 2.6 copy-start.43
  283.1 2.6 copy-start.6
  283.1 2.7 copy-start.9
  283.1 2.7 copy-start.20
  298.8 2.6 copy-start.18
  298.8 2.7 copy-start.31
  298.8 2.7 copy-start.33
  304.0 1.5 copy-start.14
  305.4 1.6 copy-start.7
  305.4 2.2 copy-start.12
  305.4 3.3 copy-start.21
  315.1 1.9 copy-start.25
  315.1 2.4 copy-start.24
  317.1 3.6 copy-start.23
  317.5 18.4 %copy-start.10 = (f32[256,640]{0,1:T(8,128)S(1)}, f32[256,640]{0,1:T(8,128)}, u32[]{:S(2)}) copy-start(f32[256,640]{0,1:T(8,128)} %slice_reduce_fusion) | copy-start | bytes 1966084
  317.5 18.4 %copy-start.13 = (f32[256,640]{0,1:T(8,128)S(1)}, f32[256,640]{0,1:T(8,128)}, u32[]{:S(2)}) copy-start(f32[256,640]{0,1:T(8,128)} %copy-done.11) | copy-start | bytes 1966084
  317.7 18.2 %collective-permute-start.12 = (bf16[1,256,1280]{1,2,0:T(8,128)(2,1)}, bf16[1,256,1280]{1,2,0:T(8,128)(2,1)S(1)}, u32[]{:S(2)}, u32[]{:S(2)}) collective-permute-start(bf16[1,256,1280]{1,2,0:T(8,128)(2,1)} %fusion.133), channel_id=1, source_target_pairs={{2,0},{10,8},{18,16},{26,24},{34,32},{42,40},{50,48},{58,56},{66,6... | collective-permute-start | bytes 1966088 | tf_op jit(solution)/shard_map/ppermute | solution.py:27
  319.1 16.8 %collective-permute-start.11 = (bf16[1,256,1280]{1,2,0:T(8,128)(2,1)}, bf16[1,256,1280]{1,2,0:T(8,128)(2,1)S(1)}, u32[]{:S(2)}, u32[]{:S(2)}) collective-permute-start(bf16[1,256,1280]{1,2,0:T(8,128)(2,1)} %fusion.133), channel_id=1, source_target_pairs={{1,0},{9,8},{17,16},{25,24},{33,32},{41,40},{49,48},{57,56},{65,64... | collective-permute-start | bytes 1966088 | tf_op jit(solution)/shard_map/ppermute | solution.py:27
  320.7 15.2 %copy-start.22 = (bf16[16,8,25610]{2,1,0:T(8,128)(2,1)}, bf16[16,8,25610]{2,1,0:T(8,128)(2,1)S(1)}, u32[]{:S(2)}) copy-start(bf16[16,8,25610]{2,1,0:T(8,128)(2,1)S(1)} %constant_dynamic-update-slice_fusion.1) | copy-start | bytes 19668484
  338.5 1.4 copy-start.19
  339.9 1.7 copy-start.15
  340.7 2.0 copy-start.2
  343.5 1.6 copy-start.3
  347.0 18.5 %copy-start.27 = (bf16[1,2,256,1280]{3,2,1,0:T(8,128)(2,1)S(1)}, bf16[1,2,256,1280]{3,2,1,0:T(8,128)(2,1)}, u32[]{:S(2)}) copy-start(bf16[1,2,256,1280]{3,2,1,0:T(8,128)(2,1)} %get-tuple-element.38) | copy-start | bytes 3932164
  348.5 12.7 %collective-permute-start.7 = (bf16[1,1,256,1280]{3,2,1,0:T(8,128)(2,1)S(1)}, bf16[1,1,256,1280]{3,2,1,0:T(8,128)(2,1)S(1)}, u32[]{:S(2)}, u32[]{:S(2)}) collective-permute-start(bf16[1,1,256,1280]{3,2,1,0:T(8,128)(2,1)S(1)} %get-tuple-element.30), channel_id=1, source_target_pairs={{0,1},{1,2},{2,3},{3,4},{4,5},{5,6},{6,7},{8,9},{9,10},{10,11},{11... | collective-permute-start | bytes 1966088 | tf_op jit(solution)/shard_map/ppermute | solution.py:63
  349.9 15.9 %copy-start.47 = (bf16[1,2,256,1280]{3,2,1,0:T(8,128)(2,1)S(1)}, bf16[1,2,256,1280]{3,2,1,0:T(8,128)(2,1)}, u32[]{:S(2)}) copy-start(bf16[1,2,256,1280]{3,2,1,0:T(8,128)(2,1)} %copy-done.46) | copy-start | bytes 3932164
  349.9 15.6 %collective-permute-start.8 = (bf16[1,1,256,1280]{3,2,1,0:T(8,128)(2,1)S(1)}, bf16[1,1,256,1280]{3,2,1,0:T(8,128)(2,1)S(1)}, u32[]{:S(2)}, u32[]{:S(2)}) collective-permute-start(bf16[1,1,256,1280]{3,2,1,0:T(8,128)(2,1)S(1)} %get-tuple-element.31), channel_id=1, source_target_pairs={{1,0},{2,1},{3,2},{4,3},{5,4},{6,5},{7,6},{9,8},{10,9},{11,10},{12... | collective-permute-start | bytes 1966088 | tf_op jit(solution)/shard_map/ppermute | solution.py:64
  439.9 16.4 %all-to-all-start = ((f32[8,1,25610]{2,1,0:T(1,128)}), f32[8,1,25610]{2,1,0:T(1,128)}, u32[]{:S(2)}, u32[]{:S(2)}) async-start(f32[8,1,25610]{2,1,0:T(1,128)} %copy.65), calls=%async_computation | async-start | bytes 1646592 | tf_op jit(solution)/shard_map/all_to_all | solution.py:37
  (4 other events, 4.3 us)
Sparse Core Ops, SparseCore 0:
  347.2 89.8 reduce-scatter.3

commit v7 on v6

--- a/solution.py
+++ b/solution.py
@@ -31,9 +31,9 @@
 
 def scatter_sum(parts, outer, inner):
     count = lax.axis_size(outer) * lax.axis_size(inner)
-    packed = jnp.concatenate([p.reshape(count, -1) for p in parts], axis=1)
+    packed = jnp.concatenate([p.astype(jnp.bfloat16).reshape(count, -1) for p in parts], axis=1)
     share = packed.reshape((lax.axis_size(outer), -1) + packed.shape[1:])
-    share = lax.psum_scatter(share.astype(jnp.bfloat16), outer, scatter_dimension=0, tiled=True)[0]
+    share = lax.psum_scatter(share, outer, scatter_dimension=0, tiled=True)[0]
     share = lax.all_to_all(share.astype(jnp.float32), inner, 0, 0, tiled=True)
     share = jnp.sum(share, axis=0)
     outs, start = [], 0
@@ -99,7 +99,7 @@
     top_score = jnp.max(scores, axis=-1, keepdims=True)
     expd = jnp.exp(scores - top_score)
     prob_f32 = expd / jnp.sum(expd, axis=-1, keepdims=True)
-    prob_b = prob_f32.astype(jnp.bfloat16)
+    prob_b = lax.optimization_barrier(prob_f32.astype(jnp.bfloat16))
     mixed = jnp.einsum(
         "lfhst,lfthd->lfshd", prob_b, split_heads(val_all), preferred_element_type=jnp.float32
     )
@@ -114,6 +114,7 @@
     )
     centre = jnp.sum(grad_prob * prob_f32, axis=-1, keepdims=True)
     grad_score = (prob_f32 * (grad_prob - centre) * HD ** (-0.5)).astype(jnp.bfloat16)
+    grad_score = lax.optimization_barrier(grad_score)
     grad_queries = jnp.einsum(
         "lfhst,lfthd->lfshd", grad_score, split_heads(key_all), preferred_element_type=jnp.float32
     )

time: 475 us -> 379 us (0.80)
  matrix products: 198 us -> 85.2 us
  other arithmetic: 34.6 us -> 52.5 us
    dot_general x1, matrix products: 43.1 us -> 1.02 us  [attend_back(): jnp.einsum('lfhst,lfshd->lfthd', grad_score, split_heads(queries), prefer...]
    dot_general x1, matrix products: 42.6 us -> 4.71 us  [attend_back(): jnp.einsum('lfhst,lfthd->lfshd', grad_score, split_heads(key_all), prefer...]
    dot_general x1, matrix products: 17.6 us -> 1.69 us  [attend(): jnp.einsum('lfhst,lfthd->lfshd', prob_b, split_heads(val_all), preferred_...]
    dot_general x1, matrix products: 18.6 us -> 3.72 us  [attend_back(): jnp.einsum('lfhst,lfshd->lfthd', prob_b, grad_heads, preferred_element_ty...]
    div x0 -> x1, other arithmetic: none -> 14.3 us  [attend(): prob_f32 = expd / jnp.sum(expd, axis=-1, keepdims=True)]
    convert_element_type x0 -> x1, other arithmetic: none -> 4.79 us  [attend(): prob_b = lax.optimization_barrier(prob_f32.astype(jnp.bfloat16))]
    unnamed x103 -> x111, local copies, waits for them, and re-layouts: 17.2 us -> 18.5 us
    concatenate x6 -> x5, local copies, waits for them, and re-layouts: 17.8 us -> 17.8 us  [scatter_sum(): jnp.concatenate([p.astype(jnp.bfloat16).reshape(count, -1) for p in parts...]
  transfers between devices with their start and end apart: 20 -> 20, of which waited for: 9 -> 9; matrix products, arithmetic and copies ran while one was open for 27% -> 31% of each run, Pallas kernels for 0% -> 0%
where the time goes in v7:
time: 379 us; the launch traced here: 373 us
  waiting for transfers between devices  119 us (31%)
  matrix products  85.2 us (22%)
  local copies, waits for them, and re-layouts  61.3 us (16%)
  other arithmetic  52.5 us (14%)
  starting transfers between devices  40.1 us (11%)
  between operations  15 us (4%)
    unnamed x2, waiting for transfers between devices  60.4 us
    ppermute x7, waiting for transfers between devices, from_owner(): got = lax.ppermute(block, axis, [(0, target)])  21.1 us
    unnamed x111, local copies, waits for them, and re-layouts  18.5 us
    concatenate x5, local copies, waits for them, and re-layouts, scatter_sum(): jnp.concatenate([p.astype(jnp.bfloat16).reshape(count, -1) for p in parts...  17.8 us
    ppermute x7, starting transfers between devices, from_owner(): got = lax.ppermute(block, axis, [(0, target)])  16.6 us
    sub x1, other arithmetic, attend_back(): grad_prob - centre  16.2 us
    ppermute x7, waiting for transfers between devices, to_owner(): got = lax.ppermute(block.astype(jnp.bfloat16), axis, [(source, 0)])  15.1 us
    div x1, other arithmetic, attend(): prob_f32 = expd / jnp.sum(expd, axis=-1, keepdims=True)  14.3 us
  transfers between devices with their start and end apart: 20, of which 9 were waited for; matrix products, arithmetic and copies ran while one was open for 31% of the time, Pallas kernels for 0%

profile of v7, /device:TPU:0, one launch (start us, length us, event | category | flops | bytes accessed | tf_op | source)
XLA Modules:
  0.0 372.9 jit_solution(11833754410333085858)
XLA Ops:
  7.2 2.1 slice_bitcast_fusion.1
  9.4 3.7 collective-permute-start.6
  13.0 2.2 collective-permute-start.5
  15.3 2.1 collective-permute-start.4
  17.4 2.1 collective-permute-start.3
  19.6 2.2 collective-permute-start.2
  22.5 2.2 fusion.107
  24.7 2.1 fusion.104
  26.9 1.5 collective-permute-done.6
  28.4 2.1 collective-permute-start.1
  30.5 11.9 %collective-permute-done.5 = bf16[1,256,1280]{2,1,0:T(8,128)(2,1)S(1)} collective-permute-done((bf16[1,256,1280]{2,1,0:T(8,128)(2,1)}, bf16[1,256,1280]{2,1,0:T(8,128)(2,1)S(1)}, u32[]{:S(2)}, u32[]{:S(2)}) %collective-permute-start.5) | collective-permute-done | bytes 655392 | tf_op jit(solution)/shard_map/ppermute | solution.py:19
  42.5 2.1 collective-permute-start
  44.6 2.2 fusion.101
  46.8 2.2 copy.53
  49.0 2.2 copy.52
  51.2 2.2 copy.50
  53.3 2.6 fusion.179
  57.3 5.7 %collective-permute-start.10 = (bf16[1,1,256,1280]{3,2,1,0:T(8,128)(2,1)}, bf16[1,1,256,1280]{3,2,1,0:T(8,128)(2,1)}, u32[]{:S(2)}, u32[]{:S(2)}) collective-permute-start(bf16[1,1,256,1280]{3,2,1,0:T(8,128)(2,1)} %get-tuple-element.27), channel_id=1, source_target_pairs={{0,1},{1,2},{2,3},{3,4},{4,5},{5,6},{6,7},{8,9},{9,10},{10,11},{11... | collective-permute-start | bytes 1966088 | tf_op jit(solution)/shard_map/ppermute | solution.py:63
  63.0 7.6 %collective-permute-done.1 = bf16[1,256,1280]{2,1,0:T(8,128)(2,1)} collective-permute-done((bf16[1,256,1280]{2,1,0:T(8,128)(2,1)}, bf16[1,256,1280]{2,1,0:T(8,128)(2,1)}, u32[]{:S(2)}, u32[]{:S(2)}) %collective-permute-start.1) | collective-permute-done | bytes 655392 | tf_op jit(solution)/shard_map/ppermute | solution.py:19
  72.6 1.5 convolution_convert_fusion.1
  78.1 6.7 %fusion.135 = f32[2,10,256,512]{3,2,1,0:T(8,128)} fusion(bf16[2,256,10,64]{1,3,2,0:T(8,128)(2,1)} %bitcast.254, bf16[1,2,256,10,64]{2,4,3,1,0:T(8,128)(2,1)S(1)} %broadcast_in_dim.15, bf16[1,2,256,10,64]{2,4,3,1,0:T(8,128)(2,1)} %bitcast.258), kind=kOutput, calls=%fused_computation.144 | convolution fusion | flops 338165760 | bytes 12451840 | tf_op jit(solution)/shard_map/lfshd,lfthd->lfhst/dot_general | solution.py:93
  84.8 14.3 %fusion.22 = f32[2,10,256,512]{3,2,1,0:T(8,128)} fusion(f32[2,10,256,512]{3,2,1,0:T(8,128)} %fusion.135), kind=kOutput, calls=%fused_computation.23 | output fusion | flops 10497022 | bytes 20971520 | tf_op jit(solution)/shard_map/div | solution.py:101
  99.1 4.8 %convert_bitcast_fusion = bf16[1,2,10,256,512]{4,3,2,1,0:T(8,128)(2,1)S(1)} fusion(f32[2,10,256,512]{3,2,1,0:T(8,128)} %fusion.22), kind=kLoop, calls=%fused_computation.21 | loop fusion | flops 2621440 | bytes 15728640 | tf_op jit(solution)/shard_map/convert_element_type | solution.py:102
  104.0 1.7 fusion.113
  106.6 2.6 fusion.80
  109.3 2.0 fusion.124
  111.3 10.0 %fusion.61 = bf16[1,2,256,1280]{3,2,1,0:T(8,128)(2,1)S(1)} fusion(bf16[1280,3,1280]{2,0,1:T(8,128)(2,1)} %param.16, bf16[1,2,256,1,1280]{4,2,3,1,0:T(8,128)(2,1)S(1)} %get-tuple-element.25, bf16[1,2,256,1,1280]{4,2,3,1,0:T(8,128)(2,1)S(1)} %bitcast.262, bf16[1,2,256,1,1280]{4,2,3,1,0:T(8,128)(2,1)S(1)} %get-tuple-element.24, ...), kind=kOutput, calls=%fused_computation.68 | convolution fusion | flops 5044961280 | bytes 17694720 | tf_op jit(solution)/shard_map/lfsjo,cjo->lfsc/dot_general | solution.py:186
  122.5 2.1 fusion.110
  124.5 2.2 copy.56
  126.7 3.7 fusion.17
  132.4 2.2 fusion.50
  134.7 5.4 %fusion.129 = f32[2,10,256,512]{3,2,1,0:T(8,128)} fusion(bf16[2,256,10,64]{1,3,2,0:T(8,128)(2,1)S(1)} %bitcast.257, bf16[2,256,10,64]{1,3,2,0:T(8,128)(2,1)S(1)} %broadcast_in_dim.16, bf16[2,256,10,64]{1,3,2,0:T(8,128)(2,1)S(1)} %bitcast.261), kind=kOutput, calls=%fused_computation.134 | convolution fusion | flops 338165760 | bytes 12451840 | tf_op jit(solution)/shard_map/lfshd,lfthd->lfhst/dot_general | solution.py:112
  140.1 16.2 %fusion.83 = bf16[1,2,10,256,512]{4,3,2,1,0:T(8,128)(2,1)} fusion(f32[2,10,256,512]{3,2,1,0:T(8,128)} %fusion.22, f32[2,10,256,512]{3,2,1,0:T(8,128)} %fusion.129), kind=kOutput, calls=%fused_computation.90 | output fusion | flops 13112831 | bytes 26214400 | tf_op jit(solution)/shard_map/sub | solution.py:116
  156.4 4.7 %fusion.116 = bf16[2,10,64,256]{3,2,1,0:T(8,128)(2,1)S(1)} fusion(bf16[1,2,10,256,512]{4,3,2,1,0:T(8,128)(2,1)} %fusion.83, bf16[1,2,256,10,64]{2,4,3,1,0:T(8,128)(2,1)} %copy-done.32, bf16[1,2,256,10,64]{2,4,3,1,0:T(8,128)(2,1)} %bitcast.259), kind=kOutput, calls=%fused_computation.114 | convolution fusion | flops 338493440 | bytes 7208960 | tf_op jit(solution)/shard_map/lfhst,lfthd->lfshd/dot_general | solution.py:118
  163.9 2.6 fusion.155
  173.9 2.6 fusion.49
  176.6 2.8 fusion.92
  179.4 2.5 fusion.158
  181.9 2.2 copy.75
  184.1 4.1 %concatenate.70 = bf16[16,8,6400]{2,1,0:T(8,128)(2,1)} reshape(bf16[640,1280]{1,0:T(8,128)(2,1)} %fusion.50) | data formatting | bytes 3276800 | tf_op jit(solution)/shard_map/concatenate | solution.py:34
  188.2 2.6 convolution_bitcast_fusion.1
  190.8 2.1 fusion.48
  192.9 4.4 %concatenate.69 = bf16[16,8,6400]{2,1,0:T(8,128)(2,1)} reshape(bf16[1280,640]{1,0:T(8,128)(2,1)} %fusion.48) | data formatting | bytes 3276800 | tf_op jit(solution)/shard_map/concatenate | solution.py:34
  197.3 2.2 copy.74
  199.5 4.4 %concatenate.67 = bf16[16,8,6400]{2,1,0:T(8,128)(2,1)} reshape(bf16[1280,640]{1,0:T(8,128)(2,1)} %fusion.49) | data formatting | bytes 3276800 | tf_op jit(solution)/shard_map/concatenate | solution.py:34
  203.8 2.6 convolution_bitcast_fusion.2
  210.5 1.6 copy.76
  213.7 2.1 fusion.47
  215.8 4.4 %concatenate.68 = bf16[16,8,6400]{2,1,0:T(8,128)(2,1)} reshape(bf16[1280,640]{1,0:T(8,128)(2,1)} %fusion.47) | data formatting | bytes 3276800 | tf_op jit(solution)/shard_map/concatenate | solution.py:34
  220.2 1.7 constant_dynamic-update-slice_fusion.4
  225.1 1.5 collective-permute-start.11
  226.8 1.6 collective-permute-done.14
  228.4 13.6 %collective-permute-done.12 = bf16[1,256,1280]{1,2,0:T(8,128)(2,1)S(1)} collective-permute-done((bf16[1,256,1280]{1,2,0:T(8,128)(2,1)}, bf16[1,256,1280]{1,2,0:T(8,128)(2,1)S(1)}, u32[]{:S(2)}, u32[]{:S(2)}) %collective-permute-start.12) | collective-permute-done | bytes 655392 | tf_op jit(solution)/shard_map/ppermute | solution.py:27
  241.9 2.6 convert_add_fusion.2
  251.8 1.5 fusion.180
  256.1 9.9 %collective-permute-done.7 = bf16[1,1,256,1280]{3,2,1,0:T(8,128)(2,1)S(1)} collective-permute-done((bf16[1,1,256,1280]{3,2,1,0:T(8,128)(2,1)S(1)}, bf16[1,1,256,1280]{3,2,1,0:T(8,128)(2,1)S(1)}, u32[]{:S(2)}, u32[]{:S(2)}) %collective-permute-start.7) | collective-permute-done | bytes 655392 | tf_op jit(solution)/shard_map/ppermute | solution.py:63
  266.0 4.3 %collective-permute-done.8 = bf16[1,1,256,1280]{3,2,1,0:T(8,128)(2,1)S(1)} collective-permute-done((bf16[1,1,256,1280]{3,2,1,0:T(8,128)(2,1)S(1)}, bf16[1,1,256,1280]{3,2,1,0:T(8,128)(2,1)S(1)}, u32[]{:S(2)}, u32[]{:S(2)}) %collective-permute-start.8) | collective-permute-done | bytes 655392 | tf_op jit(solution)/shard_map/ppermute | solution.py:64
  270.5 10.8 %fusion.58 = bf16[1,2,256,1280]{3,2,1,0:T(8,128)(2,1)} fusion(bf16[1280,3,1280]{2,0,1:T(8,128)(2,1)} %param.16, bf16[1,2,256,1,1280]{4,2,1,3,0:T(8,128)(2,1)S(1)} %get-tuple-element.29, bf16[1,2,256,1,1280]{4,2,1,3,0:T(8,128)(2,1)S(1)} %bitcast.263, bf16[1,2,256,1,1280]{4,2,1,3,0:T(8,128)(2,1)S(1)} %get-tuple-element.28, ...), kind=kOutput, calls=%fused_computation.67 | convolution fusion | flops 5039063040 | bytes 16384000 | tf_op jit(solution)/shard_map/lfsjc,cjo->lfso/dot_general | solution.py:181
  281.3 60.4 %reduce-scatter.4.cloned.1.call-done = bf16[1,8,25610]{2,1,0:T(8,128)(2,1)} async-done(((bf16[16,8,25610]{2,1,0:T(8,128)(2,1)}), bf16[1,8,25610]{2,1,0:T(8,128)(2,1)}) %reduce-scatter.4.cloned.1.call-update) | async-done | bytes 409776
  342.8 1.8 copy.65
  344.5 4.3 %all-to-all-start = ((f32[8,1,25610]{2,1,0:T(1,128)}), f32[8,1,25610]{2,1,0:T(1,128)}, u32[]{:S(2)}, u32[]{:S(2)}) async-start(f32[8,1,25610]{2,1,0:T(1,128)} %copy.65), calls=%async_computation | async-start | bytes 1646592 | tf_op jit(solution)/shard_map/all_to_all | solution.py:37
  348.9 4.3 %fusion.74 = bf16[1,2,256,1280]{3,2,1,0:T(8,128)(2,1)} fusion(bf16[1,2,256,1280]{3,2,1,0:T(8,128)(2,1)S(1)} %copy-done.3, bf16[1,2,256,1280]{3,2,1,0:T(8,128)(2,1)} %copy-done.38, f32[1,2,256,1280]{3,2,1,0:T(8,128)} %copy-done.5, f32[2,256]{1,0:T(2,128)S(1)} %get-tuple-element.38, f32[2,256]{1,0:T(2,128)S(1)} %get-tuple-element.39, f32[1280]{0:T(1024)S(1)} %copy-done.46, ...), kind=kLoop, calls=%fused_computation.81 | loop fusion | flops 7208960 | bytes 6566912 | tf_op jit(solution)/shard_map/convert_element_type | solution.py:229
  353.1 7.9 %all-to-all-done = f32[8,1,25610]{2,1,0:T(1,128)} async-done(((f32[8,1,25610]{2,1,0:T(1,128)}), f32[8,1,25610]{2,1,0:T(1,128)}, u32[]{:S(2)}, u32[]{:S(2)}) %all-to-all-start) | async-done | bytes 819552 | tf_op jit(solution)/shard_map/all_to_all | solution.py:37
  361.0 1.7 reduce_sum.125
  (167 shorter events, 45.7 us)
Async XLA Ops:
  7.2 37.4 %copy-start = (bf16[1280,640]{1,0:T(8,128)(2,1)S(1)}, bf16[1280,640]{1,0:T(8,128)(2,1)}, u32[]{:S(2)}) copy-start(bf16[1280,640]{1,0:T(8,128)(2,1)} %param.14) | copy-start | bytes 4915204
  7.2 14.5 %copy-start.3 = (bf16[1,2,256,1280]{3,2,1,0:T(8,128)(2,1)S(1)}, bf16[1,2,256,1280]{3,2,1,0:T(8,128)(2,1)}, u32[]{:S(2)}) copy-start(bf16[1,2,256,1280]{3,2,1,0:T(8,128)(2,1)} %param.10) | copy-start | bytes 3932164
  7.2 334.5 %reduce-scatter.4.cloned.1.call-start = ((), (), s32[]{:S(2)}) async-start(), calls=%async_computation.2 | async-start | bytes 6998016
  9.4 13.1 %copy-start.18 = (bf16[1280,640]{1,0:T(8,128)(2,1)S(1)}, bf16[1280,640]{1,0:T(8,128)(2,1)}, u32[]{:S(2)}) copy-start(bf16[1280,640]{1,0:T(8,128)(2,1)} %param.13) | copy-start | bytes 4915204
  9.4 13.1 %copy-start.46 = (f32[1280]{0:T(1024)S(1)}, f32[1280]{0:T(1024)}, u32[]{:S(2)}) copy-start(f32[1280]{0:T(1024)} %param.11) | copy-start | bytes 15364
  9.4 19.1 %collective-permute-start.6 = (bf16[1,256,1280]{2,1,0:T(8,128)(2,1)}, bf16[1,256,1280]{2,1,0:T(8,128)(2,1)S(1)}, u32[]{:S(2)}, u32[]{:S(2)}) collective-permute-start(bf16[1,256,1280]{2,1,0:T(8,128)(2,1)} %slice_bitcast_fusion.1), channel_id=1, source_target_pairs={{0,1},{8,9},{16,17},{24,25},{32,33},{40,41},{48,49},{56,57},{64,65... | collective-permute-start | bytes 1966088 | tf_op jit(solution)/shard_map/ppermute | solution.py:19
  13.0 29.4 %collective-permute-start.5 = (bf16[1,256,1280]{2,1,0:T(8,128)(2,1)}, bf16[1,256,1280]{2,1,0:T(8,128)(2,1)S(1)}, u32[]{:S(2)}, u32[]{:S(2)}) collective-permute-start(bf16[1,256,1280]{2,1,0:T(8,128)(2,1)} %slice_bitcast_fusion.1), channel_id=1, source_target_pairs={{0,2},{8,10},{16,18},{24,26},{32,34},{40,42},{48,50},{56,58},{64,6... | collective-permute-start | bytes 1966088 | tf_op jit(solution)/shard_map/ppermute | solution.py:19
  15.3 40.7 %collective-permute-start.4 = (bf16[1,256,1280]{2,1,0:T(8,128)(2,1)}, bf16[1,256,1280]{2,1,0:T(8,128)(2,1)}, u32[]{:S(2)}, u32[]{:S(2)}) collective-permute-start(bf16[1,256,1280]{2,1,0:T(8,128)(2,1)} %slice_bitcast_fusion.1), channel_id=1, source_target_pairs={{0,3},{8,11},{16,19},{24,27},{32,35},{40,43},{48,51},{56,59},{64,6... | collective-permute-start | bytes 1966088 | tf_op jit(solution)/shard_map/ppermute | solution.py:19
  17.4 39.8 %collective-permute-start.3 = (bf16[1,256,1280]{2,1,0:T(8,128)(2,1)}, bf16[1,256,1280]{2,1,0:T(8,128)(2,1)}, u32[]{:S(2)}, u32[]{:S(2)}) collective-permute-start(bf16[1,256,1280]{2,1,0:T(8,128)(2,1)} %slice_bitcast_fusion.1), channel_id=1, source_target_pairs={{0,4},{8,12},{16,20},{24,28},{32,36},{40,44},{48,52},{56,60},{64,6... | collective-permute-start | bytes 1966088 | tf_op jit(solution)/shard_map/ppermute | solution.py:19
  19.6 43.4 %collective-permute-start.2 = (bf16[1,256,1280]{2,1,0:T(8,128)(2,1)}, bf16[1,256,1280]{2,1,0:T(8,128)(2,1)}, u32[]{:S(2)}, u32[]{:S(2)}) collective-permute-start(bf16[1,256,1280]{2,1,0:T(8,128)(2,1)} %slice_bitcast_fusion.1), channel_id=1, source_target_pairs={{0,5},{8,13},{16,21},{24,29},{32,37},{40,45},{48,53},{56,61},{64,6... | collective-permute-start | bytes 1966088 | tf_op jit(solution)/shard_map/ppermute | solution.py:19
  22.5 2.2 copy-start.48
  28.4 18.4 %copy-start.42 = (bf16[1,256,1280]{2,1,0:T(8,128)(2,1)}, bf16[1,256,1280]{2,1,0:T(8,128)(2,1)S(1)}, u32[]{:S(2)}) copy-start(bf16[1,256,1280]{2,1,0:T(8,128)(2,1)S(1)} %collective-permute-done.6) | copy-start | bytes 1966084
  28.4 42.2 %collective-permute-start.1 = (bf16[1,256,1280]{2,1,0:T(8,128)(2,1)}, bf16[1,256,1280]{2,1,0:T(8,128)(2,1)}, u32[]{:S(2)}, u32[]{:S(2)}) collective-permute-start(bf16[1,256,1280]{2,1,0:T(8,128)(2,1)} %slice_bitcast_fusion.1), channel_id=1, source_target_pairs={{0,6},{8,14},{16,22},{24,30},{32,38},{40,46},{48,54},{56,62},{64,7... | collective-permute-start | bytes 1966088 | tf_op jit(solution)/shard_map/ppermute | solution.py:19
  42.5 4.4 %copy-start.44 = (bf16[1,256,1280]{2,1,0:T(8,128)(2,1)}, bf16[1,256,1280]{2,1,0:T(8,128)(2,1)S(1)}, u32[]{:S(2)}) copy-start(bf16[1,256,1280]{2,1,0:T(8,128)(2,1)S(1)} %collective-permute-done.5) | copy-start | bytes 1966084
  42.5 28.1 %collective-permute-start = (bf16[1,256,1280]{2,1,0:T(8,128)(2,1)}, bf16[1,256,1280]{2,1,0:T(8,128)(2,1)}, u32[]{:S(2)}, u32[]{:S(2)}) collective-permute-start(bf16[1,256,1280]{2,1,0:T(8,128)(2,1)} %slice_bitcast_fusion.1), channel_id=1, source_target_pairs={{0,7},{8,15},{16,23},{24,31},{32,39},{40,47},{48,55},{56,63},{64,7... | collective-permute-start | bytes 1966088 | tf_op jit(solution)/shard_map/ppermute | solution.py:19
  53.3 17.3 %copy-start.43 = (bf16[1,256,1280]{2,1,0:T(8,128)(2,1)S(1)}, bf16[1,256,1280]{2,1,0:T(8,128)(2,1)}, u32[]{:S(2)}) copy-start(bf16[1,256,1280]{2,1,0:T(8,128)(2,1)} %copy-done.42) | copy-start | bytes 1966084
  53.3 17.3 %copy-start.45 = (bf16[1,256,1280]{2,1,0:T(8,128)(2,1)S(1)}, bf16[1,256,1280]{2,1,0:T(8,128)(2,1)}, u32[]{:S(2)}) copy-start(bf16[1,256,1280]{2,1,0:T(8,128)(2,1)} %copy-done.44) | copy-start | bytes 1966084
  55.9 53.3 %collective-permute-start.9 = (bf16[1,1,256,1280]{3,2,1,0:T(8,128)(2,1)}, bf16[1,1,256,1280]{3,2,1,0:T(8,128)(2,1)}, u32[]{:S(2)}, u32[]{:S(2)}) collective-permute-start(bf16[1,1,256,1280]{3,2,1,0:T(8,128)(2,1)} %get-tuple-element.26), channel_id=1, source_target_pairs={{1,0},{2,1},{3,2},{4,3},{5,4},{6,5},{7,6},{9,8},{10,9},{11,10},{12... | collective-permute-start | bytes 1966088 | tf_op jit(solution)/shard_map/ppermute | solution.py:64
  57.2 14.6 %copy-start.19 = (bf16[1280,640]{1,0:T(8,128)(2,1)S(1)}, bf16[1280,640]{1,0:T(8,128)(2,1)}, u32[]{:S(2)}) copy-start(bf16[1280,640]{1,0:T(8,128)(2,1)} %param.13) | copy-start | bytes 4915204
  57.3 52.0 %collective-permute-start.10 = (bf16[1,1,256,1280]{3,2,1,0:T(8,128)(2,1)}, bf16[1,1,256,1280]{3,2,1,0:T(8,128)(2,1)}, u32[]{:S(2)}, u32[]{:S(2)}) collective-permute-start(bf16[1,1,256,1280]{3,2,1,0:T(8,128)(2,1)} %get-tuple-element.27), channel_id=1, source_target_pairs={{0,1},{1,2},{2,3},{3,4},{4,5},{5,6},{6,7},{8,9},{9,10},{10,11},{11... | collective-permute-start | bytes 1966088 | tf_op jit(solution)/shard_map/ppermute | solution.py:63
  99.1 4.9 %copy-start.30 = (bf16[2,256,640]{1,2,0:T(8,128)(2,1)S(1)}, bf16[2,256,640]{1,2,0:T(8,128)(2,1)}, u32[]{:S(2)}) copy-start(bf16[2,256,640]{1,2,0:T(8,128)(2,1)} %copy.50) | copy-start | bytes 1966084
  103.9 2.4 copy-start.1
  104.0 2.7 copy-start.47
  106.2 3.0 copy-start.40
  106.6 2.6 copy-start.33
  109.3 2.1 copy-start.50
  130.5 2.0 copy-start.39
  130.5 2.0 copy-start.41
  132.4 2.3 copy-start.29
  132.4 2.3 copy-start.31
  156.4 4.7 %copy-start.2 = (bf16[1,2,10,256,512]{4,3,2,1,0:T(8,128)(2,1)S(1)}, bf16[1,2,10,256,512]{4,3,2,1,0:T(8,128)(2,1)}, u32[]{:S(2)}) copy-start(bf16[1,2,10,256,512]{4,3,2,1,0:T(8,128)(2,1)} %fusion.83) | copy-start | bytes 15728644
  156.4 4.7 %copy-start.28 = (bf16[2,256,640]{1,2,0:T(8,128)(2,1)S(1)}, bf16[2,256,640]{1,2,0:T(8,128)(2,1)}, u32[]{:S(2)}) copy-start(bf16[2,256,640]{1,2,0:T(8,128)(2,1)} %copy.52) | copy-start | bytes 1966084
  162.2 1.8 copy-start.10
  162.3 17.1 %copy-start.13 = (f32[256,640]{0,1:T(8,128)}, f32[256,640]{0,1:T(8,128)S(1)}, u32[]{:S(2)}) copy-start(f32[256,640]{0,1:T(8,128)S(1)} %slice_reduce_fusion.1) | copy-start | bytes 1966084
  167.4 56.3 %collective-permute-start.17 = (bf16[1,256,1280]{1,2,0:T(8,128)(2,1)}, bf16[1,256,1280]{1,2,0:T(8,128)(2,1)}, u32[]{:S(2)}, u32[]{:S(2)}) collective-permute-start(bf16[1,256,1280]{1,2,0:T(8,128)(2,1)} %fusion.136), channel_id=1, source_target_pairs={{7,0},{15,8},{23,16},{31,24},{39,32},{47,40},{55,48},{63,56},{71,6... | collective-permute-start | bytes 1966088 | tf_op jit(solution)/shard_map/ppermute | solution.py:27
  168.7 56.4 %collective-permute-start.16 = (bf16[1,256,1280]{1,2,0:T(8,128)(2,1)}, bf16[1,256,1280]{1,2,0:T(8,128)(2,1)}, u32[]{:S(2)}, u32[]{:S(2)}) collective-permute-start(bf16[1,256,1280]{1,2,0:T(8,128)(2,1)} %fusion.136), channel_id=1, source_target_pairs={{6,0},{14,8},{22,16},{30,24},{38,32},{46,40},{54,48},{62,56},{70,6... | collective-permute-start | bytes 1966088 | tf_op jit(solution)/shard_map/ppermute | solution.py:27
  170.0 56.8 %collective-permute-start.15 = (bf16[1,256,1280]{1,2,0:T(8,128)(2,1)}, bf16[1,256,1280]{1,2,0:T(8,128)(2,1)}, u32[]{:S(2)}, u32[]{:S(2)}) collective-permute-start(bf16[1,256,1280]{1,2,0:T(8,128)(2,1)} %fusion.136), channel_id=1, source_target_pairs={{5,0},{13,8},{21,16},{29,24},{37,32},{45,40},{53,48},{61,56},{69,6... | collective-permute-start | bytes 1966088 | tf_op jit(solution)/shard_map/ppermute | solution.py:27
  171.3 57.0 %collective-permute-start.14 = (bf16[1,256,1280]{1,2,0:T(8,128)(2,1)}, bf16[1,256,1280]{1,2,0:T(8,128)(2,1)}, u32[]{:S(2)}, u32[]{:S(2)}) collective-permute-start(bf16[1,256,1280]{1,2,0:T(8,128)(2,1)} %fusion.136), channel_id=1, source_target_pairs={{4,0},{12,8},{20,16},{28,24},{36,32},{44,40},{52,48},{60,56},{68,6... | collective-permute-start | bytes 1966088 | tf_op jit(solution)/shard_map/ppermute | solution.py:27
  172.6 55.7 %collective-permute-start.13 = (bf16[1,256,1280]{1,2,0:T(8,128)(2,1)}, bf16[1,256,1280]{1,2,0:T(8,128)(2,1)}, u32[]{:S(2)}, u32[]{:S(2)}) collective-permute-start(bf16[1,256,1280]{1,2,0:T(8,128)(2,1)} %fusion.136), channel_id=1, source_target_pairs={{3,0},{11,8},{19,16},{27,24},{35,32},{43,40},{51,48},{59,56},{67,6... | collective-permute-start | bytes 1966088 | tf_op jit(solution)/shard_map/ppermute | solution.py:27
  173.9 2.6 copy-start.49
  188.2 2.6 copy-start.8
  188.2 2.7 copy-start.11
  188.2 2.7 copy-start.22
  203.8 2.6 copy-start.20
  203.8 2.7 copy-start.36
  203.8 2.7 copy-start.37
  210.5 1.6 copy-start.9
  210.5 2.2 copy-start.14
  210.5 3.3 copy-start.23
  220.2 1.9 copy-start.27
  223.5 3.1 copy-start.25
  223.7 18.3 %copy-start.12 = (f32[256,640]{0,1:T(8,128)S(1)}, f32[256,640]{0,1:T(8,128)}, u32[]{:S(2)}) copy-start(f32[256,640]{0,1:T(8,128)} %slice_reduce_fusion) | copy-start | bytes 1966084
  223.7 18.3 %copy-start.15 = (f32[256,640]{0,1:T(8,128)S(1)}, f32[256,640]{0,1:T(8,128)}, u32[]{:S(2)}) copy-start(f32[256,640]{0,1:T(8,128)} %copy-done.13) | copy-start | bytes 1966084
  223.7 18.2 %collective-permute-start.12 = (bf16[1,256,1280]{1,2,0:T(8,128)(2,1)}, bf16[1,256,1280]{1,2,0:T(8,128)(2,1)S(1)}, u32[]{:S(2)}, u32[]{:S(2)}) collective-permute-start(bf16[1,256,1280]{1,2,0:T(8,128)(2,1)} %fusion.136), channel_id=1, source_target_pairs={{2,0},{10,8},{18,16},{26,24},{34,32},{42,40},{50,48},{58,56},{66,6... | collective-permute-start | bytes 1966088 | tf_op jit(solution)/shard_map/ppermute | solution.py:27
  225.1 16.8 %collective-permute-start.11 = (bf16[1,256,1280]{1,2,0:T(8,128)(2,1)}, bf16[1,256,1280]{1,2,0:T(8,128)(2,1)S(1)}, u32[]{:S(2)}, u32[]{:S(2)}) collective-permute-start(bf16[1,256,1280]{1,2,0:T(8,128)(2,1)} %fusion.136), channel_id=1, source_target_pairs={{1,0},{9,8},{17,16},{25,24},{33,32},{41,40},{49,48},{57,56},{65,64... | collective-permute-start | bytes 1966088 | tf_op jit(solution)/shard_map/ppermute | solution.py:27
  226.8 15.1 %copy-start.24 = (bf16[16,8,25610]{2,1,0:T(8,128)(2,1)}, bf16[16,8,25610]{2,1,0:T(8,128)(2,1)S(1)}, u32[]{:S(2)}) copy-start(bf16[16,8,25610]{2,1,0:T(8,128)(2,1)S(1)} %constant_dynamic-update-slice_fusion.1) | copy-start | bytes 19668484
  245.9 1.7 copy-start.17
  246.7 2.0 copy-start.4
  249.4 1.6 copy-start.5
  251.8 18.5 %copy-start.34 = (bf16[1,2,256,1280]{3,2,1,0:T(8,128)(2,1)S(1)}, bf16[1,2,256,1280]{3,2,1,0:T(8,128)(2,1)}, u32[]{:S(2)}) copy-start(bf16[1,2,256,1280]{3,2,1,0:T(8,128)(2,1)} %get-tuple-element.36) | copy-start | bytes 3932164
  253.3 12.7 %collective-permute-start.7 = (bf16[1,1,256,1280]{3,2,1,0:T(8,128)(2,1)S(1)}, bf16[1,1,256,1280]{3,2,1,0:T(8,128)(2,1)S(1)}, u32[]{:S(2)}, u32[]{:S(2)}) collective-permute-start(bf16[1,1,256,1280]{3,2,1,0:T(8,128)(2,1)S(1)} %get-tuple-element.30), channel_id=1, source_target_pairs={{0,1},{1,2},{2,3},{3,4},{4,5},{5,6},{6,7},{8,9},{9,10},{10,11},{11... | collective-permute-start | bytes 1966088 | tf_op jit(solution)/shard_map/ppermute | solution.py:63
  254.7 15.8 %copy-start.51 = (bf16[1,2,256,1280]{3,2,1,0:T(8,128)(2,1)S(1)}, bf16[1,2,256,1280]{3,2,1,0:T(8,128)(2,1)}, u32[]{:S(2)}) copy-start(bf16[1,2,256,1280]{3,2,1,0:T(8,128)(2,1)} %copy-done.50) | copy-start | bytes 3932164
  254.7 15.6 %collective-permute-start.8 = (bf16[1,1,256,1280]{3,2,1,0:T(8,128)(2,1)S(1)}, bf16[1,1,256,1280]{3,2,1,0:T(8,128)(2,1)S(1)}, u32[]{:S(2)}, u32[]{:S(2)}) collective-permute-start(bf16[1,1,256,1280]{3,2,1,0:T(8,128)(2,1)S(1)} %get-tuple-element.31), channel_id=1, source_target_pairs={{1,0},{2,1},{3,2},{4,3},{5,4},{6,5},{7,6},{9,8},{10,9},{11,10},{12... | collective-permute-start | bytes 1966088 | tf_op jit(solution)/shard_map/ppermute | solution.py:64
  344.5 16.5 %all-to-all-start = ((f32[8,1,25610]{2,1,0:T(1,128)}), f32[8,1,25610]{2,1,0:T(1,128)}, u32[]{:S(2)}, u32[]{:S(2)}) async-start(f32[8,1,25610]{2,1,0:T(1,128)} %copy.65), calls=%async_computation | async-start | bytes 1646592 | tf_op jit(solution)/shard_map/all_to_all | solution.py:37
  (8 other events, 9.7 us)
Sparse Core Ops, SparseCore 0:
  251.9 89.7 reduce-scatter.3

commit v8 on v7

--- a/solution.py
+++ b/solution.py
@@ -42,6 +42,12 @@
         outs.append(share[start : start + width].reshape((p.shape[0] // count,) + p.shape[1:]))
         start += width
     return outs
+
+
+def gain_sum(value, outer, inner):
+    share = value.reshape(lax.axis_size(outer), lax.axis_size(inner), -1)
+    share = jnp.sum(lax.all_to_all(share, outer, 0, 0, tiled=True), axis=0)
+    return jnp.sum(lax.all_to_all(share, inner, 0, 0, tiled=True), axis=0)
 
 
 def split_dot(wide, narrow, dims):
@@ -227,9 +233,10 @@
         - x_hat * jnp.mean(grad_hat * x_hat, axis=-1, keepdims=True)
     )
     grad_input = (grad_hidden.astype(jnp.float32) + grad_x).astype(jnp.bfloat16)
-    grad_wq, grad_wk, grad_wv, grad_out, grad_gain = scatter_sum(
-        (grad_wq, grad_wk, grad_wv, grad_out, grad_gain), "batch", "tm"
-    )
+    grad_wq, grad_wk, grad_wv, grad_out = scatter_sum(
+        (grad_wq, grad_wk, grad_wv, grad_out), "batch", "tm"
+    )
+    grad_gain = gain_sum(grad_gain, "batch", "tm")
     return (output, grad_input, grad_wq, grad_wk, grad_wv, grad_out, grad_gain)
 
 

time: 379 us -> 359 us (0.947)
  waiting for transfers between devices: 119 us -> 87.5 us
  starting transfers between devices: 40.1 us -> 55.3 us
  local copies, waits for them, and re-layouts: 61.3 us -> 51 us
  other arithmetic: 52.5 us -> 60.8 us
    unnamed x2 -> x1, waiting for transfers between devices: 60.4 us -> 0.02 us
    ppermute x7, waiting for transfers between devices: 15.1 us -> 52.3 us  [to_owner(): got = lax.ppermute(block.astype(jnp.bfloat16), axis, [(source, 0)])]
    all_to_all x0 -> x2, starting transfers between devices: none -> 11.4 us  [the longest x1 8.05 us: gain_sum(): share = jnp.sum(lax.all_to_all(share, outer, 0, 0, tiled=True), axis=0)]
    ppermute x2, waiting for transfers between devices: 9.87 us -> 0.01 us  [padded_2(): before = lax.ppermute(last, axis, up)]
    unnamed x111 -> x81, local copies, waits for them, and re-layouts: 18.5 us -> 8.97 us
    concatenate x0 -> x1, other arithmetic: none -> 5.98 us  [scatter_sum(): jnp.concatenate([p.astype(jnp.bfloat16).reshape(count, -1) for p in parts...]
    ppermute x2, starting transfers between devices: 7.06 us -> 11.1 us  [padded_2(): before = lax.ppermute(last, axis, up)]
    concatenate x5 -> x4, local copies, waits for them, and re-layouts: 17.8 us -> 17.3 us  [scatter_sum(): jnp.concatenate([p.astype(jnp.bfloat16).reshape(count, -1) for p in parts...]
  transfers between devices with their start and end apart: 20 -> 22, of which waited for: 9 -> 8; matrix products, arithmetic and copies ran while one was open for 31% -> 25% of each run, Pallas kernels for 0% -> 0%
where the time goes in v8:
time: 359 us; the launch traced here: 353 us
  waiting for transfers between devices  87.5 us (24%)
  matrix products  83.3 us (23%)
  other arithmetic  60.8 us (17%)
  starting transfers between devices  55.3 us (15%)
  local copies, waits for them, and re-layouts  51 us (14%)
  between operations  15 us (4%)
    ppermute x7, waiting for transfers between devices, to_owner(): got = lax.ppermute(block.astype(jnp.bfloat16), axis, [(source, 0)])  52.3 us
    ppermute x7, waiting for transfers between devices, from_owner(): got = lax.ppermute(block, axis, [(0, target)])  21.2 us
    concatenate x4, local copies, waits for them, and re-layouts, scatter_sum(): jnp.concatenate([p.astype(jnp.bfloat16).reshape(count, -1) for p in parts...  17.3 us
    ppermute x7, starting transfers between devices, from_owner(): got = lax.ppermute(block, axis, [(0, target)])  16.6 us
    sub x1, other arithmetic, attend_back(): grad_prob - centre  16.3 us
    div x1, other arithmetic, attend(): prob_f32 = expd / jnp.sum(expd, axis=-1, keepdims=True)  14.3 us
    ppermute x2, starting transfers between devices, padded_2(): before = lax.ppermute(last, axis, up)  11.1 us
    dot_general x4, matrix products, gram_rows(): lax.dot_general(flat_left, flat_right, (((0,), (0,)), ((), ())), preferre...  11.1 us
  transfers between devices with their start and end apart: 22, of which 8 were waited for; matrix products, arithmetic and copies ran while one was open for 25% of the time, Pallas kernels for 0%

profile of v8, /device:TPU:0, one launch (start us, length us, event | category | flops | bytes accessed | tf_op | source)
XLA Modules:
  0.0 352.8 jit_solution(16911630189149188384)
XLA Ops:
  7.2 2.1 slice_bitcast_fusion.1
  9.4 3.7 %collective-permute-start.6 = (bf16[1,256,1280]{2,1,0:T(8,128)(2,1)}, bf16[1,256,1280]{2,1,0:T(8,128)(2,1)S(1)}, u32[]{:S(2)}, u32[]{:S(2)}) collective-permute-start(bf16[1,256,1280]{2,1,0:T(8,128)(2,1)} %slice_bitcast_fusion.1), channel_id=1, source_target_pairs={{0,1},{8,9},{16,17},{24,25},{32,33},{40,41},{48,49},{56,57},{64,65... | collective-permute-start | bytes 1966088 | tf_op jit(solution)/shard_map/ppermute | solution.py:19
  13.0 2.2 collective-permute-start.5
  15.3 2.2 collective-permute-start.4
  17.4 2.1 collective-permute-start.3
  19.6 2.2 collective-permute-start.2
  22.5 2.2 fusion.107
  24.7 2.1 fusion.104
  26.8 1.6 collective-permute-done.6
  28.4 2.1 collective-permute-start.1
  30.5 11.9 %collective-permute-done.5 = bf16[1,256,1280]{2,1,0:T(8,128)(2,1)S(1)} collective-permute-done((bf16[1,256,1280]{2,1,0:T(8,128)(2,1)}, bf16[1,256,1280]{2,1,0:T(8,128)(2,1)S(1)}, u32[]{:S(2)}, u32[]{:S(2)}) %collective-permute-start.5) | collective-permute-done | bytes 655392 | tf_op jit(solution)/shard_map/ppermute | solution.py:19
  42.5 2.1 collective-permute-start
  44.6 2.2 fusion.101
  46.8 2.2 copy.73
  48.9 2.2 copy.72
  51.1 2.2 copy.70
  53.3 2.6 fusion.179
  57.2 5.7 %collective-permute-start.10 = (bf16[1,1,256,1280]{3,2,1,0:T(8,128)(2,1)}, bf16[1,1,256,1280]{3,2,1,0:T(8,128)(2,1)}, u32[]{:S(2)}, u32[]{:S(2)}) collective-permute-start(bf16[1,1,256,1280]{3,2,1,0:T(8,128)(2,1)} %get-tuple-element.27), channel_id=1, source_target_pairs={{0,1},{1,2},{2,3},{3,4},{4,5},{5,6},{6,7},{8,9},{9,10},{10,11},{11... | collective-permute-start | bytes 1966088 | tf_op jit(solution)/shard_map/ppermute | solution.py:69
  62.9 7.7 %collective-permute-done.1 = bf16[1,256,1280]{2,1,0:T(8,128)(2,1)} collective-permute-done((bf16[1,256,1280]{2,1,0:T(8,128)(2,1)}, bf16[1,256,1280]{2,1,0:T(8,128)(2,1)}, u32[]{:S(2)}, u32[]{:S(2)}) %collective-permute-start.1) | collective-permute-done | bytes 655392 | tf_op jit(solution)/shard_map/ppermute | solution.py:19
  72.6 1.5 convolution_convert_fusion.1
  78.1 6.7 %fusion.135 = f32[2,10,256,512]{3,2,1,0:T(8,128)} fusion(bf16[2,256,10,64]{1,3,2,0:T(8,128)(2,1)} %bitcast.256, bf16[1,2,256,10,64]{2,4,3,1,0:T(8,128)(2,1)S(1)} %broadcast_in_dim.15, bf16[1,2,256,10,64]{2,4,3,1,0:T(8,128)(2,1)} %bitcast.260), kind=kOutput, calls=%fused_computation.145 | convolution fusion | flops 338165760 | bytes 12451840 | tf_op jit(solution)/shard_map/lfshd,lfthd->lfhst/dot_general | solution.py:99
  84.8 14.3 %fusion.22 = f32[2,10,256,512]{3,2,1,0:T(8,128)} fusion(f32[2,10,256,512]{3,2,1,0:T(8,128)} %fusion.135), kind=kOutput, calls=%fused_computation.24 | output fusion | flops 10497022 | bytes 20971520 | tf_op jit(solution)/shard_map/div | solution.py:107
  99.1 4.8 %convert_bitcast_fusion = bf16[1,2,10,256,512]{4,3,2,1,0:T(8,128)(2,1)S(1)} fusion(f32[2,10,256,512]{3,2,1,0:T(8,128)} %fusion.22), kind=kLoop, calls=%fused_computation.22 | loop fusion | flops 2621440 | bytes 15728640 | tf_op jit(solution)/shard_map/convert_element_type | solution.py:108
  104.0 1.7 fusion.113
  106.6 2.6 fusion.80
  109.3 2.0 fusion.124
  111.3 10.0 %fusion.61 = bf16[1,2,256,1280]{3,2,1,0:T(8,128)(2,1)S(1)} fusion(bf16[1280,3,1280]{2,0,1:T(8,128)(2,1)} %param.16, bf16[1,2,256,1,1280]{4,2,3,1,0:T(8,128)(2,1)S(1)} %get-tuple-element.25, bf16[1,2,256,1,1280]{4,2,3,1,0:T(8,128)(2,1)S(1)} %bitcast.264, bf16[1,2,256,1,1280]{4,2,3,1,0:T(8,128)(2,1)S(1)} %get-tuple-element.24, ...), kind=kOutput, calls=%fused_computation.69 | convolution fusion | flops 5044961280 | bytes 17694720 | tf_op jit(solution)/shard_map/lfsjo,cjo->lfsc/dot_general | solution.py:192
  122.4 2.1 fusion.110
  124.5 2.2 copy.76
  126.7 3.7 %fusion.17 = f32[2,10,64,512]{3,2,1,0:T(8,128)S(1)} fusion(bf16[2,256,10,64]{1,3,2,0:T(8,128)(2,1)} %bitcast.258, bf16[1,2,10,256,512]{4,3,2,1,0:T(8,128)(2,1)} %copy-done.1), kind=kOutput, calls=%fused_computation.18 | convolution fusion | flops 335544320 | bytes 8519680 | tf_op jit(solution)/shard_map/lfhst,lfshd->lfthd/dot_general | solution.py:131
  132.5 2.2 fusion.50
  134.8 5.4 %fusion.129 = f32[2,10,256,512]{3,2,1,0:T(8,128)} fusion(bf16[2,256,10,64]{1,3,2,0:T(8,128)(2,1)S(1)} %bitcast.259, bf16[2,256,10,64]{1,3,2,0:T(8,128)(2,1)S(1)} %broadcast_in_dim.16, bf16[2,256,10,64]{1,3,2,0:T(8,128)(2,1)S(1)} %bitcast.263), kind=kOutput, calls=%fused_computation.135 | convolution fusion | flops 338165760 | bytes 12451840 | tf_op jit(solution)/shard_map/lfshd,lfthd->lfhst/dot_general | solution.py:118
  140.2 16.3 %fusion.83 = bf16[1,2,10,256,512]{4,3,2,1,0:T(8,128)(2,1)} fusion(f32[2,10,256,512]{3,2,1,0:T(8,128)} %fusion.22, f32[2,10,256,512]{3,2,1,0:T(8,128)} %fusion.129), kind=kOutput, calls=%fused_computation.91 | output fusion | flops 13112831 | bytes 26214400 | tf_op jit(solution)/shard_map/sub | solution.py:122
  156.5 5.6 %fusion.116 = bf16[2,10,64,256]{3,2,1,0:T(8,128)(2,1)} fusion(bf16[1,2,10,256,512]{4,3,2,1,0:T(8,128)(2,1)} %fusion.83, bf16[1,2,256,10,64]{2,4,3,1,0:T(8,128)(2,1)} %copy-done.19, bf16[1,2,256,10,64]{2,4,3,1,0:T(8,128)(2,1)} %bitcast.261), kind=kOutput, calls=%fused_computation.115 | convolution fusion | flops 338493440 | bytes 7208960 | tf_op jit(solution)/shard_map/lfhst,lfthd->lfshd/dot_general | solution.py:124
  165.0 2.2 copy.96
  167.1 4.0 %concatenate.70 = bf16[16,8,6400]{2,1,0:T(8,128)(2,1)} reshape(bf16[640,1280]{1,0:T(8,128)(2,1)} %fusion.50) | data formatting | bytes 3276800 | tf_op jit(solution)/shard_map/concatenate | solution.py:34
  171.1 2.6 convolution_bitcast_fusion.1
  174.6 2.1 fusion.48
  176.7 4.4 %concatenate.69 = bf16[16,8,6400]{2,1,0:T(8,128)(2,1)} reshape(bf16[1280,640]{1,0:T(8,128)(2,1)} %fusion.48) | data formatting | bytes 3276800 | tf_op jit(solution)/shard_map/concatenate | solution.py:34
  181.1 2.2 copy.95
  183.3 3.7 %fusion.49 = bf16[1280,640]{1,0:T(8,128)(2,1)} fusion(bf16[2,256,640]{1,2,0:T(8,128)(2,1)} %bitcast.269, bf16[1,2,256,1280]{3,2,1,0:T(8,128)(2,1)S(1)} %copy-done.3, f32[1280]{0:T(1024)S(1)} %copy-done.34, f32[2,256]{1,0:T(2,128)S(1)} %add_rsqrt_fusion, f32[2,256]{1,0:T(2,128)S(1)} %broadcast_multiply_fusion.2), kind=kOutput, calls=%fused_computation.59 | convolution fusion | flops 842956800 | bytes 3613696 | tf_op jit(solution)/shard_map/dot_general | solution.py:147
  187.0 4.5 %concatenate.67 = bf16[16,8,6400]{2,1,0:T(8,128)(2,1)} reshape(bf16[1280,640]{1,0:T(8,128)(2,1)} %fusion.49) | data formatting | bytes 3276800 | tf_op jit(solution)/shard_map/concatenate | solution.py:34
  191.6 2.6 convolution_bitcast_fusion.2
  195.1 2.1 fusion.47
  197.2 4.4 %concatenate.68 = bf16[16,8,6400]{2,1,0:T(8,128)(2,1)} reshape(bf16[1280,640]{1,0:T(8,128)(2,1)} %fusion.47) | data formatting | bytes 3276800 | tf_op jit(solution)/shard_map/concatenate | solution.py:34
  201.6 6.0 %pad_maximum_fusion = bf16[16,8,25600]{2,1,0:T(8,128)(2,1)} fusion(bf16[16,8,6400]{2,1,0:T(8,128)(2,1)} %concatenate.70, bf16[16,8,6400]{2,1,0:T(8,128)(2,1)} %concatenate.69, bf16[16,8,6400]{2,1,0:T(8,128)(2,1)} %concatenate.68, bf16[16,8,6400]{2,1,0:T(8,128)(2,1)} %concatenate.67), kind=kLoop, calls=%fused_computation.13 | loop fusion | flops 26214400 | bytes 13107200 | tf_op jit(solution)/shard_map/concatenate | solution.py:34
  207.6 1.4 fusion.136
  209.0 1.4 collective-permute-start.17
  215.7 2.7 fusion.92
  219.7 36.2 %collective-permute-done.17 = bf16[1,256,1280]{1,2,0:T(8,128)(2,1)S(1)} collective-permute-done((bf16[1,256,1280]{1,2,0:T(8,128)(2,1)S(1)}, bf16[1,256,1280]{1,2,0:T(8,128)(2,1)S(1)}, u32[]{:S(2)}, u32[]{:S(2)}) %collective-permute-start.17) | collective-permute-done | bytes 655392 | tf_op jit(solution)/shard_map/ppermute | solution.py:27
  262.2 5.4 %collective-permute-start.7 = (bf16[1,1,256,1280]{3,2,1,0:T(8,128)(2,1)}, bf16[1,1,256,1280]{3,2,1,0:T(8,128)(2,1)}, u32[]{:S(2)}, u32[]{:S(2)}) collective-permute-start(bf16[1,1,256,1280]{3,2,1,0:T(8,128)(2,1)} %get-tuple-element.30), channel_id=1, source_target_pairs={{0,1},{1,2},{2,3},{3,4},{4,5},{5,6},{6,7},{8,9},{9,10},{10,11},{11... | collective-permute-start | bytes 1966088 | tf_op jit(solution)/shard_map/ppermute | solution.py:69
  267.7 16.2 %collective-permute-done.14 = bf16[1,256,1280]{1,2,0:T(8,128)(2,1)S(1)} collective-permute-done((bf16[1,256,1280]{1,2,0:T(8,128)(2,1)S(1)}, bf16[1,256,1280]{1,2,0:T(8,128)(2,1)S(1)}, u32[]{:S(2)}, u32[]{:S(2)}) %collective-permute-start.14) | collective-permute-done | bytes 655392 | tf_op jit(solution)/shard_map/ppermute | solution.py:27
  283.8 1.5 collective-permute-start.8
  291.4 8.0 %all-to-all-start.1 = ((f32[16,8,10]{2,1,0:T(8,128)}), f32[16,8,10]{2,1,0:T(8,128)S(1)}, u32[]{:S(2)}, u32[]{:S(2)}) async-start(f32[16,8,10]{2,1,0:T(8,128)} %reshape.476), calls=%async_computation.2 | async-start | bytes 131072 | tf_op jit(solution)/shard_map/all_to_all | solution.py:49
  299.5 3.0 collective-permute-done.8
  302.5 1.9 fusion.126
  304.4 10.4 %fusion.58 = bf16[1,2,256,1280]{3,2,1,0:T(8,128)(2,1)} fusion(bf16[1280,3,1280]{2,0,1:T(8,128)(2,1)} %param.16, bf16[1,2,256,1,1280]{4,2,1,3,0:T(8,128)(2,1)S(1)} %get-tuple-element.29, bf16[1,2,256,1,1280]{4,2,1,3,0:T(8,128)(2,1)S(1)} %bitcast.265, bf16[1,2,256,1,1280]{4,2,1,3,0:T(8,128)(2,1)S(1)} %get-tuple-element.28, ...), kind=kOutput, calls=%fused_computation.68 | convolution fusion | flops 5039063040 | bytes 16384000 | tf_op jit(solution)/shard_map/lfsjc,cjo->lfso/dot_general | solution.py:187
  315.4 3.3 all-to-all-start.2
  318.7 3.6 %reduce-scatter.2.cloned.1.call-done = bf16[1,8,25600]{2,1,0:T(8,128)(2,1)} async-done(((bf16[16,8,25600]{2,1,0:T(8,128)(2,1)}), bf16[1,8,25600]{2,1,0:T(8,128)(2,1)}) %reduce-scatter.2.cloned.1.call-update) | async-done | bytes 409616 | tf_op jit(solution)/shard_map/reduce_scatter | solution.py:36
  323.4 1.8 copy.85
  325.2 4.2 %all-to-all-start = ((f32[8,1,25600]{2,1,0:T(1,128)}), f32[8,1,25600]{2,1,0:T(1,128)}, u32[]{:S(2)}, u32[]{:S(2)}) async-start(f32[8,1,25600]{2,1,0:T(1,128)} %copy.85), calls=%async_computation.1 | async-start | bytes 1638400 | tf_op jit(solution)/shard_map/all_to_all | solution.py:37
  329.4 4.2 %fusion.74 = bf16[1,2,256,1280]{3,2,1,0:T(8,128)(2,1)} fusion(bf16[1,2,256,1280]{3,2,1,0:T(8,128)(2,1)S(1)} %copy-done.3, bf16[1,2,256,1280]{3,2,1,0:T(8,128)(2,1)} %copy-done.25, f32[1,2,256,1280]{3,2,1,0:T(8,128)} %copy-done.4, f32[2,256]{1,0:T(2,128)S(1)} %get-tuple-element.38, f32[2,256]{1,0:T(2,128)S(1)} %get-tuple-element.39, f32[1280]{0:T(1024)S(1)} %copy-done.34, ...), kind=kLoop, calls=%fused_computation.82 | loop fusion | flops 7208960 | bytes 6566912 | tf_op jit(solution)/shard_map/convert_element_type | solution.py:235
  334.2 7.3 %all-to-all-done = f32[8,1,25600]{2,1,0:T(1,128)} async-done(((f32[8,1,25600]{2,1,0:T(1,128)}), f32[8,1,25600]{2,1,0:T(1,128)}, u32[]{:S(2)}, u32[]{:S(2)}) %all-to-all-start) | async-done | bytes 819232 | tf_op jit(solution)/shard_map/all_to_all | solution.py:37
  341.5 1.7 reduce_sum.142
  (142 shorter events, 40.3 us)
Async XLA Ops:
  7.2 37.4 %copy-start = (bf16[1280,640]{1,0:T(8,128)(2,1)S(1)}, bf16[1280,640]{1,0:T(8,128)(2,1)}, u32[]{:S(2)}) copy-start(bf16[1280,640]{1,0:T(8,128)(2,1)} %param.14) | copy-start | bytes 4915204
  7.2 14.5 %copy-start.3 = (bf16[1,2,256,1280]{3,2,1,0:T(8,128)(2,1)S(1)}, bf16[1,2,256,1280]{3,2,1,0:T(8,128)(2,1)}, u32[]{:S(2)}) copy-start(bf16[1,2,256,1280]{3,2,1,0:T(8,128)(2,1)} %param.10) | copy-start | bytes 3932164
  7.2 315.1 %reduce-scatter.2.cloned.1.call-start = ((), (), s32[]{:S(2)}) async-start(), calls=%async_computation.4 | async-start | bytes 6963200 | tf_op jit(solution)/shard_map/reduce_scatter | solution.py:36
  9.4 13.1 %copy-start.12 = (bf16[1280,640]{1,0:T(8,128)(2,1)S(1)}, bf16[1280,640]{1,0:T(8,128)(2,1)}, u32[]{:S(2)}) copy-start(bf16[1280,640]{1,0:T(8,128)(2,1)} %param.13) | copy-start | bytes 4915204
  9.4 13.1 %copy-start.34 = (f32[1280]{0:T(1024)S(1)}, f32[1280]{0:T(1024)}, u32[]{:S(2)}) copy-start(f32[1280]{0:T(1024)} %param.11) | copy-start | bytes 15364
  9.4 19.1 %collective-permute-start.6 = (bf16[1,256,1280]{2,1,0:T(8,128)(2,1)}, bf16[1,256,1280]{2,1,0:T(8,128)(2,1)S(1)}, u32[]{:S(2)}, u32[]{:S(2)}) collective-permute-start(bf16[1,256,1280]{2,1,0:T(8,128)(2,1)} %slice_bitcast_fusion.1), channel_id=1, source_target_pairs={{0,1},{8,9},{16,17},{24,25},{32,33},{40,41},{48,49},{56,57},{64,65... | collective-permute-start | bytes 1966088 | tf_op jit(solution)/shard_map/ppermute | solution.py:19
  13.0 29.4 %collective-permute-start.5 = (bf16[1,256,1280]{2,1,0:T(8,128)(2,1)}, bf16[1,256,1280]{2,1,0:T(8,128)(2,1)S(1)}, u32[]{:S(2)}, u32[]{:S(2)}) collective-permute-start(bf16[1,256,1280]{2,1,0:T(8,128)(2,1)} %slice_bitcast_fusion.1), channel_id=1, source_target_pairs={{0,2},{8,10},{16,18},{24,26},{32,34},{40,42},{48,50},{56,58},{64,6... | collective-permute-start | bytes 1966088 | tf_op jit(solution)/shard_map/ppermute | solution.py:19
  15.3 40.6 %collective-permute-start.4 = (bf16[1,256,1280]{2,1,0:T(8,128)(2,1)}, bf16[1,256,1280]{2,1,0:T(8,128)(2,1)}, u32[]{:S(2)}, u32[]{:S(2)}) collective-permute-start(bf16[1,256,1280]{2,1,0:T(8,128)(2,1)} %slice_bitcast_fusion.1), channel_id=1, source_target_pairs={{0,3},{8,11},{16,19},{24,27},{32,35},{40,43},{48,51},{56,59},{64,6... | collective-permute-start | bytes 1966088 | tf_op jit(solution)/shard_map/ppermute | solution.py:19
  17.4 39.8 %collective-permute-start.3 = (bf16[1,256,1280]{2,1,0:T(8,128)(2,1)}, bf16[1,256,1280]{2,1,0:T(8,128)(2,1)}, u32[]{:S(2)}, u32[]{:S(2)}) collective-permute-start(bf16[1,256,1280]{2,1,0:T(8,128)(2,1)} %slice_bitcast_fusion.1), channel_id=1, source_target_pairs={{0,4},{8,12},{16,20},{24,28},{32,36},{40,44},{48,52},{56,60},{64,6... | collective-permute-start | bytes 1966088 | tf_op jit(solution)/shard_map/ppermute | solution.py:19
  19.6 43.3 %collective-permute-start.2 = (bf16[1,256,1280]{2,1,0:T(8,128)(2,1)}, bf16[1,256,1280]{2,1,0:T(8,128)(2,1)}, u32[]{:S(2)}, u32[]{:S(2)}) collective-permute-start(bf16[1,256,1280]{2,1,0:T(8,128)(2,1)} %slice_bitcast_fusion.1), channel_id=1, source_target_pairs={{0,5},{8,13},{16,21},{24,29},{32,37},{40,45},{48,53},{56,61},{64,6... | collective-permute-start | bytes 1966088 | tf_op jit(solution)/shard_map/ppermute | solution.py:19
  22.5 2.2 copy-start.36
  28.4 18.3 %copy-start.30 = (bf16[1,256,1280]{2,1,0:T(8,128)(2,1)}, bf16[1,256,1280]{2,1,0:T(8,128)(2,1)S(1)}, u32[]{:S(2)}) copy-start(bf16[1,256,1280]{2,1,0:T(8,128)(2,1)S(1)} %collective-permute-done.6) | copy-start | bytes 1966084
  28.4 42.2 %collective-permute-start.1 = (bf16[1,256,1280]{2,1,0:T(8,128)(2,1)}, bf16[1,256,1280]{2,1,0:T(8,128)(2,1)}, u32[]{:S(2)}, u32[]{:S(2)}) collective-permute-start(bf16[1,256,1280]{2,1,0:T(8,128)(2,1)} %slice_bitcast_fusion.1), channel_id=1, source_target_pairs={{0,6},{8,14},{16,22},{24,30},{32,38},{40,46},{48,54},{56,62},{64,7... | collective-permute-start | bytes 1966088 | tf_op jit(solution)/shard_map/ppermute | solution.py:19
  42.5 4.3 %copy-start.32 = (bf16[1,256,1280]{2,1,0:T(8,128)(2,1)}, bf16[1,256,1280]{2,1,0:T(8,128)(2,1)S(1)}, u32[]{:S(2)}) copy-start(bf16[1,256,1280]{2,1,0:T(8,128)(2,1)S(1)} %collective-permute-done.5) | copy-start | bytes 1966084
  42.5 28.1 %collective-permute-start = (bf16[1,256,1280]{2,1,0:T(8,128)(2,1)}, bf16[1,256,1280]{2,1,0:T(8,128)(2,1)}, u32[]{:S(2)}, u32[]{:S(2)}) collective-permute-start(bf16[1,256,1280]{2,1,0:T(8,128)(2,1)} %slice_bitcast_fusion.1), channel_id=1, source_target_pairs={{0,7},{8,15},{16,23},{24,31},{32,39},{40,47},{48,55},{56,63},{64,7... | collective-permute-start | bytes 1966088 | tf_op jit(solution)/shard_map/ppermute | solution.py:19
  53.3 17.3 %copy-start.31 = (bf16[1,256,1280]{2,1,0:T(8,128)(2,1)S(1)}, bf16[1,256,1280]{2,1,0:T(8,128)(2,1)}, u32[]{:S(2)}) copy-start(bf16[1,256,1280]{2,1,0:T(8,128)(2,1)} %copy-done.30) | copy-start | bytes 1966084
  53.3 17.3 %copy-start.33 = (bf16[1,256,1280]{2,1,0:T(8,128)(2,1)S(1)}, bf16[1,256,1280]{2,1,0:T(8,128)(2,1)}, u32[]{:S(2)}) copy-start(bf16[1,256,1280]{2,1,0:T(8,128)(2,1)} %copy-done.32) | copy-start | bytes 1966084
  55.9 53.4 %collective-permute-start.9 = (bf16[1,1,256,1280]{3,2,1,0:T(8,128)(2,1)}, bf16[1,1,256,1280]{3,2,1,0:T(8,128)(2,1)}, u32[]{:S(2)}, u32[]{:S(2)}) collective-permute-start(bf16[1,1,256,1280]{3,2,1,0:T(8,128)(2,1)} %get-tuple-element.26), channel_id=1, source_target_pairs={{1,0},{2,1},{3,2},{4,3},{5,4},{6,5},{7,6},{9,8},{10,9},{11,10},{12... | collective-permute-start | bytes 1966088 | tf_op jit(solution)/shard_map/ppermute | solution.py:70
  57.2 14.6 %copy-start.13 = (bf16[1280,640]{1,0:T(8,128)(2,1)S(1)}, bf16[1280,640]{1,0:T(8,128)(2,1)}, u32[]{:S(2)}) copy-start(bf16[1280,640]{1,0:T(8,128)(2,1)} %param.13) | copy-start | bytes 4915204
  57.2 52.1 %collective-permute-start.10 = (bf16[1,1,256,1280]{3,2,1,0:T(8,128)(2,1)}, bf16[1,1,256,1280]{3,2,1,0:T(8,128)(2,1)}, u32[]{:S(2)}, u32[]{:S(2)}) collective-permute-start(bf16[1,1,256,1280]{3,2,1,0:T(8,128)(2,1)} %get-tuple-element.27), channel_id=1, source_target_pairs={{0,1},{1,2},{2,3},{3,4},{4,5},{5,6},{6,7},{8,9},{9,10},{10,11},{11... | collective-permute-start | bytes 1966088 | tf_op jit(solution)/shard_map/ppermute | solution.py:69
  71.5 1.1 copy-start.5
  77.2 0.9 copy-start.19
  99.1 4.9 %copy-start.17 = (bf16[2,256,640]{1,2,0:T(8,128)(2,1)S(1)}, bf16[2,256,640]{1,2,0:T(8,128)(2,1)}, u32[]{:S(2)}) copy-start(bf16[2,256,640]{1,2,0:T(8,128)(2,1)} %copy.70) | copy-start | bytes 1966084
  103.9 2.4 copy-start.1
  104.0 2.7 copy-start.35
  106.2 3.0 copy-start.28
  106.6 2.6 copy-start.20
  109.3 2.1 copy-start.37
  121.3 1.1 copy-start.25
  130.5 2.0 copy-start.26
  130.5 2.0 copy-start.29
  132.5 2.3 copy-start.16
  132.5 2.3 copy-start.18
  156.5 5.6 %copy-start.2 = (bf16[1,2,10,256,512]{4,3,2,1,0:T(8,128)(2,1)S(1)}, bf16[1,2,10,256,512]{4,3,2,1,0:T(8,128)(2,1)}, u32[]{:S(2)}) copy-start(bf16[1,2,10,256,512]{4,3,2,1,0:T(8,128)(2,1)} %fusion.83) | copy-start | bytes 15728644
  156.5 5.6 %copy-start.15 = (bf16[2,256,640]{1,2,0:T(8,128)(2,1)S(1)}, bf16[2,256,640]{1,2,0:T(8,128)(2,1)}, u32[]{:S(2)}) copy-start(bf16[2,256,640]{1,2,0:T(8,128)(2,1)} %copy.72) | copy-start | bytes 1966084
  171.1 2.6 copy-start.6
  171.1 2.6 copy-start.8
  191.6 2.6 copy-start.7
  191.6 2.6 copy-start.10
  207.6 8.1 %copy-start.27 = (bf16[2,10,64,256]{3,2,1,0:T(8,128)(2,1)S(1)}, bf16[2,10,64,256]{3,2,1,0:T(8,128)(2,1)}, u32[]{:S(2)}) copy-start(bf16[2,10,64,256]{3,2,1,0:T(8,128)(2,1)} %fusion.116) | copy-start | bytes 1966084
  209.0 9.4 %copy-start.14 = (bf16[1280,640]{1,0:T(8,128)(2,1)S(1)}, bf16[1280,640]{1,0:T(8,128)(2,1)}, u32[]{:S(2)}) copy-start(bf16[1280,640]{1,0:T(8,128)(2,1)} %param.13) | copy-start | bytes 4915204
  209.0 9.4 %copy-start.24 = (bf16[1,2,256,640]{3,2,1,0:T(8,128)(2,1)S(1)}, bf16[1,2,256,640]{3,2,1,0:T(8,128)(2,1)}, u32[]{:S(2)}) copy-start(bf16[1,2,256,640]{3,2,1,0:T(8,128)(2,1)} %copy.95) | copy-start | bytes 1966084
  209.0 46.8 %collective-permute-start.17 = (bf16[1,256,1280]{1,2,0:T(8,128)(2,1)S(1)}, bf16[1,256,1280]{1,2,0:T(8,128)(2,1)S(1)}, u32[]{:S(2)}, u32[]{:S(2)}) collective-permute-start(bf16[1,256,1280]{1,2,0:T(8,128)(2,1)S(1)} %fusion.136), channel_id=1, source_target_pairs={{7,0},{15,8},{23,16},{31,24},{39,32},{47,40},{55,48},{63,56},{71,6... | collective-permute-start | bytes 1966088 | tf_op jit(solution)/shard_map/ppermute | solution.py:27
  210.5 46.7 %collective-permute-start.16 = (bf16[1,256,1280]{1,2,0:T(8,128)(2,1)S(1)}, bf16[1,256,1280]{1,2,0:T(8,128)(2,1)S(1)}, u32[]{:S(2)}, u32[]{:S(2)}) collective-permute-start(bf16[1,256,1280]{1,2,0:T(8,128)(2,1)S(1)} %fusion.136), channel_id=1, source_target_pairs={{6,0},{14,8},{22,16},{30,24},{38,32},{46,40},{54,48},{62,56},{70,6... | collective-permute-start | bytes 1966088 | tf_op jit(solution)/shard_map/ppermute | solution.py:27
  211.8 50.4 %collective-permute-start.15 = (bf16[1,256,1280]{1,2,0:T(8,128)(2,1)S(1)}, bf16[1,256,1280]{1,2,0:T(8,128)(2,1)S(1)}, u32[]{:S(2)}, u32[]{:S(2)}) collective-permute-start(bf16[1,256,1280]{1,2,0:T(8,128)(2,1)S(1)} %fusion.136), channel_id=1, source_target_pairs={{5,0},{13,8},{21,16},{29,24},{37,32},{45,40},{53,48},{61,56},{69,6... | collective-permute-start | bytes 1966088 | tf_op jit(solution)/shard_map/ppermute | solution.py:27
  213.1 70.8 %collective-permute-start.14 = (bf16[1,256,1280]{1,2,0:T(8,128)(2,1)S(1)}, bf16[1,256,1280]{1,2,0:T(8,128)(2,1)S(1)}, u32[]{:S(2)}, u32[]{:S(2)}) collective-permute-start(bf16[1,256,1280]{1,2,0:T(8,128)(2,1)S(1)} %fusion.136), channel_id=1, source_target_pairs={{4,0},{12,8},{20,16},{28,24},{36,32},{44,40},{52,48},{60,56},{68,6... | collective-permute-start | bytes 1966088 | tf_op jit(solution)/shard_map/ppermute | solution.py:27
  214.4 71.0 %collective-permute-start.13 = (bf16[1,256,1280]{1,2,0:T(8,128)(2,1)S(1)}, bf16[1,256,1280]{1,2,0:T(8,128)(2,1)S(1)}, u32[]{:S(2)}, u32[]{:S(2)}) collective-permute-start(bf16[1,256,1280]{1,2,0:T(8,128)(2,1)S(1)} %fusion.136), channel_id=1, source_target_pairs={{3,0},{11,8},{19,16},{27,24},{35,32},{43,40},{51,48},{59,56},{67,6... | collective-permute-start | bytes 1966088 | tf_op jit(solution)/shard_map/ppermute | solution.py:27
  218.4 40.1 %copy-start.23 = (bf16[1,2,256,640]{3,2,1,0:T(8,128)(2,1)S(1)}, bf16[1,2,256,640]{3,2,1,0:T(8,128)(2,1)}, u32[]{:S(2)}) copy-start(bf16[1,2,256,640]{3,2,1,0:T(8,128)(2,1)} %copy.96) | copy-start | bytes 1966084
  255.9 29.5 %collective-permute-start.12 = (bf16[1,256,1280]{1,2,0:T(8,128)(2,1)S(1)}, bf16[1,256,1280]{1,2,0:T(8,128)(2,1)S(1)}, u32[]{:S(2)}, u32[]{:S(2)}) collective-permute-start(bf16[1,256,1280]{1,2,0:T(8,128)(2,1)S(1)} %fusion.136), channel_id=1, source_target_pairs={{2,0},{10,8},{18,16},{26,24},{34,32},{42,40},{50,48},{58,56},{66,6... | collective-permute-start | bytes 1966088 | tf_op jit(solution)/shard_map/ppermute | solution.py:27
  257.2 28.2 %collective-permute-start.11 = (bf16[1,256,1280]{1,2,0:T(8,128)(2,1)S(1)}, bf16[1,256,1280]{1,2,0:T(8,128)(2,1)S(1)}, u32[]{:S(2)}, u32[]{:S(2)}) collective-permute-start(bf16[1,256,1280]{1,2,0:T(8,128)(2,1)S(1)} %fusion.136), channel_id=1, source_target_pairs={{1,0},{9,8},{17,16},{25,24},{33,32},{41,40},{49,48},{57,56},{65,64... | collective-permute-start | bytes 1966088 | tf_op jit(solution)/shard_map/ppermute | solution.py:27
  259.7 1.3 copy-start.21
  259.9 25.4 %copy-start.9 = (f32[256,640]{0,1:T(8,128)S(1)}, f32[256,640]{0,1:T(8,128)}, u32[]{:S(2)}) copy-start(f32[256,640]{0,1:T(8,128)} %slice_reduce_fusion) | copy-start | bytes 1966084
  259.9 25.4 %copy-start.11 = (f32[256,640]{0,1:T(8,128)S(1)}, f32[256,640]{0,1:T(8,128)}, u32[]{:S(2)}) copy-start(f32[256,640]{0,1:T(8,128)} %slice_reduce_fusion.1) | copy-start | bytes 1966084
  262.2 37.3 %collective-permute-start.7 = (bf16[1,1,256,1280]{3,2,1,0:T(8,128)(2,1)}, bf16[1,1,256,1280]{3,2,1,0:T(8,128)(2,1)}, u32[]{:S(2)}, u32[]{:S(2)}) collective-permute-start(bf16[1,1,256,1280]{3,2,1,0:T(8,128)(2,1)} %get-tuple-element.30), channel_id=1, source_target_pairs={{0,1},{1,2},{2,3},{3,4},{4,5},{5,6},{6,7},{8,9},{9,10},{10,11},{11... | collective-permute-start | bytes 1966088 | tf_op jit(solution)/shard_map/ppermute | solution.py:69
  283.8 18.7 %collective-permute-start.8 = (bf16[1,1,256,1280]{3,2,1,0:T(8,128)(2,1)}, bf16[1,1,256,1280]{3,2,1,0:T(8,128)(2,1)}, u32[]{:S(2)}, u32[]{:S(2)}) collective-permute-start(bf16[1,1,256,1280]{3,2,1,0:T(8,128)(2,1)} %get-tuple-element.31), channel_id=1, source_target_pairs={{1,0},{2,1},{3,2},{4,3},{5,4},{6,5},{7,6},{9,8},{10,9},{11,10},{12... | collective-permute-start | bytes 1966088 | tf_op jit(solution)/shard_map/ppermute | solution.py:70
  289.1 1.6 copy-start.4
  291.4 23.4 %all-to-all-start.1 = ((f32[16,8,10]{2,1,0:T(8,128)}), f32[16,8,10]{2,1,0:T(8,128)S(1)}, u32[]{:S(2)}, u32[]{:S(2)}) async-start(f32[16,8,10]{2,1,0:T(8,128)} %reshape.476), calls=%async_computation.2 | async-start | bytes 131072 | tf_op jit(solution)/shard_map/all_to_all | solution.py:49
  299.4 5.0 %copy-start.22 = (bf16[1,2,256,1280]{3,2,1,0:T(8,128)(2,1)S(1)}, bf16[1,2,256,1280]{3,2,1,0:T(8,128)(2,1)}, u32[]{:S(2)}) copy-start(bf16[1,2,256,1280]{3,2,1,0:T(8,128)(2,1)} %get-tuple-element.36) | copy-start | bytes 3932164
  299.5 5.0 %copy-start.38 = (bf16[1,2,256,1280]{3,2,1,0:T(8,128)(2,1)S(1)}, bf16[1,2,256,1280]{3,2,1,0:T(8,128)(2,1)}, u32[]{:S(2)}) copy-start(bf16[1,2,256,1280]{3,2,1,0:T(8,128)(2,1)} %copy-done.37) | copy-start | bytes 3932164
  315.4 9.8 %all-to-all-start.2 = ((f32[8,1,10]{2,1,0:T(1,128)}), f32[8,1,10]{2,1,0:T(1,128)S(1)}, u32[]{:S(2)}, u32[]{:S(2)}) async-start(f32[8,1,10]{2,1,0:T(1,128)} %bitcast.74), calls=%async_computation.3 | async-start | bytes 8192 | tf_op jit(solution)/shard_map/all_to_all | solution.py:50
  325.2 16.3 %all-to-all-start = ((f32[8,1,25600]{2,1,0:T(1,128)}), f32[8,1,25600]{2,1,0:T(1,128)}, u32[]{:S(2)}, u32[]{:S(2)}) async-start(f32[8,1,25600]{2,1,0:T(1,128)} %copy.85), calls=%async_computation.1 | async-start | bytes 1638400 | tf_op jit(solution)/shard_map/all_to_all | solution.py:37
Sparse Core Ops, SparseCore 0:
  207.7 114.5 reduce-scatter.1

commit v9 on v8

--- a/solution.py
+++ b/solution.py
@@ -34,8 +34,8 @@
     packed = jnp.concatenate([p.astype(jnp.bfloat16).reshape(count, -1) for p in parts], axis=1)
     share = packed.reshape((lax.axis_size(outer), -1) + packed.shape[1:])
     share = lax.psum_scatter(share, outer, scatter_dimension=0, tiled=True)[0]
-    share = lax.all_to_all(share.astype(jnp.float32), inner, 0, 0, tiled=True)
-    share = jnp.sum(share, axis=0)
+    share = lax.all_to_all(share, inner, 0, 0, tiled=True)
+    share = jnp.sum(share.astype(jnp.float32), axis=0)
     outs, start = [], 0
     for p in parts:
         width = p.size // count

time: 359 us -> 355 us (0.989)
  waiting for transfers between devices: 87.5 us -> 83.4 us
    all_to_all x1, waiting for transfers between devices: 7.27 us -> 3.27 us  [scatter_sum(): share = lax.all_to_all(share, inner, 0, 0, tiled=True)]
    unnamed x81 -> x83, local copies, waits for them, and re-layouts: 8.97 us -> 10.4 us
where the time goes in v9:
time: 355 us; the launch traced here: 349 us
  waiting for transfers between devices  83.4 us (23%)
  matrix products  83.1 us (23%)
  other arithmetic  60.8 us (17%)
  starting transfers between devices  55.6 us (16%)
  local copies, waits for them, and re-layouts  51.1 us (14%)
  between operations  15.1 us (4%)
    ppermute x7, waiting for transfers between devices, to_owner(): got = lax.ppermute(block.astype(jnp.bfloat16), axis, [(source, 0)])  52.4 us
    ppermute x7, waiting for transfers between devices, from_owner(): got = lax.ppermute(block, axis, [(0, target)])  21.2 us
    concatenate x4, local copies, waits for them, and re-layouts, scatter_sum(): jnp.concatenate([p.astype(jnp.bfloat16).reshape(count, -1) for p in parts...  17.3 us
    ppermute x7, starting transfers between devices, from_owner(): got = lax.ppermute(block, axis, [(0, target)])  16.6 us
    sub x1, other arithmetic, attend_back(): grad_prob - centre  16.3 us
    div x1, other arithmetic, attend(): prob_f32 = expd / jnp.sum(expd, axis=-1, keepdims=True)  14.3 us
    ppermute x2, starting transfers between devices, padded_2(): before = lax.ppermute(last, axis, up)  11.1 us
    dot_general x4, matrix products, gram_rows(): lax.dot_general(flat_left, flat_right, (((0,), (0,)), ((), ())), preferre...  11.1 us
  transfers between devices with their start and end apart: 22, of which 8 were waited for; matrix products, arithmetic and copies ran while one was open for 25% of the time, Pallas kernels for 0%

profile of v9, /device:TPU:0, one launch (start us, length us, event | category | flops | bytes accessed | tf_op | source)
XLA Modules:
  0.0 349.1 jit_solution(13941347255042697915)
XLA Ops:
  7.2 2.1 slice_bitcast_fusion.1
  9.4 3.7 %collective-permute-start.6 = (bf16[1,256,1280]{2,1,0:T(8,128)(2,1)}, bf16[1,256,1280]{2,1,0:T(8,128)(2,1)S(1)}, u32[]{:S(2)}, u32[]{:S(2)}) collective-permute-start(bf16[1,256,1280]{2,1,0:T(8,128)(2,1)} %slice_bitcast_fusion.1), channel_id=1, source_target_pairs={{0,1},{8,9},{16,17},{24,25},{32,33},{40,41},{48,49},{56,57},{64,65... | collective-permute-start | bytes 1966088 | tf_op jit(solution)/shard_map/ppermute | solution.py:19
  13.0 2.2 collective-permute-start.5
  15.3 2.2 collective-permute-start.4
  17.4 2.1 collective-permute-start.3
  19.6 2.2 collective-permute-start.2
  22.5 2.2 fusion.107
  24.7 2.1 fusion.104
  26.8 1.6 collective-permute-done.6
  28.4 2.1 collective-permute-start.1
  30.5 11.9 %collective-permute-done.5 = bf16[1,256,1280]{2,1,0:T(8,128)(2,1)S(1)} collective-permute-done((bf16[1,256,1280]{2,1,0:T(8,128)(2,1)}, bf16[1,256,1280]{2,1,0:T(8,128)(2,1)S(1)}, u32[]{:S(2)}, u32[]{:S(2)}) %collective-permute-start.5) | collective-permute-done | bytes 655392 | tf_op jit(solution)/shard_map/ppermute | solution.py:19
  42.5 2.2 collective-permute-start
  44.6 2.1 fusion.101
  46.8 2.2 copy.69
  48.9 2.2 copy.68
  51.1 2.2 copy.66
  53.3 2.6 fusion.179
  57.2 5.7 %collective-permute-start.10 = (bf16[1,1,256,1280]{3,2,1,0:T(8,128)(2,1)}, bf16[1,1,256,1280]{3,2,1,0:T(8,128)(2,1)}, u32[]{:S(2)}, u32[]{:S(2)}) collective-permute-start(bf16[1,1,256,1280]{3,2,1,0:T(8,128)(2,1)} %get-tuple-element.27), channel_id=1, source_target_pairs={{0,1},{1,2},{2,3},{3,4},{4,5},{5,6},{6,7},{8,9},{9,10},{10,11},{11... | collective-permute-start | bytes 1966088 | tf_op jit(solution)/shard_map/ppermute | solution.py:69
  62.9 7.7 %collective-permute-done.1 = bf16[1,256,1280]{2,1,0:T(8,128)(2,1)} collective-permute-done((bf16[1,256,1280]{2,1,0:T(8,128)(2,1)}, bf16[1,256,1280]{2,1,0:T(8,128)(2,1)}, u32[]{:S(2)}, u32[]{:S(2)}) %collective-permute-start.1) | collective-permute-done | bytes 655392 | tf_op jit(solution)/shard_map/ppermute | solution.py:19
  72.6 1.5 convolution_convert_fusion.1
  78.1 6.7 %fusion.135 = f32[2,10,256,512]{3,2,1,0:T(8,128)} fusion(bf16[2,256,10,64]{1,3,2,0:T(8,128)(2,1)} %bitcast.254, bf16[1,2,256,10,64]{2,4,3,1,0:T(8,128)(2,1)S(1)} %broadcast_in_dim.15, bf16[1,2,256,10,64]{2,4,3,1,0:T(8,128)(2,1)} %bitcast.258), kind=kOutput, calls=%fused_computation.145 | convolution fusion | flops 338165760 | bytes 12451840 | tf_op jit(solution)/shard_map/lfshd,lfthd->lfhst/dot_general | solution.py:99
  84.7 14.3 %fusion.22 = f32[2,10,256,512]{3,2,1,0:T(8,128)} fusion(f32[2,10,256,512]{3,2,1,0:T(8,128)} %fusion.135), kind=kOutput, calls=%fused_computation.24 | output fusion | flops 10497022 | bytes 20971520 | tf_op jit(solution)/shard_map/div | solution.py:107
  99.0 4.8 %convert_bitcast_fusion = bf16[1,2,10,256,512]{4,3,2,1,0:T(8,128)(2,1)S(1)} fusion(f32[2,10,256,512]{3,2,1,0:T(8,128)} %fusion.22), kind=kLoop, calls=%fused_computation.22 | loop fusion | flops 2621440 | bytes 15728640 | tf_op jit(solution)/shard_map/convert_element_type | solution.py:108
  103.9 1.7 fusion.113
  106.6 2.6 fusion.80
  109.2 2.0 fusion.124
  111.3 10.0 %fusion.61 = bf16[1,2,256,1280]{3,2,1,0:T(8,128)(2,1)S(1)} fusion(bf16[1280,3,1280]{2,0,1:T(8,128)(2,1)} %param.16, bf16[1,2,256,1,1280]{4,2,3,1,0:T(8,128)(2,1)S(1)} %get-tuple-element.25, bf16[1,2,256,1,1280]{4,2,3,1,0:T(8,128)(2,1)S(1)} %bitcast.262, bf16[1,2,256,1,1280]{4,2,3,1,0:T(8,128)(2,1)S(1)} %get-tuple-element.24, ...), kind=kOutput, calls=%fused_computation.69 | convolution fusion | flops 5044961280 | bytes 17694720 | tf_op jit(solution)/shard_map/lfsjo,cjo->lfsc/dot_general | solution.py:192
  122.4 2.1 fusion.110
  124.5 2.2 copy.72
  126.6 3.7 %fusion.17 = f32[2,10,64,512]{3,2,1,0:T(8,128)S(1)} fusion(bf16[2,256,10,64]{1,3,2,0:T(8,128)(2,1)} %bitcast.256, bf16[1,2,10,256,512]{4,3,2,1,0:T(8,128)(2,1)} %copy-done.1), kind=kOutput, calls=%fused_computation.18 | convolution fusion | flops 335544320 | bytes 8519680 | tf_op jit(solution)/shard_map/lfhst,lfshd->lfthd/dot_general | solution.py:131
  132.4 2.2 fusion.50
  134.7 5.4 %fusion.129 = f32[2,10,256,512]{3,2,1,0:T(8,128)} fusion(bf16[2,256,10,64]{1,3,2,0:T(8,128)(2,1)S(1)} %bitcast.257, bf16[2,256,10,64]{1,3,2,0:T(8,128)(2,1)S(1)} %broadcast_in_dim.16, bf16[2,256,10,64]{1,3,2,0:T(8,128)(2,1)S(1)} %bitcast.261), kind=kOutput, calls=%fused_computation.135 | convolution fusion | flops 338165760 | bytes 12451840 | tf_op jit(solution)/shard_map/lfshd,lfthd->lfhst/dot_general | solution.py:118
  140.1 16.3 %fusion.83 = bf16[1,2,10,256,512]{4,3,2,1,0:T(8,128)(2,1)} fusion(f32[2,10,256,512]{3,2,1,0:T(8,128)} %fusion.22, f32[2,10,256,512]{3,2,1,0:T(8,128)} %fusion.129), kind=kOutput, calls=%fused_computation.91 | output fusion | flops 13112831 | bytes 26214400 | tf_op jit(solution)/shard_map/sub | solution.py:122
  156.4 5.6 %fusion.116 = bf16[2,10,64,256]{3,2,1,0:T(8,128)(2,1)} fusion(bf16[1,2,10,256,512]{4,3,2,1,0:T(8,128)(2,1)} %fusion.83, bf16[1,2,256,10,64]{2,4,3,1,0:T(8,128)(2,1)} %copy-done.19, bf16[1,2,256,10,64]{2,4,3,1,0:T(8,128)(2,1)} %bitcast.259), kind=kOutput, calls=%fused_computation.115 | convolution fusion | flops 338493440 | bytes 7208960 | tf_op jit(solution)/shard_map/lfhst,lfthd->lfshd/dot_general | solution.py:124
  164.9 2.2 copy.92
  167.0 4.0 %concatenate.70 = bf16[16,8,6400]{2,1,0:T(8,128)(2,1)} reshape(bf16[640,1280]{1,0:T(8,128)(2,1)} %fusion.50) | data formatting | bytes 3276800 | tf_op jit(solution)/shard_map/concatenate | solution.py:34
  171.0 2.6 convolution_bitcast_fusion.1
  174.5 2.1 fusion.48
  176.6 4.4 %concatenate.69 = bf16[16,8,6400]{2,1,0:T(8,128)(2,1)} reshape(bf16[1280,640]{1,0:T(8,128)(2,1)} %fusion.48) | data formatting | bytes 3276800 | tf_op jit(solution)/shard_map/concatenate | solution.py:34
  181.0 2.2 copy.91
  183.1 3.7 %fusion.49 = bf16[1280,640]{1,0:T(8,128)(2,1)} fusion(bf16[2,256,640]{1,2,0:T(8,128)(2,1)} %bitcast.267, bf16[1,2,256,1280]{3,2,1,0:T(8,128)(2,1)S(1)} %copy-done.3, f32[1280]{0:T(1024)S(1)} %copy-done.34, f32[2,256]{1,0:T(2,128)S(1)} %add_rsqrt_fusion, f32[2,256]{1,0:T(2,128)S(1)} %broadcast_multiply_fusion.2), kind=kOutput, calls=%fused_computation.59 | convolution fusion | flops 842956800 | bytes 3613696 | tf_op jit(solution)/shard_map/dot_general | solution.py:147
  186.9 4.5 %concatenate.67 = bf16[16,8,6400]{2,1,0:T(8,128)(2,1)} reshape(bf16[1280,640]{1,0:T(8,128)(2,1)} %fusion.49) | data formatting | bytes 3276800 | tf_op jit(solution)/shard_map/concatenate | solution.py:34
  191.4 2.6 convolution_bitcast_fusion.2
  194.9 2.1 fusion.47
  197.0 4.4 %concatenate.68 = bf16[16,8,6400]{2,1,0:T(8,128)(2,1)} reshape(bf16[1280,640]{1,0:T(8,128)(2,1)} %fusion.47) | data formatting | bytes 3276800 | tf_op jit(solution)/shard_map/concatenate | solution.py:34
  201.4 6.0 %pad_maximum_fusion = bf16[16,8,25600]{2,1,0:T(8,128)(2,1)} fusion(bf16[16,8,6400]{2,1,0:T(8,128)(2,1)} %concatenate.70, bf16[16,8,6400]{2,1,0:T(8,128)(2,1)} %concatenate.69, bf16[16,8,6400]{2,1,0:T(8,128)(2,1)} %concatenate.68, bf16[16,8,6400]{2,1,0:T(8,128)(2,1)} %concatenate.67), kind=kLoop, calls=%fused_computation.13 | loop fusion | flops 26214400 | bytes 13107200 | tf_op jit(solution)/shard_map/concatenate | solution.py:34
  207.4 1.4 fusion.136
  208.9 1.4 collective-permute-start.17
  210.3 1.3 collective-permute-start.16
  215.5 2.7 fusion.92
  219.5 36.2 %collective-permute-done.17 = bf16[1,256,1280]{1,2,0:T(8,128)(2,1)S(1)} collective-permute-done((bf16[1,256,1280]{1,2,0:T(8,128)(2,1)S(1)}, bf16[1,256,1280]{1,2,0:T(8,128)(2,1)S(1)}, u32[]{:S(2)}, u32[]{:S(2)}) %collective-permute-start.17) | collective-permute-done | bytes 655392 | tf_op jit(solution)/shard_map/ppermute | solution.py:27
  262.0 5.5 %collective-permute-start.7 = (bf16[1,1,256,1280]{3,2,1,0:T(8,128)(2,1)}, bf16[1,1,256,1280]{3,2,1,0:T(8,128)(2,1)}, u32[]{:S(2)}, u32[]{:S(2)}) collective-permute-start(bf16[1,1,256,1280]{3,2,1,0:T(8,128)(2,1)} %get-tuple-element.30), channel_id=1, source_target_pairs={{0,1},{1,2},{2,3},{3,4},{4,5},{5,6},{6,7},{8,9},{9,10},{10,11},{11... | collective-permute-start | bytes 1966088 | tf_op jit(solution)/shard_map/ppermute | solution.py:69
  267.5 16.2 %collective-permute-done.14 = bf16[1,256,1280]{1,2,0:T(8,128)(2,1)S(1)} collective-permute-done((bf16[1,256,1280]{1,2,0:T(8,128)(2,1)S(1)}, bf16[1,256,1280]{1,2,0:T(8,128)(2,1)S(1)}, u32[]{:S(2)}, u32[]{:S(2)}) %collective-permute-start.14) | collective-permute-done | bytes 655392 | tf_op jit(solution)/shard_map/ppermute | solution.py:27
  283.7 1.5 collective-permute-start.8
  291.2 8.0 %all-to-all-start.1 = ((f32[16,8,10]{2,1,0:T(8,128)}), f32[16,8,10]{2,1,0:T(8,128)S(1)}, u32[]{:S(2)}, u32[]{:S(2)}) async-start(f32[16,8,10]{2,1,0:T(8,128)} %reshape.466), calls=%async_computation.2 | async-start | bytes 131072 | tf_op jit(solution)/shard_map/all_to_all | solution.py:49
  299.3 3.0 collective-permute-done.8
  302.3 1.9 fusion.126
  304.3 10.3 %fusion.58 = bf16[1,2,256,1280]{3,2,1,0:T(8,128)(2,1)} fusion(bf16[1280,3,1280]{2,0,1:T(8,128)(2,1)} %param.16, bf16[1,2,256,1,1280]{4,2,1,3,0:T(8,128)(2,1)S(1)} %get-tuple-element.29, bf16[1,2,256,1,1280]{4,2,1,3,0:T(8,128)(2,1)S(1)} %bitcast.263, bf16[1,2,256,1,1280]{4,2,1,3,0:T(8,128)(2,1)S(1)} %get-tuple-element.28, ...), kind=kOutput, calls=%fused_computation.68 | convolution fusion | flops 5039063040 | bytes 16384000 | tf_op jit(solution)/shard_map/lfsjc,cjo->lfso/dot_general | solution.py:187
  315.2 3.3 all-to-all-start.2
  318.5 3.5 %reduce-scatter.2.cloned.1.call-done = bf16[1,8,25600]{2,1,0:T(8,128)(2,1)} async-done(((bf16[16,8,25600]{2,1,0:T(8,128)(2,1)}), bf16[1,8,25600]{2,1,0:T(8,128)(2,1)}) %reduce-scatter.2.cloned.1.call-update) | async-done | bytes 409616 | tf_op jit(solution)/shard_map/reduce_scatter | solution.py:36
  322.6 1.9 reduce.18
  325.6 4.5 %all-to-all-start = ((bf16[8,2,12800]{2,1,0:T(2,128)(2,1)}), bf16[8,2,12800]{2,1,0:T(2,128)(2,1)S(1)}, u32[]{:S(2)}, u32[]{:S(2)}) async-start(bf16[8,2,12800]{2,1,0:T(2,128)(2,1)} %reshape.478), calls=%async_computation.1 | async-start | bytes 819200 | tf_op jit(solution)/shard_map/all_to_all | solution.py:37
  330.1 4.2 %fusion.74 = bf16[1,2,256,1280]{3,2,1,0:T(8,128)(2,1)} fusion(bf16[1,2,256,1280]{3,2,1,0:T(8,128)(2,1)S(1)} %copy-done.3, bf16[1,2,256,1280]{3,2,1,0:T(8,128)(2,1)} %copy-done.25, f32[1,2,256,1280]{3,2,1,0:T(8,128)} %copy-done.4, f32[2,256]{1,0:T(2,128)S(1)} %get-tuple-element.38, f32[2,256]{1,0:T(2,128)S(1)} %get-tuple-element.39, f32[1280]{0:T(1024)S(1)} %copy-done.34, ...), kind=kLoop, calls=%fused_computation.82 | loop fusion | flops 7208960 | bytes 6566912 | tf_op jit(solution)/shard_map/convert_element_type | solution.py:235
  334.9 3.3 all-to-all-done
  (144 shorter events, 40.9 us)
Async XLA Ops:
  7.2 37.4 %copy-start = (bf16[1280,640]{1,0:T(8,128)(2,1)S(1)}, bf16[1280,640]{1,0:T(8,128)(2,1)}, u32[]{:S(2)}) copy-start(bf16[1280,640]{1,0:T(8,128)(2,1)} %param.14) | copy-start | bytes 4915204
  7.2 14.5 %copy-start.3 = (bf16[1,2,256,1280]{3,2,1,0:T(8,128)(2,1)S(1)}, bf16[1,2,256,1280]{3,2,1,0:T(8,128)(2,1)}, u32[]{:S(2)}) copy-start(bf16[1,2,256,1280]{3,2,1,0:T(8,128)(2,1)} %param.10) | copy-start | bytes 3932164
  7.2 314.9 %reduce-scatter.2.cloned.1.call-start = ((), (), s32[]{:S(2)}) async-start(), calls=%async_computation.4 | async-start | bytes 6963200 | tf_op jit(solution)/shard_map/reduce_scatter | solution.py:36
  9.4 13.1 %copy-start.12 = (bf16[1280,640]{1,0:T(8,128)(2,1)S(1)}, bf16[1280,640]{1,0:T(8,128)(2,1)}, u32[]{:S(2)}) copy-start(bf16[1280,640]{1,0:T(8,128)(2,1)} %param.13) | copy-start | bytes 4915204
  9.4 13.1 %copy-start.34 = (f32[1280]{0:T(1024)S(1)}, f32[1280]{0:T(1024)}, u32[]{:S(2)}) copy-start(f32[1280]{0:T(1024)} %param.11) | copy-start | bytes 15364
  9.4 19.1 %collective-permute-start.6 = (bf16[1,256,1280]{2,1,0:T(8,128)(2,1)}, bf16[1,256,1280]{2,1,0:T(8,128)(2,1)S(1)}, u32[]{:S(2)}, u32[]{:S(2)}) collective-permute-start(bf16[1,256,1280]{2,1,0:T(8,128)(2,1)} %slice_bitcast_fusion.1), channel_id=1, source_target_pairs={{0,1},{8,9},{16,17},{24,25},{32,33},{40,41},{48,49},{56,57},{64,65... | collective-permute-start | bytes 1966088 | tf_op jit(solution)/shard_map/ppermute | solution.py:19
  13.0 29.4 %collective-permute-start.5 = (bf16[1,256,1280]{2,1,0:T(8,128)(2,1)}, bf16[1,256,1280]{2,1,0:T(8,128)(2,1)S(1)}, u32[]{:S(2)}, u32[]{:S(2)}) collective-permute-start(bf16[1,256,1280]{2,1,0:T(8,128)(2,1)} %slice_bitcast_fusion.1), channel_id=1, source_target_pairs={{0,2},{8,10},{16,18},{24,26},{32,34},{40,42},{48,50},{56,58},{64,6... | collective-permute-start | bytes 1966088 | tf_op jit(solution)/shard_map/ppermute | solution.py:19
  15.3 40.6 %collective-permute-start.4 = (bf16[1,256,1280]{2,1,0:T(8,128)(2,1)}, bf16[1,256,1280]{2,1,0:T(8,128)(2,1)}, u32[]{:S(2)}, u32[]{:S(2)}) collective-permute-start(bf16[1,256,1280]{2,1,0:T(8,128)(2,1)} %slice_bitcast_fusion.1), channel_id=1, source_target_pairs={{0,3},{8,11},{16,19},{24,27},{32,35},{40,43},{48,51},{56,59},{64,6... | collective-permute-start | bytes 1966088 | tf_op jit(solution)/shard_map/ppermute | solution.py:19
  17.4 39.8 %collective-permute-start.3 = (bf16[1,256,1280]{2,1,0:T(8,128)(2,1)}, bf16[1,256,1280]{2,1,0:T(8,128)(2,1)}, u32[]{:S(2)}, u32[]{:S(2)}) collective-permute-start(bf16[1,256,1280]{2,1,0:T(8,128)(2,1)} %slice_bitcast_fusion.1), channel_id=1, source_target_pairs={{0,4},{8,12},{16,20},{24,28},{32,36},{40,44},{48,52},{56,60},{64,6... | collective-permute-start | bytes 1966088 | tf_op jit(solution)/shard_map/ppermute | solution.py:19
  19.6 43.3 %collective-permute-start.2 = (bf16[1,256,1280]{2,1,0:T(8,128)(2,1)}, bf16[1,256,1280]{2,1,0:T(8,128)(2,1)}, u32[]{:S(2)}, u32[]{:S(2)}) collective-permute-start(bf16[1,256,1280]{2,1,0:T(8,128)(2,1)} %slice_bitcast_fusion.1), channel_id=1, source_target_pairs={{0,5},{8,13},{16,21},{24,29},{32,37},{40,45},{48,53},{56,61},{64,6... | collective-permute-start | bytes 1966088 | tf_op jit(solution)/shard_map/ppermute | solution.py:19
  22.5 2.2 copy-start.36
  28.4 18.3 %copy-start.30 = (bf16[1,256,1280]{2,1,0:T(8,128)(2,1)}, bf16[1,256,1280]{2,1,0:T(8,128)(2,1)S(1)}, u32[]{:S(2)}) copy-start(bf16[1,256,1280]{2,1,0:T(8,128)(2,1)S(1)} %collective-permute-done.6) | copy-start | bytes 1966084
  28.4 42.2 %collective-permute-start.1 = (bf16[1,256,1280]{2,1,0:T(8,128)(2,1)}, bf16[1,256,1280]{2,1,0:T(8,128)(2,1)}, u32[]{:S(2)}, u32[]{:S(2)}) collective-permute-start(bf16[1,256,1280]{2,1,0:T(8,128)(2,1)} %slice_bitcast_fusion.1), channel_id=1, source_target_pairs={{0,6},{8,14},{16,22},{24,30},{32,38},{40,46},{48,54},{56,62},{64,7... | collective-permute-start | bytes 1966088 | tf_op jit(solution)/shard_map/ppermute | solution.py:19
  42.5 4.3 %copy-start.32 = (bf16[1,256,1280]{2,1,0:T(8,128)(2,1)}, bf16[1,256,1280]{2,1,0:T(8,128)(2,1)S(1)}, u32[]{:S(2)}) copy-start(bf16[1,256,1280]{2,1,0:T(8,128)(2,1)S(1)} %collective-permute-done.5) | copy-start | bytes 1966084
  42.5 28.1 %collective-permute-start = (bf16[1,256,1280]{2,1,0:T(8,128)(2,1)}, bf16[1,256,1280]{2,1,0:T(8,128)(2,1)}, u32[]{:S(2)}, u32[]{:S(2)}) collective-permute-start(bf16[1,256,1280]{2,1,0:T(8,128)(2,1)} %slice_bitcast_fusion.1), channel_id=1, source_target_pairs={{0,7},{8,15},{16,23},{24,31},{32,39},{40,47},{48,55},{56,63},{64,7... | collective-permute-start | bytes 1966088 | tf_op jit(solution)/shard_map/ppermute | solution.py:19
  53.3 17.3 %copy-start.31 = (bf16[1,256,1280]{2,1,0:T(8,128)(2,1)S(1)}, bf16[1,256,1280]{2,1,0:T(8,128)(2,1)}, u32[]{:S(2)}) copy-start(bf16[1,256,1280]{2,1,0:T(8,128)(2,1)} %copy-done.30) | copy-start | bytes 1966084
  53.3 17.3 %copy-start.33 = (bf16[1,256,1280]{2,1,0:T(8,128)(2,1)S(1)}, bf16[1,256,1280]{2,1,0:T(8,128)(2,1)}, u32[]{:S(2)}) copy-start(bf16[1,256,1280]{2,1,0:T(8,128)(2,1)} %copy-done.32) | copy-start | bytes 1966084
  55.9 53.3 %collective-permute-start.9 = (bf16[1,1,256,1280]{3,2,1,0:T(8,128)(2,1)}, bf16[1,1,256,1280]{3,2,1,0:T(8,128)(2,1)}, u32[]{:S(2)}, u32[]{:S(2)}) collective-permute-start(bf16[1,1,256,1280]{3,2,1,0:T(8,128)(2,1)} %get-tuple-element.26), channel_id=1, source_target_pairs={{1,0},{2,1},{3,2},{4,3},{5,4},{6,5},{7,6},{9,8},{10,9},{11,10},{12... | collective-permute-start | bytes 1966088 | tf_op jit(solution)/shard_map/ppermute | solution.py:70
  57.2 14.6 %copy-start.13 = (bf16[1280,640]{1,0:T(8,128)(2,1)S(1)}, bf16[1280,640]{1,0:T(8,128)(2,1)}, u32[]{:S(2)}) copy-start(bf16[1280,640]{1,0:T(8,128)(2,1)} %param.13) | copy-start | bytes 4915204
  57.2 52.0 %collective-permute-start.10 = (bf16[1,1,256,1280]{3,2,1,0:T(8,128)(2,1)}, bf16[1,1,256,1280]{3,2,1,0:T(8,128)(2,1)}, u32[]{:S(2)}, u32[]{:S(2)}) collective-permute-start(bf16[1,1,256,1280]{3,2,1,0:T(8,128)(2,1)} %get-tuple-element.27), channel_id=1, source_target_pairs={{0,1},{1,2},{2,3},{3,4},{4,5},{5,6},{6,7},{8,9},{9,10},{10,11},{11... | collective-permute-start | bytes 1966088 | tf_op jit(solution)/shard_map/ppermute | solution.py:69
  71.5 1.1 copy-start.5
  77.2 0.9 copy-start.19
  99.0 4.9 %copy-start.17 = (bf16[2,256,640]{1,2,0:T(8,128)(2,1)S(1)}, bf16[2,256,640]{1,2,0:T(8,128)(2,1)}, u32[]{:S(2)}) copy-start(bf16[2,256,640]{1,2,0:T(8,128)(2,1)} %copy.66) | copy-start | bytes 1966084
  103.8 2.4 copy-start.1
  103.9 2.7 copy-start.35
  106.2 3.0 copy-start.28
  106.6 2.6 copy-start.20
  109.2 2.1 copy-start.37
  121.3 1.1 copy-start.25
  130.4 2.0 copy-start.26
  130.4 2.0 copy-start.29
  132.4 2.3 copy-start.16
  132.4 2.3 copy-start.18
  156.4 5.6 %copy-start.2 = (bf16[1,2,10,256,512]{4,3,2,1,0:T(8,128)(2,1)S(1)}, bf16[1,2,10,256,512]{4,3,2,1,0:T(8,128)(2,1)}, u32[]{:S(2)}) copy-start(bf16[1,2,10,256,512]{4,3,2,1,0:T(8,128)(2,1)} %fusion.83) | copy-start | bytes 15728644
  156.4 5.6 %copy-start.15 = (bf16[2,256,640]{1,2,0:T(8,128)(2,1)S(1)}, bf16[2,256,640]{1,2,0:T(8,128)(2,1)}, u32[]{:S(2)}) copy-start(bf16[2,256,640]{1,2,0:T(8,128)(2,1)} %copy.68) | copy-start | bytes 1966084
  171.0 2.6 copy-start.6
  171.0 2.6 copy-start.8
  191.4 2.6 copy-start.7
  191.4 2.6 copy-start.10
  207.4 8.1 %copy-start.27 = (bf16[2,10,64,256]{3,2,1,0:T(8,128)(2,1)S(1)}, bf16[2,10,64,256]{3,2,1,0:T(8,128)(2,1)}, u32[]{:S(2)}) copy-start(bf16[2,10,64,256]{3,2,1,0:T(8,128)(2,1)} %fusion.116) | copy-start | bytes 1966084
  208.8 9.4 %copy-start.14 = (bf16[1280,640]{1,0:T(8,128)(2,1)S(1)}, bf16[1280,640]{1,0:T(8,128)(2,1)}, u32[]{:S(2)}) copy-start(bf16[1280,640]{1,0:T(8,128)(2,1)} %param.13) | copy-start | bytes 4915204
  208.8 9.4 %copy-start.24 = (bf16[1,2,256,640]{3,2,1,0:T(8,128)(2,1)S(1)}, bf16[1,2,256,640]{3,2,1,0:T(8,128)(2,1)}, u32[]{:S(2)}) copy-start(bf16[1,2,256,640]{3,2,1,0:T(8,128)(2,1)} %copy.91) | copy-start | bytes 1966084
  208.9 46.8 %collective-permute-start.17 = (bf16[1,256,1280]{1,2,0:T(8,128)(2,1)S(1)}, bf16[1,256,1280]{1,2,0:T(8,128)(2,1)S(1)}, u32[]{:S(2)}, u32[]{:S(2)}) collective-permute-start(bf16[1,256,1280]{1,2,0:T(8,128)(2,1)S(1)} %fusion.136), channel_id=1, source_target_pairs={{7,0},{15,8},{23,16},{31,24},{39,32},{47,40},{55,48},{63,56},{71,6... | collective-permute-start | bytes 1966088 | tf_op jit(solution)/shard_map/ppermute | solution.py:27
  210.3 46.7 %collective-permute-start.16 = (bf16[1,256,1280]{1,2,0:T(8,128)(2,1)S(1)}, bf16[1,256,1280]{1,2,0:T(8,128)(2,1)S(1)}, u32[]{:S(2)}, u32[]{:S(2)}) collective-permute-start(bf16[1,256,1280]{1,2,0:T(8,128)(2,1)S(1)} %fusion.136), channel_id=1, source_target_pairs={{6,0},{14,8},{22,16},{30,24},{38,32},{46,40},{54,48},{62,56},{70,6... | collective-permute-start | bytes 1966088 | tf_op jit(solution)/shard_map/ppermute | solution.py:27
  211.6 50.5 %collective-permute-start.15 = (bf16[1,256,1280]{1,2,0:T(8,128)(2,1)S(1)}, bf16[1,256,1280]{1,2,0:T(8,128)(2,1)S(1)}, u32[]{:S(2)}, u32[]{:S(2)}) collective-permute-start(bf16[1,256,1280]{1,2,0:T(8,128)(2,1)S(1)} %fusion.136), channel_id=1, source_target_pairs={{5,0},{13,8},{21,16},{29,24},{37,32},{45,40},{53,48},{61,56},{69,6... | collective-permute-start | bytes 1966088 | tf_op jit(solution)/shard_map/ppermute | solution.py:27
  212.9 70.8 %collective-permute-start.14 = (bf16[1,256,1280]{1,2,0:T(8,128)(2,1)S(1)}, bf16[1,256,1280]{1,2,0:T(8,128)(2,1)S(1)}, u32[]{:S(2)}, u32[]{:S(2)}) collective-permute-start(bf16[1,256,1280]{1,2,0:T(8,128)(2,1)S(1)} %fusion.136), channel_id=1, source_target_pairs={{4,0},{12,8},{20,16},{28,24},{36,32},{44,40},{52,48},{60,56},{68,6... | collective-permute-start | bytes 1966088 | tf_op jit(solution)/shard_map/ppermute | solution.py:27
  214.2 71.0 %collective-permute-start.13 = (bf16[1,256,1280]{1,2,0:T(8,128)(2,1)S(1)}, bf16[1,256,1280]{1,2,0:T(8,128)(2,1)S(1)}, u32[]{:S(2)}, u32[]{:S(2)}) collective-permute-start(bf16[1,256,1280]{1,2,0:T(8,128)(2,1)S(1)} %fusion.136), channel_id=1, source_target_pairs={{3,0},{11,8},{19,16},{27,24},{35,32},{43,40},{51,48},{59,56},{67,6... | collective-permute-start | bytes 1966088 | tf_op jit(solution)/shard_map/ppermute | solution.py:27
  218.2 40.1 %copy-start.23 = (bf16[1,2,256,640]{3,2,1,0:T(8,128)(2,1)S(1)}, bf16[1,2,256,640]{3,2,1,0:T(8,128)(2,1)}, u32[]{:S(2)}) copy-start(bf16[1,2,256,640]{3,2,1,0:T(8,128)(2,1)} %copy.92) | copy-start | bytes 1966084
  255.7 29.5 %collective-permute-start.12 = (bf16[1,256,1280]{1,2,0:T(8,128)(2,1)S(1)}, bf16[1,256,1280]{1,2,0:T(8,128)(2,1)S(1)}, u32[]{:S(2)}, u32[]{:S(2)}) collective-permute-start(bf16[1,256,1280]{1,2,0:T(8,128)(2,1)S(1)} %fusion.136), channel_id=1, source_target_pairs={{2,0},{10,8},{18,16},{26,24},{34,32},{42,40},{50,48},{58,56},{66,6... | collective-permute-start | bytes 1966088 | tf_op jit(solution)/shard_map/ppermute | solution.py:27
  257.0 28.2 %collective-permute-start.11 = (bf16[1,256,1280]{1,2,0:T(8,128)(2,1)S(1)}, bf16[1,256,1280]{1,2,0:T(8,128)(2,1)S(1)}, u32[]{:S(2)}, u32[]{:S(2)}) collective-permute-start(bf16[1,256,1280]{1,2,0:T(8,128)(2,1)S(1)} %fusion.136), channel_id=1, source_target_pairs={{1,0},{9,8},{17,16},{25,24},{33,32},{41,40},{49,48},{57,56},{65,64... | collective-permute-start | bytes 1966088 | tf_op jit(solution)/shard_map/ppermute | solution.py:27
  259.6 1.3 copy-start.21
  259.8 25.4 %copy-start.9 = (f32[256,640]{0,1:T(8,128)S(1)}, f32[256,640]{0,1:T(8,128)}, u32[]{:S(2)}) copy-start(f32[256,640]{0,1:T(8,128)} %slice_reduce_fusion) | copy-start | bytes 1966084
  259.8 25.4 %copy-start.11 = (f32[256,640]{0,1:T(8,128)S(1)}, f32[256,640]{0,1:T(8,128)}, u32[]{:S(2)}) copy-start(f32[256,640]{0,1:T(8,128)} %slice_reduce_fusion.1) | copy-start | bytes 1966084
  262.0 37.3 %collective-permute-start.7 = (bf16[1,1,256,1280]{3,2,1,0:T(8,128)(2,1)}, bf16[1,1,256,1280]{3,2,1,0:T(8,128)(2,1)}, u32[]{:S(2)}, u32[]{:S(2)}) collective-permute-start(bf16[1,1,256,1280]{3,2,1,0:T(8,128)(2,1)} %get-tuple-element.30), channel_id=1, source_target_pairs={{0,1},{1,2},{2,3},{3,4},{4,5},{5,6},{6,7},{8,9},{9,10},{10,11},{11... | collective-permute-start | bytes 1966088 | tf_op jit(solution)/shard_map/ppermute | solution.py:69
  283.7 18.7 %collective-permute-start.8 = (bf16[1,1,256,1280]{3,2,1,0:T(8,128)(2,1)}, bf16[1,1,256,1280]{3,2,1,0:T(8,128)(2,1)}, u32[]{:S(2)}, u32[]{:S(2)}) collective-permute-start(bf16[1,1,256,1280]{3,2,1,0:T(8,128)(2,1)} %get-tuple-element.31), channel_id=1, source_target_pairs={{1,0},{2,1},{3,2},{4,3},{5,4},{6,5},{7,6},{9,8},{10,9},{11,10},{12... | collective-permute-start | bytes 1966088 | tf_op jit(solution)/shard_map/ppermute | solution.py:70
  288.9 1.6 copy-start.4
  291.2 23.4 %all-to-all-start.1 = ((f32[16,8,10]{2,1,0:T(8,128)}), f32[16,8,10]{2,1,0:T(8,128)S(1)}, u32[]{:S(2)}, u32[]{:S(2)}) async-start(f32[16,8,10]{2,1,0:T(8,128)} %reshape.466), calls=%async_computation.2 | async-start | bytes 131072 | tf_op jit(solution)/shard_map/all_to_all | solution.py:49
  299.3 5.0 %copy-start.22 = (bf16[1,2,256,1280]{3,2,1,0:T(8,128)(2,1)S(1)}, bf16[1,2,256,1280]{3,2,1,0:T(8,128)(2,1)}, u32[]{:S(2)}) copy-start(bf16[1,2,256,1280]{3,2,1,0:T(8,128)(2,1)} %get-tuple-element.36) | copy-start | bytes 3932164
  299.3 5.0 %copy-start.38 = (bf16[1,2,256,1280]{3,2,1,0:T(8,128)(2,1)S(1)}, bf16[1,2,256,1280]{3,2,1,0:T(8,128)(2,1)}, u32[]{:S(2)}) copy-start(bf16[1,2,256,1280]{3,2,1,0:T(8,128)(2,1)} %copy-done.37) | copy-start | bytes 3932164
  315.2 10.4 %all-to-all-start.2 = ((f32[8,1,10]{2,1,0:T(1,128)}), f32[8,1,10]{2,1,0:T(1,128)S(1)}, u32[]{:S(2)}, u32[]{:S(2)}) async-start(f32[8,1,10]{2,1,0:T(1,128)} %bitcast.74), calls=%async_computation.3 | async-start | bytes 8192 | tf_op jit(solution)/shard_map/all_to_all | solution.py:50
  325.6 12.6 %all-to-all-start = ((bf16[8,2,12800]{2,1,0:T(2,128)(2,1)}), bf16[8,2,12800]{2,1,0:T(2,128)(2,1)S(1)}, u32[]{:S(2)}, u32[]{:S(2)}) async-start(bf16[8,2,12800]{2,1,0:T(2,128)(2,1)} %reshape.478), calls=%async_computation.1 | async-start | bytes 819200 | tf_op jit(solution)/shard_map/all_to_all | solution.py:37
Sparse Core Ops, SparseCore 0:
  207.5 114.5 reduce-scatter.1

commit v10 on v9

--- a/solution.py
+++ b/solution.py
@@ -214,17 +214,20 @@
     first_sum = to_owner(jnp.concatenate([key_first_grad, val_first_grad], axis=-1), "tm")
     width = key_first_grad.shape[-1]
 
+    first_flat = normed_first.reshape(-1, normed_first.shape[-1])
+    extra_key = split_dot(key_first_grad.reshape(-1, width), first_flat, (((0,), (0,)), ((), ()))).T
+    extra_val = split_dot(val_first_grad.reshape(-1, width), first_flat, (((0,), (0,)), ((), ()))).T
+    grad_wq = gram_rows(normed, grad_queries)
+    grad_wk = gram_rows(normed, key_b) + extra_key
+    grad_wv = gram_rows(normed, val_b) + extra_val
+    grad_wq, grad_wk, grad_wv, grad_out, first_sum = lax.optimization_barrier(
+        (grad_wq, grad_wk, grad_wv, grad_out, first_sum)
+    )
     dims = (((2,), (1,)), ((), ()))
     first_rows = split_dot(first_sum[..., :width], w_key, dims)
     first_rows = first_rows + split_dot(first_sum[..., width:], w_value, dims)
     first_rows = jnp.where(is_owner, first_rows, jnp.zeros_like(first_rows))
-    first_flat = normed_first.reshape(-1, normed_first.shape[-1])
-    extra_key = split_dot(key_first_grad.reshape(-1, width), first_flat, (((0,), (0,)), ((), ()))).T
-    extra_val = split_dot(val_first_grad.reshape(-1, width), first_flat, (((0,), (0,)), ((), ()))).T
     grad_normed = grad_normed.at[:, 0].add(first_rows)
-    grad_wq = gram_rows(normed, grad_queries)
-    grad_wk = gram_rows(normed, key_b) + extra_key
-    grad_wv = gram_rows(normed, val_b) + extra_val
     grad_gain = jnp.sum(grad_normed * x_hat, axis=(0, 1, 2))
     grad_hat = grad_normed * norm_gain
     grad_x = inv_std * (

time: 355 us -> 381 us (1.073)
  waiting for transfers between devices: 83.4 us -> 105 us
    reduce_scatter x1, waiting for transfers between devices: 3.54 us -> 49 us  [scatter_sum(): share = lax.psum_scatter(share, outer, scatter_dimension=0, tiled=True)[0]]
    ppermute x7, waiting for transfers between devices: 52.4 us -> 31.4 us  [to_owner(): got = lax.ppermute(block.astype(jnp.bfloat16), axis, [(source, 0)])]
    unnamed x83 -> x93, local copies, waits for them, and re-layouts: 10.4 us -> 12 us
  transfers between devices with their start and end apart: 22 -> 22, of which waited for: 8 -> 8; matrix products, arithmetic and copies ran while one was open for 25% -> 29% of each run, Pallas kernels for 0% -> 0%
where the time goes in v10:
time: 381 us; the launch traced here: 375 us
  waiting for transfers between devices  105 us (28%)
  matrix products  85.1 us (22%)
  other arithmetic  62.7 us (16%)
  local copies, waits for them, and re-layouts  54.1 us (14%)
  starting transfers between devices  53.2 us (14%)
  between operations  15 us (4%)
    reduce_scatter x1, waiting for transfers between devices, scatter_sum(): share = lax.psum_scatter(share, outer, scatter_dimension=0, tiled=True)[0]  49 us
    ppermute x7, waiting for transfers between devices, to_owner(): got = lax.ppermute(block.astype(jnp.bfloat16), axis, [(source, 0)])  31.4 us
    ppermute x7, waiting for transfers between devices, from_owner(): got = lax.ppermute(block, axis, [(0, target)])  21.2 us
    concatenate x4, local copies, waits for them, and re-layouts, scatter_sum(): jnp.concatenate([p.astype(jnp.bfloat16).reshape(count, -1) for p in parts...  17.1 us
    ppermute x7, starting transfers between devices, from_owner(): got = lax.ppermute(block, axis, [(0, target)])  16.6 us
    sub x1, other arithmetic, attend_back(): grad_prob - centre  16.3 us
    div x1, other arithmetic, attend(): prob_f32 = expd / jnp.sum(expd, axis=-1, keepdims=True)  14.3 us
    dot_general x8, matrix products, split_dot(): lax.dot_general(part, narrow, dims, preferred_element_type=jnp.float32)  12.3 us
  transfers between devices with their start and end apart: 22, of which 8 were waited for; matrix products, arithmetic and copies ran while one was open for 29% of the time, Pallas kernels for 0%

profile of v10, /device:TPU:0, one launch (start us, length us, event | category | flops | bytes accessed | tf_op | source)
XLA Modules:
  0.0 375.1 jit_solution(18338386183836983775)
XLA Ops:
  7.2 2.1 slice_bitcast_fusion.1
  9.4 3.7 collective-permute-start.6
  13.0 2.2 collective-permute-start.5
  15.3 2.2 collective-permute-start.4
  17.4 2.1 collective-permute-start.3
  19.6 2.2 collective-permute-start.2
  22.5 2.2 fusion.103
  24.7 2.1 fusion.100
  26.8 1.6 collective-permute-done.6
  28.4 2.1 collective-permute-start.1
  30.5 11.9 %collective-permute-done.5 = bf16[1,256,1280]{2,1,0:T(8,128)(2,1)S(1)} collective-permute-done((bf16[1,256,1280]{2,1,0:T(8,128)(2,1)}, bf16[1,256,1280]{2,1,0:T(8,128)(2,1)S(1)}, u32[]{:S(2)}, u32[]{:S(2)}) %collective-permute-start.5) | collective-permute-done | bytes 655392 | tf_op jit(solution)/shard_map/ppermute | solution.py:19
  42.5 2.1 collective-permute-start
  44.6 2.2 fusion.97
  46.7 2.2 copy.69
  48.9 2.2 copy.68
  51.1 2.2 copy.66
  53.3 2.6 fusion.175
  57.2 5.7 %collective-permute-start.10 = (bf16[1,1,256,1280]{3,2,1,0:T(8,128)(2,1)}, bf16[1,1,256,1280]{3,2,1,0:T(8,128)(2,1)}, u32[]{:S(2)}, u32[]{:S(2)}) collective-permute-start(bf16[1,1,256,1280]{3,2,1,0:T(8,128)(2,1)} %get-tuple-element.37), channel_id=1, source_target_pairs={{0,1},{1,2},{2,3},{3,4},{4,5},{5,6},{6,7},{8,9},{9,10},{10,11},{11... | collective-permute-start | bytes 1966088 | tf_op jit(solution)/shard_map/ppermute | solution.py:69
  62.9 7.7 %collective-permute-done.1 = bf16[1,256,1280]{2,1,0:T(8,128)(2,1)} collective-permute-done((bf16[1,256,1280]{2,1,0:T(8,128)(2,1)}, bf16[1,256,1280]{2,1,0:T(8,128)(2,1)}, u32[]{:S(2)}, u32[]{:S(2)}) %collective-permute-start.1) | collective-permute-done | bytes 655392 | tf_op jit(solution)/shard_map/ppermute | solution.py:19
  78.1 6.7 %fusion.131 = f32[2,10,256,512]{3,2,1,0:T(8,128)} fusion(bf16[2,256,10,64]{1,3,2,0:T(8,128)(2,1)} %bitcast.250, bf16[1,2,256,10,64]{2,4,3,1,0:T(8,128)(2,1)S(1)} %broadcast_in_dim.15, bf16[1,2,256,10,64]{2,4,3,1,0:T(8,128)(2,1)} %bitcast.254), kind=kOutput, calls=%fused_computation.141 | convolution fusion | flops 338165760 | bytes 12451840 | tf_op jit(solution)/shard_map/lfshd,lfthd->lfhst/dot_general | solution.py:99
  84.8 14.3 %fusion.22 = f32[2,10,256,512]{3,2,1,0:T(8,128)} fusion(f32[2,10,256,512]{3,2,1,0:T(8,128)} %fusion.131), kind=kOutput, calls=%fused_computation.24 | output fusion | flops 10497022 | bytes 20971520 | tf_op jit(solution)/shard_map/div | solution.py:107
  99.1 4.8 %convert_bitcast_fusion = bf16[1,2,10,256,512]{4,3,2,1,0:T(8,128)(2,1)S(1)} fusion(f32[2,10,256,512]{3,2,1,0:T(8,128)} %fusion.22), kind=kLoop, calls=%fused_computation.22 | loop fusion | flops 2621440 | bytes 15728640 | tf_op jit(solution)/shard_map/convert_element_type | solution.py:108
  104.0 1.7 fusion.109
  106.6 2.6 fusion.76
  109.2 2.0 fusion.120
  111.3 9.8 %fusion.57 = bf16[1,2,256,1280]{3,2,1,0:T(8,128)(2,1)S(1)} fusion(bf16[1280,3,1280]{2,0,1:T(8,128)(2,1)} %param.16, bf16[1,2,256,1,1280]{4,2,3,1,0:T(8,128)(2,1)S(1)} %get-tuple-element.35, bf16[1,2,256,1,1280]{4,2,3,1,0:T(8,128)(2,1)S(1)} %bitcast.258, bf16[1,2,256,1,1280]{4,2,3,1,0:T(8,128)(2,1)S(1)} %get-tuple-element.34, ...), kind=kOutput, calls=%fused_computation.65 | convolution fusion | flops 5044961280 | bytes 17694720 | tf_op jit(solution)/shard_map/lfsjo,cjo->lfsc/dot_general | solution.py:192
  122.2 2.1 fusion.106
  124.2 2.2 copy.72
  126.5 3.7 fusion.17
  132.7 5.4 %fusion.125 = f32[2,10,256,512]{3,2,1,0:T(8,128)} fusion(bf16[2,256,10,64]{1,3,2,0:T(8,128)(2,1)S(1)} %bitcast.253, bf16[2,256,10,64]{1,3,2,0:T(8,128)(2,1)S(1)} %broadcast_in_dim.16, bf16[2,256,10,64]{1,3,2,0:T(8,128)(2,1)S(1)} %bitcast.257), kind=kOutput, calls=%fused_computation.131 | convolution fusion | flops 338165760 | bytes 12451840 | tf_op jit(solution)/shard_map/lfshd,lfthd->lfhst/dot_general | solution.py:118
  138.1 16.3 %fusion.79 = bf16[1,2,10,256,512]{4,3,2,1,0:T(8,128)(2,1)} fusion(f32[2,10,256,512]{3,2,1,0:T(8,128)} %fusion.22, f32[2,10,256,512]{3,2,1,0:T(8,128)} %fusion.125), kind=kOutput, calls=%fused_computation.87 | output fusion | flops 13112831 | bytes 26214400 | tf_op jit(solution)/shard_map/sub | solution.py:122
  154.4 5.6 %fusion.112 = bf16[2,10,64,256]{3,2,1,0:T(8,128)(2,1)} fusion(bf16[1,2,10,256,512]{4,3,2,1,0:T(8,128)(2,1)} %fusion.79, bf16[1,2,256,10,64]{2,4,3,1,0:T(8,128)(2,1)} %copy-done.22, bf16[1,2,256,10,64]{2,4,3,1,0:T(8,128)(2,1)} %bitcast.255), kind=kOutput, calls=%fused_computation.111 | convolution fusion | flops 338493440 | bytes 7208960 | tf_op jit(solution)/shard_map/lfhst,lfthd->lfshd/dot_general | solution.py:124
  162.8 2.5 fusion.151
  171.4 1.7 collective-permute-start.13
  173.1 2.6 fusion.154
  175.7 2.2 copy.92
  177.9 4.2 %convolution_bitcast_fusion.1 = f32[1280,640]{1,0:T(8,128)} fusion(bf16[1,2,256,640]{3,2,1,0:T(8,128)(2,1)} %copy.92, bf16[1,2,256,1280]{3,2,1,0:T(8,128)(2,1)S(1)} %copy-done.3, f32[1280]{0:T(1024)S(1)} %copy-done.38, f32[2,256]{1,0:T(2,128)S(1)} %add_rsqrt_fusion, f32[2,256]{1,0:T(2,128)S(1)} %broadcast_multiply_fusion.2), kind=kOutput, calls=%fused_computation.47 | convolution fusion | flops 842137600 | bytes 5252096 | tf_op jit(solution)/shard_map/dot_general | solution.py:147
  182.1 2.2 copy.91
  184.3 2.6 convolution_bitcast_fusion.2
  187.0 2.6 convolution_bitcast_fusion.3
  189.6 2.1 fusion.31
  191.7 21.5 %collective-permute-done.17 = bf16[1,256,1280]{1,2,0:T(8,128)(2,1)} collective-permute-done((bf16[1,256,1280]{1,2,0:T(8,128)(2,1)}, bf16[1,256,1280]{1,2,0:T(8,128)(2,1)}, u32[]{:S(2)}, u32[]{:S(2)}) %collective-permute-start.17) | collective-permute-done | bytes 655392 | tf_op jit(solution)/shard_map/ppermute | solution.py:27
  216.0 2.2 convolution_bitcast_fusion
  218.2 2.1 fusion.32
  220.3 6.9 %collective-permute-done.14 = bf16[1,256,1280]{1,2,0:T(8,128)(2,1)} collective-permute-done((bf16[1,256,1280]{1,2,0:T(8,128)(2,1)}, bf16[1,256,1280]{1,2,0:T(8,128)(2,1)}, u32[]{:S(2)}, u32[]{:S(2)}) %collective-permute-start.14) | collective-permute-done | bytes 655392 | tf_op jit(solution)/shard_map/ppermute | solution.py:27
  227.2 3.0 collective-permute-done.12
  230.2 3.7 convert_add_fusion.2
  233.9 4.4 %concatenate.67 = bf16[16,8,6400]{2,1,0:T(8,128)(2,1)} reshape(bf16[1280,640]{1,0:T(8,128)(2,1)} %convolution_bitcast_fusion.3) | data formatting | bytes 3276800 | tf_op jit(solution)/shard_map/concatenate | solution.py:34
  238.3 4.4 %concatenate.68 = bf16[16,8,6400]{2,1,0:T(8,128)(2,1)} reshape(bf16[1280,640]{1,0:T(8,128)(2,1)} %fusion.32) | data formatting | bytes 3276800 | tf_op jit(solution)/shard_map/concatenate | solution.py:34
  242.7 4.4 %concatenate.69 = bf16[16,8,6400]{2,1,0:T(8,128)(2,1)} reshape(bf16[1280,640]{1,0:T(8,128)(2,1)} %fusion.31) | data formatting | bytes 3276800 | tf_op jit(solution)/shard_map/concatenate | solution.py:34
  247.0 4.0 %concatenate.70 = bf16[16,8,6400]{2,1,0:T(8,128)(2,1)} reshape(bf16[640,1280]{1,0:T(8,128)(2,1)} %convolution_bitcast_fusion) | data formatting | bytes 3276800 | tf_op jit(solution)/shard_map/concatenate | solution.py:34
  251.0 6.0 %pad_maximum_fusion = bf16[16,8,25600]{2,1,0:T(8,128)(2,1)} fusion(bf16[16,8,6400]{2,1,0:T(8,128)(2,1)} %concatenate.70, bf16[16,8,6400]{2,1,0:T(8,128)(2,1)} %concatenate.69, bf16[16,8,6400]{2,1,0:T(8,128)(2,1)} %concatenate.68, bf16[16,8,6400]{2,1,0:T(8,128)(2,1)} %concatenate.67), kind=kLoop, calls=%fused_computation.13 | loop fusion | flops 26214400 | bytes 13107200 | tf_op jit(solution)/shard_map/concatenate | solution.py:34
  257.0 2.6 fusion.176
  259.6 2.2 collective-permute-start.7
  261.8 1.6 collective-permute-start.8
  274.0 8.0 %all-to-all-start.1 = ((f32[16,8,10]{2,1,0:T(8,128)}), f32[16,8,10]{2,1,0:T(8,128)S(1)}, u32[]{:S(2)}, u32[]{:S(2)}) async-start(f32[16,8,10]{2,1,0:T(8,128)} %reshape.466), calls=%async_computation.2 | async-start | bytes 131072 | tf_op jit(solution)/shard_map/all_to_all | solution.py:49
  282.1 2.1 fusion.122
  284.6 10.1 %fusion.54 = bf16[1,2,256,1280]{3,2,1,0:T(8,128)(2,1)} fusion(bf16[1280,3,1280]{2,0,1:T(8,128)(2,1)} %param.16, bf16[1,2,256,1,1280]{4,2,1,3,0:T(8,128)(2,1)S(1)} %get-tuple-element.39, bf16[1,2,256,1,1280]{4,2,1,3,0:T(8,128)(2,1)S(1)} %bitcast.259, bf16[1,2,256,1,1280]{4,2,1,3,0:T(8,128)(2,1)S(1)} %get-tuple-element.38, ...), kind=kOutput, calls=%fused_computation.64 | convolution fusion | flops 5039063040 | bytes 16384000 | tf_op jit(solution)/shard_map/lfsjc,cjo->lfso/dot_general | solution.py:187
  295.3 3.9 %all-to-all-start.2 = ((f32[8,1,10]{2,1,0:T(1,128)}), f32[8,1,10]{2,1,0:T(1,128)S(1)}, u32[]{:S(2)}, u32[]{:S(2)}) async-start(f32[8,1,10]{2,1,0:T(1,128)} %bitcast.74), calls=%async_computation.3 | async-start | bytes 8192 | tf_op jit(solution)/shard_map/all_to_all | solution.py:50
  299.2 49.0 %reduce-scatter.2.cloned.1.call-done = bf16[1,8,25600]{2,1,0:T(8,128)(2,1)} async-done(((bf16[16,8,25600]{2,1,0:T(8,128)(2,1)}), bf16[1,8,25600]{2,1,0:T(8,128)(2,1)}) %reduce-scatter.2.cloned.1.call-update) | async-done | bytes 409616 | tf_op jit(solution)/shard_map/reduce_scatter | solution.py:36
  348.7 1.9 reduce.18
  351.7 4.3 %all-to-all-start = ((bf16[8,2,12800]{2,1,0:T(2,128)(2,1)}), bf16[8,2,12800]{2,1,0:T(2,128)(2,1)S(1)}, u32[]{:S(2)}, u32[]{:S(2)}) async-start(bf16[8,2,12800]{2,1,0:T(2,128)(2,1)} %reshape.478), calls=%async_computation.1 | async-start | bytes 819200 | tf_op jit(solution)/shard_map/all_to_all | solution.py:37
  356.0 4.2 %fusion.70 = bf16[1,2,256,1280]{3,2,1,0:T(8,128)(2,1)} fusion(bf16[1,2,256,1280]{3,2,1,0:T(8,128)(2,1)S(1)} %copy-done.3, bf16[1,2,256,1280]{3,2,1,0:T(8,128)(2,1)} %copy-done.28, f32[1,2,256,1280]{3,2,1,0:T(8,128)} %copy-done.4, f32[2,256]{1,0:T(2,128)S(1)} %get-tuple-element.48, f32[2,256]{1,0:T(2,128)S(1)} %get-tuple-element.49, f32[1280]{0:T(1024)S(1)} %copy-done.38, ...), kind=kLoop, calls=%fused_computation.78 | loop fusion | flops 7208960 | bytes 6566912 | tf_op jit(solution)/shard_map/convert_element_type | solution.py:238
  360.8 3.3 all-to-all-done
  (154 shorter events, 43.2 us)
Async XLA Ops:
  7.2 37.4 %copy-start = (bf16[1280,640]{1,0:T(8,128)(2,1)S(1)}, bf16[1280,640]{1,0:T(8,128)(2,1)}, u32[]{:S(2)}) copy-start(bf16[1280,640]{1,0:T(8,128)(2,1)} %param.14) | copy-start | bytes 4915204
  7.2 14.6 %copy-start.3 = (bf16[1,2,256,1280]{3,2,1,0:T(8,128)(2,1)S(1)}, bf16[1,2,256,1280]{3,2,1,0:T(8,128)(2,1)}, u32[]{:S(2)}) copy-start(bf16[1,2,256,1280]{3,2,1,0:T(8,128)(2,1)} %param.10) | copy-start | bytes 3932164
  7.2 341.0 %reduce-scatter.2.cloned.1.call-start = ((), (), s32[]{:S(2)}) async-start(), calls=%async_computation.4 | async-start | bytes 6963200 | tf_op jit(solution)/shard_map/reduce_scatter | solution.py:36
  9.4 13.1 %copy-start.12 = (bf16[1280,640]{1,0:T(8,128)(2,1)S(1)}, bf16[1280,640]{1,0:T(8,128)(2,1)}, u32[]{:S(2)}) copy-start(bf16[1280,640]{1,0:T(8,128)(2,1)} %param.13) | copy-start | bytes 4915204
  9.4 13.1 %copy-start.38 = (f32[1280]{0:T(1024)S(1)}, f32[1280]{0:T(1024)}, u32[]{:S(2)}) copy-start(f32[1280]{0:T(1024)} %param.11) | copy-start | bytes 15364
  9.4 19.1 %collective-permute-start.6 = (bf16[1,256,1280]{2,1,0:T(8,128)(2,1)}, bf16[1,256,1280]{2,1,0:T(8,128)(2,1)S(1)}, u32[]{:S(2)}, u32[]{:S(2)}) collective-permute-start(bf16[1,256,1280]{2,1,0:T(8,128)(2,1)} %slice_bitcast_fusion.1), channel_id=1, source_target_pairs={{0,1},{8,9},{16,17},{24,25},{32,33},{40,41},{48,49},{56,57},{64,65... | collective-permute-start | bytes 1966088 | tf_op jit(solution)/shard_map/ppermute | solution.py:19
  13.0 29.4 %collective-permute-start.5 = (bf16[1,256,1280]{2,1,0:T(8,128)(2,1)}, bf16[1,256,1280]{2,1,0:T(8,128)(2,1)S(1)}, u32[]{:S(2)}, u32[]{:S(2)}) collective-permute-start(bf16[1,256,1280]{2,1,0:T(8,128)(2,1)} %slice_bitcast_fusion.1), channel_id=1, source_target_pairs={{0,2},{8,10},{16,18},{24,26},{32,34},{40,42},{48,50},{56,58},{64,6... | collective-permute-start | bytes 1966088 | tf_op jit(solution)/shard_map/ppermute | solution.py:19
  15.3 40.6 %collective-permute-start.4 = (bf16[1,256,1280]{2,1,0:T(8,128)(2,1)}, bf16[1,256,1280]{2,1,0:T(8,128)(2,1)}, u32[]{:S(2)}, u32[]{:S(2)}) collective-permute-start(bf16[1,256,1280]{2,1,0:T(8,128)(2,1)} %slice_bitcast_fusion.1), channel_id=1, source_target_pairs={{0,3},{8,11},{16,19},{24,27},{32,35},{40,43},{48,51},{56,59},{64,6... | collective-permute-start | bytes 1966088 | tf_op jit(solution)/shard_map/ppermute | solution.py:19
  17.4 39.8 %collective-permute-start.3 = (bf16[1,256,1280]{2,1,0:T(8,128)(2,1)}, bf16[1,256,1280]{2,1,0:T(8,128)(2,1)}, u32[]{:S(2)}, u32[]{:S(2)}) collective-permute-start(bf16[1,256,1280]{2,1,0:T(8,128)(2,1)} %slice_bitcast_fusion.1), channel_id=1, source_target_pairs={{0,4},{8,12},{16,20},{24,28},{32,36},{40,44},{48,52},{56,60},{64,6... | collective-permute-start | bytes 1966088 | tf_op jit(solution)/shard_map/ppermute | solution.py:19
  19.6 43.3 %collective-permute-start.2 = (bf16[1,256,1280]{2,1,0:T(8,128)(2,1)}, bf16[1,256,1280]{2,1,0:T(8,128)(2,1)}, u32[]{:S(2)}, u32[]{:S(2)}) collective-permute-start(bf16[1,256,1280]{2,1,0:T(8,128)(2,1)} %slice_bitcast_fusion.1), channel_id=1, source_target_pairs={{0,5},{8,13},{16,21},{24,29},{32,37},{40,45},{48,53},{56,61},{64,6... | collective-permute-start | bytes 1966088 | tf_op jit(solution)/shard_map/ppermute | solution.py:19
  22.5 2.2 copy-start.40
  28.4 18.3 %copy-start.34 = (bf16[1,256,1280]{2,1,0:T(8,128)(2,1)}, bf16[1,256,1280]{2,1,0:T(8,128)(2,1)S(1)}, u32[]{:S(2)}) copy-start(bf16[1,256,1280]{2,1,0:T(8,128)(2,1)S(1)} %collective-permute-done.6) | copy-start | bytes 1966084
  28.4 42.2 %collective-permute-start.1 = (bf16[1,256,1280]{2,1,0:T(8,128)(2,1)}, bf16[1,256,1280]{2,1,0:T(8,128)(2,1)}, u32[]{:S(2)}, u32[]{:S(2)}) collective-permute-start(bf16[1,256,1280]{2,1,0:T(8,128)(2,1)} %slice_bitcast_fusion.1), channel_id=1, source_target_pairs={{0,6},{8,14},{16,22},{24,30},{32,38},{40,46},{48,54},{56,62},{64,7... | collective-permute-start | bytes 1966088 | tf_op jit(solution)/shard_map/ppermute | solution.py:19
  42.5 4.3 %copy-start.36 = (bf16[1,256,1280]{2,1,0:T(8,128)(2,1)}, bf16[1,256,1280]{2,1,0:T(8,128)(2,1)S(1)}, u32[]{:S(2)}) copy-start(bf16[1,256,1280]{2,1,0:T(8,128)(2,1)S(1)} %collective-permute-done.5) | copy-start | bytes 1966084
  42.5 28.1 %collective-permute-start = (bf16[1,256,1280]{2,1,0:T(8,128)(2,1)}, bf16[1,256,1280]{2,1,0:T(8,128)(2,1)}, u32[]{:S(2)}, u32[]{:S(2)}) collective-permute-start(bf16[1,256,1280]{2,1,0:T(8,128)(2,1)} %slice_bitcast_fusion.1), channel_id=1, source_target_pairs={{0,7},{8,15},{16,23},{24,31},{32,39},{40,47},{48,55},{56,63},{64,7... | collective-permute-start | bytes 1966088 | tf_op jit(solution)/shard_map/ppermute | solution.py:19
  53.3 17.3 %copy-start.35 = (bf16[1,256,1280]{2,1,0:T(8,128)(2,1)S(1)}, bf16[1,256,1280]{2,1,0:T(8,128)(2,1)}, u32[]{:S(2)}) copy-start(bf16[1,256,1280]{2,1,0:T(8,128)(2,1)} %copy-done.34) | copy-start | bytes 1966084
  53.3 17.3 %copy-start.37 = (bf16[1,256,1280]{2,1,0:T(8,128)(2,1)S(1)}, bf16[1,256,1280]{2,1,0:T(8,128)(2,1)}, u32[]{:S(2)}) copy-start(bf16[1,256,1280]{2,1,0:T(8,128)(2,1)} %copy-done.36) | copy-start | bytes 1966084
  55.9 53.3 %collective-permute-start.9 = (bf16[1,1,256,1280]{3,2,1,0:T(8,128)(2,1)}, bf16[1,1,256,1280]{3,2,1,0:T(8,128)(2,1)}, u32[]{:S(2)}, u32[]{:S(2)}) collective-permute-start(bf16[1,1,256,1280]{3,2,1,0:T(8,128)(2,1)} %get-tuple-element.36), channel_id=1, source_target_pairs={{1,0},{2,1},{3,2},{4,3},{5,4},{6,5},{7,6},{9,8},{10,9},{11,10},{12... | collective-permute-start | bytes 1966088 | tf_op jit(solution)/shard_map/ppermute | solution.py:70
  57.2 14.6 %copy-start.13 = (bf16[1280,640]{1,0:T(8,128)(2,1)S(1)}, bf16[1280,640]{1,0:T(8,128)(2,1)}, u32[]{:S(2)}) copy-start(bf16[1280,640]{1,0:T(8,128)(2,1)} %param.13) | copy-start | bytes 4915204
  57.2 52.0 %collective-permute-start.10 = (bf16[1,1,256,1280]{3,2,1,0:T(8,128)(2,1)}, bf16[1,1,256,1280]{3,2,1,0:T(8,128)(2,1)}, u32[]{:S(2)}, u32[]{:S(2)}) collective-permute-start(bf16[1,1,256,1280]{3,2,1,0:T(8,128)(2,1)} %get-tuple-element.37), channel_id=1, source_target_pairs={{0,1},{1,2},{2,3},{3,4},{4,5},{5,6},{6,7},{8,9},{9,10},{10,11},{11... | collective-permute-start | bytes 1966088 | tf_op jit(solution)/shard_map/ppermute | solution.py:69
  71.5 1.1 copy-start.5
  99.1 4.9 %copy-start.20 = (bf16[2,256,640]{1,2,0:T(8,128)(2,1)S(1)}, bf16[2,256,640]{1,2,0:T(8,128)(2,1)}, u32[]{:S(2)}) copy-start(bf16[2,256,640]{1,2,0:T(8,128)(2,1)} %copy.66) | copy-start | bytes 1966084
  103.9 2.4 copy-start.1
  103.9 2.7 copy-start.39
  106.2 3.0 copy-start.32
  106.6 2.6 copy-start.23
  109.2 2.1 copy-start.42
  131.2 1.3 copy-start.19
  131.2 1.5 copy-start.21
  154.4 5.6 %copy-start.2 = (bf16[1,2,10,256,512]{4,3,2,1,0:T(8,128)(2,1)S(1)}, bf16[1,2,10,256,512]{4,3,2,1,0:T(8,128)(2,1)}, u32[]{:S(2)}) copy-start(bf16[1,2,10,256,512]{4,3,2,1,0:T(8,128)(2,1)} %fusion.79) | copy-start | bytes 15728644
  154.4 5.6 %copy-start.18 = (bf16[2,256,640]{1,2,0:T(8,128)(2,1)S(1)}, bf16[2,256,640]{1,2,0:T(8,128)(2,1)}, u32[]{:S(2)}) copy-start(bf16[2,256,640]{1,2,0:T(8,128)(2,1)} %copy.68) | copy-start | bytes 1966084
  161.0 1.1 copy-start.6
  161.0 1.8 copy-start.8
  161.2 11.9 %copy-start.10 = (f32[256,640]{0,1:T(8,128)}, f32[256,640]{0,1:T(8,128)S(1)}, u32[]{:S(2)}) copy-start(f32[256,640]{0,1:T(8,128)S(1)} %slice_reduce_fusion.1) | copy-start | bytes 1966084
  166.2 47.0 %collective-permute-start.17 = (bf16[1,256,1280]{1,2,0:T(8,128)(2,1)}, bf16[1,256,1280]{1,2,0:T(8,128)(2,1)}, u32[]{:S(2)}, u32[]{:S(2)}) collective-permute-start(bf16[1,256,1280]{1,2,0:T(8,128)(2,1)} %fusion.132), channel_id=1, source_target_pairs={{7,0},{15,8},{23,16},{31,24},{39,32},{47,40},{55,48},{63,56},{71,6... | collective-permute-start | bytes 1966088 | tf_op jit(solution)/shard_map/ppermute | solution.py:27
  167.5 47.0 %collective-permute-start.16 = (bf16[1,256,1280]{1,2,0:T(8,128)(2,1)}, bf16[1,256,1280]{1,2,0:T(8,128)(2,1)}, u32[]{:S(2)}, u32[]{:S(2)}) collective-permute-start(bf16[1,256,1280]{1,2,0:T(8,128)(2,1)} %fusion.132), channel_id=1, source_target_pairs={{6,0},{14,8},{22,16},{30,24},{38,32},{46,40},{54,48},{62,56},{70,6... | collective-permute-start | bytes 1966088 | tf_op jit(solution)/shard_map/ppermute | solution.py:27
  168.8 51.5 %collective-permute-start.15 = (bf16[1,256,1280]{1,2,0:T(8,128)(2,1)}, bf16[1,256,1280]{1,2,0:T(8,128)(2,1)}, u32[]{:S(2)}, u32[]{:S(2)}) collective-permute-start(bf16[1,256,1280]{1,2,0:T(8,128)(2,1)} %fusion.132), channel_id=1, source_target_pairs={{5,0},{13,8},{21,16},{29,24},{37,32},{45,40},{53,48},{61,56},{69,6... | collective-permute-start | bytes 1966088 | tf_op jit(solution)/shard_map/ppermute | solution.py:27
  170.1 57.0 %collective-permute-start.14 = (bf16[1,256,1280]{1,2,0:T(8,128)(2,1)}, bf16[1,256,1280]{1,2,0:T(8,128)(2,1)}, u32[]{:S(2)}, u32[]{:S(2)}) collective-permute-start(bf16[1,256,1280]{1,2,0:T(8,128)(2,1)} %fusion.132), channel_id=1, source_target_pairs={{4,0},{12,8},{20,16},{28,24},{36,32},{44,40},{52,48},{60,56},{68,6... | collective-permute-start | bytes 1966088 | tf_op jit(solution)/shard_map/ppermute | solution.py:27
  171.4 55.7 %collective-permute-start.13 = (bf16[1,256,1280]{1,2,0:T(8,128)(2,1)}, bf16[1,256,1280]{1,2,0:T(8,128)(2,1)}, u32[]{:S(2)}, u32[]{:S(2)}) collective-permute-start(bf16[1,256,1280]{1,2,0:T(8,128)(2,1)} %fusion.132), channel_id=1, source_target_pairs={{3,0},{11,8},{19,16},{27,24},{35,32},{43,40},{51,48},{59,56},{67,6... | collective-permute-start | bytes 1966088 | tf_op jit(solution)/shard_map/ppermute | solution.py:27
  184.3 2.6 copy-start.30
  184.3 5.3 %copy-start.25 = (f32[1280,640]{1,0:T(8,128)S(1)}, f32[1280,640]{1,0:T(8,128)}, u32[]{:S(2)}) copy-start(f32[1280,640]{1,0:T(8,128)} %convolution_bitcast_fusion.1) | copy-start | bytes 9830404
  187.0 2.7 copy-start.7
  187.0 2.7 copy-start.9
  187.0 2.6 copy-start.15
  189.6 26.4 %copy-start.29 = (bf16[1,2,256,1280]{3,2,1,0:T(8,128)(2,1)S(1)}, bf16[1,2,256,1280]{3,2,1,0:T(8,128)(2,1)}, u32[]{:S(2)}) copy-start(bf16[1,2,256,1280]{3,2,1,0:T(8,128)(2,1)} %copy-done.28) | copy-start | bytes 3932164
  189.6 26.4 %copy-start.33 = (bf16[2,10,64,256]{3,2,1,0:T(8,128)(2,1)S(1)}, bf16[2,10,64,256]{3,2,1,0:T(8,128)(2,1)}, u32[]{:S(2)}) copy-start(bf16[2,10,64,256]{3,2,1,0:T(8,128)(2,1)} %copy-done.32) | copy-start | bytes 1966084
  191.7 26.5 %copy-start.11 = (f32[256,640]{0,1:T(8,128)S(1)}, f32[256,640]{0,1:T(8,128)}, u32[]{:S(2)}) copy-start(f32[256,640]{0,1:T(8,128)} %copy-done.10) | copy-start | bytes 1966084
  213.2 16.9 %collective-permute-start.12 = (bf16[1,256,1280]{1,2,0:T(8,128)(2,1)}, bf16[1,256,1280]{1,2,0:T(8,128)(2,1)S(1)}, u32[]{:S(2)}, u32[]{:S(2)}) collective-permute-start(bf16[1,256,1280]{1,2,0:T(8,128)(2,1)} %fusion.132), channel_id=1, source_target_pairs={{2,0},{10,8},{18,16},{26,24},{34,32},{42,40},{50,48},{58,56},{66,6... | collective-permute-start | bytes 1966088 | tf_op jit(solution)/shard_map/ppermute | solution.py:27
  214.5 15.6 %collective-permute-start.11 = (bf16[1,256,1280]{1,2,0:T(8,128)(2,1)}, bf16[1,256,1280]{1,2,0:T(8,128)(2,1)S(1)}, u32[]{:S(2)}, u32[]{:S(2)}) collective-permute-start(bf16[1,256,1280]{1,2,0:T(8,128)(2,1)} %fusion.132), channel_id=1, source_target_pairs={{1,0},{9,8},{17,16},{25,24},{33,32},{41,40},{49,48},{57,56},{65,64... | collective-permute-start | bytes 1966088 | tf_op jit(solution)/shard_map/ppermute | solution.py:27
  216.0 2.2 copy-start.16
  257.0 6.5 %copy-start.31 = (bf16[2,10,64,256]{3,2,1,0:T(8,128)(2,1)S(1)}, bf16[2,10,64,256]{3,2,1,0:T(8,128)(2,1)}, u32[]{:S(2)}) copy-start(bf16[2,10,64,256]{3,2,1,0:T(8,128)(2,1)} %fusion.112) | copy-start | bytes 1966084
  257.0 6.5 %copy-start.41 = (bf16[1280,640]{1,0:T(8,128)(2,1)S(1)}, bf16[1280,640]{1,0:T(8,128)(2,1)}, u32[]{:S(2)}) copy-start(bf16[1280,640]{1,0:T(8,128)(2,1)} %param.12) | copy-start | bytes 4915204
  259.6 22.5 %collective-permute-start.7 = (bf16[1,1,256,1280]{3,2,1,0:T(8,128)(2,1)}, bf16[1,1,256,1280]{3,2,1,0:T(8,128)(2,1)}, u32[]{:S(2)}, u32[]{:S(2)}) collective-permute-start(bf16[1,1,256,1280]{3,2,1,0:T(8,128)(2,1)} %get-tuple-element.40), channel_id=1, source_target_pairs={{0,1},{1,2},{2,3},{3,4},{4,5},{5,6},{6,7},{8,9},{9,10},{10,11},{11... | collective-permute-start | bytes 1966088 | tf_op jit(solution)/shard_map/ppermute | solution.py:69
  261.8 2.9 copy-start.14
  261.8 2.9 copy-start.27
  261.8 20.3 %collective-permute-start.8 = (bf16[1,1,256,1280]{3,2,1,0:T(8,128)(2,1)}, bf16[1,1,256,1280]{3,2,1,0:T(8,128)(2,1)}, u32[]{:S(2)}, u32[]{:S(2)}) collective-permute-start(bf16[1,1,256,1280]{3,2,1,0:T(8,128)(2,1)} %get-tuple-element.41), channel_id=1, source_target_pairs={{1,0},{2,1},{3,2},{4,3},{5,4},{6,5},{7,6},{9,8},{10,9},{11,10},{12... | collective-permute-start | bytes 1966088 | tf_op jit(solution)/shard_map/ppermute | solution.py:70
  264.7 1.2 copy-start.26
  267.2 1.4 copy-start.17
  271.7 1.6 copy-start.4
  274.0 20.7 %all-to-all-start.1 = ((f32[16,8,10]{2,1,0:T(8,128)}), f32[16,8,10]{2,1,0:T(8,128)S(1)}, u32[]{:S(2)}, u32[]{:S(2)}) async-start(f32[16,8,10]{2,1,0:T(8,128)} %reshape.466), calls=%async_computation.2 | async-start | bytes 131072 | tf_op jit(solution)/shard_map/all_to_all | solution.py:49
  282.1 2.1 copy-start.24
  282.1 2.5 copy-start.43
  295.3 56.4 %all-to-all-start.2 = ((f32[8,1,10]{2,1,0:T(1,128)}), f32[8,1,10]{2,1,0:T(1,128)S(1)}, u32[]{:S(2)}, u32[]{:S(2)}) async-start(f32[8,1,10]{2,1,0:T(1,128)} %bitcast.74), calls=%async_computation.3 | async-start | bytes 8192 | tf_op jit(solution)/shard_map/all_to_all | solution.py:50
  351.7 12.4 %all-to-all-start = ((bf16[8,2,12800]{2,1,0:T(2,128)(2,1)}), bf16[8,2,12800]{2,1,0:T(2,128)(2,1)S(1)}, u32[]{:S(2)}, u32[]{:S(2)}) async-start(bf16[8,2,12800]{2,1,0:T(2,128)(2,1)} %reshape.478), calls=%async_computation.1 | async-start | bytes 819200 | tf_op jit(solution)/shard_map/all_to_all | solution.py:37
  (2 other events, 1.9 us)
Sparse Core Ops, SparseCore 0:
  257.1 91.0 reduce-scatter.1

commit v11 on v9

--- a/solution.py
+++ b/solution.py
@@ -219,12 +219,22 @@
     first_rows = first_rows + split_dot(first_sum[..., width:], w_value, dims)
     first_rows = jnp.where(is_owner, first_rows, jnp.zeros_like(first_rows))
     first_flat = normed_first.reshape(-1, normed_first.shape[-1])
-    extra_key = split_dot(key_first_grad.reshape(-1, width), first_flat, (((0,), (0,)), ((), ()))).T
-    extra_val = split_dot(val_first_grad.reshape(-1, width), first_flat, (((0,), (0,)), ((), ()))).T
     grad_normed = grad_normed.at[:, 0].add(first_rows)
-    grad_wq = gram_rows(normed, grad_queries)
-    grad_wk = gram_rows(normed, key_b) + extra_key
-    grad_wv = gram_rows(normed, val_b) + extra_val
+    own = jnp.concatenate([grad_queries, key_b, val_b], axis=-1).reshape(-1, 3 * width)
+    first_grads = jnp.concatenate([key_first_grad, val_first_grad], axis=-1).reshape(-1, 2 * width)
+    first_high = first_grads.astype(jnp.bfloat16)
+    first_low = (first_grads - first_high.astype(jnp.float32)).astype(jnp.bfloat16)
+    blank = jnp.zeros((first_grads.shape[0], width), jnp.bfloat16)
+    rhs = jnp.concatenate(
+        [
+            own,
+            jnp.concatenate([blank, first_high], axis=-1),
+            jnp.concatenate([blank, first_low], axis=-1),
+        ],
+        axis=0,
+    )
+    lhs = jnp.concatenate([normed.reshape(-1, normed.shape[-1]), first_flat, first_flat], axis=0)
+    grad_qkv = gram_rows(lhs, rhs)
     grad_gain = jnp.sum(grad_normed * x_hat, axis=(0, 1, 2))
     grad_hat = grad_normed * norm_gain
     grad_x = inv_std * (
@@ -233,9 +243,8 @@
         - x_hat * jnp.mean(grad_hat * x_hat, axis=-1, keepdims=True)
     )
     grad_input = (grad_hidden.astype(jnp.float32) + grad_x).astype(jnp.bfloat16)
-    grad_wq, grad_wk, grad_wv, grad_out = scatter_sum(
-        (grad_wq, grad_wk, grad_wv, grad_out), "batch", "tm"
-    )
+    grad_qkv, grad_out = scatter_sum((grad_qkv, grad_out), "batch", "tm")
+    grad_wq, grad_wk, grad_wv = jnp.split(grad_qkv, 3, axis=-1)
     grad_gain = gain_sum(grad_gain, "batch", "tm")
     return (output, grad_input, grad_wq, grad_wk, grad_wv, grad_out, grad_gain)
 

time: 355 us -> 355 us (level)
  local copies, waits for them, and re-layouts: 51.1 us -> 56.2 us
  matrix products: 83.1 us -> 78.4 us
    dot_general x8 -> x4, matrix products: 8.96 us -> 3.06 us  [split_dot(): lax.dot_general(part, narrow, dims, preferred_element_type=jnp.float32)]
    concatenate x0 -> x2, local copies, waits for them, and re-layouts: none -> 4.4 us  [on_device(): jnp.concatenate([grad_queries, key_b, val_b], axis=-1)]
    unnamed x83 -> x82, local copies, waits for them, and re-layouts: 10.4 us -> 12.8 us
    concatenate x4 -> x2, local copies, waits for them, and re-layouts: 17.3 us -> 15 us  [scatter_sum(): jnp.concatenate([p.astype(jnp.bfloat16).reshape(count, -1) for p in parts...]
    dot_general x4 -> x2, matrix products: 11.1 us -> 12.4 us  [gram_rows(): lax.dot_general(flat_left, flat_right, (((0,), (0,)), ((), ())), preferre...]
where the time goes in v11:
time: 355 us; the launch traced here: 349 us
  waiting for transfers between devices  82.6 us (23%)
  matrix products  78.4 us (22%)
  other arithmetic  61.7 us (17%)
  local copies, waits for them, and re-layouts  56.2 us (16%)
  starting transfers between devices  55.2 us (16%)
  between operations  15 us (4%)
    ppermute x7, waiting for transfers between devices, to_owner(): got = lax.ppermute(block.astype(jnp.bfloat16), axis, [(source, 0)])  52.1 us
    ppermute x7, waiting for transfers between devices, from_owner(): got = lax.ppermute(block, axis, [(0, target)])  20.7 us
    ppermute x7, starting transfers between devices, from_owner(): got = lax.ppermute(block, axis, [(0, target)])  16.5 us
    sub x1, other arithmetic, attend_back(): grad_prob - centre  16.3 us
    concatenate x2, local copies, waits for them, and re-layouts, scatter_sum(): jnp.concatenate([p.astype(jnp.bfloat16).reshape(count, -1) for p in parts...  15 us
    div x1, other arithmetic, attend(): prob_f32 = expd / jnp.sum(expd, axis=-1, keepdims=True)  14.3 us
    unnamed x82, local copies, waits for them, and re-layouts  12.8 us
    dot_general x2, matrix products, gram_rows(): lax.dot_general(flat_left, flat_right, (((0,), (0,)), ((), ())), preferre...  12.4 us
  transfers between devices with their start and end apart: 22, of which 8 were waited for; matrix products, arithmetic and copies ran while one was open for 25% of the time, Pallas kernels for 0%

profile of v11, /device:TPU:0, one launch (start us, length us, event | category | flops | bytes accessed | tf_op | source)
XLA Modules:
  0.0 349.0 jit_solution(9245467214271708234)
XLA Ops:
  7.2 2.1 slice_bitcast_fusion.1
  9.4 3.5 %collective-permute-start.6 = (bf16[1,256,1280]{2,1,0:T(8,128)(2,1)}, bf16[1,256,1280]{2,1,0:T(8,128)(2,1)S(1)}, u32[]{:S(2)}, u32[]{:S(2)}) collective-permute-start(bf16[1,256,1280]{2,1,0:T(8,128)(2,1)} %slice_bitcast_fusion.1), channel_id=1, source_target_pairs={{0,1},{8,9},{16,17},{24,25},{32,33},{40,41},{48,49},{56,57},{64,65... | collective-permute-start | bytes 1966088 | tf_op jit(solution)/shard_map/ppermute | solution.py:19
  12.9 2.2 collective-permute-start.5
  15.2 2.1 collective-permute-start.4
  17.3 2.1 collective-permute-start.3
  19.4 2.2 collective-permute-start.2
  23.3 2.0 fusion.121
  25.3 2.0 fusion.124
  28.3 2.1 collective-permute-start.1
  30.4 11.9 %collective-permute-done.5 = bf16[1,256,1280]{2,1,0:T(8,128)(2,1)S(1)} collective-permute-done((bf16[1,256,1280]{2,1,0:T(8,128)(2,1)}, bf16[1,256,1280]{2,1,0:T(8,128)(2,1)S(1)}, u32[]{:S(2)}, u32[]{:S(2)}) %collective-permute-start.5) | collective-permute-done | bytes 655392 | tf_op jit(solution)/shard_map/ppermute | solution.py:19
  42.3 2.2 collective-permute-start
  44.5 2.1 fusion.118
  46.6 2.2 copy.62
  48.8 2.2 copy.63
  51.0 2.2 copy.60
  53.2 2.6 fusion.179
  55.7 1.3 collective-permute-start.9
  57.0 5.6 %collective-permute-start.10 = (bf16[1,1,256,1280]{3,2,1,0:T(8,128)(2,1)}, bf16[1,1,256,1280]{3,2,1,0:T(8,128)(2,1)}, u32[]{:S(2)}, u32[]{:S(2)}) collective-permute-start(bf16[1,1,256,1280]{3,2,1,0:T(8,128)(2,1)} %get-tuple-element.29), channel_id=1, source_target_pairs={{0,1},{1,2},{2,3},{3,4},{4,5},{5,6},{6,7},{8,9},{9,10},{10,11},{11... | collective-permute-start | bytes 1966088 | tf_op jit(solution)/shard_map/ppermute | solution.py:69
  62.6 7.8 %collective-permute-done.1 = bf16[1,256,1280]{2,1,0:T(8,128)(2,1)} collective-permute-done((bf16[1,256,1280]{2,1,0:T(8,128)(2,1)}, bf16[1,256,1280]{2,1,0:T(8,128)(2,1)}, u32[]{:S(2)}, u32[]{:S(2)}) %collective-permute-start.1) | collective-permute-done | bytes 655392 | tf_op jit(solution)/shard_map/ppermute | solution.py:19
  73.6 1.4 convolution_convert_fusion.2
  79.0 6.7 %fusion.155 = f32[2,10,256,512]{3,2,1,0:T(8,128)} fusion(bf16[2,256,10,64]{1,3,2,0:T(8,128)(2,1)} %bitcast.253, bf16[1,2,256,10,64]{2,4,3,1,0:T(8,128)(2,1)S(1)} %broadcast_in_dim.15, bf16[1,2,256,10,64]{2,4,3,1,0:T(8,128)(2,1)} %bitcast.257), kind=kOutput, calls=%fused_computation.164 | convolution fusion | flops 338165760 | bytes 12451840 | tf_op jit(solution)/shard_map/lfshd,lfthd->lfhst/dot_general | solution.py:99
  85.7 14.3 %fusion.25 = f32[2,10,256,512]{3,2,1,0:T(8,128)} fusion(f32[2,10,256,512]{3,2,1,0:T(8,128)} %fusion.155), kind=kOutput, calls=%fused_computation.31 | output fusion | flops 10497022 | bytes 20971520 | tf_op jit(solution)/shard_map/div | solution.py:107
  100.0 4.8 %convert_bitcast_fusion = bf16[1,2,10,256,512]{4,3,2,1,0:T(8,128)(2,1)S(1)} fusion(f32[2,10,256,512]{3,2,1,0:T(8,128)} %fusion.25), kind=kLoop, calls=%fused_computation.29 | loop fusion | flops 2621440 | bytes 15728640 | tf_op jit(solution)/shard_map/convert_element_type | solution.py:108
  104.9 1.7 fusion.130
  107.5 2.6 fusion.91
  110.2 2.0 fusion.140
  112.2 10.1 %fusion.72 = bf16[1,2,256,1280]{3,2,1,0:T(8,128)(2,1)S(1)} fusion(bf16[1280,3,1280]{2,0,1:T(8,128)(2,1)} %param.16, bf16[1,2,256,1,1280]{4,2,3,1,0:T(8,128)(2,1)S(1)} %get-tuple-element.27, bf16[1,2,256,1,1280]{4,2,3,1,0:T(8,128)(2,1)S(1)} %bitcast.263, bf16[1,2,256,1,1280]{4,2,3,1,0:T(8,128)(2,1)S(1)} %get-tuple-element.26, ...), kind=kOutput, calls=%fused_computation.77 | convolution fusion | flops 5044961280 | bytes 17694720 | tf_op jit(solution)/shard_map/lfsjo,cjo->lfsc/dot_general | solution.py:192
  123.4 2.1 fusion.127
  125.4 2.2 copy.66
  127.7 3.7 %fusion.20 = f32[2,10,64,512]{3,2,1,0:T(8,128)S(1)} fusion(bf16[2,256,10,64]{1,3,2,0:T(8,128)(2,1)} %bitcast.255, bf16[1,2,10,256,512]{4,3,2,1,0:T(8,128)(2,1)} %copy-done.1), kind=kOutput, calls=%fused_computation.25 | convolution fusion | flops 335544320 | bytes 8519680 | tf_op jit(solution)/shard_map/lfhst,lfshd->lfthd/dot_general | solution.py:131
  133.4 2.2 fusion.61
  135.6 5.4 %fusion.145 = f32[2,10,256,512]{3,2,1,0:T(8,128)} fusion(bf16[2,256,10,64]{1,3,2,0:T(8,128)(2,1)S(1)} %bitcast.256, bf16[2,256,10,64]{1,3,2,0:T(8,128)(2,1)S(1)} %broadcast_in_dim.16, bf16[2,256,10,64]{1,3,2,0:T(8,128)(2,1)S(1)} %bitcast.260), kind=kOutput, calls=%fused_computation.148 | convolution fusion | flops 338165760 | bytes 12451840 | tf_op jit(solution)/shard_map/lfshd,lfthd->lfhst/dot_general | solution.py:118
  141.0 16.3 %fusion.99 = bf16[1,2,10,256,512]{4,3,2,1,0:T(8,128)(2,1)} fusion(f32[2,10,256,512]{3,2,1,0:T(8,128)} %fusion.25, f32[2,10,256,512]{3,2,1,0:T(8,128)} %fusion.145), kind=kOutput, calls=%fused_computation.104 | output fusion | flops 13112831 | bytes 26214400 | tf_op jit(solution)/shard_map/sub | solution.py:122
  157.3 5.6 %fusion.133 = bf16[2,10,64,256]{3,2,1,0:T(8,128)(2,1)} fusion(bf16[1,2,10,256,512]{4,3,2,1,0:T(8,128)(2,1)} %fusion.99, bf16[1,2,256,10,64]{2,4,3,1,0:T(8,128)(2,1)} %copy-done.18, bf16[1,2,256,10,64]{2,4,3,1,0:T(8,128)(2,1)} %bitcast.258), kind=kOutput, calls=%fused_computation.129 | convolution fusion | flops 338493440 | bytes 7208960 | tf_op jit(solution)/shard_map/lfhst,lfthd->lfshd/dot_general | solution.py:124
  167.3 2.2 copy.81
  169.4 2.2 copy.73
  171.7 4.0 %concatenate.92 = bf16[16,8,6400]{2,1,0:T(8,128)(2,1)} reshape(bf16[640,1280]{1,0:T(8,128)(2,1)} %fusion.61) | data formatting | bytes 3276800 | tf_op jit(solution)/shard_map/concatenate | solution.py:34
  175.6 1.8 copy.71
  178.4 2.2 copy.80
  180.5 2.2 copy.72
  182.7 10.2 %convolution_convert_fusion = bf16[1280,1920]{1,0:T(8,128)(2,1)} fusion(bf16[256,1280]{0,1:T(8,128)(2,1)} %fusion.149, bf16[256,1280]{0,1:T(8,128)(2,1)} %get-tuple-element.24, bf16[512,640]{0,1:T(8,128)(2,1)} %copy.73, bf16[512,640]{0,1:T(8,128)(2,1)} %copy.72, bf16[512,640]{0,1:T(8,128)(2,1)} %bitcast.274, bf16[256,1280]{1,0:T(8,128)(2,1)} %copy-done.28, ...), kind=kOutput, calls=%fused_computation.19 | convolution fusion | flops 5074944000 | bytes 10158080 | tf_op jit(solution)/shard_map/dot_general | solution.py:147
  192.9 11.0 %concatenate.91 = bf16[16,8,19200]{2,1,0:T(8,128)(2,1)} reshape(bf16[1280,1920]{1,0:T(8,128)(2,1)} %convolution_convert_fusion) | data formatting | bytes 9830400 | tf_op jit(solution)/shard_map/concatenate | solution.py:34
  204.0 6.2 %pad_maximum_fusion = bf16[16,8,25600]{2,1,0:T(8,128)(2,1)} fusion(bf16[16,8,6400]{2,1,0:T(8,128)(2,1)} %concatenate.92, bf16[16,8,19200]{2,1,0:T(8,128)(2,1)} %concatenate.91), kind=kLoop, calls=%fused_computation.20 | loop fusion | flops 13107200 | bytes 13107200 | tf_op jit(solution)/shard_map/concatenate | solution.py:34
  210.2 1.3 collective-permute-start.17
  211.5 1.3 collective-permute-start.16
  212.8 1.3 collective-permute-start.15
  214.1 1.3 collective-permute-start.14
  215.4 1.5 collective-permute-start.13
  216.9 3.0 fusion.109
  221.2 35.9 %collective-permute-done.17 = bf16[1,256,1280]{1,2,0:T(8,128)(2,1)S(1)} collective-permute-done((bf16[1,256,1280]{1,2,0:T(8,128)(2,1)}, bf16[1,256,1280]{1,2,0:T(8,128)(2,1)S(1)}, u32[]{:S(2)}, u32[]{:S(2)}) %collective-permute-start.17) | collective-permute-done | bytes 655392 | tf_op jit(solution)/shard_map/ppermute | solution.py:27
  257.1 1.3 collective-permute-start.12
  258.4 1.3 collective-permute-start.11
  263.4 5.4 %collective-permute-start.7 = (bf16[1,1,256,1280]{3,2,1,0:T(8,128)(2,1)}, bf16[1,1,256,1280]{3,2,1,0:T(8,128)(2,1)}, u32[]{:S(2)}, u32[]{:S(2)}) collective-permute-start(bf16[1,1,256,1280]{3,2,1,0:T(8,128)(2,1)} %get-tuple-element.32), channel_id=1, source_target_pairs={{0,1},{1,2},{2,3},{3,4},{4,5},{5,6},{6,7},{8,9},{9,10},{10,11},{11... | collective-permute-start | bytes 1966088 | tf_op jit(solution)/shard_map/ppermute | solution.py:69
  268.9 16.2 %collective-permute-done.14 = bf16[1,256,1280]{1,2,0:T(8,128)(2,1)S(1)} collective-permute-done((bf16[1,256,1280]{1,2,0:T(8,128)(2,1)}, bf16[1,256,1280]{1,2,0:T(8,128)(2,1)S(1)}, u32[]{:S(2)}, u32[]{:S(2)}) %collective-permute-start.14) | collective-permute-done | bytes 655392 | tf_op jit(solution)/shard_map/ppermute | solution.py:27
  292.4 8.3 %all-to-all-start.1 = ((f32[16,8,10]{2,1,0:T(8,128)}), f32[16,8,10]{2,1,0:T(8,128)S(1)}, u32[]{:S(2)}, u32[]{:S(2)}) async-start(f32[16,8,10]{2,1,0:T(8,128)} %reshape.416), calls=%async_computation.2 | async-start | bytes 131072 | tf_op jit(solution)/shard_map/all_to_all | solution.py:49
  300.7 3.0 collective-permute-done.8
  303.7 1.9 fusion.142
  305.7 10.3 %fusion.69 = bf16[1,2,256,1280]{3,2,1,0:T(8,128)(2,1)} fusion(bf16[1280,3,1280]{2,0,1:T(8,128)(2,1)} %param.16, bf16[1,2,256,1,1280]{4,2,1,3,0:T(8,128)(2,1)S(1)} %get-tuple-element.31, bf16[1,2,256,1,1280]{4,2,1,3,0:T(8,128)(2,1)S(1)} %bitcast.264, bf16[1,2,256,1,1280]{4,2,1,3,0:T(8,128)(2,1)S(1)} %get-tuple-element.30, ...), kind=kOutput, calls=%fused_computation.76 | convolution fusion | flops 5039063040 | bytes 16384000 | tf_op jit(solution)/shard_map/lfsjc,cjo->lfso/dot_general | solution.py:187
  316.6 3.3 all-to-all-start.2
  319.9 3.5 %reduce-scatter.2.cloned.1.call-done = bf16[1,8,25600]{2,1,0:T(8,128)(2,1)} async-done(((bf16[16,8,25600]{2,1,0:T(8,128)(2,1)}), bf16[1,8,25600]{2,1,0:T(8,128)(2,1)}) %reduce-scatter.2.cloned.1.call-update) | async-done | bytes 409616 | tf_op jit(solution)/shard_map/reduce_scatter | solution.py:36
  324.0 1.9 reduce.18
  327.0 4.3 %all-to-all-start = ((bf16[8,2,12800]{2,1,0:T(2,128)(2,1)}), bf16[8,2,12800]{2,1,0:T(2,128)(2,1)S(1)}, u32[]{:S(2)}, u32[]{:S(2)}) async-start(bf16[8,2,12800]{2,1,0:T(2,128)(2,1)} %reshape.425), calls=%async_computation.1 | async-start | bytes 819200 | tf_op jit(solution)/shard_map/all_to_all | solution.py:37
  331.2 4.2 %fusion.85 = bf16[1,2,256,1280]{3,2,1,0:T(8,128)(2,1)} fusion(bf16[1,2,256,1280]{3,2,1,0:T(8,128)(2,1)S(1)} %copy-done.3, bf16[1,2,256,1280]{3,2,1,0:T(8,128)(2,1)} %copy-done.23, f32[1,2,256,1280]{3,2,1,0:T(8,128)} %copy-done.4, f32[2,256]{1,0:T(2,128)S(1)} %get-tuple-element.39, f32[2,256]{1,0:T(2,128)S(1)} %get-tuple-element.40, f32[1280]{0:T(1024)S(1)} %copy-done.33, ...), kind=kLoop, calls=%fused_computation.90 | loop fusion | flops 7208960 | bytes 6566912 | tf_op jit(solution)/shard_map/convert_element_type | solution.py:245
  336.0 3.3 all-to-all-done
  (141 shorter events, 36.9 us)
Async XLA Ops:
  7.2 37.4 %copy-start = (bf16[1280,640]{1,0:T(8,128)(2,1)S(1)}, bf16[1280,640]{1,0:T(8,128)(2,1)}, u32[]{:S(2)}) copy-start(bf16[1280,640]{1,0:T(8,128)(2,1)} %param.14) | copy-start | bytes 4915204
  7.2 14.4 %copy-start.3 = (bf16[1,2,256,1280]{3,2,1,0:T(8,128)(2,1)S(1)}, bf16[1,2,256,1280]{3,2,1,0:T(8,128)(2,1)}, u32[]{:S(2)}) copy-start(bf16[1,2,256,1280]{3,2,1,0:T(8,128)(2,1)} %param.10) | copy-start | bytes 3932164
  7.2 15.2 %copy-start.33 = (f32[1280]{0:T(1024)S(1)}, f32[1280]{0:T(1024)}, u32[]{:S(2)}) copy-start(f32[1280]{0:T(1024)} %param.11) | copy-start | bytes 15364
  7.2 316.3 %reduce-scatter.2.cloned.1.call-start = ((), (), s32[]{:S(2)}) async-start(), calls=%async_computation.4 | async-start | bytes 6963200 | tf_op jit(solution)/shard_map/reduce_scatter | solution.py:36
  9.4 18.9 %collective-permute-start.6 = (bf16[1,256,1280]{2,1,0:T(8,128)(2,1)}, bf16[1,256,1280]{2,1,0:T(8,128)(2,1)S(1)}, u32[]{:S(2)}, u32[]{:S(2)}) collective-permute-start(bf16[1,256,1280]{2,1,0:T(8,128)(2,1)} %slice_bitcast_fusion.1), channel_id=1, source_target_pairs={{0,1},{8,9},{16,17},{24,25},{32,33},{40,41},{48,49},{56,57},{64,65... | collective-permute-start | bytes 1966088 | tf_op jit(solution)/shard_map/ppermute | solution.py:19
  12.9 29.4 %collective-permute-start.5 = (bf16[1,256,1280]{2,1,0:T(8,128)(2,1)}, bf16[1,256,1280]{2,1,0:T(8,128)(2,1)S(1)}, u32[]{:S(2)}, u32[]{:S(2)}) collective-permute-start(bf16[1,256,1280]{2,1,0:T(8,128)(2,1)} %slice_bitcast_fusion.1), channel_id=1, source_target_pairs={{0,2},{8,10},{16,18},{24,26},{32,34},{40,42},{48,50},{56,58},{64,6... | collective-permute-start | bytes 1966088 | tf_op jit(solution)/shard_map/ppermute | solution.py:19
  15.2 40.6 %collective-permute-start.4 = (bf16[1,256,1280]{2,1,0:T(8,128)(2,1)}, bf16[1,256,1280]{2,1,0:T(8,128)(2,1)}, u32[]{:S(2)}, u32[]{:S(2)}) collective-permute-start(bf16[1,256,1280]{2,1,0:T(8,128)(2,1)} %slice_bitcast_fusion.1), channel_id=1, source_target_pairs={{0,3},{8,11},{16,19},{24,27},{32,35},{40,43},{48,51},{56,59},{64,6... | collective-permute-start | bytes 1966088 | tf_op jit(solution)/shard_map/ppermute | solution.py:19
  17.3 39.7 %collective-permute-start.3 = (bf16[1,256,1280]{2,1,0:T(8,128)(2,1)}, bf16[1,256,1280]{2,1,0:T(8,128)(2,1)}, u32[]{:S(2)}, u32[]{:S(2)}) collective-permute-start(bf16[1,256,1280]{2,1,0:T(8,128)(2,1)} %slice_bitcast_fusion.1), channel_id=1, source_target_pairs={{0,4},{8,12},{16,20},{24,28},{32,36},{40,44},{48,52},{56,60},{64,6... | collective-permute-start | bytes 1966088 | tf_op jit(solution)/shard_map/ppermute | solution.py:19
  19.4 43.2 %collective-permute-start.2 = (bf16[1,256,1280]{2,1,0:T(8,128)(2,1)}, bf16[1,256,1280]{2,1,0:T(8,128)(2,1)}, u32[]{:S(2)}, u32[]{:S(2)}) collective-permute-start(bf16[1,256,1280]{2,1,0:T(8,128)(2,1)} %slice_bitcast_fusion.1), channel_id=1, source_target_pairs={{0,5},{8,13},{16,21},{24,29},{32,37},{40,45},{48,53},{56,61},{64,6... | collective-permute-start | bytes 1966088 | tf_op jit(solution)/shard_map/ppermute | solution.py:19
  21.8 1.4 copy-start.35
  23.3 21.2 %copy-start.22 = (bf16[1,2,256,1280]{3,2,1,0:T(8,128)(2,1)}, bf16[1,2,256,1280]{3,2,1,0:T(8,128)(2,1)S(1)}, u32[]{:S(2)}) copy-start(bf16[1,2,256,1280]{3,2,1,0:T(8,128)(2,1)S(1)} %fusion.80) | copy-start | bytes 3932164
  23.3 2.0 copy-start.5
  28.3 18.3 %copy-start.29 = (bf16[1,256,1280]{2,1,0:T(8,128)(2,1)}, bf16[1,256,1280]{2,1,0:T(8,128)(2,1)S(1)}, u32[]{:S(2)}) copy-start(bf16[1,256,1280]{2,1,0:T(8,128)(2,1)S(1)} %collective-permute-done.6) | copy-start | bytes 1966084
  28.3 42.2 %collective-permute-start.1 = (bf16[1,256,1280]{2,1,0:T(8,128)(2,1)}, bf16[1,256,1280]{2,1,0:T(8,128)(2,1)}, u32[]{:S(2)}, u32[]{:S(2)}) collective-permute-start(bf16[1,256,1280]{2,1,0:T(8,128)(2,1)} %slice_bitcast_fusion.1), channel_id=1, source_target_pairs={{0,6},{8,14},{16,22},{24,30},{32,38},{40,46},{48,54},{56,62},{64,7... | collective-permute-start | bytes 1966088 | tf_op jit(solution)/shard_map/ppermute | solution.py:19
  42.3 4.3 %copy-start.31 = (bf16[1,256,1280]{2,1,0:T(8,128)(2,1)}, bf16[1,256,1280]{2,1,0:T(8,128)(2,1)S(1)}, u32[]{:S(2)}) copy-start(bf16[1,256,1280]{2,1,0:T(8,128)(2,1)S(1)} %collective-permute-done.5) | copy-start | bytes 1966084
  42.3 28.1 %collective-permute-start = (bf16[1,256,1280]{2,1,0:T(8,128)(2,1)}, bf16[1,256,1280]{2,1,0:T(8,128)(2,1)}, u32[]{:S(2)}, u32[]{:S(2)}) collective-permute-start(bf16[1,256,1280]{2,1,0:T(8,128)(2,1)} %slice_bitcast_fusion.1), channel_id=1, source_target_pairs={{0,7},{8,15},{16,23},{24,31},{32,39},{40,47},{48,55},{56,63},{64,7... | collective-permute-start | bytes 1966088 | tf_op jit(solution)/shard_map/ppermute | solution.py:19
  53.1 17.3 %copy-start.30 = (bf16[1,256,1280]{2,1,0:T(8,128)(2,1)S(1)}, bf16[1,256,1280]{2,1,0:T(8,128)(2,1)}, u32[]{:S(2)}) copy-start(bf16[1,256,1280]{2,1,0:T(8,128)(2,1)} %copy-done.29) | copy-start | bytes 1966084
  53.2 17.3 %copy-start.32 = (bf16[1,256,1280]{2,1,0:T(8,128)(2,1)S(1)}, bf16[1,256,1280]{2,1,0:T(8,128)(2,1)}, u32[]{:S(2)}) copy-start(bf16[1,256,1280]{2,1,0:T(8,128)(2,1)} %copy-done.31) | copy-start | bytes 1966084
  55.7 54.4 %collective-permute-start.9 = (bf16[1,1,256,1280]{3,2,1,0:T(8,128)(2,1)}, bf16[1,1,256,1280]{3,2,1,0:T(8,128)(2,1)}, u32[]{:S(2)}, u32[]{:S(2)}) collective-permute-start(bf16[1,1,256,1280]{3,2,1,0:T(8,128)(2,1)} %get-tuple-element.28), channel_id=1, source_target_pairs={{1,0},{2,1},{3,2},{4,3},{5,4},{6,5},{7,6},{9,8},{10,9},{11,10},{12... | collective-permute-start | bytes 1966088 | tf_op jit(solution)/shard_map/ppermute | solution.py:70
  57.0 53.1 %collective-permute-start.10 = (bf16[1,1,256,1280]{3,2,1,0:T(8,128)(2,1)}, bf16[1,1,256,1280]{3,2,1,0:T(8,128)(2,1)}, u32[]{:S(2)}, u32[]{:S(2)}) collective-permute-start(bf16[1,1,256,1280]{3,2,1,0:T(8,128)(2,1)} %get-tuple-element.29), channel_id=1, source_target_pairs={{0,1},{1,2},{2,3},{3,4},{4,5},{5,6},{6,7},{8,9},{9,10},{10,11},{11... | collective-permute-start | bytes 1966088 | tf_op jit(solution)/shard_map/ppermute | solution.py:69
  71.4 1.4 copy-start.6
  72.8 0.8 copy-start.28
  78.1 0.9 copy-start.18
  100.0 4.9 %copy-start.14 = (bf16[2,256,640]{1,2,0:T(8,128)(2,1)S(1)}, bf16[2,256,640]{1,2,0:T(8,128)(2,1)}, u32[]{:S(2)}) copy-start(bf16[2,256,640]{1,2,0:T(8,128)(2,1)} %copy.60) | copy-start | bytes 1966084
  104.8 2.4 copy-start.1
  104.9 2.7 copy-start.34
  107.1 3.0 copy-start.26
  107.5 2.6 copy-start.19
  110.1 2.1 copy-start.36
  122.3 1.1 copy-start.23
  131.4 2.0 copy-start.24
  131.4 2.0 copy-start.27
  133.4 2.3 copy-start.13
  133.4 2.3 copy-start.15
  157.3 5.6 %copy-start.2 = (bf16[1,2,10,256,512]{4,3,2,1,0:T(8,128)(2,1)S(1)}, bf16[1,2,10,256,512]{4,3,2,1,0:T(8,128)(2,1)}, u32[]{:S(2)}) copy-start(bf16[1,2,10,256,512]{4,3,2,1,0:T(8,128)(2,1)} %fusion.99) | copy-start | bytes 15728644
  157.3 5.6 %copy-start.12 = (bf16[2,256,640]{1,2,0:T(8,128)(2,1)S(1)}, bf16[2,256,640]{1,2,0:T(8,128)(2,1)}, u32[]{:S(2)}) copy-start(bf16[2,256,640]{1,2,0:T(8,128)(2,1)} %copy.62) | copy-start | bytes 1966084
  163.9 1.1 copy-start.8
  164.1 2.0 copy-start.10
  210.2 46.9 %collective-permute-start.17 = (bf16[1,256,1280]{1,2,0:T(8,128)(2,1)}, bf16[1,256,1280]{1,2,0:T(8,128)(2,1)S(1)}, u32[]{:S(2)}, u32[]{:S(2)}) collective-permute-start(bf16[1,256,1280]{1,2,0:T(8,128)(2,1)} %get-tuple-element.25), channel_id=1, source_target_pairs={{7,0},{15,8},{23,16},{31,24},{39,32},{47,40},{55,48},{63,56},{71,6... | collective-permute-start | bytes 1966088 | tf_op jit(solution)/shard_map/ppermute | solution.py:27
  211.5 46.9 %collective-permute-start.16 = (bf16[1,256,1280]{1,2,0:T(8,128)(2,1)}, bf16[1,256,1280]{1,2,0:T(8,128)(2,1)S(1)}, u32[]{:S(2)}, u32[]{:S(2)}) collective-permute-start(bf16[1,256,1280]{1,2,0:T(8,128)(2,1)} %get-tuple-element.25), channel_id=1, source_target_pairs={{6,0},{14,8},{22,16},{30,24},{38,32},{46,40},{54,48},{62,56},{70,6... | collective-permute-start | bytes 1966088 | tf_op jit(solution)/shard_map/ppermute | solution.py:27
  212.8 50.7 %collective-permute-start.15 = (bf16[1,256,1280]{1,2,0:T(8,128)(2,1)}, bf16[1,256,1280]{1,2,0:T(8,128)(2,1)S(1)}, u32[]{:S(2)}, u32[]{:S(2)}) collective-permute-start(bf16[1,256,1280]{1,2,0:T(8,128)(2,1)} %get-tuple-element.25), channel_id=1, source_target_pairs={{5,0},{13,8},{21,16},{29,24},{37,32},{45,40},{53,48},{61,56},{69,6... | collective-permute-start | bytes 1966088 | tf_op jit(solution)/shard_map/ppermute | solution.py:27
  214.1 71.0 %collective-permute-start.14 = (bf16[1,256,1280]{1,2,0:T(8,128)(2,1)}, bf16[1,256,1280]{1,2,0:T(8,128)(2,1)S(1)}, u32[]{:S(2)}, u32[]{:S(2)}) collective-permute-start(bf16[1,256,1280]{1,2,0:T(8,128)(2,1)} %get-tuple-element.25), channel_id=1, source_target_pairs={{4,0},{12,8},{20,16},{28,24},{36,32},{44,40},{52,48},{60,56},{68,6... | collective-permute-start | bytes 1966088 | tf_op jit(solution)/shard_map/ppermute | solution.py:27
  215.4 71.0 %collective-permute-start.13 = (bf16[1,256,1280]{1,2,0:T(8,128)(2,1)}, bf16[1,256,1280]{1,2,0:T(8,128)(2,1)S(1)}, u32[]{:S(2)}, u32[]{:S(2)}) collective-permute-start(bf16[1,256,1280]{1,2,0:T(8,128)(2,1)} %get-tuple-element.25), channel_id=1, source_target_pairs={{3,0},{11,8},{19,16},{27,24},{35,32},{43,40},{51,48},{59,56},{67,6... | collective-permute-start | bytes 1966088 | tf_op jit(solution)/shard_map/ppermute | solution.py:27
  216.9 3.0 copy-start.7
  216.9 3.0 copy-start.17
  219.9 37.2 %copy-start.25 = (bf16[1,256,1280]{1,2,0:T(8,128)(2,1)S(1)}, bf16[1,256,1280]{1,2,0:T(8,128)(2,1)}, u32[]{:S(2)}) copy-start(bf16[1,256,1280]{1,2,0:T(8,128)(2,1)} %get-tuple-element.25) | copy-start | bytes 1966084
  219.9 39.8 %copy-start.16 = (bf16[1,2,256,640]{3,2,1,0:T(8,128)(2,1)S(1)}, bf16[1,2,256,640]{3,2,1,0:T(8,128)(2,1)}, u32[]{:S(2)}) copy-start(bf16[1,2,256,640]{3,2,1,0:T(8,128)(2,1)} %copy.81) | copy-start | bytes 1966084
  257.1 29.3 %collective-permute-start.12 = (bf16[1,256,1280]{1,2,0:T(8,128)(2,1)S(1)}, bf16[1,256,1280]{1,2,0:T(8,128)(2,1)S(1)}, u32[]{:S(2)}, u32[]{:S(2)}) collective-permute-start(bf16[1,256,1280]{1,2,0:T(8,128)(2,1)S(1)} %copy-done.25), channel_id=1, source_target_pairs={{2,0},{10,8},{18,16},{26,24},{34,32},{42,40},{50,48},{58,56},{66,6... | collective-permute-start | bytes 1966088 | tf_op jit(solution)/shard_map/ppermute | solution.py:27
  258.4 28.0 %collective-permute-start.11 = (bf16[1,256,1280]{1,2,0:T(8,128)(2,1)S(1)}, bf16[1,256,1280]{1,2,0:T(8,128)(2,1)S(1)}, u32[]{:S(2)}, u32[]{:S(2)}) collective-permute-start(bf16[1,256,1280]{1,2,0:T(8,128)(2,1)S(1)} %copy-done.25), channel_id=1, source_target_pairs={{1,0},{9,8},{17,16},{25,24},{33,32},{41,40},{49,48},{57,56},{65,64... | collective-permute-start | bytes 1966088 | tf_op jit(solution)/shard_map/ppermute | solution.py:27
  261.0 1.3 copy-start.20
  261.2 25.2 %copy-start.9 = (f32[256,640]{0,1:T(8,128)S(1)}, f32[256,640]{0,1:T(8,128)}, u32[]{:S(2)}) copy-start(f32[256,640]{0,1:T(8,128)} %slice_reduce_fusion) | copy-start | bytes 1966084
  261.2 25.2 %copy-start.11 = (f32[256,640]{0,1:T(8,128)S(1)}, f32[256,640]{0,1:T(8,128)}, u32[]{:S(2)}) copy-start(f32[256,640]{0,1:T(8,128)} %copy-done.10) | copy-start | bytes 1966084
  263.4 37.3 %collective-permute-start.7 = (bf16[1,1,256,1280]{3,2,1,0:T(8,128)(2,1)}, bf16[1,1,256,1280]{3,2,1,0:T(8,128)(2,1)}, u32[]{:S(2)}, u32[]{:S(2)}) collective-permute-start(bf16[1,1,256,1280]{3,2,1,0:T(8,128)(2,1)} %get-tuple-element.32), channel_id=1, source_target_pairs={{0,1},{1,2},{2,3},{3,4},{4,5},{5,6},{6,7},{8,9},{9,10},{10,11},{11... | collective-permute-start | bytes 1966088 | tf_op jit(solution)/shard_map/ppermute | solution.py:69
  285.1 18.7 %collective-permute-start.8 = (bf16[1,1,256,1280]{3,2,1,0:T(8,128)(2,1)}, bf16[1,1,256,1280]{3,2,1,0:T(8,128)(2,1)}, u32[]{:S(2)}, u32[]{:S(2)}) collective-permute-start(bf16[1,1,256,1280]{3,2,1,0:T(8,128)(2,1)} %get-tuple-element.33), channel_id=1, source_target_pairs={{1,0},{2,1},{3,2},{4,3},{5,4},{6,5},{7,6},{9,8},{10,9},{11,10},{12... | collective-permute-start | bytes 1966088 | tf_op jit(solution)/shard_map/ppermute | solution.py:70
  290.1 1.6 copy-start.4
  292.4 23.6 %all-to-all-start.1 = ((f32[16,8,10]{2,1,0:T(8,128)}), f32[16,8,10]{2,1,0:T(8,128)S(1)}, u32[]{:S(2)}, u32[]{:S(2)}) async-start(f32[16,8,10]{2,1,0:T(8,128)} %reshape.416), calls=%async_computation.2 | async-start | bytes 131072 | tf_op jit(solution)/shard_map/all_to_all | solution.py:49
  300.7 5.0 %copy-start.21 = (bf16[1,2,256,1280]{3,2,1,0:T(8,128)(2,1)S(1)}, bf16[1,2,256,1280]{3,2,1,0:T(8,128)(2,1)}, u32[]{:S(2)}) copy-start(bf16[1,2,256,1280]{3,2,1,0:T(8,128)(2,1)} %get-tuple-element.37) | copy-start | bytes 3932164
  300.7 5.0 %copy-start.37 = (bf16[1,2,256,1280]{3,2,1,0:T(8,128)(2,1)S(1)}, bf16[1,2,256,1280]{3,2,1,0:T(8,128)(2,1)}, u32[]{:S(2)}) copy-start(bf16[1,2,256,1280]{3,2,1,0:T(8,128)(2,1)} %copy-done.36) | copy-start | bytes 3932164
  316.6 10.3 %all-to-all-start.2 = ((f32[8,1,10]{2,1,0:T(1,128)}), f32[8,1,10]{2,1,0:T(1,128)S(1)}, u32[]{:S(2)}, u32[]{:S(2)}) async-start(f32[8,1,10]{2,1,0:T(1,128)} %bitcast.74), calls=%async_computation.3 | async-start | bytes 8192 | tf_op jit(solution)/shard_map/all_to_all | solution.py:50
  327.0 12.3 %all-to-all-start = ((bf16[8,2,12800]{2,1,0:T(2,128)(2,1)}), bf16[8,2,12800]{2,1,0:T(2,128)(2,1)S(1)}, u32[]{:S(2)}, u32[]{:S(2)}) async-start(bf16[8,2,12800]{2,1,0:T(2,128)(2,1)} %reshape.425), calls=%async_computation.1 | async-start | bytes 819200 | tf_op jit(solution)/shard_map/all_to_all | solution.py:37
Sparse Core Ops, SparseCore 0:
  210.3 113.1 reduce-scatter.1
